TPU v7x, 128 devices: a whole 4x4x4 slice. The times are simulated.
128 devices in a mesh: req: 32 (over x, z, core), tensor: 4 (over y).
Axes of the slice: x: 4, y: 4, z: 4, core: 2. Of those that a mesh axis runs over, the one named last changes fastest.
Arguments:
- hidden_in: bfloat16 [32768, 2048], P('req', 'tensor'), may hold values from -6 to 6
- segment: int32 [32768], P('req'), may hold values from 0 to 15, never falling along the last dimension, each value on 1 to 4096 neighbouring positions
- w_query: bfloat16 [2048, 1024], P(None, 'tensor'), may hold values from -0.125 to 0.125
- w_key: bfloat16 [2048, 1024], P(None, 'tensor'), may hold values from -0.125 to 0.125
- w_value: bfloat16 [2048, 2048], P(None, 'tensor'), may hold values from -0.125 to 0.125
- w_outgate: bfloat16 [2048, 2048], P(None, 'tensor'), may hold values from -0.125 to 0.125
- w_gate_down: bfloat16 [2048, 16], replicated, may hold values from -0.125 to 0.125
- w_gate_up: bfloat16 [16, 1024], P(None, 'tensor'), may hold values from -1.5 to 1.5
- gate_bias: float32 [1024], P('tensor'), may hold values from -2 to 8
- norm_gain: float32 [512], replicated, may hold values from 0.5 to 1.5
- w_out: bfloat16 [2048, 2048], P('tensor'), may hold values from -0.125 to 0.125
Outputs:
- mixed: bfloat16 [32768, 2048], P('req', 'tensor')
Inputs may be any that keep to these rules, and one draw needn't show every extreme that they name: segment never falls along the tokens; each prompt covers 1 to 4096 consecutive tokens and one covers exactly 4096.
All inputs are finite; a program needn't handle non-finite values.
Results may differ from a plain program's by a relative error of at most 0.014.
Values may be sent and summed in bfloat16 or wider, within the bound.
No kernel may reach another device: no remote copies, remote signals or barrier semaphores. Data moves between devices by JAX's collectives and lax.ppermute only.
A program may use at most 128 MiB of HBM per device.

v0:
```python
import jax
import jax.numpy as jnp
from jax import lax
from jax.sharding import PartitionSpec as P

GROUP = 64


def carried_in(shard, axis, combine, identity):
    devices, index = (lax.axis_size(axis), lax.axis_index(axis))
    everything = jax.tree.map(
        lambda part, kind: lax.all_gather(part.astype(kind), axis),
        shard,
        jax.tree.map(lambda a: jnp.bfloat16 if a.dtype == jnp.float32 else a.dtype, shard),
    )
    start = jax.tree.map(
        lambda part, zero: jnp.broadcast_to(jnp.asarray(zero, part.dtype), part.shape),
        shard,
        identity,
    )

    def lap(k, before):
        reached = k < index
        new = combine(
            before, jax.tree.map(lambda part, own: part[k].astype(own.dtype), everything, shard)
        )
        return jax.tree.map(lambda a, b: jnp.where(reached, a, b), new, before)

    return lax.fori_loop(0, devices, lap, start)


def combine(earlier, later):
    first_a, last_a, decay_a, state_a = earlier
    first_b, last_b, decay_b, state_b = later
    linked = ((first_b == last_a) | (last_a == 0.0) | (first_b == 0.0)).astype(jnp.float32)
    decay_new = decay_b * decay_a * linked
    state_new = state_b + (linked * decay_b)[:, None] * state_a
    first_new = jnp.where(first_a > 0.0, first_a, first_b)
    last_new = jnp.where(last_b > 0.0, last_b, last_a)
    return (first_new, last_new, decay_new, state_new)


def body(
    hidden_in,
    segment,
    w_query,
    w_key,
    w_value,
    w_outgate,
    w_gate_down,
    w_gate_up,
    gate_bias,
    norm_gain,
    w_out,
):
    tok_rows = hidden_in.shape[0]
    key_width = w_query.shape[1]
    value_width = w_value.shape[1]
    weights = (w_query, w_key, w_value, w_outgate, w_gate_down)
    piece = lax.all_gather(hidden_in, "tensor", axis=1, tiled=True)
    query_sum, key_sum, value_sum, outgate, low = tuple(
        (jnp.dot(piece, weight, preferred_element_type=jnp.float32) for weight in weights)
    )
    query = query_sum.astype(jnp.bfloat16)
    key = key_sum.astype(jnp.bfloat16)
    value = value_sum.astype(jnp.bfloat16)
    pre_gate = (
        jnp.dot(low, w_gate_up.astype(jnp.float32), precision=lax.Precision.HIGHEST) + gate_bias
    )
    logdecay = jax.nn.log_sigmoid(pre_gate) / 16.0
    blocks = tok_rows // GROUP
    starts = jnp.concatenate(
        [jnp.zeros((1,), jnp.int32), (segment[1:] != segment[:-1]).astype(jnp.int32)]
    )
    live_device = (jnp.cumsum(starts) == 0).astype(jnp.float32)
    seg_blocks = segment.reshape(blocks, GROUP)
    live_blocks = (jnp.cumsum(starts.reshape(blocks, GROUP), axis=1) == 0).astype(jnp.float32)
    cumul = jnp.cumsum(logdecay.reshape(blocks, GROUP, key_width), axis=1)
    block_totals = cumul[:, -1, :]
    before = jnp.cumsum(block_totals, axis=0) - block_totals
    device_cumul = (cumul + before[:, None, :]).reshape(tok_rows, key_width)
    positions = jnp.arange(GROUP)
    causal = positions[None, :] <= positions[:, None]
    middle_row = GROUP // 2

    def block_step(state, inputs):
        q_block, k_block, v_block, c_block, s_block, l_block = inputs
        q_float = q_block.astype(jnp.float32)
        k_float = k_block.astype(jnp.float32)
        v_float = v_block.astype(jnp.float32)
        inter = (
            jnp.dot(q_float * jnp.exp(c_block), state, precision=lax.Precision.HIGHEST)
            * l_block[:, None]
        )
        allowed = causal & (s_block[:, None] == s_block[None, :])
        centre = c_block[middle_row]
        q_scaled = q_float * jnp.exp(c_block - centre[None, :])
        k_scaled = k_float * jnp.exp(centre[None, :] - c_block)
        raw_scores = jnp.dot(q_scaled, k_scaled.T, precision=lax.Precision.HIGHEST)
        scores = jnp.where(allowed, raw_scores, 0.0)
        intra = jnp.dot(scores, v_float, precision=lax.Precision.HIGHEST)
        last_cumul = c_block[-1]
        same_last = (s_block == s_block[-1]).astype(jnp.float32)
        k_decayed = k_float * jnp.exp(last_cumul[None, :] - c_block) * same_last[:, None]
        state = l_block[-1] * jnp.exp(last_cumul)[:, None] * state + jnp.dot(
            k_decayed.T, v_float, precision=lax.Precision.HIGHEST
        )
        return (state, inter + intra)

    zero_state = jnp.zeros((key_width, value_width), jnp.float32)
    final_state, local_out = lax.scan(
        block_step,
        zero_state,
        (
            query.reshape(blocks, GROUP, key_width),
            key.reshape(blocks, GROUP, key_width),
            value.reshape(blocks, GROUP, value_width),
            cumul,
            seg_blocks,
            live_blocks,
        ),
    )
    local_out = local_out.reshape(tok_rows, value_width)
    first_id = (segment[0] + 1).astype(jnp.float32)
    last_id = (segment[-1] + 1).astype(jnp.float32)
    decay_device = jnp.exp(device_cumul[-1]) * live_device[-1]
    mine = (first_id, last_id, decay_device, final_state)
    identity = (
        jnp.zeros((), jnp.float32),
        jnp.zeros((), jnp.float32),
        jnp.ones((key_width,), jnp.float32),
        jnp.zeros((key_width, value_width), jnp.float32),
    )
    incoming = carried_in(mine, "req", combine, identity)
    first_in, last_in, decay_in, state_in = incoming
    linked = ((first_id == last_in) | (last_in == 0.0)).astype(jnp.float32)
    carried = jnp.dot(
        query.astype(jnp.float32) * jnp.exp(device_cumul), state_in, precision=lax.Precision.HIGHEST
    )
    attn = (local_out + carried * (live_device * linked)[:, None]) * key_width ** (-0.5)
    normed = attn * lax.rsqrt(jnp.mean(attn * attn, axis=-1, keepdims=True) + 1e-05) * norm_gain
    gated = (normed * jax.nn.silu(outgate)).astype(jnp.bfloat16)
    head_term = jnp.dot(gated, w_out, preferred_element_type=jnp.float32)
    return lax.psum_scatter(
        head_term.astype(jnp.bfloat16), "tensor", scatter_dimension=1, tiled=True
    )


def solution(mesh):
    in_specs = (
        P("req", "tensor"),
        P("req"),
        P(None, "tensor"),
        P(None, "tensor"),
        P(None, "tensor"),
        P(None, "tensor"),
        P(),
        P(None, "tensor"),
        P("tensor"),
        P(),
        P("tensor", None),
    )
    out_specs = P("req", "tensor")
    return jax.shard_map(body, mesh=mesh, in_specs=in_specs, out_specs=out_specs, check_vma=False)
```

profile of v0, /device:TPU:2, one launch (start us, length us, event | category | flops | bytes accessed | tf_op | source)
XLA Modules:
  0.0 538.8 jit_solution(2485547177089798620)
XLA Ops:
  9.3 50.3 %all-gather.5.cloned.1.call-done = bf16[1024,2048]{1,0:T(8,128)(2,1)} async-done(((bf16[1024,512]{1,0:T(8,128)(2,1)}), bf16[1024,2048]{1,0:T(8,128)(2,1)}) %all-gather.5.cloned.1.call-update) | async-done | bytes 4194320 | tf_op jit(solution)/shard_map/all_gather | solution.py:60
  59.6 3.4 fusion.69
  64.2 1.6 fusion.49
  67.4 3.4 convolution_convert_fusion.1
  70.8 2.0 convolution_convert_fusion.3
  72.8 133.2 %while.29 = (s32[]{:T(128)}, f32[256,512]{1,0:T(8,128)S(1)}, f32[16,64,512]{2,1,0:T(8,128)}, f32[16,64]{1,0:T(8,128)S(1)}, f32[16,64,256]{2,0,1:T(8,128)}, /*ind...) while((s32[]{:T(128)}, f32[256,512]{1,0:T(8,128)S(1)}, ...), condition=%wide.region_3.4_spmd.clone, body=%wide.region_2.3_spmd.clone.sunk | while | flops 239878528 | bytes 2676648 | solution.py:111
  79.7 1.4 convolution_add_fusion.3
  88.0 1.4 convolution_add_fusion.3
  96.3 1.4 convolution_add_fusion.3
  104.7 1.4 convolution_add_fusion.3
  113.0 1.4 convolution_add_fusion.3
  121.3 1.4 convolution_add_fusion.3
  129.6 1.4 convolution_add_fusion.3
  138.0 1.4 convolution_add_fusion.3
  146.3 1.4 convolution_add_fusion.3
  154.6 1.4 convolution_add_fusion.3
  162.9 1.4 convolution_add_fusion.3
  171.3 1.4 convolution_add_fusion.3
  179.6 1.4 convolution_add_fusion.3
  187.9 1.4 convolution_add_fusion.3
  196.2 1.4 convolution_add_fusion.3
  204.5 1.4 convolution_add_fusion.3
  206.8 1.4 fusion.66
  210.3 1.4 dynamic-update-slice
  211.7 56.1 %all-reduce.2 = (bf16[32]{0:T(256)(128)(2,1)S(1)}, bf16[32]{0:T(256)(128)(2,1)S(1)}) all-reduce(bf16[32]{0:T(256)(128)(2,1)S(1)} %dynamic-update-slice, bf16[32]{0:T(256)(128)(2,1)S(1)} %dynamic-update-slice.1), channel_id=1, replica_groups=mesh['req'=32,'tensor'=4] {'req'}, use_global_device_ids=true, to_apply=%add | all-reduce | flops 64 | bytes 256
  271.1 1.3 broadcast_add_fusion
  274.0 33.8 %all-gather.1 = bf16[32,1,256]{2,1,0:T(2,128)(2,1)S(1)} all-gather(bf16[1,1,256]{2,1,0:T(2,128)(2,1)S(1)} %fusion.62), channel_id=1, replica_groups=mesh['req'=32,'tensor'=4] {'req'}, dimensions={0}, use_global_device_ids=true | all-gather | bytes 16896 | tf_op jit(solution)/shard_map/all_gather | solution.py:12
  307.8 2.9 copy.41
  310.7 160.3 %while.30 = (s32[]{:T(128)}, f32[]{:T(128)}, f32[256,512]{1,0:T(8,128)S(1)}, s32[]{:T(128)}, bf16[32]{0:T(256)(128)(2,1)S(1)}, /*index=5*/bf16[32,256,512]{2,1,0...) while((s32[]{:T(128)}, f32[]{:T(128)}, ...), condition=%wide.region_8.9_spmd.clone, body=%wide.region_7.8_spmd.clone.sunk | while | flops 655885 | bytes 1313502 | solution.py:29
  471.2 5.6 %multiply_reduce_fusion = (f32[1024]{0:T(1024)S(1)}, f32[1024,512]{0,1:T(8,128)}) fusion(f32[1024,512]{0,1:T(8,128)} %copy.41, f32[1024]{0:T(1024)S(1)} %select_bitcast_fusion, f32[256,512]{1,0:T(8,128)S(1)} %get-tuple-element.200, f32[1024,256]{1,0:T(8,128)} %bitcast.116, bf16[1024,256]{1,0:T(8,128)(2,1)S(1)} %bitcast.119), kind=kOutput, calls=%fused_computation.59 | convolution fusion | flops 1613757440 | bytes 6299648 | tf_op jit(solution)/shard_map/dot_general | solution.py:137
  476.8 10.3 %convolution_convert_fusion = bf16[1024,2048]{1,0:T(8,128)(2,1)} fusion(bf16[512,2048]{1,0:T(8,128)(2,1)S(1)} %copy-done, f32[1024,512]{0,1:T(8,128)} %get-tuple-element.340, f32[512]{0:T(512)S(1)} %copy-done.7, f32[1024]{0:T(1024)S(1)} %rsqrt_multiply_fusion, bf16[1024,2048]{1,0:T(8,128)(2,1)} %all-gather.5.cloned.1.call-done, bf16[2048,512]{1,0:T(8,128)(2,1)} %param.20), kind=kOutput, calls=%fused_computation.56 | convolution fusion | flops 4301258752 | bytes 14686208 | tf_op jit(solution)/shard_map/dot_general | solution.py:143
  487.1 45.2 %reduce-scatter.2.cloned.1.call-done = bf16[1024,512]{1,0:T(8,128)(2,1)} async-done(((bf16[1024,2048]{1,0:T(8,128)(2,1)}), bf16[1024,512]{1,0:T(8,128)(2,1)}) %reduce-scatter.2.cloned.1.call-update) | async-done | bytes 1048592 | tf_op jit(solution)/shard_map/reduce_scatter | solution.py:144
  (425 shorter events, 198.3 us)
Async XLA Ops:
  6.5 470.2 %copy-start = (bf16[512,2048]{1,0:T(8,128)(2,1)S(1)}, bf16[512,2048]{1,0:T(8,128)(2,1)}, u32[]{:S(2)}) copy-start(bf16[512,2048]{1,0:T(8,128)(2,1)} %param.25) | copy-start | bytes 6291460
  6.5 53.1 %all-gather.5.cloned.1.call-start = ((), (), s32[]{:S(2)}) async-start(), calls=%async_computation.1 | async-start | bytes 5242880 | tf_op jit(solution)/shard_map/all_gather | solution.py:60
  7.3 303.5 %all-gather.7.cloned.1.call-start = ((), (), s32[]{:S(2)}) async-start(), calls=%async_computation.3 | async-start | bytes 8650752 | tf_op jit(solution)/shard_map/all_gather | solution.py:12
  9.3 53.7 %copy-start.6 = (bf16[16,256]{1,0:T(8,128)(2,1)S(1)}, bf16[16,256]{1,0:T(8,128)(2,1)}, u32[]{:S(2)}) copy-start(bf16[16,256]{1,0:T(8,128)(2,1)} %param.22) | copy-start | bytes 24580
  9.3 53.7 %copy-start.8 = (f32[256]{0:T(256)S(1)}, f32[256]{0:T(256)}, u32[]{:S(2)}) copy-start(f32[256]{0:T(256)} %param.23) | copy-start | bytes 3076
  63.0 2.8 copy-start.1
  63.0 2.8 copy-start.4
  65.8 1.6 copy-start.3
  67.4 3.4 copy-start.5
  72.8 136.1 %copy-start.9 = (u32[128]{0:T(128)S(1)}, u32[128]{0:T(128)}, u32[]{:S(2)}) copy-start(u32[128]{0:T(128)} %constant.99) | copy-start | bytes 1540
  206.7 325.6 %reduce-scatter.2.cloned.1.call-start = ((), (), s32[]{:S(2)}) async-start(), calls=%async_computation.2 | async-start | bytes 5242880 | tf_op jit(solution)/shard_map/reduce_scatter | solution.py:144
  273.0 1.0 copy-start.2
  471.2 5.6 %copy-start.7 = (f32[512]{0:T(512)S(1)}, f32[512]{0:T(512)}, u32[]{:S(2)}) copy-start(f32[512]{0:T(512)} %param.24) | copy-start | bytes 6148
Sparse Core Ops, SparseCore 0:
  9.0 50.5 all-gather.4
  206.8 53.3 all-gather.6
  487.2 45.0 reduce-scatter.1
where the time goes:
time: 546 us; the launch traced here: 539 us
  matrix products  99.8 us (18%)
  waiting for transfers between devices  96.3 us (18%)
  local copies, waits for them, and re-layouts  90.8 us (17%)
  blocking collectives  89.9 us (16%)
  loops' own time  84.8 us (16%)
  other arithmetic  62.7 us (11%)
  between operations  14.6 us (3%)
    another operation x1, loops' own time, carried_in(): return lax.fori_loop(0, devices, lap, start)  83.2 us
    unnamed x1, blocking collectives  56.1 us
    all_gather x1, waiting for transfers between devices, body(): piece = lax.all_gather(hidden_in, 'tensor', axis=1, tiled=True)  50.3 us
    reduce_scatter x1, waiting for transfers between devices, body(): lax.psum_scatter(head_term.astype(jnp.bfloat16), 'tensor', scatter_dimens...  45.2 us
    dynamic_slice x64, local copies, waits for them, and re-layouts, lap(): part[k].astype(own.dtype)  41.7 us
    select_n x32, other arithmetic, lap(): return jax.tree.map(lambda a, b: jnp.where(reached, a, b), new, before)  34.9 us
    all_gather x1, blocking collectives, carried_in(): lax.all_gather(part.astype(kind), axis)  33.8 us
    dot_general x16, matrix products, block_step(): jnp.dot(k_decayed.T, v_float, precision=lax.Precision.HIGHEST)  22.6 us
  transfers between devices with their start and end apart: 3, of which 2 were waited for; matrix products, arithmetic and copies ran while one was open for 3% of the time, Pallas kernels for 0%

commit v1 on v0

v1 whole, which is shorter than its diff:
```python
import jax
import jax.numpy as jnp
from jax import lax
from jax.sharding import PartitionSpec as P

GROUP = 64
SEG_MOST = 4096
HIGHEST = lax.Precision.HIGHEST


def shifted(x, axis, shift, devices):
    pairs = [(i, i + shift) for i in range(devices - shift)]
    return lax.ppermute(x, axis, pairs)


def body(
    hidden_in,
    segment,
    w_query,
    w_key,
    w_value,
    w_outgate,
    w_gate_down,
    w_gate_up,
    gate_bias,
    norm_gain,
    w_out,
):
    tok_rows = hidden_in.shape[0]
    key_width = w_query.shape[1]
    value_width = w_value.shape[1]
    weights = (w_query, w_key, w_value, w_outgate, w_gate_down)
    piece = lax.all_gather(hidden_in, "tensor", axis=1, tiled=True)
    query_sum, key_sum, value_sum, outgate, low = tuple(
        (jnp.dot(piece, weight, preferred_element_type=jnp.float32) for weight in weights)
    )
    query = query_sum.astype(jnp.bfloat16)
    key = key_sum.astype(jnp.bfloat16)
    value = value_sum.astype(jnp.bfloat16)
    pre_gate = jnp.dot(low, w_gate_up.astype(jnp.float32), precision=HIGHEST) + gate_bias
    logdecay = jax.nn.log_sigmoid(pre_gate) / 16.0

    blocks = tok_rows // GROUP
    starts = jnp.concatenate(
        [jnp.zeros((1,), jnp.int32), (segment[1:] != segment[:-1]).astype(jnp.int32)]
    )
    live_device = (jnp.cumsum(starts) == 0).astype(jnp.float32)
    seg_blocks = segment.reshape(blocks, GROUP)
    live_blocks = (jnp.cumsum(starts.reshape(blocks, GROUP), axis=1) == 0).astype(jnp.float32)
    cumul = jnp.cumsum(logdecay.reshape(blocks, GROUP, key_width), axis=1)
    block_totals = cumul[:, -1, :]
    before = jnp.cumsum(block_totals, axis=0) - block_totals
    device_cumul = (cumul + before[:, None, :]).reshape(tok_rows, key_width)

    q_float = query.astype(jnp.float32).reshape(blocks, GROUP, key_width)
    k_float = key.astype(jnp.float32).reshape(blocks, GROUP, key_width)
    v_float = value.astype(jnp.float32).reshape(blocks, GROUP, value_width)

    positions = jnp.arange(GROUP)
    causal = positions[None, :] <= positions[:, None]
    centre = cumul[:, GROUP // 2, :]
    q_scaled = q_float * jnp.exp(cumul - centre[:, None, :])
    k_scaled = k_float * jnp.exp(centre[:, None, :] - cumul)
    raw_scores = jnp.einsum("ncd,nsd->ncs", q_scaled, k_scaled, precision=HIGHEST)
    allowed = causal[None] & (seg_blocks[:, :, None] == seg_blocks[:, None, :])
    scores = jnp.where(allowed, raw_scores, 0.0)
    intra = jnp.einsum("ncs,nsv->ncv", scores, v_float, precision=HIGHEST)

    same_last = (seg_blocks == seg_blocks[:, -1:]).astype(jnp.float32)
    k_decayed = k_float * jnp.exp(block_totals[:, None, :] - cumul) * same_last[:, :, None]
    chunk_states = jnp.einsum("ncd,ncv->ndv", k_decayed, v_float, precision=HIGHEST)
    chunk_decay = jnp.exp(block_totals) * live_blocks[:, -1:]

    entering = [jnp.zeros((key_width, value_width), jnp.float32)]
    for n in range(blocks):
        entering.append(chunk_decay[n][:, None] * entering[-1] + chunk_states[n])
    final_state = entering[-1]
    entering = jnp.stack(entering[:-1])
    inter = (
        jnp.einsum("ncd,ndv->ncv", q_float * jnp.exp(cumul), entering, precision=HIGHEST)
        * live_blocks[:, :, None]
    )
    local_out = (intra + inter).reshape(tok_rows, value_width)

    devices = lax.axis_size("req")
    window = min(devices - 1, -(-SEG_MOST // tok_rows))
    first_id = (segment[0] + 1).astype(jnp.float32)
    last_id = (segment[-1] + 1).astype(jnp.float32)
    decay_device = jnp.exp(device_cumul[-1]) * live_device[-1]
    ids = jnp.stack([first_id, last_id])
    sent_state = final_state.astype(jnp.bfloat16)
    got = [
        (
            shifted(ids, "req", j, devices),
            shifted(decay_device, "req", j, devices),
            shifted(sent_state, "req", j, devices).astype(jnp.float32),
        )
        for j in range(1, window + 1)
    ]
    ids_far, _, state_in = got[-1]
    for j in range(window - 1, 0, -1):
        ids_j, decay_j, state_j = got[j - 1]
        link = (ids_j[0] == ids_far[1]).astype(jnp.float32)
        state_in = state_j + (link * decay_j)[:, None] * state_in
        ids_far = ids_j
    linked = (first_id == ids_far[1]).astype(jnp.float32)
    carried = jnp.dot(
        query.astype(jnp.float32) * jnp.exp(device_cumul), state_in, precision=HIGHEST
    )
    attn = (local_out + carried * (live_device * linked)[:, None]) * key_width ** (-0.5)
    normed = attn * lax.rsqrt(jnp.mean(attn * attn, axis=-1, keepdims=True) + 1e-05) * norm_gain
    gated = (normed * jax.nn.silu(outgate)).astype(jnp.bfloat16)
    head_term = jnp.dot(gated, w_out, preferred_element_type=jnp.float32)
    return lax.psum_scatter(
        head_term.astype(jnp.bfloat16), "tensor", scatter_dimension=1, tiled=True
    )


def solution(mesh):
    in_specs = (
        P("req", "tensor"),
        P("req"),
        P(None, "tensor"),
        P(None, "tensor"),
        P(None, "tensor"),
        P(None, "tensor"),
        P(),
        P(None, "tensor"),
        P("tensor"),
        P(),
        P("tensor", None),
    )
    out_specs = P("req", "tensor")
    return jax.shard_map(body, mesh=mesh, in_specs=in_specs, out_specs=out_specs, check_vma=False)
```

time: 546 us -> 195 us (0.36); the launches traced: 539 us -> 193 us
  blocking collectives: 89.9 us -> 0 us
  loops' own time: 84.8 us -> 0 us
  local copies, waits for them, and re-layouts: 90.8 us -> 10.6 us
  matrix products: 99.8 us -> 40.4 us
  other arithmetic: 62.7 us -> 7.99 us
  starting transfers between devices: 0.08 us -> 36.8 us
  waiting for transfers between devices: 96.3 us -> 77 us
  between operations: 14.6 us -> 20.6 us
    another operation x2 -> x0, loops' own time: 84.8 us -> none  [the longest x1 83.2 us: carried_in(): return lax.fori_loop(0, devices, lap, start)]
    dynamic_slice x112 -> x0, local copies, waits for them, and re-layouts: 59.6 us -> none  [the longest x64 41.7 us: lap(): part[k].astype(own.dtype)]
    dot_general x65 -> x5, matrix products: 73.8 us -> 15.7 us  [the longest x1 6.94 us: body(): jnp.einsum('ncd,ndv->ncv', q_float * jnp.exp(cumul), entering, precision=...]
    unnamed x1 -> x0, blocking collectives: 56.1 us -> none
    ppermute x0 -> x11, starting transfers between devices: none -> 36.8 us  [shifted(): return lax.ppermute(x, axis, pairs)]
    select_n x32 -> x0, other arithmetic: 34.9 us -> none  [lap(): return jax.tree.map(lambda a, b: jnp.where(reached, a, b), new, before)]
    all_gather x1 -> x0, blocking collectives: 33.8 us -> none  [carried_in(): lax.all_gather(part.astype(kind), axis)]
    all_gather x1, waiting for transfers between devices: 50.3 us -> 22.6 us  [body(): piece = lax.all_gather(hidden_in, 'tensor', axis=1, tiled=True)]
  transfers between devices with their start and end apart: 3 -> 13, of which waited for: 2 -> 4; matrix products, arithmetic and copies ran while one was open for 3% -> 13% of each run, Pallas kernels for 0% -> 0%
where the time goes in v1:
time: 195 us; the launch traced here: 193 us
  waiting for transfers between devices  77 us (39%)
  matrix products  40.4 us (21%)
  starting transfers between devices  36.8 us (19%)
  between operations  20.6 us (11%)
  local copies, waits for them, and re-layouts  10.6 us (5%)
  other arithmetic  7.99 us (4%)
    reduce_scatter x1, waiting for transfers between devices, body(): lax.psum_scatter(head_term.astype(jnp.bfloat16), 'tensor', scatter_dimens...  44.4 us
    ppermute x11, starting transfers between devices, shifted(): return lax.ppermute(x, axis, pairs)  36.8 us
    all_gather x1, waiting for transfers between devices, body(): piece = lax.all_gather(hidden_in, 'tensor', axis=1, tiled=True)  22.6 us
    dot_general x1, matrix products, body(): head_term = jnp.dot(gated, w_out, preferred_element_type=jnp.float32)  10.3 us
    ppermute x11, waiting for transfers between devices, shifted(): return lax.ppermute(x, axis, pairs)  9.26 us
    dot_general x4, matrix products, body(): jnp.dot(piece, weight, preferred_element_type=jnp.float32)  8.35 us
    dot_general x1, matrix products, body(): jnp.einsum('ncd,ndv->ncv', q_float * jnp.exp(cumul), entering, precision=...  6.94 us
    dot_general x1, matrix products, body(): jnp.dot(query.astype(jnp.float32) * jnp.exp(device_cumul), state_in, prec...  6.02 us
  transfers between devices with their start and end apart: 13, of which 4 were waited for; matrix products, arithmetic and copies ran while one was open for 13% of the time, Pallas kernels for 0%

profile of v1, /device:TPU:2, one launch (start us, length us, event | category | flops | bytes accessed | tf_op | source)
XLA Modules:
  0.0 193.4 jit_solution(17621551754248473050)
XLA Ops:
  7.3 1.3 fusion.60
  10.0 1.9 collective-permute-start.1
  11.9 5.5 %collective-permute-start.5 = (f32[2]{0:T(128)S(1)}, f32[2]{0:T(128)S(1)}, u32[]{:S(2)}, u32[]{:S(2)}) collective-permute-start(f32[2]{0:T(128)S(1)} %pad_maximum_fusion), channel_id=1, source_target_pairs={{0,12},{4,16},{8,20},{12,24},{16,28},{20,32},{24,36},{28,40},{32,4... | collective-permute-start | bytes 32 | tf_op jit(solution)/shard_map/ppermute | solution.py:13
  17.4 3.7 %collective-permute-start.8 = (f32[2]{0:T(128)S(1)}, f32[2]{0:T(128)S(1)}, u32[]{:S(2)}, u32[]{:S(2)}) collective-permute-start(f32[2]{0:T(128)S(1)} %pad_maximum_fusion), channel_id=1, source_target_pairs={{0,16},{4,20},{8,24},{12,28},{16,32},{20,36},{24,40},{28,44},{32,4... | collective-permute-start | bytes 32 | tf_op jit(solution)/shard_map/ppermute | solution.py:13
  21.1 3.2 %collective-permute-start.2 = (f32[2]{0:T(128)S(1)}, f32[2]{0:T(128)S(1)}, u32[]{:S(2)}, u32[]{:S(2)}) collective-permute-start(f32[2]{0:T(128)S(1)} %pad_maximum_fusion), channel_id=1, source_target_pairs={{0,8},{4,12},{8,16},{12,20},{16,24},{20,28},{24,32},{28,36},{32,40... | collective-permute-start | bytes 32 | tf_op jit(solution)/shard_map/ppermute | solution.py:13
  27.3 0.9 broadcast_dynamic-update-slice_fusion
  37.0 22.6 %all-gather.2.cloned.1.call-done = bf16[1024,2048]{1,0:T(8,128)(2,1)} async-done(((bf16[1024,512]{1,0:T(8,128)(2,1)}), bf16[1024,2048]{1,0:T(8,128)(2,1)}) %all-gather.2.cloned.1.call-update) | async-done | bytes 4194320 | tf_op jit(solution)/shard_map/all_gather | solution.py:33
  59.6 3.5 %fusion.66 = f32[1024,16]{0,1:T(8,128)S(1)} fusion(bf16[1024,2048]{1,0:T(8,128)(2,1)} %all-gather.2.cloned.1.call-done, bf16[2048,16]{0,1:T(8,128)(2,1)} %param.17), kind=kOutput, calls=%fused_computation.141 | convolution fusion | flops 67108864 | bytes 4325376 | tf_op jit(solution)/shard_map/dot_general | solution.py:35
  63.1 2.0 %fusion.3 = f32[1024,256]{1,0:T(8,128)S(1)} fusion(f32[1024,16]{0,1:T(8,128)S(1)} %fusion.66, bf16[16,256]{1,0:T(8,128)(2,1)} %param.18, f32[256]{0:T(256)} %param.19), kind=kOutput, calls=%fused_computation.14 | convolution fusion | flops 52953088 | bytes 1123328 | tf_op jit(solution)/shard_map/dot_general | solution.py:40
  65.1 0.8 fusion.9
  66.0 1.3 convolution_convert_fusion.2
  67.5 1.2 fusion.1
  68.8 1.7 multiply_multiply_fusion
  70.4 2.3 %convolution_convert_fusion.1 = bf16[1024,512]{1,0:T(8,128)(2,1)S(1)} fusion(bf16[1024,2048]{1,0:T(8,128)(2,1)S(1)} %copy-done.1, bf16[2048,512]{1,0:T(8,128)(2,1)S(1)} %copy-done.3), kind=kOutput, calls=%fused_computation.6 | convolution fusion | flops 2148007936 | bytes 7340032 | tf_op jit(solution)/shard_map/dot_general | solution.py:35
  72.8 3.6 %fusion.5 = f32[16,256,512]{2,1,0:T(8,128)S(1)} fusion(bf16[16,64,512]{2,1,0:T(8,128)(2,1)S(1)} %bitcast.159, f32[16,64,256]{2,0,1:T(8,128)S(1)} %get-tuple-element.23), kind=kOutput, calls=%fused_computation.16 | convolution fusion | flops 1610612736 | bytes 10485760 | tf_op jit(solution)/shard_map/ncd,ncv->ndv/dot_general | solution.py:71
  76.4 1.5 fusion.17
  77.9 5.1 %collective-permute-start.10 = (bf16[256,512]{1,0:T(8,128)(2,1)}, bf16[256,512]{1,0:T(8,128)(2,1)S(1)}, u32[]{:S(2)}, u32[]{:S(2)}) collective-permute-start(bf16[256,512]{1,0:T(8,128)(2,1)} %fusion.17), channel_id=1, source_target_pairs={{0,16},{4,20},{8,24},{12,28},{16,32},{20,36},{24,40},{28,44},{32,4... | collective-permute-start | bytes 786440 | tf_op jit(solution)/shard_map/ppermute | solution.py:13
  83.0 1.9 collective-permute-start.7
  84.9 2.6 %collective-permute-start.4 = (bf16[256,512]{1,0:T(8,128)(2,1)}, bf16[256,512]{1,0:T(8,128)(2,1)}, u32[]{:S(2)}, u32[]{:S(2)}) collective-permute-start(bf16[256,512]{1,0:T(8,128)(2,1)} %fusion.17), channel_id=1, source_target_pairs={{0,8},{4,12},{8,16},{12,20},{16,24},{20,28},{24,32},{28,36},{32,40... | collective-permute-start | bytes 786440 | tf_op jit(solution)/shard_map/ppermute | solution.py:13
  87.5 4.1 %collective-permute-start = (bf16[256,512]{1,0:T(8,128)(2,1)}, bf16[256,512]{1,0:T(8,128)(2,1)}, u32[]{:S(2)}, u32[]{:S(2)}) collective-permute-start(bf16[256,512]{1,0:T(8,128)(2,1)} %fusion.17), channel_id=1, source_target_pairs={{0,4},{4,8},{8,12},{12,16},{16,20},{20,24},{24,28},{28,32},{32,36}... | collective-permute-start | bytes 786440 | tf_op jit(solution)/shard_map/ppermute | solution.py:13
  91.6 2.2 %convolution_select_fusion = f32[16,64,64]{2,1,0:T(8,128)S(1)} fusion(f32[16,64,256]{2,0,1:T(8,128)S(1)} %get-tuple-element.24, f32[16,64,256]{2,0,1:T(8,128)S(1)} %get-tuple-element.25, s32[16,64]{1,0:T(8,128)S(1)} %eq.64, pred[64,64]{1,0:T(8,128)(4,1)S(1)} %iota_compare_fusion), kind=kOutput, calls=%fused_computation.12 | convolution fusion | flops 201523200 | bytes 2367488 | tf_op jit(solution)/shard_map/ncd,nsd->ncs/dot_general | solution.py:64
  93.9 1.0 fusion.67
  97.6 3.5 %collective-permute-start.9 = (f32[256]{0:T(256)S(1)}, f32[256]{0:T(256)S(1)}, u32[]{:S(2)}, u32[]{:S(2)}) collective-permute-start(f32[256]{0:T(256)S(1)} %bitcast.203), channel_id=1, source_target_pairs={{0,12},{4,16},{8,20},{12,24},{16,28},{20,32},{24,36},{28,40},{32,4... | collective-permute-start | bytes 3080 | tf_op jit(solution)/shard_map/ppermute | solution.py:13
  101.2 6.9 %multiply_add_fusion.1 = f32[16,64,512]{2,1,0:T(8,128)} fusion(f32[16,64,512]{2,1,0:T(8,128)S(1)} %fusion.67, f32[16,256,512]{2,1,0:T(8,128)S(1)} %add_dynamic-update-slice_fusion, f32[16,64,256]{2,0,1:T(8,128)S(1)} %get-tuple-element.26, f32[16,64]{1,0:T(8,128)S(1)} %compare_convert_fusion.1), kind=kOutput, calls=%fused_computation.5 | convolution fusion | flops 1611661312 | bytes 13635584 | tf_op jit(solution)/shard_map/ncd,ndv->ncv/dot_general | solution.py:80
  108.2 2.9 %copy.54 = f32[1024,512]{0,1:T(8,128)} copy(f32[1024,512]{1,0:T(8,128)} %bitcast.156) | data formatting | bytes 4194304 | tf_op jit(solution)/shard_map/reshape | solution.py:83
  111.1 2.9 %collective-permute-start.6 = (f32[256]{0:T(256)S(1)}, f32[256]{0:T(256)S(1)}, u32[]{:S(2)}, u32[]{:S(2)}) collective-permute-start(f32[256]{0:T(256)S(1)} %bitcast.204), channel_id=1, source_target_pairs={{0,8},{4,12},{8,16},{12,20},{16,24},{20,28},{24,32},{28,36},{32,40... | collective-permute-start | bytes 3080 | tf_op jit(solution)/shard_map/ppermute | solution.py:13
  114.0 4.6 %collective-permute-done.6 = f32[256]{0:T(256)S(1)} collective-permute-done((f32[256]{0:T(256)S(1)}, f32[256]{0:T(256)S(1)}, u32[]{:S(2)}, u32[]{:S(2)}) %collective-permute-start.6) | collective-permute-done | bytes 1056 | tf_op jit(solution)/shard_map/ppermute | solution.py:13
  118.7 2.4 %collective-permute-start.3 = (f32[256]{0:T(256)S(1)}, f32[256]{0:T(256)S(1)}, u32[]{:S(2)}, u32[]{:S(2)}) collective-permute-start(f32[256]{0:T(256)S(1)} %bitcast.205), channel_id=1, source_target_pairs={{0,4},{4,8},{8,12},{12,16},{16,20},{20,24},{24,28},{28,32},{32,36}... | collective-permute-start | bytes 3080 | tf_op jit(solution)/shard_map/ppermute | solution.py:13
  121.1 4.6 %collective-permute-done.3 = f32[256]{0:T(256)S(1)} collective-permute-done((f32[256]{0:T(256)S(1)}, f32[256]{0:T(256)S(1)}, u32[]{:S(2)}, u32[]{:S(2)}) %collective-permute-start.3) | collective-permute-done | bytes 1056 | tf_op jit(solution)/shard_map/ppermute | solution.py:13
  125.7 6.0 %multiply_reduce_fusion = (f32[1024]{0:T(1024)S(1)}, f32[1024,512]{0,1:T(8,128)}) fusion(f32[1024,512]{0,1:T(8,128)} %copy.54, f32[1024]{0:T(1024)S(1)} %get-tuple-element.5, bf16[256,512]{1,0:T(8,128)(2,1)S(1)} %collective-permute-done.10, bf16[256,512]{1,0:T(8,128)(2,1)} %collective-permute-done.7, bf16[256,512]{1,0:T(8,128)(2,1)} %collective-permute-done.4, ...), kind=kOutput, calls=%fused_computation.3 | convolution fusion | flops 1614806016 | bytes 7351296 | tf_op jit(solution)/shard_map/dot_general | solution.py:107
  131.8 10.3 %convolution_convert_fusion = bf16[1024,2048]{1,0:T(8,128)(2,1)} fusion(bf16[512,2048]{1,0:T(8,128)(2,1)S(1)} %copy-done, f32[1024,512]{0,1:T(8,128)} %get-tuple-element.58, f32[512]{0:T(512)S(1)} %copy-done.6, f32[1024]{0:T(1024)S(1)} %rsqrt_multiply_fusion, bf16[1024,2048]{1,0:T(8,128)(2,1)} %all-gather.2.cloned.1.call-done, bf16[2048,512]{1,0:T(8,128)(2,1)} %param.16), kind=kOutput, calls=%fused_computation | convolution fusion | flops 4301258752 | bytes 14686208 | tf_op jit(solution)/shard_map/dot_general | solution.py:113
  142.1 44.4 %reduce-scatter.2.cloned.1.call-done = bf16[1024,512]{1,0:T(8,128)(2,1)} async-done(((bf16[1024,2048]{1,0:T(8,128)(2,1)}), bf16[1024,512]{1,0:T(8,128)(2,1)}) %reduce-scatter.2.cloned.1.call-update) | async-done | bytes 1048592 | tf_op jit(solution)/shard_map/reduce_scatter | solution.py:114
  (81 shorter events, 10.2 us)
Async XLA Ops:
  6.5 125.2 %copy-start = (bf16[512,2048]{1,0:T(8,128)(2,1)S(1)}, bf16[512,2048]{1,0:T(8,128)(2,1)}, u32[]{:S(2)}) copy-start(bf16[512,2048]{1,0:T(8,128)(2,1)} %param.21) | copy-start | bytes 6291460
  6.5 59.4 %copy-start.4 = (bf16[2048,256]{1,0:T(8,128)(2,1)S(1)}, bf16[2048,256]{1,0:T(8,128)(2,1)}, u32[]{:S(2)}) copy-start(bf16[2048,256]{1,0:T(8,128)(2,1)} %param.14) | copy-start | bytes 3145732
  6.5 53.1 %all-gather.2.cloned.1.call-start = ((), (), s32[]{:S(2)}) async-start(), calls=%async_computation.1 | async-start | bytes 5242880 | tf_op jit(solution)/shard_map/all_gather | solution.py:33
  7.3 179.3 %reduce-scatter.2.cloned.1.call-start = ((), (), s32[]{:S(2)}) async-start(), calls=%async_computation.2 | async-start | bytes 5242880 | tf_op jit(solution)/shard_map/reduce_scatter | solution.py:114
  10.0 18.2 %collective-permute-start.1 = (f32[2]{0:T(128)S(1)}, f32[2]{0:T(128)S(1)}, u32[]{:S(2)}, u32[]{:S(2)}) collective-permute-start(f32[2]{0:T(128)S(1)} %pad_maximum_fusion), channel_id=1, source_target_pairs={{0,4},{4,8},{8,12},{12,16},{16,20},{20,24},{24,28},{28,32},{32,36}... | collective-permute-start | bytes 32 | tf_op jit(solution)/shard_map/ppermute | solution.py:13
  11.9 19.8 %collective-permute-start.5 = (f32[2]{0:T(128)S(1)}, f32[2]{0:T(128)S(1)}, u32[]{:S(2)}, u32[]{:S(2)}) collective-permute-start(f32[2]{0:T(128)S(1)} %pad_maximum_fusion), channel_id=1, source_target_pairs={{0,12},{4,16},{8,20},{12,24},{16,28},{20,32},{24,36},{28,40},{32,4... | collective-permute-start | bytes 32 | tf_op jit(solution)/shard_map/ppermute | solution.py:13
  17.4 13.6 %collective-permute-start.8 = (f32[2]{0:T(128)S(1)}, f32[2]{0:T(128)S(1)}, u32[]{:S(2)}, u32[]{:S(2)}) collective-permute-start(f32[2]{0:T(128)S(1)} %pad_maximum_fusion), channel_id=1, source_target_pairs={{0,16},{4,20},{8,24},{12,28},{16,32},{20,36},{24,40},{28,44},{32,4... | collective-permute-start | bytes 32 | tf_op jit(solution)/shard_map/ppermute | solution.py:13
  21.1 12.6 %collective-permute-start.2 = (f32[2]{0:T(128)S(1)}, f32[2]{0:T(128)S(1)}, u32[]{:S(2)}, u32[]{:S(2)}) collective-permute-start(f32[2]{0:T(128)S(1)} %pad_maximum_fusion), channel_id=1, source_target_pairs={{0,8},{4,12},{8,16},{12,20},{16,24},{20,28},{24,32},{28,36},{32,40... | collective-permute-start | bytes 32 | tf_op jit(solution)/shard_map/ppermute | solution.py:13
  59.6 6.3 %copy-start.1 = (bf16[1024,2048]{1,0:T(8,128)(2,1)S(1)}, bf16[1024,2048]{1,0:T(8,128)(2,1)}, u32[]{:S(2)}) copy-start(bf16[1024,2048]{1,0:T(8,128)(2,1)} %all-gather.2.cloned.1.call-done) | copy-start | bytes 12582916
  63.1 4.4 %copy-start.5 = (bf16[2048,256]{1,0:T(8,128)(2,1)S(1)}, bf16[2048,256]{1,0:T(8,128)(2,1)}, u32[]{:S(2)}) copy-start(bf16[2048,256]{1,0:T(8,128)(2,1)} %param.13) | copy-start | bytes 3145732
  67.3 3.1 %copy-start.3 = (bf16[2048,512]{1,0:T(8,128)(2,1)S(1)}, bf16[2048,512]{1,0:T(8,128)(2,1)}, u32[]{:S(2)}) copy-start(bf16[2048,512]{1,0:T(8,128)(2,1)} %param.15) | copy-start | bytes 6291460
  68.8 4.0 %copy-start.2 = (f32[1024,256]{1,0:T(8,128)}, f32[1024,256]{1,0:T(8,128)S(1)}, u32[]{:S(2)}) copy-start(f32[1024,256]{1,0:T(8,128)S(1)} %fusion.1) | copy-start | bytes 3145732
  72.8 22.1 %slice-start = ((s8[8388608]{0:T(1024)(128)(4,1)}), s8[4194304]{0:T(1024)(128)(4,1)S(1)}, s32[]{:S(2)}) async-start(s8[8388608]{0:T(1024)(128)(4,1)} %bitcast.154), calls=%async_computation.3 | async-start | bytes 8388608
  76.4 18.5 %slice-start.1 = ((s8[8388608]{0:T(1024)(128)(4,1)}), s8[4194304]{0:T(1024)(128)(4,1)S(1)}, s32[]{:S(2)}) async-start(s8[8388608]{0:T(1024)(128)(4,1)} %bitcast.154), calls=%async_computation.4 | async-start | bytes 8388608
  77.9 47.8 %collective-permute-start.10 = (bf16[256,512]{1,0:T(8,128)(2,1)}, bf16[256,512]{1,0:T(8,128)(2,1)S(1)}, u32[]{:S(2)}, u32[]{:S(2)}) collective-permute-start(bf16[256,512]{1,0:T(8,128)(2,1)} %fusion.17), channel_id=1, source_target_pairs={{0,16},{4,20},{8,24},{12,28},{16,32},{20,36},{24,40},{28,44},{32,4... | collective-permute-start | bytes 786440 | tf_op jit(solution)/shard_map/ppermute | solution.py:13
  83.0 42.7 %collective-permute-start.7 = (bf16[256,512]{1,0:T(8,128)(2,1)}, bf16[256,512]{1,0:T(8,128)(2,1)}, u32[]{:S(2)}, u32[]{:S(2)}) collective-permute-start(bf16[256,512]{1,0:T(8,128)(2,1)} %fusion.17), channel_id=1, source_target_pairs={{0,12},{4,16},{8,20},{12,24},{16,28},{20,32},{24,36},{28,40},{32,4... | collective-permute-start | bytes 786440 | tf_op jit(solution)/shard_map/ppermute | solution.py:13
  84.9 40.8 %collective-permute-start.4 = (bf16[256,512]{1,0:T(8,128)(2,1)}, bf16[256,512]{1,0:T(8,128)(2,1)}, u32[]{:S(2)}, u32[]{:S(2)}) collective-permute-start(bf16[256,512]{1,0:T(8,128)(2,1)} %fusion.17), channel_id=1, source_target_pairs={{0,8},{4,12},{8,16},{12,20},{16,24},{20,28},{24,32},{28,36},{32,40... | collective-permute-start | bytes 786440 | tf_op jit(solution)/shard_map/ppermute | solution.py:13
  87.5 38.2 %collective-permute-start = (bf16[256,512]{1,0:T(8,128)(2,1)}, bf16[256,512]{1,0:T(8,128)(2,1)}, u32[]{:S(2)}, u32[]{:S(2)}) collective-permute-start(bf16[256,512]{1,0:T(8,128)(2,1)} %fusion.17), channel_id=1, source_target_pairs={{0,4},{4,8},{8,12},{12,16},{16,20},{20,24},{24,28},{28,32},{32,36}... | collective-permute-start | bytes 786440 | tf_op jit(solution)/shard_map/ppermute | solution.py:13
  97.6 13.5 %collective-permute-start.9 = (f32[256]{0:T(256)S(1)}, f32[256]{0:T(256)S(1)}, u32[]{:S(2)}, u32[]{:S(2)}) collective-permute-start(f32[256]{0:T(256)S(1)} %bitcast.203), channel_id=1, source_target_pairs={{0,12},{4,16},{8,20},{12,24},{16,28},{20,32},{24,36},{28,40},{32,4... | collective-permute-start | bytes 3080 | tf_op jit(solution)/shard_map/ppermute | solution.py:13
  108.2 23.6 %copy-start.6 = (f32[512]{0:T(512)S(1)}, f32[512]{0:T(512)}, u32[]{:S(2)}) copy-start(f32[512]{0:T(512)} %param.20) | copy-start | bytes 6148
  111.1 7.6 %collective-permute-start.6 = (f32[256]{0:T(256)S(1)}, f32[256]{0:T(256)S(1)}, u32[]{:S(2)}, u32[]{:S(2)}) collective-permute-start(f32[256]{0:T(256)S(1)} %bitcast.204), channel_id=1, source_target_pairs={{0,8},{4,12},{8,16},{12,20},{16,24},{20,28},{24,32},{28,36},{32,40... | collective-permute-start | bytes 3080 | tf_op jit(solution)/shard_map/ppermute | solution.py:13
  118.7 7.0 %collective-permute-start.3 = (f32[256]{0:T(256)S(1)}, f32[256]{0:T(256)S(1)}, u32[]{:S(2)}, u32[]{:S(2)}) collective-permute-start(f32[256]{0:T(256)S(1)} %bitcast.205), channel_id=1, source_target_pairs={{0,4},{4,8},{8,12},{12,16},{16,20},{20,24},{24,28},{28,32},{32,36}... | collective-permute-start | bytes 3080 | tf_op jit(solution)/shard_map/ppermute | solution.py:13
Sparse Core Ops, SparseCore 0:
  9.0 50.5 all-gather.1
  142.2 44.2 reduce-scatter.1

commit v2 on v1

v2 whole, which is shorter than its diff:
```python
import jax
import jax.numpy as jnp
from jax import lax
from jax.sharding import PartitionSpec as P

GROUP = 64
PIECES = 4
SEG_MOST = 4096
HIGHEST = lax.Precision.HIGHEST


def shifted(x, axis, shift, devices):
    pairs = [(i, i + shift) for i in range(devices - shift)]
    return lax.ppermute(x, axis, pairs)


def body(
    hidden_in,
    segment,
    w_query,
    w_key,
    w_value,
    w_outgate,
    w_gate_down,
    w_gate_up,
    gate_bias,
    norm_gain,
    w_out,
):
    tok_rows = hidden_in.shape[0]
    key_width = w_query.shape[1]
    value_width = w_value.shape[1]
    weights = (w_query, w_key, w_value, w_outgate, w_gate_down)
    piece_rows = tok_rows // PIECES
    piece_blocks = piece_rows // GROUP
    blocks = tok_rows // GROUP
    positions = jnp.arange(GROUP)
    causal = positions[None, :] <= positions[:, None]

    starts = jnp.concatenate(
        [jnp.zeros((1,), jnp.int32), (segment[1:] != segment[:-1]).astype(jnp.int32)]
    )
    live_device = (jnp.cumsum(starts) == 0).astype(jnp.float32)
    seg_all = segment.reshape(blocks, GROUP)
    live_all = (jnp.cumsum(starts.reshape(blocks, GROUP), axis=1) == 0).astype(jnp.float32)

    parts = []
    for p in range(PIECES):
        rows = slice(p * piece_rows, (p + 1) * piece_rows)
        piece = lax.all_gather(hidden_in[rows], "tensor", axis=1, tiled=True)
        query_sum, key_sum, value_sum, outgate, low = tuple(
            (jnp.dot(piece, weight, preferred_element_type=jnp.float32) for weight in weights)
        )
        query = query_sum.astype(jnp.bfloat16)
        key = key_sum.astype(jnp.bfloat16)
        value = value_sum.astype(jnp.bfloat16)
        pre_gate = jnp.dot(low, w_gate_up.astype(jnp.float32), precision=HIGHEST) + gate_bias
        logdecay = jax.nn.log_sigmoid(pre_gate) / 16.0

        chunks = slice(p * piece_blocks, (p + 1) * piece_blocks)
        seg_blocks = seg_all[chunks]
        live_blocks = live_all[chunks]
        cumul = jnp.cumsum(logdecay.reshape(piece_blocks, GROUP, key_width), axis=1)
        q_float = query.astype(jnp.float32).reshape(piece_blocks, GROUP, key_width)
        k_float = key.astype(jnp.float32).reshape(piece_blocks, GROUP, key_width)
        v_float = value.astype(jnp.float32).reshape(piece_blocks, GROUP, value_width)

        centre = cumul[:, GROUP // 2, :]
        q_scaled = q_float * jnp.exp(cumul - centre[:, None, :])
        k_scaled = k_float * jnp.exp(centre[:, None, :] - cumul)
        raw_scores = jnp.einsum("ncd,nsd->ncs", q_scaled, k_scaled, precision=HIGHEST)
        allowed = causal[None] & (seg_blocks[:, :, None] == seg_blocks[:, None, :])
        scores = jnp.where(allowed, raw_scores, 0.0)
        intra = jnp.einsum("ncs,nsv->ncv", scores, v_float, precision=HIGHEST)

        block_totals = cumul[:, -1, :]
        same_last = (seg_blocks == seg_blocks[:, -1:]).astype(jnp.float32)
        k_decayed = k_float * jnp.exp(block_totals[:, None, :] - cumul) * same_last[:, :, None]
        chunk_states = jnp.einsum("ncd,ncv->ndv", k_decayed, v_float, precision=HIGHEST)
        chunk_decay = jnp.exp(block_totals) * live_blocks[:, -1:]
        parts.append(
            (query, outgate, q_float, cumul, live_blocks, intra, chunk_states, chunk_decay, block_totals)
        )

    entering = jnp.zeros((key_width, value_width), jnp.float32)
    local_outs = []
    for p in range(PIECES):
        query, outgate, q_float, cumul, live_blocks, intra, chunk_states, chunk_decay, _ = parts[p]
        states = []
        for n in range(piece_blocks):
            states.append(entering)
            entering = chunk_decay[n][:, None] * entering + chunk_states[n]
        inter = (
            jnp.einsum("ncd,ndv->ncv", q_float * jnp.exp(cumul), jnp.stack(states), precision=HIGHEST)
            * live_blocks[:, :, None]
        )
        local_outs.append((intra + inter).reshape(piece_rows, value_width))
    final_state = entering

    block_totals = jnp.concatenate([part[8] for part in parts])
    before = jnp.cumsum(block_totals, axis=0) - block_totals
    cumul = jnp.concatenate([part[3] for part in parts])
    device_cumul = (cumul + before[:, None, :]).reshape(tok_rows, key_width)

    devices = lax.axis_size("req")
    window = min(devices - 1, -(-SEG_MOST // tok_rows))
    first_id = (segment[0] + 1).astype(jnp.float32)
    last_id = (segment[-1] + 1).astype(jnp.float32)
    decay_device = jnp.exp(device_cumul[-1]) * live_device[-1]
    tail = jnp.zeros((2, value_width), jnp.float32)
    tail = tail.at[0, :key_width].set(decay_device).at[1, 0].set(first_id).at[1, 1].set(last_id)
    message = jnp.concatenate([final_state, tail]).astype(jnp.bfloat16)
    got = [shifted(message, "req", j, devices).astype(jnp.float32) for j in range(1, window + 1)]
    state_in = got[-1][:key_width]
    last_far = got[-1][key_width + 1, 1]
    for j in range(window - 1, 0, -1):
        msg = got[j - 1]
        link = (msg[key_width + 1, 0] == last_far).astype(jnp.float32)
        state_in = msg[:key_width] + (link * msg[key_width, :key_width])[:, None] * state_in
        last_far = msg[key_width + 1, 1]
    linked = (first_id == last_far).astype(jnp.float32)
    mask = live_device * linked

    outs = []
    for p in range(PIECES):
        rows = slice(p * piece_rows, (p + 1) * piece_rows)
        query, outgate = parts[p][0], parts[p][1]
        carried = jnp.dot(
            query.astype(jnp.float32) * jnp.exp(device_cumul[rows]), state_in, precision=HIGHEST
        )
        attn = (local_outs[p] + carried * mask[rows][:, None]) * key_width ** (-0.5)
        normed = attn * lax.rsqrt(jnp.mean(attn * attn, axis=-1, keepdims=True) + 1e-05) * norm_gain
        gated = (normed * jax.nn.silu(outgate)).astype(jnp.bfloat16)
        head_term = jnp.dot(gated, w_out, preferred_element_type=jnp.float32)
        outs.append(
            lax.psum_scatter(head_term.astype(jnp.bfloat16), "tensor", scatter_dimension=1, tiled=True)
        )
    return jnp.concatenate(outs, axis=0)


def solution(mesh):
    in_specs = (
        P("req", "tensor"),
        P("req"),
        P(None, "tensor"),
        P(None, "tensor"),
        P(None, "tensor"),
        P(None, "tensor"),
        P(),
        P(None, "tensor"),
        P("tensor"),
        P(),
        P("tensor", None),
    )
    out_specs = P("req", "tensor")
    return jax.shard_map(body, mesh=mesh, in_specs=in_specs, out_specs=out_specs, check_vma=False)
```

time: 195 us -> 293 us (1.50)
  waiting for transfers between devices: 77 us -> 157 us
  starting transfers between devices: 36.8 us -> 14.1 us
  matrix products: 40.4 us -> 59.7 us
  local copies, waits for them, and re-layouts: 10.6 us -> 21.5 us
  other arithmetic: 7.99 us -> 18.3 us
    all_gather x1 -> x4, waiting for transfers between devices: 22.6 us -> 84.1 us  [body(): piece = lax.all_gather(hidden_in[rows], 'tensor', axis=1, tiled=True)]
    reduce_scatter x1 -> x4, waiting for transfers between devices: 44.4 us -> 69.7 us  [body(): lax.psum_scatter(head_term.astype(jnp.bfloat16), 'tensor', scatter_dimens...]
    ppermute x11 -> x4, starting transfers between devices: 36.8 us -> 13.6 us  [shifted(): return lax.ppermute(x, axis, pairs)]
    dot_general x4 -> x16, matrix products: 8.35 us -> 19 us  [body(): jnp.dot(piece, weight, preferred_element_type=jnp.float32)]
    ppermute x11 -> x4, waiting for transfers between devices: 9.26 us -> 1.11 us  [shifted(): return lax.ppermute(x, axis, pairs)]
    slice x6 -> x18, local copies, waits for them, and re-layouts: 2.72 us -> 10.5 us  [the longest x4 2.44 us: body(): centre = cumul[:, GROUP // 2, :]]
    dot_general x1 -> x4, matrix products: 10.3 us -> 17.3 us  [body(): head_term = jnp.dot(gated, w_out, preferred_element_type=jnp.float32)]
    add x0 -> x2, other arithmetic: none -> 3.98 us  [the longest x1 3.8 us: body(): entering = chunk_decay[n][:, None] * entering + chunk_states[n]]
  transfers between devices with their start and end apart: 13 -> 12, of which waited for: 4 -> 9; matrix products, arithmetic and copies ran while one was open for 13% -> 19% of each run, Pallas kernels for 0% -> 0%
where the time goes in v2:
time: 293 us; the launch traced here: 292 us
  waiting for transfers between devices  157 us (54%)
  matrix products  59.7 us (20%)
  between operations  21.6 us (7%)
  local copies, waits for them, and re-layouts  21.5 us (7%)
  other arithmetic  18.3 us (6%)
  starting transfers between devices  14.1 us (5%)
    all_gather x4, waiting for transfers between devices, body(): piece = lax.all_gather(hidden_in[rows], 'tensor', axis=1, tiled=True)  84.1 us
    reduce_scatter x4, waiting for transfers between devices, body(): lax.psum_scatter(head_term.astype(jnp.bfloat16), 'tensor', scatter_dimens...  69.7 us
    dot_general x16, matrix products, body(): jnp.dot(piece, weight, preferred_element_type=jnp.float32)  19 us
    dot_general x4, matrix products, body(): head_term = jnp.dot(gated, w_out, preferred_element_type=jnp.float32)  17.3 us
    ppermute x4, starting transfers between devices, shifted(): return lax.ppermute(x, axis, pairs)  13.6 us
    dot_general x4, matrix products, body(): jnp.einsum('ncd,ndv->ncv', q_float * jnp.exp(cumul), jnp.stack(states), p...  7.04 us
  transfers between devices with their start and end apart: 12, of which 9 were waited for; matrix products, arithmetic and copies ran while one was open for 19% of the time, Pallas kernels for 0%

profile of v2, /device:TPU:2, one launch (start us, length us, event | category | flops | bytes accessed | tf_op | source)
XLA Modules:
  0.0 292.1 jit_solution(15862725786038252527)
XLA Ops:
  6.6 2.3 fusion.172
  19.7 15.8 %all-gather.5.cloned.1.call-done = bf16[256,2048]{1,0:T(8,128)(2,1)} async-done(((bf16[256,512]{1,0:T(8,128)(2,1)}), bf16[256,2048]{1,0:T(8,128)(2,1)}) %all-gather.5.cloned.1.call-update) | async-done | bytes 1048592 | tf_op jit(solution)/shard_map/all_gather | solution.py:50
  35.6 1.6 fusion.194
  38.5 23.2 %all-gather.7.cloned.1.call-done = bf16[256,2048]{1,0:T(8,128)(2,1)} async-done(((bf16[256,512]{1,0:T(8,128)(2,1)}), bf16[256,2048]{1,0:T(8,128)(2,1)}) %all-gather.7.cloned.1.call-update) | async-done | bytes 1048592 | tf_op jit(solution)/shard_map/all_gather | solution.py:50
  61.7 1.6 fusion.196
  64.6 23.2 %all-gather.11.cloned.1.call-done = bf16[256,2048]{1,0:T(8,128)(2,1)} async-done(((bf16[256,512]{1,0:T(8,128)(2,1)}), bf16[256,2048]{1,0:T(8,128)(2,1)}) %all-gather.11.cloned.1.call-update) | async-done | bytes 1048592 | tf_op jit(solution)/shard_map/all_gather | solution.py:50
  87.8 1.6 fusion.198
  92.0 21.8 %all-gather.9.cloned.1.call-done = bf16[256,2048]{1,0:T(8,128)(2,1)} async-done(((bf16[256,512]{1,0:T(8,128)(2,1)}), bf16[256,2048]{1,0:T(8,128)(2,1)}) %all-gather.9.cloned.1.call-update) | async-done | bytes 1048592 | tf_op jit(solution)/shard_map/all_gather | solution.py:50
  113.8 1.6 fusion.197
  130.7 3.8 %multiply_add_fusion = (f32[1,256,512]{2,1,0:T(8,128)}, f32[1,256,512]{2,1,0:T(8,128)}, f32[1,256,512]{2,1,0:T(8,128)}, f32[1,256,512]{2,1,0:T(8,128)}, f32[1,25...) fusion(f32[4,256,512]{2,1,0:T(8,128)S(1)} %fusion.91, ...), kind=kLoop, calls=%fused_computation.127 | loop fusion | flops 3801088 | bytes 15744000 | tf_op jit(solution)/shard_map/add | solution.py:92
  134.5 1.5 fusion.65
  139.6 5.2 %collective-permute-start.3 = (bf16[258,512]{1,0:T(8,128)(2,1)S(1)}, bf16[258,512]{1,0:T(8,128)(2,1)S(1)}, u32[]{:S(2)}, u32[]{:S(2)}) collective-permute-start(bf16[258,512]{1,0:T(8,128)(2,1)S(1)} %pad_maximum_fusion.1), channel_id=1, source_target_pairs={{0,16},{4,20},{8,24},{12,28},{16,32},{20,36},{24,40},{28,44},{32,4... | collective-permute-start | bytes 792584 | tf_op jit(solution)/shard_map/ppermute | solution.py:14
  144.8 1.9 collective-permute-start.2
  146.7 2.6 collective-permute-start.1
  149.3 3.9 %collective-permute-start = (bf16[258,512]{1,0:T(8,128)(2,1)S(1)}, bf16[258,512]{1,0:T(8,128)(2,1)S(1)}, u32[]{:S(2)}, u32[]{:S(2)}) collective-permute-start(bf16[258,512]{1,0:T(8,128)(2,1)S(1)} %pad_maximum_fusion.1), channel_id=1, source_target_pairs={{0,4},{4,8},{8,12},{12,16},{16,20},{20,24},{24,28},{28,32},{32,36}... | collective-permute-start | bytes 792584 | tf_op jit(solution)/shard_map/ppermute | solution.py:14
  153.2 2.4 bitcast_multiply_fusion
  173.9 1.5 multiply_reduce_fusion
  176.0 4.4 %convolution_convert_fusion = bf16[256,2048]{1,0:T(8,128)(2,1)} fusion(bf16[512,2048]{1,0:T(8,128)(2,1)S(1)} %copy-done, f32[256,512]{1,0:T(8,128)} %get-tuple-element.117, f32[256]{0:T(256)} %rsqrt_multiply_fusion, f32[512]{0:T(512)} %param.26, bf16[256,2048]{1,0:T(8,128)(2,1)} %all-gather.11.cloned.1.call-done, bf16[2048,512]{1,0:T(8,128)(2,1)} %param.22), kind=kOutput, calls=%fused_computation | convolution fusion | flops 1075314688 | bytes 6818816 | tf_op jit(solution)/shard_map/dot_general | solution.py:134
  180.5 1.9 bitcast_multiply_fusion.1
  182.4 2.1 fusion.34
  185.6 1.5 multiply_reduce_fusion.1
  187.6 4.4 %convolution_convert_fusion.1 = bf16[256,2048]{1,0:T(8,128)(2,1)} fusion(bf16[512,2048]{1,0:T(8,128)(2,1)S(1)} %copy-done, f32[256,512]{1,0:T(8,128)} %get-tuple-element.121, f32[256]{0:T(256)} %rsqrt_multiply_fusion.1, f32[512]{0:T(512)} %param.26, bf16[256,2048]{1,0:T(8,128)(2,1)} %all-gather.9.cloned.1.call-done, bf16[2048,512]{1,0:T(8,128)(2,1)} %param.22), kind=kOutput, calls=%fused_computation.1 | convolution fusion | flops 1075314688 | bytes 6818816 | tf_op jit(solution)/shard_map/dot_general | solution.py:134
  192.4 1.8 bitcast_multiply_fusion.2
  194.3 2.1 fusion.37
  199.0 4.4 %convolution_convert_fusion.2 = bf16[256,2048]{1,0:T(8,128)(2,1)} fusion(bf16[512,2048]{1,0:T(8,128)(2,1)S(1)} %copy-done, f32[256,512]{1,0:T(8,128)} %get-tuple-element.125, f32[256]{0:T(256)S(1)} %rsqrt_multiply_fusion.2, f32[512]{0:T(512)S(1)} %copy-done.102, bf16[256,2048]{1,0:T(8,128)(2,1)} %all-gather.7.cloned.1.call-done, bf16[2048,512]{1,0:T(8,128)(2,1)} %param.22), kind=kOutput, calls=%fused_computation.2 | convolution fusion | flops 1075314688 | bytes 6818816 | tf_op jit(solution)/shard_map/dot_general | solution.py:134
  203.6 1.8 bitcast_multiply_fusion.3
  207.8 1.5 multiply_reduce_fusion.3
  209.3 4.1 %convolution_convert_fusion.3 = bf16[256,2048]{1,0:T(8,128)(2,1)} fusion(bf16[512,2048]{1,0:T(8,128)(2,1)S(1)} %copy-done, f32[256,512]{1,0:T(8,128)} %get-tuple-element.129, f32[512]{0:T(512)S(1)} %copy-done.103, f32[256]{0:T(256)S(1)} %rsqrt_multiply_fusion.3, bf16[256,2048]{1,0:T(8,128)(2,1)S(1)} %copy-done.8, bf16[2048,512]{1,0:T(8,128)(2,1)} %param.22), kind=kOutput, calls=%fused_computation.3 | convolution fusion | flops 1075314688 | bytes 6818816 | tf_op jit(solution)/shard_map/dot_general | solution.py:134
  213.4 17.8 %reduce-scatter.9.cloned.1.call-done = bf16[256,512]{1,0:T(8,128)(2,1)} async-done(((bf16[256,2048]{1,0:T(8,128)(2,1)}), bf16[256,512]{1,0:T(8,128)(2,1)}) %reduce-scatter.9.cloned.1.call-update) | async-done | bytes 262160 | tf_op jit(solution)/shard_map/reduce_scatter | solution.py:136
  231.2 25.9 %reduce-scatter.7.cloned.1.call-done = bf16[256,512]{1,0:T(8,128)(2,1)} async-done(((bf16[256,2048]{1,0:T(8,128)(2,1)}), bf16[256,512]{1,0:T(8,128)(2,1)}) %reduce-scatter.7.cloned.1.call-update) | async-done | bytes 262160 | tf_op jit(solution)/shard_map/reduce_scatter | solution.py:136
  257.1 25.9 %reduce-scatter.5.cloned.1.call-done = bf16[256,512]{1,0:T(8,128)(2,1)} async-done(((bf16[256,2048]{1,0:T(8,128)(2,1)}), bf16[256,512]{1,0:T(8,128)(2,1)}) %reduce-scatter.5.cloned.1.call-update) | async-done | bytes 262160 | tf_op jit(solution)/shard_map/reduce_scatter | solution.py:136
  283.0 2.2 pad_maximum_fusion
  (337 shorter events, 53.2 us)
Async XLA Ops:
  6.5 169.4 %copy-start = (bf16[512,2048]{1,0:T(8,128)(2,1)S(1)}, bf16[512,2048]{1,0:T(8,128)(2,1)}, u32[]{:S(2)}) copy-start(bf16[512,2048]{1,0:T(8,128)(2,1)} %param.27) | copy-start | bytes 6291460
  6.5 29.0 %copy-start.27 = (bf16[2048,16]{0,1:T(8,128)(2,1)S(1)}, bf16[2048,16]{0,1:T(8,128)(2,1)}, u32[]{:S(2)}) copy-start(bf16[2048,16]{0,1:T(8,128)(2,1)} %param.23) | copy-start | bytes 196612
  6.5 30.6 %copy-start.104 = (f32[256]{0:T(256)S(1)}, f32[256]{0:T(256)}, u32[]{:S(2)}) copy-start(f32[256]{0:T(256)} %param.25) | copy-start | bytes 3076
  6.5 30.7 %copy-start.101 = (bf16[16,256]{1,0:T(8,128)(2,1)S(1)}, bf16[16,256]{1,0:T(8,128)(2,1)}, u32[]{:S(2)}) copy-start(bf16[16,256]{1,0:T(8,128)(2,1)} %param.24) | copy-start | bytes 24580
  6.5 29.0 %all-gather.5.cloned.1.call-start = ((), (), s32[]{:S(2)}) async-start(), calls=%async_computation.4 | async-start | bytes 1310720 | tf_op jit(solution)/shard_map/all_gather | solution.py:50
  8.9 52.8 %all-gather.7.cloned.1.call-start = ((), (), s32[]{:S(2)}) async-start(), calls=%async_computation.5 | async-start | bytes 1310720 | tf_op jit(solution)/shard_map/all_gather | solution.py:50
  9.7 78.2 %all-gather.11.cloned.1.call-start = ((), (), s32[]{:S(2)}) async-start(), calls=%async_computation.7 | async-start | bytes 1310720 | tf_op jit(solution)/shard_map/all_gather | solution.py:50
  10.4 103.4 %all-gather.9.cloned.1.call-start = ((), (), s32[]{:S(2)}) async-start(), calls=%async_computation.6 | async-start | bytes 1310720 | tf_op jit(solution)/shard_map/all_gather | solution.py:50
  11.0 202.4 %reduce-scatter.11.cloned.1.call-start = ((), (), s32[]{:S(2)}) async-start(), calls=%async_computation.11 | async-start | bytes 1310720 | tf_op jit(solution)/shard_map/reduce_scatter | solution.py:136
  16.1 19.5 %copy-start.63 = (s32[4,64]{1,0:T(4,128)}, s32[4,64]{1,0:T(4,128)S(1)}, u32[]{:S(2)}) copy-start(s32[4,64]{1,0:T(4,128)S(1)} %slice.469) | copy-start | bytes 3076
  16.9 18.6 %copy-start.67 = (s32[4,64]{1,0:T(4,128)}, s32[4,64]{1,0:T(4,128)S(1)}, u32[]{:S(2)}) copy-start(s32[4,64]{1,0:T(4,128)S(1)} %slice.485) | copy-start | bytes 3076
  18.1 17.5 %copy-start.59 = (s32[8,128]{1,0:T(8,128)}, s32[8,128]{1,0:T(8,128)S(1)}, u32[]{:S(2)}) copy-start(s32[8,128]{1,0:T(8,128)S(1)} %reduce-window.9) | copy-start | bytes 12292
  18.3 17.3 %copy-start.93 = (s32[8]{0:T(128)}, s32[8]{0:T(128)S(1)}, u32[]{:S(2)}) copy-start(s32[8]{0:T(128)S(1)} %slice_reduce_fusion) | copy-start | bytes 100
  37.9 83.6 %copy-start.16 = (f32[4,64,256]{2,1,0:T(8,128)}, f32[4,64,256]{2,1,0:T(8,128)S(1)}, u32[]{:S(2)}) copy-start(f32[4,64,256]{2,1,0:T(8,128)S(1)} %reduce_window_sum.64) | copy-start | bytes 786436
  90.2 36.5 %copy-start.14 = (f32[4,64,256]{2,1,0:T(8,128)}, f32[4,64,256]{2,1,0:T(8,128)S(1)}, u32[]{:S(2)}) copy-start(f32[4,64,256]{2,1,0:T(8,128)S(1)} %reduce_window_sum.68) | copy-start | bytes 786436
  90.8 27.5 %copy-start.55 = (f32[4,1,256]{2,0,1:T(4,128)}, f32[4,1,256]{2,0,1:T(4,128)S(1)}, u32[]{:S(2)}) copy-start(f32[4,1,256]{2,0,1:T(4,128)S(1)} %copy.57) | copy-start | bytes 12292
  134.5 18.7 %copy-start.73 = (f32[4,1,256]{2,1,0:T(1,128)S(1)}, f32[4,1,256]{2,1,0:T(1,128)}, u32[]{:S(2)}) copy-start(f32[4,1,256]{2,1,0:T(1,128)} %get-tuple-element.80) | copy-start | bytes 12292
  134.5 18.7 %copy-start.2 = (bf16[2048,256]{1,0:T(8,128)(2,1)S(1)}, bf16[2048,256]{1,0:T(8,128)(2,1)}, u32[]{:S(2)}) copy-start(bf16[2048,256]{1,0:T(8,128)(2,1)} %param.19) | copy-start | bytes 3145732
  136.0 19.6 %copy-start.68 = (s32[4,64]{1,0:T(4,128)S(1)}, s32[4,64]{1,0:T(4,128)}, u32[]{:S(2)}) copy-start(s32[4,64]{1,0:T(4,128)} %copy-done.67) | copy-start | bytes 3076
  138.5 17.2 %copy-start.15 = (f32[4,64,256]{2,1,0:T(8,128)S(1)}, f32[4,64,256]{2,1,0:T(8,128)}, u32[]{:S(2)}) copy-start(f32[4,64,256]{2,1,0:T(8,128)} %copy-done.14) | copy-start | bytes 786436
  138.5 17.2 %copy-start.24 = (bf16[256,256]{1,0:T(8,128)(2,1)S(1)}, bf16[256,256]{1,0:T(8,128)(2,1)}, u32[]{:S(2)}) copy-start(bf16[256,256]{1,0:T(8,128)(2,1)} %copy-done.23) | copy-start | bytes 393220
  139.5 16.6 %copy-start.46 = (f32[1,256,512]{2,1,0:T(8,128)S(1)}, f32[1,256,512]{2,1,0:T(8,128)}, u32[]{:S(2)}) copy-start(f32[1,256,512]{2,1,0:T(8,128)} %get-tuple-element.45) | copy-start | bytes 1572868
  139.5 16.6 %copy-start.47 = (f32[1,256,512]{2,1,0:T(8,128)S(1)}, f32[1,256,512]{2,1,0:T(8,128)}, u32[]{:S(2)}) copy-start(f32[1,256,512]{2,1,0:T(8,128)} %get-tuple-element.46) | copy-start | bytes 1572868
  139.5 16.6 %copy-start.48 = (f32[1,256,512]{2,1,0:T(8,128)S(1)}, f32[1,256,512]{2,1,0:T(8,128)}, u32[]{:S(2)}) copy-start(f32[1,256,512]{2,1,0:T(8,128)} %get-tuple-element.47) | copy-start | bytes 1572868
  139.5 16.6 %copy-start.49 = (f32[1,256,512]{2,1,0:T(8,128)S(1)}, f32[1,256,512]{2,1,0:T(8,128)}, u32[]{:S(2)}) copy-start(f32[1,256,512]{2,1,0:T(8,128)} %get-tuple-element.48) | copy-start | bytes 1572868
  139.6 19.2 %collective-permute-start.3 = (bf16[258,512]{1,0:T(8,128)(2,1)S(1)}, bf16[258,512]{1,0:T(8,128)(2,1)S(1)}, u32[]{:S(2)}, u32[]{:S(2)}) collective-permute-start(bf16[258,512]{1,0:T(8,128)(2,1)S(1)} %pad_maximum_fusion.1), channel_id=1, source_target_pairs={{0,16},{4,20},{8,24},{12,28},{16,32},{20,36},{24,40},{28,44},{32,4... | collective-permute-start | bytes 792584 | tf_op jit(solution)/shard_map/ppermute | solution.py:14
  144.8 14.7 %collective-permute-start.2 = (bf16[258,512]{1,0:T(8,128)(2,1)S(1)}, bf16[258,512]{1,0:T(8,128)(2,1)S(1)}, u32[]{:S(2)}, u32[]{:S(2)}) collective-permute-start(bf16[258,512]{1,0:T(8,128)(2,1)S(1)} %pad_maximum_fusion.1), channel_id=1, source_target_pairs={{0,12},{4,16},{8,20},{12,24},{16,28},{20,32},{24,36},{28,40},{32,4... | collective-permute-start | bytes 792584 | tf_op jit(solution)/shard_map/ppermute | solution.py:14
  146.7 15.5 %collective-permute-start.1 = (bf16[258,512]{1,0:T(8,128)(2,1)S(1)}, bf16[258,512]{1,0:T(8,128)(2,1)S(1)}, u32[]{:S(2)}, u32[]{:S(2)}) collective-permute-start(bf16[258,512]{1,0:T(8,128)(2,1)S(1)} %pad_maximum_fusion.1), channel_id=1, source_target_pairs={{0,8},{4,12},{8,16},{12,20},{16,24},{20,28},{24,32},{28,36},{32,40... | collective-permute-start | bytes 792584 | tf_op jit(solution)/shard_map/ppermute | solution.py:14
  149.3 16.5 %collective-permute-start = (bf16[258,512]{1,0:T(8,128)(2,1)S(1)}, bf16[258,512]{1,0:T(8,128)(2,1)S(1)}, u32[]{:S(2)}, u32[]{:S(2)}) collective-permute-start(bf16[258,512]{1,0:T(8,128)(2,1)S(1)} %pad_maximum_fusion.1), channel_id=1, source_target_pairs={{0,4},{4,8},{8,12},{12,16},{16,20},{20,24},{24,28},{28,32},{32,36}... | collective-permute-start | bytes 792584 | tf_op jit(solution)/shard_map/ppermute | solution.py:14
  180.4 50.8 %reduce-scatter.9.cloned.1.call-start = ((), (), s32[]{:S(2)}) async-start(), calls=%async_computation.10 | async-start | bytes 1310720 | tf_op jit(solution)/shard_map/reduce_scatter | solution.py:136
  192.1 65.0 %reduce-scatter.7.cloned.1.call-start = ((), (), s32[]{:S(2)}) async-start(), calls=%async_computation.9 | async-start | bytes 1310720 | tf_op jit(solution)/shard_map/reduce_scatter | solution.py:136
  203.4 79.6 %reduce-scatter.5.cloned.1.call-start = ((), (), s32[]{:S(2)}) async-start(), calls=%async_computation.8 | async-start | bytes 1310720 | tf_op jit(solution)/shard_map/reduce_scatter | solution.py:136
  (85 other events, 212.1 us)
Sparse Core Ops, SparseCore 0:
  9.1 26.4 all-gather.4
  37.2 24.4 all-gather.6
  63.4 24.4 all-gather.10
  89.4 24.4 all-gather.8
  180.5 24.8 reduce-scatter.10
  207.6 23.5 reduce-scatter.8
  233.6 23.4 reduce-scatter.6
  259.5 23.4 reduce-scatter.4

commit v3 on v1

--- a/solution.py
+++ b/solution.py
@@ -6,6 +6,7 @@
 GROUP = 64
 SEG_MOST = 4096
 HIGHEST = lax.Precision.HIGHEST
+HIGH = lax.Precision.HIGH
 
 
 def shifted(x, axis, shift, devices):
@@ -61,14 +62,14 @@
     centre = cumul[:, GROUP // 2, :]
     q_scaled = q_float * jnp.exp(cumul - centre[:, None, :])
     k_scaled = k_float * jnp.exp(centre[:, None, :] - cumul)
-    raw_scores = jnp.einsum("ncd,nsd->ncs", q_scaled, k_scaled, precision=HIGHEST)
+    raw_scores = jnp.einsum("ncd,nsd->ncs", q_scaled, k_scaled, precision=HIGH)
     allowed = causal[None] & (seg_blocks[:, :, None] == seg_blocks[:, None, :])
     scores = jnp.where(allowed, raw_scores, 0.0)
-    intra = jnp.einsum("ncs,nsv->ncv", scores, v_float, precision=HIGHEST)
+    intra = jnp.einsum("ncs,nsv->ncv", scores, v_float, precision=HIGH)
 
     same_last = (seg_blocks == seg_blocks[:, -1:]).astype(jnp.float32)
     k_decayed = k_float * jnp.exp(block_totals[:, None, :] - cumul) * same_last[:, :, None]
-    chunk_states = jnp.einsum("ncd,ncv->ndv", k_decayed, v_float, precision=HIGHEST)
+    chunk_states = jnp.einsum("ncd,ncv->ndv", k_decayed, v_float, precision=HIGH)
     chunk_decay = jnp.exp(block_totals) * live_blocks[:, -1:]
 
     entering = [jnp.zeros((key_width, value_width), jnp.float32)]
@@ -77,7 +78,7 @@
     final_state = entering[-1]
     entering = jnp.stack(entering[:-1])
     inter = (
-        jnp.einsum("ncd,ndv->ncv", q_float * jnp.exp(cumul), entering, precision=HIGHEST)
+        jnp.einsum("ncd,ndv->ncv", q_float * jnp.exp(cumul), entering, precision=HIGH)
         * live_blocks[:, :, None]
     )
     local_out = (intra + inter).reshape(tok_rows, value_width)
@@ -87,25 +88,20 @@
     first_id = (segment[0] + 1).astype(jnp.float32)
     last_id = (segment[-1] + 1).astype(jnp.float32)
     decay_device = jnp.exp(device_cumul[-1]) * live_device[-1]
-    ids = jnp.stack([first_id, last_id])
-    sent_state = final_state.astype(jnp.bfloat16)
-    got = [
-        (
-            shifted(ids, "req", j, devices),
-            shifted(decay_device, "req", j, devices),
-            shifted(sent_state, "req", j, devices).astype(jnp.float32),
-        )
-        for j in range(1, window + 1)
-    ]
-    ids_far, _, state_in = got[-1]
+    tail = jnp.zeros((2, value_width), jnp.float32)
+    tail = tail.at[0, :key_width].set(decay_device).at[1, 0].set(first_id).at[1, 1].set(last_id)
+    message = jnp.concatenate([final_state, tail]).astype(jnp.bfloat16)
+    got = [shifted(message, "req", j, devices).astype(jnp.float32) for j in range(1, window + 1)]
+    state_in = got[-1][:key_width]
+    last_far = got[-1][key_width + 1, 1]
     for j in range(window - 1, 0, -1):
-        ids_j, decay_j, state_j = got[j - 1]
-        link = (ids_j[0] == ids_far[1]).astype(jnp.float32)
-        state_in = state_j + (link * decay_j)[:, None] * state_in
-        ids_far = ids_j
-    linked = (first_id == ids_far[1]).astype(jnp.float32)
+        msg = got[j - 1]
+        link = (msg[key_width + 1, 0] == last_far).astype(jnp.float32)
+        state_in = msg[:key_width] + (link * msg[key_width, :key_width])[:, None] * state_in
+        last_far = msg[key_width + 1, 1]
+    linked = (first_id == last_far).astype(jnp.float32)
     carried = jnp.dot(
-        query.astype(jnp.float32) * jnp.exp(device_cumul), state_in, precision=HIGHEST
+        query.astype(jnp.float32) * jnp.exp(device_cumul), state_in, precision=HIGH
     )
     attn = (local_out + carried * (live_device * linked)[:, None]) * key_width ** (-0.5)
     normed = attn * lax.rsqrt(jnp.mean(attn * attn, axis=-1, keepdims=True) + 1e-05) * norm_gain

time: 195 us -> 228 us (1.17)
  other arithmetic: 7.99 us -> 44.5 us
  starting transfers between devices: 36.8 us -> 13 us
  waiting for transfers between devices: 77 us -> 93 us
  local copies, waits for them, and re-layouts: 10.6 us -> 13.8 us
    unnamed x15 -> x14, other arithmetic: 1.95 us -> 29 us
    ppermute x11 -> x4, starting transfers between devices: 36.8 us -> 13 us  [shifted(): return lax.ppermute(x, axis, pairs)]
    all_gather x1, waiting for transfers between devices: 22.6 us -> 44.3 us  [body(): piece = lax.all_gather(hidden_in, 'tensor', axis=1, tiled=True)]
    ppermute x11 -> x4, waiting for transfers between devices: 9.26 us -> 0.01 us  [shifted(): return lax.ppermute(x, axis, pairs)]
    another operation x3 -> x4, other arithmetic: 0.38 us -> 4.37 us
    reduce_scatter x1, waiting for transfers between devices: 44.4 us -> 47.9 us  [body(): lax.psum_scatter(head_term.astype(jnp.bfloat16), 'tensor', scatter_dimens...]
  transfers between devices with their start and end apart: 13 -> 6, of which waited for: 4 -> 2; matrix products, arithmetic and copies ran while one was open for 13% -> 24% of each run, Pallas kernels for 0% -> 0%
where the time goes in v3:
time: 228 us; the launch traced here: 226 us
  waiting for transfers between devices  93 us (41%)
  other arithmetic  44.5 us (20%)
  matrix products  41.5 us (18%)
  between operations  20 us (9%)
  local copies, waits for them, and re-layouts  13.8 us (6%)
  starting transfers between devices  13 us (6%)
    reduce_scatter x1, waiting for transfers between devices, body(): lax.psum_scatter(head_term.astype(jnp.bfloat16), 'tensor', scatter_dimens...  47.9 us
    all_gather x1, waiting for transfers between devices, body(): piece = lax.all_gather(hidden_in, 'tensor', axis=1, tiled=True)  44.3 us
    unnamed x14, other arithmetic  29 us
    ppermute x4, starting transfers between devices, shifted(): return lax.ppermute(x, axis, pairs)  13 us
    dot_general x1, matrix products, body(): head_term = jnp.dot(gated, w_out, preferred_element_type=jnp.float32)  10.3 us
    dot_general x4, matrix products, body(): jnp.dot(piece, weight, preferred_element_type=jnp.float32)  8.35 us
    dot_general x1, matrix products, body(): jnp.einsum('ncd,ndv->ncv', q_float * jnp.exp(cumul), entering, precision=...  7.93 us
    dot_general x1, matrix products, body(): jnp.einsum('ncd,ncv->ndv', k_decayed, v_float, precision=HIGH)  5.73 us
  transfers between devices with their start and end apart: 6, of which 2 were waited for; matrix products, arithmetic and copies ran while one was open for 24% of the time, Pallas kernels for 0%

profile of v3, /device:TPU:2, one launch (start us, length us, event | category | flops | bytes accessed | tf_op | source)
XLA Modules:
  0.0 225.9 jit_solution(16146995661903344463)
XLA Ops:
  15.3 44.3 %all-gather.2.cloned.1.call-done = bf16[1024,2048]{1,0:T(8,128)(2,1)} async-done(((bf16[1024,512]{1,0:T(8,128)(2,1)}), bf16[1024,2048]{1,0:T(8,128)(2,1)}) %all-gather.2.cloned.1.call-update) | async-done | bytes 4194320 | tf_op jit(solution)/shard_map/all_gather | solution.py:34
  59.6 3.5 %fusion.65 = f32[1024,16]{0,1:T(8,128)S(1)} fusion(bf16[1024,2048]{1,0:T(8,128)(2,1)} %all-gather.2.cloned.1.call-done, bf16[2048,16]{0,1:T(8,128)(2,1)} %param.23), kind=kOutput, calls=%fused_computation.140 | convolution fusion | flops 67108864 | bytes 4325376 | tf_op jit(solution)/shard_map/dot_general | solution.py:36
  63.1 2.0 fusion.3
  68.6 3.2 %multiply_multiply_fusion = (f32[16,64,256]{2,0,1:T(8,128)S(1)}, f32[16,64,256]{2,0,1:T(8,128)}, f32[16,64,256]{2,0,1:T(8,128)}, f32[16,64,256]{2,0,1:T(8,128)}, f32[16,64,256]{2,0,1:T(8,128)S(1)}) fusion(f32[16,64,256]{2,0,1:T(8,128)S(1)} %fusion.9, f32[16,64,256]{2,1,0:T(8,128)S(1)} %convert.17, f32[16,64]{0,1:T(8,128)S(1)} %copy.48, ...), kind=kLoop, calls=%fused_computation.27 | loop fusion | flops 2359296 | bytes 8441856 | tf_op jit(solution)/shard_map/mul | solution.py:71
  72.4 2.3 %convolution_convert_fusion.1 = bf16[1024,512]{1,0:T(8,128)(2,1)S(1)} fusion(bf16[1024,2048]{1,0:T(8,128)(2,1)S(1)} %copy-done.1, bf16[2048,512]{1,0:T(8,128)(2,1)S(1)} %copy-done.8), kind=kOutput, calls=%fused_computation.6 | convolution fusion | flops 2148007936 | bytes 7340032 | tf_op jit(solution)/shard_map/dot_general | solution.py:36
  75.8 5.7 %fusion.5 = f32[16,256,512]{2,1,0:T(8,128)} fusion(bf16[16,64,512]{2,1,0:T(8,128)(2,1)S(1)} %bitcast.163, f32[16,64,256]{2,0,1:T(8,128)S(1)} %get-tuple-element.57), kind=kOutput, calls=%fused_computation.16 | convolution fusion | flops 805306368 | bytes 10485760 | tf_op jit(solution)/shard_map/ncd,ncv->ndv/dot_general | solution.py:72
  81.9 4.0 %fusion.26 = bf16[256,512]{1,0:T(8,128)(2,1)S(1)} fusion(f32[16,256,512]{2,1,0:T(8,128)} %fusion.5, f32[256]{0:T(256)S(1)} %bitcast.168, f32[256]{0:T(256)S(1)} %bitcast.189, f32[256]{0:T(256)S(1)} %bitcast.186, f32[256]{0:T(256)S(1)} %bitcast.201, f32[256]{0:T(256)S(1)} %bitcast.183, f32[256]{0:T(256)S(1)} %bitcast.199, f32[256]{0:T(256)S(1)} %bitcast.180, ...), kind=kLoop, calls=%fused_computation.42 | loop fusion | flops 4194304 | bytes 8667136 | tf_op jit(solution)/shard_map/convert.9
  86.6 1.9 collective-permute-start
  88.6 5.1 %collective-permute-start.3 = (bf16[258,512]{1,0:T(8,128)(2,1)}, bf16[258,512]{1,0:T(8,128)(2,1)}, u32[]{:S(2)}, u32[]{:S(2)}) collective-permute-start(bf16[258,512]{1,0:T(8,128)(2,1)} %pad_maximum_fusion), channel_id=1, source_target_pairs={{0,16},{4,20},{8,24},{12,28},{16,32},{20,36},{24,40},{28,44},{32,4... | collective-permute-start | bytes 792584 | tf_op jit(solution)/shard_map/ppermute | solution.py:14
  93.6 3.2 %collective-permute-start.2 = (bf16[258,512]{1,0:T(8,128)(2,1)}, bf16[258,512]{1,0:T(8,128)(2,1)}, u32[]{:S(2)}, u32[]{:S(2)}) collective-permute-start(bf16[258,512]{1,0:T(8,128)(2,1)} %pad_maximum_fusion), channel_id=1, source_target_pairs={{0,12},{4,16},{8,20},{12,24},{16,28},{20,32},{24,36},{28,40},{32,4... | collective-permute-start | bytes 792584 | tf_op jit(solution)/shard_map/ppermute | solution.py:14
  96.8 2.8 %collective-permute-start.1 = (bf16[258,512]{1,0:T(8,128)(2,1)}, bf16[258,512]{1,0:T(8,128)(2,1)}, u32[]{:S(2)}, u32[]{:S(2)}) collective-permute-start(bf16[258,512]{1,0:T(8,128)(2,1)} %pad_maximum_fusion), channel_id=1, source_target_pairs={{0,8},{4,12},{8,16},{12,20},{16,24},{20,28},{24,32},{28,36},{32,40... | collective-permute-start | bytes 792584 | tf_op jit(solution)/shard_map/ppermute | solution.py:14
  99.7 1.7 convolution_select_fusion
  102.2 2.0 fusion.42
  104.2 2.2 constant_dynamic-update-slice_fusion.6
  106.3 1.9 fusion.46
  108.3 2.2 constant_dynamic-update-slice_fusion.5
  110.4 1.9 fusion.47
  112.4 2.2 constant_dynamic-update-slice_fusion.4
  114.5 2.0 fusion.48
  116.5 2.3 %constant_dynamic-update-slice_fusion.3 = (f32[16,256,512]{2,1,0:T(8,128)}, f32[1,256,512]{2,1,0:T(8,128)S(1)}) fusion(f32[16,256,512]{2,1,0:T(8,128)} %fusion.48, f32[16,256,512]{2,1,0:T(8,128)} %fusion.5, f32[1,256,512]{2,1,0:T(8,128)S(1)} %get-tuple-element.50, f32[256]{0:T(256)S(1)} %bitcast.182, f32[256]{0:T(256)S(1)} %bitcast.198), kind=kLoop, calls=%fused_computation.104 | loop fusion | flops 524288 | bytes 2623488
  118.8 2.0 fusion.49
  120.8 2.2 constant_dynamic-update-slice_fusion.2
  122.9 1.9 fusion.50
  124.8 2.2 constant_dynamic-update-slice_fusion.1
  127.0 2.0 fusion.51
  129.0 2.2 constant_dynamic-update-slice_fusion
  131.1 2.0 add_dynamic-update-slice_fusion
  133.1 7.9 %multiply_add_fusion.1 = f32[16,64,512]{2,1,0:T(8,128)} fusion(f32[16,64,512]{2,1,0:T(8,128)S(1)} %fusion.66, f32[16,256,512]{2,1,0:T(8,128)} %add_dynamic-update-slice_fusion, f32[16,64,256]{2,0,1:T(8,128)S(1)} %copy-done.4, f32[16,64]{1,0:T(8,128)S(1)} %compare_convert_fusion.1), kind=kOutput, calls=%fused_computation.5 | convolution fusion | flops 806354944 | bytes 13635584 | tf_op jit(solution)/shard_map/ncd,ndv->ncv/dot_general | solution.py:81
  141.0 2.9 %copy.54 = f32[1024,512]{0,1:T(8,128)} copy(f32[1024,512]{1,0:T(8,128)} %bitcast.160) | data formatting | bytes 4194304 | tf_op jit(solution)/shard_map/reshape | solution.py:84
  156.0 4.8 %multiply_reduce_fusion = (f32[1024]{0:T(1024)S(1)}, f32[1024,512]{0,1:T(8,128)}) fusion(f32[1024,512]{0,1:T(8,128)} %copy.54, f32[1024]{0:T(1024)S(1)} %select_bitcast_fusion, f32[258,512]{1,0:T(8,128)S(1)} %convert_element_type.101, f32[258,512]{1,0:T(8,128)S(1)} %convert_element_type.98, f32[258,512]{1,0:T(8,128)S(1)} %convert_element_type.95, ...), kind=kOutput, calls=%fused_computation.3 | convolution fusion | flops 808975360 | bytes 8399872 | tf_op jit(solution)/shard_map/dot_general | solution.py:103
  160.8 10.3 %convolution_convert_fusion = bf16[1024,2048]{1,0:T(8,128)(2,1)} fusion(bf16[512,2048]{1,0:T(8,128)(2,1)S(1)} %copy-done, f32[1024,512]{0,1:T(8,128)} %get-tuple-element.92, f32[512]{0:T(512)S(1)} %copy-done.11, f32[1024]{0:T(1024)S(1)} %rsqrt_multiply_fusion, bf16[1024,2048]{1,0:T(8,128)(2,1)} %all-gather.2.cloned.1.call-done, bf16[2048,512]{1,0:T(8,128)(2,1)} %param.22), kind=kOutput, calls=%fused_computation | convolution fusion | flops 4301258752 | bytes 14686208 | tf_op jit(solution)/shard_map/dot_general | solution.py:109
  171.1 47.9 %reduce-scatter.2.cloned.1.call-done = bf16[1024,512]{1,0:T(8,128)(2,1)} async-done(((bf16[1024,2048]{1,0:T(8,128)(2,1)}), bf16[1024,512]{1,0:T(8,128)(2,1)}) %reduce-scatter.2.cloned.1.call-update) | async-done | bytes 1048592 | tf_op jit(solution)/shard_map/reduce_scatter | solution.py:110
  (80 shorter events, 21.3 us)
Async XLA Ops:
  6.5 154.2 %copy-start = (bf16[512,2048]{1,0:T(8,128)(2,1)S(1)}, bf16[512,2048]{1,0:T(8,128)(2,1)}, u32[]{:S(2)}) copy-start(bf16[512,2048]{1,0:T(8,128)(2,1)} %param.27) | copy-start | bytes 6291460
  6.5 59.2 %copy-start.9 = (bf16[2048,256]{1,0:T(8,128)(2,1)S(1)}, bf16[2048,256]{1,0:T(8,128)(2,1)}, u32[]{:S(2)}) copy-start(bf16[2048,256]{1,0:T(8,128)(2,1)} %param.20) | copy-start | bytes 3145732
  6.5 53.1 %all-gather.2.cloned.1.call-start = ((), (), s32[]{:S(2)}) async-start(), calls=%async_computation.1 | async-start | bytes 5242880 | tf_op jit(solution)/shard_map/all_gather | solution.py:34
  7.3 211.8 %reduce-scatter.2.cloned.1.call-start = ((), (), s32[]{:S(2)}) async-start(), calls=%async_computation.2 | async-start | bytes 5242880 | tf_op jit(solution)/shard_map/reduce_scatter | solution.py:110
  59.6 6.2 %copy-start.1 = (bf16[1024,2048]{1,0:T(8,128)(2,1)S(1)}, bf16[1024,2048]{1,0:T(8,128)(2,1)}, u32[]{:S(2)}) copy-start(bf16[1024,2048]{1,0:T(8,128)(2,1)} %all-gather.2.cloned.1.call-done) | copy-start | bytes 12582916
  63.1 4.2 %copy-start.10 = (bf16[2048,256]{1,0:T(8,128)(2,1)S(1)}, bf16[2048,256]{1,0:T(8,128)(2,1)}, u32[]{:S(2)}) copy-start(bf16[2048,256]{1,0:T(8,128)(2,1)} %param.19) | copy-start | bytes 3145732
  67.3 5.1 %copy-start.8 = (bf16[2048,512]{1,0:T(8,128)(2,1)S(1)}, bf16[2048,512]{1,0:T(8,128)(2,1)}, u32[]{:S(2)}) copy-start(bf16[2048,512]{1,0:T(8,128)(2,1)} %param.21) | copy-start | bytes 6291460
  68.6 6.2 %copy-start.7 = (f32[1024,256]{1,0:T(8,128)}, f32[1024,256]{1,0:T(8,128)S(1)}, u32[]{:S(2)}) copy-start(f32[1024,256]{1,0:T(8,128)S(1)} %fusion.1) | copy-start | bytes 3145732
  74.8 1.0 copy-start.2
  81.9 17.8 %copy-start.5 = (f32[16,64,256]{2,0,1:T(8,128)S(1)}, f32[16,64,256]{2,0,1:T(8,128)}, u32[]{:S(2)}) copy-start(f32[16,64,256]{2,0,1:T(8,128)} %get-tuple-element.58) | copy-start | bytes 3145732
  81.9 17.8 %copy-start.6 = (f32[16,64,256]{2,0,1:T(8,128)S(1)}, f32[16,64,256]{2,0,1:T(8,128)}, u32[]{:S(2)}) copy-start(f32[16,64,256]{2,0,1:T(8,128)} %get-tuple-element.59) | copy-start | bytes 3145732
  81.9 19.5 %copy-start.3 = (bf16[1024,512]{1,0:T(8,128)(2,1)S(1)}, bf16[1024,512]{1,0:T(8,128)(2,1)}, u32[]{:S(2)}) copy-start(bf16[1024,512]{1,0:T(8,128)(2,1)} %copy-done.2) | copy-start | bytes 3145732
  86.6 57.3 %collective-permute-start = (bf16[258,512]{1,0:T(8,128)(2,1)}, bf16[258,512]{1,0:T(8,128)(2,1)S(1)}, u32[]{:S(2)}, u32[]{:S(2)}) collective-permute-start(bf16[258,512]{1,0:T(8,128)(2,1)} %pad_maximum_fusion), channel_id=1, source_target_pairs={{0,4},{4,8},{8,12},{12,16},{16,20},{20,24},{24,28},{28,32},{32,36}... | collective-permute-start | bytes 792584 | tf_op jit(solution)/shard_map/ppermute | solution.py:14
  88.6 57.9 %collective-permute-start.3 = (bf16[258,512]{1,0:T(8,128)(2,1)}, bf16[258,512]{1,0:T(8,128)(2,1)}, u32[]{:S(2)}, u32[]{:S(2)}) collective-permute-start(bf16[258,512]{1,0:T(8,128)(2,1)} %pad_maximum_fusion), channel_id=1, source_target_pairs={{0,16},{4,20},{8,24},{12,28},{16,32},{20,36},{24,40},{28,44},{32,4... | collective-permute-start | bytes 792584 | tf_op jit(solution)/shard_map/ppermute | solution.py:14
  93.6 50.9 %collective-permute-start.2 = (bf16[258,512]{1,0:T(8,128)(2,1)}, bf16[258,512]{1,0:T(8,128)(2,1)}, u32[]{:S(2)}, u32[]{:S(2)}) collective-permute-start(bf16[258,512]{1,0:T(8,128)(2,1)} %pad_maximum_fusion), channel_id=1, source_target_pairs={{0,12},{4,16},{8,20},{12,24},{16,28},{20,32},{24,36},{28,40},{32,4... | collective-permute-start | bytes 792584 | tf_op jit(solution)/shard_map/ppermute | solution.py:14
  96.8 52.2 %collective-permute-start.1 = (bf16[258,512]{1,0:T(8,128)(2,1)}, bf16[258,512]{1,0:T(8,128)(2,1)}, u32[]{:S(2)}, u32[]{:S(2)}) collective-permute-start(bf16[258,512]{1,0:T(8,128)(2,1)} %pad_maximum_fusion), channel_id=1, source_target_pairs={{0,8},{4,12},{8,16},{12,20},{16,24},{20,28},{24,32},{28,36},{32,40... | collective-permute-start | bytes 792584 | tf_op jit(solution)/shard_map/ppermute | solution.py:14
  116.5 16.6 %copy-start.4 = (f32[16,64,256]{2,0,1:T(8,128)S(1)}, f32[16,64,256]{2,0,1:T(8,128)}, u32[]{:S(2)}) copy-start(f32[16,64,256]{2,0,1:T(8,128)} %get-tuple-element.60) | copy-start | bytes 3145732
  141.0 19.8 %copy-start.11 = (f32[512]{0:T(512)S(1)}, f32[512]{0:T(512)}, u32[]{:S(2)}) copy-start(f32[512]{0:T(512)} %param.26) | copy-start | bytes 6148
Sparse Core Ops, SparseCore 0:
  9.0 50.5 all-gather.1
  171.2 47.7 reduce-scatter.1

commit v4 on v3

--- a/solution.py
+++ b/solution.py
@@ -12,6 +12,52 @@
 def shifted(x, axis, shift, devices):
     pairs = [(i, i + shift) for i in range(devices - shift)]
     return lax.ppermute(x, axis, pairs)
+
+
+def ring(x, step):
+    size = lax.axis_size("tensor")
+    return lax.ppermute(x, "tensor", [(i, (i + step) % size) for i in range(size)])
+
+
+def gathered_blocks(local):
+    half = local.shape[0] // 2
+    from_left = ring(local, 1)
+    from_right = ring(local, -1)
+    far = jnp.concatenate([ring(from_left[:half], 1), ring(from_right[half:], -1)])
+    return ((0, local), (-1, from_left), (1, from_right), (2, far))
+
+
+def block_dot(blocks_in, weight):
+    size = lax.axis_size("tensor")
+    index = lax.axis_index("tensor")
+    width = blocks_in[0][1].shape[1]
+    total = None
+    for offset, block in blocks_in:
+        rows = lax.dynamic_slice_in_dim(weight, ((index + offset) % size) * width, width, 0)
+        term = jnp.dot(block, rows, preferred_element_type=jnp.float32)
+        total = term if total is None else total + term
+    return total
+
+
+def scattered_sum(gated, w_out):
+    size = lax.axis_size("tensor")
+    index = lax.axis_index("tensor")
+    width = w_out.shape[1] // size
+
+    def term(offset):
+        cols = lax.dynamic_slice_in_dim(w_out, ((index + offset) % size) * width, width, 1)
+        return jnp.dot(gated, cols, preferred_element_type=jnp.float32).astype(jnp.bfloat16)
+
+    half = gated.shape[0] // 2
+    far = term(2)
+    far_from_left = ring(far[:half], 1)
+    far_from_right = ring(far[half:], -1)
+    from_left = ring(term(1), 1)
+    from_right = ring(term(-1), -1)
+    relayed = jnp.concatenate([ring(far_from_left, 1), ring(far_from_right, -1)])
+    total = term(0).astype(jnp.float32) + from_left.astype(jnp.float32)
+    total = total + from_right.astype(jnp.float32) + relayed.astype(jnp.float32)
+    return total
 
 
 def body(
@@ -31,9 +77,9 @@
     key_width = w_query.shape[1]
     value_width = w_value.shape[1]
     weights = (w_query, w_key, w_value, w_outgate, w_gate_down)
-    piece = lax.all_gather(hidden_in, "tensor", axis=1, tiled=True)
+    blocks_in = gathered_blocks(hidden_in)
     query_sum, key_sum, value_sum, outgate, low = tuple(
-        (jnp.dot(piece, weight, preferred_element_type=jnp.float32) for weight in weights)
+        (block_dot(blocks_in, weight) for weight in weights)
     )
     query = query_sum.astype(jnp.bfloat16)
     key = key_sum.astype(jnp.bfloat16)
@@ -72,15 +118,14 @@
     chunk_states = jnp.einsum("ncd,ncv->ndv", k_decayed, v_float, precision=HIGH)
     chunk_decay = jnp.exp(block_totals) * live_blocks[:, -1:]
 
-    entering = [jnp.zeros((key_width, value_width), jnp.float32)]
+    q_decayed = q_float * jnp.exp(cumul)
+    entering = jnp.zeros((key_width, value_width), jnp.float32)
+    inters = []
     for n in range(blocks):
-        entering.append(chunk_decay[n][:, None] * entering[-1] + chunk_states[n])
-    final_state = entering[-1]
-    entering = jnp.stack(entering[:-1])
-    inter = (
-        jnp.einsum("ncd,ndv->ncv", q_float * jnp.exp(cumul), entering, precision=HIGH)
-        * live_blocks[:, :, None]
-    )
+        inters.append(jnp.dot(q_decayed[n], entering, precision=HIGH))
+        entering = chunk_decay[n][:, None] * entering + chunk_states[n]
+    final_state = entering
+    inter = jnp.stack(inters) * live_blocks[:, :, None]
     local_out = (intra + inter).reshape(tok_rows, value_width)
 
     devices = lax.axis_size("req")
@@ -106,10 +151,7 @@
     attn = (local_out + carried * (live_device * linked)[:, None]) * key_width ** (-0.5)
     normed = attn * lax.rsqrt(jnp.mean(attn * attn, axis=-1, keepdims=True) + 1e-05) * norm_gain
     gated = (normed * jax.nn.silu(outgate)).astype(jnp.bfloat16)
-    head_term = jnp.dot(gated, w_out, preferred_element_type=jnp.float32)
-    return lax.psum_scatter(
-        head_term.astype(jnp.bfloat16), "tensor", scatter_dimension=1, tiled=True
-    )
+    return scattered_sum(gated, w_out).astype(jnp.bfloat16)
 
 
 def solution(mesh):

time: 228 us -> 188 us (0.82)
  waiting for transfers between devices: 93 us -> 42.8 us
  other arithmetic: 44.5 us -> 16.5 us
  matrix products: 41.5 us -> 65.1 us
  starting transfers between devices: 13 us -> 31.7 us
  between operations: 20 us -> 6.93 us
  local copies, waits for them, and re-layouts: 13.8 us -> 23.7 us
    reduce_scatter x1 -> x0, waiting for transfers between devices: 47.9 us -> none  [body(): lax.psum_scatter(head_term.astype(jnp.bfloat16), 'tensor', scatter_dimens...]
    all_gather x1 -> x0, waiting for transfers between devices: 44.3 us -> none  [body(): piece = lax.all_gather(hidden_in, 'tensor', axis=1, tiled=True)]
    ppermute x0 -> x10, waiting for transfers between devices: none -> 42.8 us  [ring(): lax.ppermute(x, 'tensor', [(i, (i + step) % size) for i in range(size)])]
    unnamed x14 -> x0, other arithmetic: 29 us -> none
    dot_general x6 -> x40, matrix products: 26.6 us -> 51.3 us  [the longest x20 42.1 us: block_dot(): term = jnp.dot(block, rows, preferred_element_type=jnp.float32)]
    ppermute x0 -> x10, starting transfers between devices: none -> 16.7 us  [ring(): lax.ppermute(x, 'tensor', [(i, (i + step) % size) for i in range(size)])]
    convert_element_type x0 -> x2, local copies, waits for them, and re-layouts: none -> 4.1 us  [the longest x1 2.52 us: body(): q_float = query.astype(jnp.float32).reshape(blocks, GROUP, key_width)]
    reshape x0 -> x1, local copies, waits for them, and re-layouts: none -> 2.73 us  [body(): k_float = key.astype(jnp.float32).reshape(blocks, GROUP, key_width)]
  transfers between devices with their start and end apart: 6 -> 14, of which waited for: 2 -> 3; matrix products, arithmetic and copies ran while one was open for 24% -> 29% of each run, Pallas kernels for 0% -> 0%
where the time goes in v4:
time: 188 us; the launch traced here: 187 us
  matrix products  65.1 us (35%)
  waiting for transfers between devices  42.8 us (23%)
  starting transfers between devices  31.7 us (17%)
  local copies, waits for them, and re-layouts  23.7 us (13%)
  other arithmetic  16.5 us (9%)
  between operations  6.93 us (4%)
    ppermute x10, waiting for transfers between devices, ring(): lax.ppermute(x, 'tensor', [(i, (i + step) % size) for i in range(size)])  42.8 us
    dot_general x20, matrix products, block_dot(): term = jnp.dot(block, rows, preferred_element_type=jnp.float32)  42.1 us
    ppermute x10, starting transfers between devices, ring(): lax.ppermute(x, 'tensor', [(i, (i + step) % size) for i in range(size)])  16.7 us
    ppermute x4, starting transfers between devices, shifted(): return lax.ppermute(x, axis, pairs)  15 us
    dot_general x1, matrix products, body(): jnp.einsum('ncd,ncv->ndv', k_decayed, v_float, precision=HIGH)  5.73 us
    dot_general x16, matrix products, body(): inters.append(jnp.dot(q_decayed[n], entering, precision=HIGH))  5.06 us
    mul x1, other arithmetic, body(): q_scaled = q_float * jnp.exp(cumul - centre[:, None, :])  4.76 us
    another operation x4, other arithmetic  4.37 us
  transfers between devices with their start and end apart: 14, of which 3 were waited for; matrix products, arithmetic and copies ran while one was open for 29% of the time, Pallas kernels for 0%

profile of v4, /device:TPU:2, one launch (start us, length us, event | category | flops | bytes accessed | tf_op | source)
XLA Modules:
  0.0 186.8 jit_solution(16871772410497039624)
XLA Ops:
  6.5 2.8 %fusion.124 = f32[256,1024]{1,0:T(8,128)} fusion(bf16[1024,512]{1,0:T(8,128)(2,1)} %param.17, bf16[2048,256]{1,0:T(8,128)(2,1)} %param.19, s32[]{:T(128)S(6)} %select_n.101), kind=kOutput, calls=%fused_computation.190 | convolution fusion | flops 268435456 | bytes 2359300 | tf_op jit(solution)/shard_map/dot_general | solution.py:37
  14.7 1.9 %fusion.118 = f32[256,1024]{1,0:T(8,128)S(1)} fusion(bf16[1024,512]{1,0:T(8,128)(2,1)} %param.17, bf16[2048,256]{1,0:T(8,128)(2,1)} %param.20, s32[]{:T(128)S(6)} %select_n.101), kind=kOutput, calls=%fused_computation.184 | convolution fusion | flops 268435456 | bytes 2359300 | tf_op jit(solution)/shard_map/dot_general | solution.py:37
  16.6 2.1 %fusion.105 = f32[512,1024]{1,0:T(8,128)} fusion(bf16[1024,512]{1,0:T(8,128)(2,1)S(1)} %copy-done.3, bf16[2048,512]{1,0:T(8,128)(2,1)S(1)} %copy-done, s32[]{:T(128)S(6)} %select_n.101), kind=kOutput, calls=%fused_computation.169 | convolution fusion | flops 536870912 | bytes 3670020 | tf_op jit(solution)/shard_map/dot_general | solution.py:37
  18.7 2.2 %fusion.93 = f32[512,1024]{1,0:T(8,128)} fusion(bf16[1024,512]{1,0:T(8,128)(2,1)S(1)} %copy-done.3, bf16[2048,512]{1,0:T(8,128)(2,1)S(1)} %copy-done.19, s32[]{:T(128)S(6)} %select_n.101), kind=kOutput, calls=%fused_computation.145 | convolution fusion | flops 536870912 | bytes 3670020 | tf_op jit(solution)/shard_map/dot_general | solution.py:37
  20.9 5.6 %collective-permute-done = bf16[1024,512]{1,0:T(8,128)(2,1)} collective-permute-done((bf16[1024,512]{1,0:T(8,128)(2,1)}, bf16[1024,512]{1,0:T(8,128)(2,1)}, u32[]{:S(2)}, u32[]{:S(2)}) %collective-permute-start) | collective-permute-done | bytes 1048608 | tf_op jit(solution)/shard_map/ppermute | solution.py:19
  28.0 3.0 %collective-permute-start.3 = (bf16[512,512]{1,0:T(8,128)(2,1)S(1)}, bf16[512,512]{1,0:T(8,128)(2,1)S(1)}, u32[]{:S(2)}, u32[]{:S(2)}) collective-permute-start(bf16[512,512]{1,0:T(8,128)(2,1)S(1)} %slice.412), channel_id=1, source_target_pairs={{0,3},{1,0},{2,1},{3,2},{4,7},{5,4},{6,5},{7,6},{8,11},{9,8},{10,9... | collective-permute-start | bytes 1572872 | tf_op jit(solution)/shard_map/ppermute | solution.py:19
  31.0 3.3 %fusion.103 = f32[512,1024]{1,0:T(8,128)} fusion(bf16[1024,512]{1,0:T(8,128)(2,1)} %collective-permute-done, bf16[2048,512]{1,0:T(8,128)(2,1)S(1)} %copy-done, s32[]{:T(128)S(6)} %select_n.103), kind=kOutput, calls=%fused_computation.167 | convolution fusion | flops 536870912 | bytes 3670020 | tf_op jit(solution)/shard_map/dot_general | solution.py:37
  34.3 3.3 %fusion.91 = f32[512,1024]{1,0:T(8,128)} fusion(bf16[1024,512]{1,0:T(8,128)(2,1)} %collective-permute-done, bf16[2048,512]{1,0:T(8,128)(2,1)S(1)} %copy-done.19, s32[]{:T(128)S(6)} %select_n.103), kind=kOutput, calls=%fused_computation.143 | convolution fusion | flops 536870912 | bytes 3670020 | tf_op jit(solution)/shard_map/dot_general | solution.py:37
  37.6 2.1 %fusion.101 = f32[512,1024]{1,0:T(8,128)} fusion(bf16[1024,512]{1,0:T(8,128)(2,1)S(1)} %collective-permute-done.1, bf16[2048,512]{1,0:T(8,128)(2,1)S(1)} %copy-done, s32[]{:T(128)S(6)} %select_n.105), kind=kOutput, calls=%fused_computation.165 | convolution fusion | flops 536870912 | bytes 3670020 | tf_op jit(solution)/shard_map/dot_general | solution.py:37
  39.7 2.1 %fusion.89 = f32[512,1024]{1,0:T(8,128)} fusion(bf16[1024,512]{1,0:T(8,128)(2,1)S(1)} %collective-permute-done.1, bf16[2048,512]{1,0:T(8,128)(2,1)S(1)} %copy-done.19, s32[]{:T(128)S(6)} %select_n.105), kind=kOutput, calls=%fused_computation.141 | convolution fusion | flops 536870912 | bytes 3670020 | tf_op jit(solution)/shard_map/dot_general | solution.py:37
  45.3 2.8 %convolution_add_fusion.2 = f32[256,1024]{1,0:T(8,128)} fusion(f32[256,1024]{1,0:T(8,128)S(1)} %fusion.118, bf16[1024,512]{1,0:T(8,128)(2,1)} %collective-permute-done, bf16[2048,256]{1,0:T(8,128)(2,1)S(1)} %copy-done.21, s32[]{:T(128)S(6)} %select_n.103), kind=kOutput, calls=%fused_computation.18 | convolution fusion | flops 268697600 | bytes 3407876 | tf_op jit(solution)/shard_map/dot_general | solution.py:37
  55.5 2.5 %copy.51 = f32[1024,256]{1,0:T(8,128)} copy(f32[1024,256]{0,1:T(8,128)} %fusion.7) | data formatting | bytes 2097152 | tf_op jit(solution)/shard_map/convert_element_type | solution.py:102
  58.0 3.1 %fusion.9 = f32[1024,256]{0,1:T(8,128)} fusion(f32[1024,256]{0,1:T(8,128)} %fusion.114, f32[256,1024]{1,0:T(8,128)} %convolution_add_fusion.2, bf16[1024,512]{1,0:T(8,128)(2,1)S(1)} %collective-permute-done.1, bf16[2048,256]{1,0:T(8,128)(2,1)} %param.20, s32[]{:T(128)S(6)} %select_n.105), kind=kOutput, calls=%fused_computation.26 | convolution fusion | flops 269484032 | bytes 4456452 | tf_op jit(solution)/shard_map/dot_general | solution.py:37
  61.2 2.7 %copy.55 = f32[1024,256]{1,0:T(8,128)} copy(f32[1024,256]{0,1:T(8,128)} %fusion.9) | data formatting | bytes 2097152 | tf_op jit(solution)/shard_map/reshape | solution.py:103
  63.9 4.6 %fusion = bf16[1024,512]{0,1:T(8,128)(2,1)} fusion(f32[512,1024]{1,0:T(8,128)} %fusion.101, f32[512,1024]{1,0:T(8,128)} %fusion.105, f32[512,1024]{1,0:T(8,128)} %fusion.103, bf16[1024,512]{1,0:T(8,128)(2,1)S(1)} %copy-done.5, bf16[2048,512]{1,0:T(8,128)(2,1)S(1)} %copy-done, s32[]{:T(128)S(6)} %select_n.107), kind=kOutput, calls=%fused_computation.3 | convolution fusion | flops 538968064 | bytes 8912900 | tf_op jit(solution)/shard_map/dot_general | solution.py:37
  70.2 4.8 %exponential_multiply_fusion.2 = (f32[16,64,256]{2,0,1:T(8,128)}, f32[16,64,256]{2,0,1:T(8,128)}, f32[16,64,256]{2,0,1:T(8,128)S(1)}, f32[16,64,256]{2,0,1:T(8,128)}, f32[16,64,256]{2,0,1:T(8,128)S(1)}) fusion(f32[16,64,256]{2,0,1:T(8,128)S(1)} %copy-done.10, f32[16,64,256]{2,1,0:T(8,128)} %bitcast.361, f32[16,256]{1,0:T(8,128)S(1)} %get-tuple-element.59, ...), kind=kLoop, calls=%fused_computation.77 | loop fusion | flops 2359296 | bytes 8441856 | tf_op jit(solution)/shard_map/mul | solution.py:109
  75.6 5.7 %fusion.30 = f32[16,256,512]{2,1,0:T(8,128)} fusion(bf16[16,64,512]{2,1,0:T(8,128)(2,1)S(1)} %bitcast.356, f32[16,64,256]{2,0,1:T(8,128)S(1)} %get-tuple-element.52), kind=kOutput, calls=%fused_computation.66 | convolution fusion | flops 805306368 | bytes 10485760 | tf_op jit(solution)/shard_map/ncd,ncv->ndv/dot_general | solution.py:118
  81.5 4.0 %fusion.48 = bf16[256,512]{1,0:T(8,128)(2,1)S(1)} fusion(f32[16,256,512]{2,1,0:T(8,128)} %fusion.30, f32[256]{0:T(256)S(1)} %bitcast.364, f32[256]{0:T(256)S(1)} %bitcast.397, f32[256]{0:T(256)S(1)} %bitcast.382, f32[256]{0:T(256)S(1)} %bitcast.395, f32[256]{0:T(256)S(1)} %bitcast.379, f32[256]{0:T(256)S(1)} %bitcast.393, f32[256]{0:T(256)S(1)} %bitcast.376, ...), kind=kLoop, calls=%fused_computation.89 | loop fusion | flops 4194304 | bytes 8667136 | tf_op jit(solution)/shard_map/convert.9
  86.2 3.9 %collective-permute-start.5 = (bf16[258,512]{1,0:T(8,128)(2,1)}, bf16[258,512]{1,0:T(8,128)(2,1)S(1)}, u32[]{:S(2)}, u32[]{:S(2)}) collective-permute-start(bf16[258,512]{1,0:T(8,128)(2,1)} %pad_maximum_fusion), channel_id=1, source_target_pairs={{0,8},{4,12},{8,16},{12,20},{16,24},{20,28},{24,32},{28,36},{32,40... | collective-permute-start | bytes 792584 | tf_op jit(solution)/shard_map/ppermute | solution.py:14
  90.2 1.9 %collective-permute-start.4 = (bf16[258,512]{1,0:T(8,128)(2,1)}, bf16[258,512]{1,0:T(8,128)(2,1)}, u32[]{:S(2)}, u32[]{:S(2)}) collective-permute-start(bf16[258,512]{1,0:T(8,128)(2,1)} %pad_maximum_fusion), channel_id=1, source_target_pairs={{0,4},{4,8},{8,12},{12,16},{16,20},{20,24},{24,28},{28,32},{32,36}... | collective-permute-start | bytes 792584 | tf_op jit(solution)/shard_map/ppermute | solution.py:14
  92.1 5.2 %collective-permute-start.6 = (bf16[258,512]{1,0:T(8,128)(2,1)}, bf16[258,512]{1,0:T(8,128)(2,1)}, u32[]{:S(2)}, u32[]{:S(2)}) collective-permute-start(bf16[258,512]{1,0:T(8,128)(2,1)} %pad_maximum_fusion), channel_id=1, source_target_pairs={{0,12},{4,16},{8,20},{12,24},{16,28},{20,32},{24,36},{28,40},{32,4... | collective-permute-start | bytes 792584 | tf_op jit(solution)/shard_map/ppermute | solution.py:14
  97.3 4.0 %collective-permute-start.7 = (bf16[258,512]{1,0:T(8,128)(2,1)}, bf16[258,512]{1,0:T(8,128)(2,1)}, u32[]{:S(2)}, u32[]{:S(2)}) collective-permute-start(bf16[258,512]{1,0:T(8,128)(2,1)} %pad_maximum_fusion), channel_id=1, source_target_pairs={{0,16},{4,20},{8,24},{12,28},{16,32},{20,36},{24,40},{28,44},{32,4... | collective-permute-start | bytes 792584 | tf_op jit(solution)/shard_map/ppermute | solution.py:14
  110.4 2.2 %multiply_add_fusion.1 = f32[16,64,512]{2,1,0:T(8,128)} fusion(f32[16,64,512]{2,1,0:T(8,128)S(1)} %fusion.10, f32[16,64,64]{2,1,0:T(8,128)S(1)} %convolution_select_fusion, bf16[16,64,512]{2,1,0:T(8,128)(2,1)S(1)} %bitcast.357, f32[16,64]{1,0:T(8,128)S(1)} %compare_convert_fusion.1), kind=kOutput, calls=%fused_computation.8 | convolution fusion | flops 202375168 | bytes 5509120 | tf_op jit(solution)/shard_map/ncs,nsv->ncv/dot_general | solution.py:114
  112.6 2.7 %copy.68 = f32[1024,256]{0,1:T(8,128)} copy(f32[1024,256]{1,0:T(8,128)} %bitcast.360) | data formatting | bytes 2097152 | tf_op jit(solution)/shard_map/add | solution.py:100
  129.6 3.0 %multiply_reduce_fusion = (f32[1024]{0:T(1024)S(1)}, f32[1024,512]{0,1:T(8,128)S(1)}) fusion(f32[1024,512]{0,1:T(8,128)S(1)} %copy-done.8, f32[1024]{0:T(1024)S(1)} %select_bitcast_fusion, f32[258,512]{1,0:T(8,128)S(1)} %convert_element_type.125, f32[258,512]{1,0:T(8,128)S(1)} %convert_element_type.122, f32[258,512]{1,0:T(8,128)S(1)} %convert_element_type.119, ...), kind=kOutput, calls=%fused_computation.6 | convolution fusion | flops 808975360 | bytes 8399872 | tf_op jit(solution)/shard_map/dot_general | solution.py:148
  132.7 2.5 %multiply_convert_fusion = bf16[1024,512]{0,1:T(8,128)(2,1)S(1)} fusion(f32[512,1024]{1,0:T(8,128)S(1)} %copy-done.18, f32[512,1024]{1,0:T(8,128)S(1)} %copy-done.16, f32[512,1024]{1,0:T(8,128)S(1)} %copy-done.17, f32[1024,512]{0,1:T(8,128)S(1)} %get-tuple-element.103, f32[512]{0:T(512)S(1)} %copy-done.25, f32[1024]{0:T(1024)S(1)} %rsqrt_multiply_fusion, ...), kind=kOutput, calls=%fused_computation.5 | convolution fusion | flops 542638080 | bytes 11016196 | tf_op jit(solution)/shard_map/dot_general | solution.py:37
  137.1 3.2 %collective-permute-start.12 = (bf16[512,512]{1,0:T(8,128)(2,1)S(1)}, bf16[512,512]{1,0:T(8,128)(2,1)S(1)}, u32[]{:S(2)}, u32[]{:S(2)}) collective-permute-start(bf16[512,512]{1,0:T(8,128)(2,1)S(1)} %get-tuple-element.55), channel_id=1, source_target_pairs={{0,3},{1,0},{2,1},{3,2},{4,7},{5,4},{6,5},{7,6},{8,11},{9,8},{10,9... | collective-permute-start | bytes 1572872 | tf_op jit(solution)/shard_map/ppermute | solution.py:19
  141.2 3.2 %collective-permute-start.9 = (bf16[1024,512]{1,0:T(8,128)(2,1)S(1)}, bf16[1024,512]{1,0:T(8,128)(2,1)S(1)}, u32[]{:S(2)}, u32[]{:S(2)}) collective-permute-start(bf16[1024,512]{1,0:T(8,128)(2,1)S(1)} %convolution_convert_fusion.1), channel_id=1, source_target_pairs={{0,3},{1,0},{2,1},{3,2},{4,7},{5,4},{6,5},{7,6},{8,11},{9,8},{10,9... | collective-permute-start | bytes 3145736 | tf_op jit(solution)/shard_map/ppermute | solution.py:19
  144.4 8.7 %collective-permute-done.10 = bf16[512,512]{1,0:T(8,128)(2,1)S(1)} collective-permute-done((bf16[512,512]{1,0:T(8,128)(2,1)S(1)}, bf16[512,512]{1,0:T(8,128)(2,1)S(1)}, u32[]{:S(2)}, u32[]{:S(2)}) %collective-permute-start.10) | collective-permute-done | bytes 524320 | tf_op jit(solution)/shard_map/ppermute | solution.py:19
  153.1 3.2 %collective-permute-start.13 = (bf16[512,512]{1,0:T(8,128)(2,1)S(1)}, bf16[512,512]{1,0:T(8,128)(2,1)S(1)}, u32[]{:S(2)}, u32[]{:S(2)}) collective-permute-start(bf16[512,512]{1,0:T(8,128)(2,1)S(1)} %collective-permute-done.12), channel_id=1, source_target_pairs={{0,3},{1,0},{2,1},{3,2},{4,7},{5,4},{6,5},{7,6},{8,11},{9,8},{10,9... | collective-permute-start | bytes 1572872 | tf_op jit(solution)/shard_map/ppermute | solution.py:19
  156.3 28.5 %collective-permute-done.11 = bf16[512,512]{1,0:T(8,128)(2,1)S(1)} collective-permute-done((bf16[512,512]{1,0:T(8,128)(2,1)S(1)}, bf16[512,512]{1,0:T(8,128)(2,1)S(1)}, u32[]{:S(2)}, u32[]{:S(2)}) %collective-permute-start.11) | collective-permute-done | bytes 524320 | tf_op jit(solution)/shard_map/ppermute | solution.py:19
  184.8 1.9 %add_convert_fusion = bf16[1024,512]{1,0:T(8,128)(2,1)} fusion(bf16[1024,512]{1,0:T(8,128)(2,1)S(1)} %collective-permute-done.9, bf16[1024,512]{1,0:T(8,128)(2,1)S(1)} %collective-permute-done.8, bf16[512,512]{1,0:T(8,128)(2,1)S(1)} %collective-permute-done.13, bf16[512,512]{1,0:T(8,128)(2,1)S(1)} %collective-permute-done.11, ...), kind=kOutput, calls=%fused_computation.4 | convolution fusion | flops 543162368 | bytes 5767172 | tf_op jit(solution)/shard_map/dot_general | solution.py:49
  (152 shorter events, 47.0 us)
Async XLA Ops:
  0.0 16.6 %copy-start = (bf16[2048,512]{1,0:T(8,128)(2,1)S(1)}, bf16[2048,512]{1,0:T(8,128)(2,1)}, u32[]{:S(2)}) copy-start(bf16[2048,512]{1,0:T(8,128)(2,1)} %param.21) | copy-start | bytes 6291460
  0.0 26.5 %collective-permute-start = (bf16[1024,512]{1,0:T(8,128)(2,1)}, bf16[1024,512]{1,0:T(8,128)(2,1)}, u32[]{:S(2)}, u32[]{:S(2)}) collective-permute-start(bf16[1024,512]{1,0:T(8,128)(2,1)} %param.17), channel_id=1, source_target_pairs={{0,1},{1,2},{2,3},{3,0},{4,5},{5,6},{6,7},{7,4},{8,9},{9,10},{10,1... | collective-permute-start | bytes 3145736 | tf_op jit(solution)/shard_map/ppermute | solution.py:19
  1.6 26.4 %collective-permute-start.1 = (bf16[1024,512]{1,0:T(8,128)(2,1)}, bf16[1024,512]{1,0:T(8,128)(2,1)S(1)}, u32[]{:S(2)}, u32[]{:S(2)}) collective-permute-start(bf16[1024,512]{1,0:T(8,128)(2,1)} %param.17), channel_id=1, source_target_pairs={{0,3},{1,0},{2,1},{3,2},{4,7},{5,4},{6,5},{7,6},{8,11},{9,8},{10,9... | collective-permute-start | bytes 3145736 | tf_op jit(solution)/shard_map/ppermute | solution.py:19
  14.5 2.1 %copy-start.3 = (bf16[1024,512]{1,0:T(8,128)(2,1)S(1)}, bf16[1024,512]{1,0:T(8,128)(2,1)}, u32[]{:S(2)}) copy-start(bf16[1024,512]{1,0:T(8,128)(2,1)} %param.17) | copy-start | bytes 3145732
  16.6 2.1 %copy-start.19 = (bf16[2048,512]{1,0:T(8,128)(2,1)S(1)}, bf16[2048,512]{1,0:T(8,128)(2,1)}, u32[]{:S(2)}) copy-start(bf16[2048,512]{1,0:T(8,128)(2,1)} %param.22) | copy-start | bytes 6291460
  27.6 20.5 %collective-permute-start.2 = (bf16[512,512]{1,0:T(8,128)(2,1)S(1)}, bf16[512,512]{1,0:T(8,128)(2,1)S(1)}, u32[]{:S(2)}, u32[]{:S(2)}) collective-permute-start(bf16[512,512]{1,0:T(8,128)(2,1)S(1)} %slice.411), channel_id=1, source_target_pairs={{0,1},{1,2},{2,3},{3,0},{4,5},{5,6},{6,7},{7,4},{8,9},{9,10},{10,1... | collective-permute-start | bytes 1572872 | tf_op jit(solution)/shard_map/ppermute | solution.py:19
  28.0 20.1 %collective-permute-start.3 = (bf16[512,512]{1,0:T(8,128)(2,1)S(1)}, bf16[512,512]{1,0:T(8,128)(2,1)S(1)}, u32[]{:S(2)}, u32[]{:S(2)}) collective-permute-start(bf16[512,512]{1,0:T(8,128)(2,1)S(1)} %slice.412), channel_id=1, source_target_pairs={{0,3},{1,0},{2,1},{3,2},{4,7},{5,4},{6,5},{7,6},{8,11},{9,8},{10,9... | collective-permute-start | bytes 1572872 | tf_op jit(solution)/shard_map/ppermute | solution.py:19
  41.8 3.4 %copy-start.21 = (bf16[2048,256]{1,0:T(8,128)(2,1)S(1)}, bf16[2048,256]{1,0:T(8,128)(2,1)}, u32[]{:S(2)}) copy-start(bf16[2048,256]{1,0:T(8,128)(2,1)} %param.20) | copy-start | bytes 3145732
  48.2 2.4 %copy-start.4 = (bf16[1024,512]{1,0:T(8,128)(2,1)}, bf16[1024,512]{1,0:T(8,128)(2,1)S(1)}, u32[]{:S(2)}) copy-start(bf16[1024,512]{1,0:T(8,128)(2,1)S(1)} %constant_dynamic-update-slice_fusion) | copy-start | bytes 3145732
  61.1 2.7 %copy-start.5 = (bf16[1024,512]{1,0:T(8,128)(2,1)S(1)}, bf16[1024,512]{1,0:T(8,128)(2,1)}, u32[]{:S(2)}) copy-start(bf16[1024,512]{1,0:T(8,128)(2,1)} %copy-done.4) | copy-start | bytes 3145732
  75.6 5.7 %copy-start.11 = (f32[16,64,256]{2,1,0:T(8,128)}, f32[16,64,256]{2,1,0:T(8,128)S(1)}, u32[]{:S(2)}) copy-start(f32[16,64,256]{2,1,0:T(8,128)S(1)} %copy.67) | copy-start | bytes 3145732
  81.5 19.8 %copy-start.2 = (f32[16,256,512]{2,1,0:T(8,128)S(1)}, f32[16,256,512]{2,1,0:T(8,128)}, u32[]{:S(2)}) copy-start(f32[16,256,512]{2,1,0:T(8,128)} %fusion.30) | copy-start | bytes 25165828
  86.2 16.2 %copy-start.15 = (f32[16,64,256]{2,0,1:T(8,128)S(1)}, f32[16,64,256]{2,0,1:T(8,128)}, u32[]{:S(2)}) copy-start(f32[16,64,256]{2,0,1:T(8,128)} %get-tuple-element.49) | copy-start | bytes 3145732
  86.2 30.9 %collective-permute-start.5 = (bf16[258,512]{1,0:T(8,128)(2,1)}, bf16[258,512]{1,0:T(8,128)(2,1)S(1)}, u32[]{:S(2)}, u32[]{:S(2)}) collective-permute-start(bf16[258,512]{1,0:T(8,128)(2,1)} %pad_maximum_fusion), channel_id=1, source_target_pairs={{0,8},{4,12},{8,16},{12,20},{16,24},{20,28},{24,32},{28,36},{32,40... | collective-permute-start | bytes 792584 | tf_op jit(solution)/shard_map/ppermute | solution.py:14
  90.2 27.6 %collective-permute-start.4 = (bf16[258,512]{1,0:T(8,128)(2,1)}, bf16[258,512]{1,0:T(8,128)(2,1)}, u32[]{:S(2)}, u32[]{:S(2)}) collective-permute-start(bf16[258,512]{1,0:T(8,128)(2,1)} %pad_maximum_fusion), channel_id=1, source_target_pairs={{0,4},{4,8},{8,12},{12,16},{16,20},{20,24},{24,28},{28,32},{32,36}... | collective-permute-start | bytes 792584 | tf_op jit(solution)/shard_map/ppermute | solution.py:14
  92.1 28.3 %collective-permute-start.6 = (bf16[258,512]{1,0:T(8,128)(2,1)}, bf16[258,512]{1,0:T(8,128)(2,1)}, u32[]{:S(2)}, u32[]{:S(2)}) collective-permute-start(bf16[258,512]{1,0:T(8,128)(2,1)} %pad_maximum_fusion), channel_id=1, source_target_pairs={{0,12},{4,16},{8,20},{12,24},{16,28},{20,32},{24,36},{28,40},{32,4... | collective-permute-start | bytes 792584 | tf_op jit(solution)/shard_map/ppermute | solution.py:14
  97.3 25.7 %collective-permute-start.7 = (bf16[258,512]{1,0:T(8,128)(2,1)}, bf16[258,512]{1,0:T(8,128)(2,1)}, u32[]{:S(2)}, u32[]{:S(2)}) collective-permute-start(bf16[258,512]{1,0:T(8,128)(2,1)} %pad_maximum_fusion), channel_id=1, source_target_pairs={{0,16},{4,20},{8,24},{12,28},{16,32},{20,36},{24,40},{28,44},{32,4... | collective-permute-start | bytes 792584 | tf_op jit(solution)/shard_map/ppermute | solution.py:14
  112.6 2.7 %copy-start.7 = (f32[16,64,512]{2,1,0:T(8,128)S(1)}, f32[16,64,512]{2,1,0:T(8,128)}, u32[]{:S(2)}) copy-start(f32[16,64,512]{2,1,0:T(8,128)} %multiply_add_fusion.1) | copy-start | bytes 6291460
  117.1 12.4 %copy-start.6 = (f32[1024,256]{0,1:T(8,128)S(1)}, f32[1024,256]{0,1:T(8,128)}, u32[]{:S(2)}) copy-start(f32[1024,256]{0,1:T(8,128)} %fusion.7) | copy-start | bytes 3145732
  126.1 3.4 %copy-start.8 = (f32[1024,512]{0,1:T(8,128)S(1)}, f32[1024,512]{0,1:T(8,128)}, u32[]{:S(2)}) copy-start(f32[1024,512]{0,1:T(8,128)} %copy.69) | copy-start | bytes 6291460
  129.5 3.1 %copy-start.16 = (f32[512,1024]{1,0:T(8,128)S(1)}, f32[512,1024]{1,0:T(8,128)}, u32[]{:S(2)}) copy-start(f32[512,1024]{1,0:T(8,128)} %fusion.93) | copy-start | bytes 6291460
  129.5 3.1 %copy-start.17 = (f32[512,1024]{1,0:T(8,128)S(1)}, f32[512,1024]{1,0:T(8,128)}, u32[]{:S(2)}) copy-start(f32[512,1024]{1,0:T(8,128)} %fusion.91) | copy-start | bytes 6291460
  129.5 3.2 %copy-start.18 = (f32[512,1024]{1,0:T(8,128)S(1)}, f32[512,1024]{1,0:T(8,128)}, u32[]{:S(2)}) copy-start(f32[512,1024]{1,0:T(8,128)} %fusion.89) | copy-start | bytes 6291460
  129.5 3.2 %copy-start.25 = (f32[512]{0:T(512)S(1)}, f32[512]{0:T(512)}, u32[]{:S(2)}) copy-start(f32[512]{0:T(512)} %param.26) | copy-start | bytes 6148
  132.7 2.5 %copy-start.23 = (bf16[512,2048]{1,0:T(8,128)(2,1)S(1)}, bf16[512,2048]{1,0:T(8,128)(2,1)}, u32[]{:S(2)}) copy-start(bf16[512,2048]{1,0:T(8,128)(2,1)} %param.27) | copy-start | bytes 6291460
  136.8 16.3 %collective-permute-start.10 = (bf16[512,512]{1,0:T(8,128)(2,1)S(1)}, bf16[512,512]{1,0:T(8,128)(2,1)S(1)}, u32[]{:S(2)}, u32[]{:S(2)}) collective-permute-start(bf16[512,512]{1,0:T(8,128)(2,1)S(1)} %get-tuple-element.54), channel_id=1, source_target_pairs={{0,1},{1,2},{2,3},{3,0},{4,5},{5,6},{6,7},{7,4},{8,9},{9,10},{10,1... | collective-permute-start | bytes 1572872 | tf_op jit(solution)/shard_map/ppermute | solution.py:19
  137.1 16.0 %collective-permute-start.12 = (bf16[512,512]{1,0:T(8,128)(2,1)S(1)}, bf16[512,512]{1,0:T(8,128)(2,1)S(1)}, u32[]{:S(2)}, u32[]{:S(2)}) collective-permute-start(bf16[512,512]{1,0:T(8,128)(2,1)S(1)} %get-tuple-element.55), channel_id=1, source_target_pairs={{0,3},{1,0},{2,1},{3,2},{4,7},{5,4},{6,5},{7,6},{8,11},{9,8},{10,9... | collective-permute-start | bytes 1572872 | tf_op jit(solution)/shard_map/ppermute | solution.py:19
  140.3 46.4 %copy-start.1 = (bf16[2048,512]{1,0:T(8,128)(2,1)S(1)}, bf16[2048,512]{1,0:T(8,128)(2,1)}, u32[]{:S(2)}) copy-start(bf16[2048,512]{1,0:T(8,128)(2,1)} %param.21) | copy-start | bytes 6291460
  141.1 43.7 %collective-permute-start.8 = (bf16[1024,512]{1,0:T(8,128)(2,1)S(1)}, bf16[1024,512]{1,0:T(8,128)(2,1)S(1)}, u32[]{:S(2)}, u32[]{:S(2)}) collective-permute-start(bf16[1024,512]{1,0:T(8,128)(2,1)S(1)} %convolution_convert_fusion.2), channel_id=1, source_target_pairs={{0,1},{1,2},{2,3},{3,0},{4,5},{5,6},{6,7},{7,4},{8,9},{9,10},{10,1... | collective-permute-start | bytes 3145736 | tf_op jit(solution)/shard_map/ppermute | solution.py:19
  141.2 43.6 %collective-permute-start.9 = (bf16[1024,512]{1,0:T(8,128)(2,1)S(1)}, bf16[1024,512]{1,0:T(8,128)(2,1)S(1)}, u32[]{:S(2)}, u32[]{:S(2)}) collective-permute-start(bf16[1024,512]{1,0:T(8,128)(2,1)S(1)} %convolution_convert_fusion.1), channel_id=1, source_target_pairs={{0,3},{1,0},{2,1},{3,2},{4,7},{5,4},{6,5},{7,6},{8,11},{9,8},{10,9... | collective-permute-start | bytes 3145736 | tf_op jit(solution)/shard_map/ppermute | solution.py:19
  153.1 31.7 %collective-permute-start.11 = (bf16[512,512]{1,0:T(8,128)(2,1)S(1)}, bf16[512,512]{1,0:T(8,128)(2,1)S(1)}, u32[]{:S(2)}, u32[]{:S(2)}) collective-permute-start(bf16[512,512]{1,0:T(8,128)(2,1)S(1)} %collective-permute-done.10), channel_id=1, source_target_pairs={{0,1},{1,2},{2,3},{3,0},{4,5},{5,6},{6,7},{7,4},{8,9},{9,10},{10,1... | collective-permute-start | bytes 1572872 | tf_op jit(solution)/shard_map/ppermute | solution.py:19
  153.1 31.7 %collective-permute-start.13 = (bf16[512,512]{1,0:T(8,128)(2,1)S(1)}, bf16[512,512]{1,0:T(8,128)(2,1)S(1)}, u32[]{:S(2)}, u32[]{:S(2)}) collective-permute-start(bf16[512,512]{1,0:T(8,128)(2,1)S(1)} %collective-permute-done.12), channel_id=1, source_target_pairs={{0,3},{1,0},{2,1},{3,2},{4,7},{5,4},{6,5},{7,6},{8,11},{9,8},{10,9... | collective-permute-start | bytes 1572872 | tf_op jit(solution)/shard_map/ppermute | solution.py:19
  (9 other events, 15.3 us)

commit v5 on v4

--- a/solution.py
+++ b/solution.py
@@ -19,44 +19,46 @@
     return lax.ppermute(x, "tensor", [(i, (i + step) % size) for i in range(size)])
 
 
-def gathered_blocks(local):
+def gathered(local):
     half = local.shape[0] // 2
     from_left = ring(local, 1)
     from_right = ring(local, -1)
     far = jnp.concatenate([ring(from_left[:half], 1), ring(from_right[half:], -1)])
-    return ((0, local), (-1, from_left), (1, from_right), (2, far))
+    return jnp.concatenate([local, from_right, far, from_left], axis=1)
 
 
-def block_dot(blocks_in, weight):
+def projected(full, weights):
     size = lax.axis_size("tensor")
     index = lax.axis_index("tensor")
-    width = blocks_in[0][1].shape[1]
-    total = None
-    for offset, block in blocks_in:
-        rows = lax.dynamic_slice_in_dim(weight, ((index + offset) % size) * width, width, 0)
-        term = jnp.dot(block, rows, preferred_element_type=jnp.float32)
-        total = term if total is None else total + term
-    return total
+    width = full.shape[1] // size
+    joined = jnp.concatenate(weights, axis=1)
+    doubled = jnp.concatenate([joined, joined], axis=0)
+    rolled = lax.dynamic_slice_in_dim(doubled, index * width, joined.shape[0], 0)
+    out = jnp.dot(full, rolled, preferred_element_type=jnp.float32)
+    parts, at = [], 0
+    for weight in weights:
+        parts.append(out[:, at : at + weight.shape[1]])
+        at += weight.shape[1]
+    return parts
 
 
 def scattered_sum(gated, w_out):
     size = lax.axis_size("tensor")
     index = lax.axis_index("tensor")
     width = w_out.shape[1] // size
+    rows = gated.shape[0]
+    half = rows // 2
 
     def term(offset):
         cols = lax.dynamic_slice_in_dim(w_out, ((index + offset) % size) * width, width, 1)
         return jnp.dot(gated, cols, preferred_element_type=jnp.float32).astype(jnp.bfloat16)
 
-    half = gated.shape[0] // 2
     far = term(2)
-    far_from_left = ring(far[:half], 1)
-    far_from_right = ring(far[half:], -1)
-    from_left = ring(term(1), 1)
-    from_right = ring(term(-1), -1)
-    relayed = jnp.concatenate([ring(far_from_left, 1), ring(far_from_right, -1)])
-    total = term(0).astype(jnp.float32) + from_left.astype(jnp.float32)
-    total = total + from_right.astype(jnp.float32) + relayed.astype(jnp.float32)
+    from_left = ring(jnp.concatenate([term(1), far[:half]]), 1)
+    from_right = ring(jnp.concatenate([term(-1), far[half:]]), -1)
+    relayed = jnp.concatenate([ring(from_left[rows:], 1), ring(from_right[rows:], -1)])
+    total = term(0).astype(jnp.float32) + from_left[:rows].astype(jnp.float32)
+    total = total + from_right[:rows].astype(jnp.float32) + relayed.astype(jnp.float32)
     return total
 
 
@@ -77,10 +79,7 @@
     key_width = w_query.shape[1]
     value_width = w_value.shape[1]
     weights = (w_query, w_key, w_value, w_outgate, w_gate_down)
-    blocks_in = gathered_blocks(hidden_in)
-    query_sum, key_sum, value_sum, outgate, low = tuple(
-        (block_dot(blocks_in, weight) for weight in weights)
-    )
+    query_sum, key_sum, value_sum, outgate, low = projected(gathered(hidden_in), weights)
     query = query_sum.astype(jnp.bfloat16)
     key = key_sum.astype(jnp.bfloat16)
     value = value_sum.astype(jnp.bfloat16)

time: 188 us -> 204 us (1.085)
  waiting for transfers between devices: 42.8 us -> 72.1 us
  matrix products: 65.1 us -> 40.6 us
  local copies, waits for them, and re-layouts: 23.7 us -> 37.2 us
  starting transfers between devices: 31.7 us -> 24.1 us
  other arithmetic: 16.5 us -> 22 us
    ppermute x10 -> x8, waiting for transfers between devices: 42.8 us -> 72.1 us  [ring(): lax.ppermute(x, 'tensor', [(i, (i + step) % size) for i in range(size)])]
    dot_general x20 -> x1, matrix products: 42.1 us -> 15.3 us  [projected(): out = jnp.dot(full, rolled, preferred_element_type=jnp.float32)]
    slice x3 -> x7, local copies, waits for them, and re-layouts: 1.18 us -> 8.63 us  [the longest x2 3.8 us: projected(): parts.append(out[:, at:at + weight.shape[1]])]
    unnamed x55 -> x39, local copies, waits for them, and re-layouts: 1.36 us -> 7.91 us
    ppermute x10 -> x8, starting transfers between devices: 16.7 us -> 10.5 us  [ring(): lax.ppermute(x, 'tensor', [(i, (i + step) % size) for i in range(size)])]
    another operation x4, other arithmetic: 4.37 us -> 1.2 us
    reshape x0 -> x1, other arithmetic: none -> 2.82 us  [body(): k_float = key.astype(jnp.float32).reshape(blocks, GROUP, key_width)]
    add x1, other arithmetic: 1.16 us -> 3.69 us  [body(): entering = chunk_decay[n][:, None] * entering + chunk_states[n]]
  transfers between devices with their start and end apart: 14 -> 12, of which waited for: 3 -> 6; matrix products, arithmetic and copies ran while one was open for 29% -> 17% of each run, Pallas kernels for 0% -> 0%
where the time goes in v5:
time: 204 us; the launch traced here: 203 us
  waiting for transfers between devices  72.1 us (35%)
  matrix products  40.6 us (20%)
  local copies, waits for them, and re-layouts  37.2 us (18%)
  starting transfers between devices  24.1 us (12%)
  other arithmetic  22 us (11%)
  between operations  6.74 us (3%)
    ppermute x8, waiting for transfers between devices, ring(): lax.ppermute(x, 'tensor', [(i, (i + step) % size) for i in range(size)])  72.1 us
    dot_general x1, matrix products, projected(): out = jnp.dot(full, rolled, preferred_element_type=jnp.float32)  15.3 us
    ppermute x4, starting transfers between devices, shifted(): return lax.ppermute(x, axis, pairs)  13.6 us
    ppermute x8, starting transfers between devices, ring(): lax.ppermute(x, 'tensor', [(i, (i + step) % size) for i in range(size)])  10.5 us
    unnamed x39, local copies, waits for them, and re-layouts  7.91 us
    dot_general x4, matrix products, term(): jnp.dot(gated, cols, preferred_element_type=jnp.float32)  5.97 us
    dot_general x1, matrix products, body(): jnp.einsum('ncd,ncv->ndv', k_decayed, v_float, precision=HIGH)  5.69 us
    mul x1, other arithmetic, body(): q_scaled = q_float * jnp.exp(cumul - centre[:, None, :])  5.06 us
  transfers between devices with their start and end apart: 12, of which 6 were waited for; matrix products, arithmetic and copies ran while one was open for 17% of the time, Pallas kernels for 0%

profile of v5, /device:TPU:2, one launch (start us, length us, event | category | flops | bytes accessed | tf_op | source)
XLA Modules:
  0.0 202.8 jit_solution(10579799216027386615)
XLA Ops:
  0.0 1.6 collective-permute-start.1
  1.6 1.7 collective-permute-start
  8.3 18.2 %collective-permute-done = bf16[1024,512]{1,0:T(8,128)(2,1)} collective-permute-done((bf16[1024,512]{1,0:T(8,128)(2,1)}, bf16[1024,512]{1,0:T(8,128)(2,1)}, u32[]{:S(2)}, u32[]{:S(2)}) %collective-permute-start) | collective-permute-done | bytes 1048608 | tf_op jit(solution)/shard_map/ppermute | solution.py:19
  27.6 3.1 %collective-permute-start.3 = (bf16[512,512]{1,0:T(8,128)(2,1)S(1)}, bf16[512,512]{1,0:T(8,128)(2,1)}, u32[]{:S(2)}, u32[]{:S(2)}) collective-permute-start(bf16[512,512]{1,0:T(8,128)(2,1)S(1)} %slice.451), channel_id=1, source_target_pairs={{0,3},{1,0},{2,1},{3,2},{4,7},{5,4},{6,5},{7,6},{8,11},{9,8},{10,9... | collective-permute-start | bytes 1572872 | tf_op jit(solution)/shard_map/ppermute | solution.py:19
  30.7 1.9 slice.450
  36.9 3.1 %constant_dynamic-update-slice_fusion.1 = bf16[2048,1552]{1,0:T(8,128)(2,1)} fusion(bf16[2048,1552]{1,0:T(8,128)(2,1)} %copy-done.12, bf16[2048,512]{1,0:T(8,128)(2,1)} %param.22), kind=kLoop, calls=%fused_computation.196 | loop fusion | bytes 4194304
  40.9 5.6 %collective-permute-done.2 = bf16[512,512]{1,0:T(8,128)(2,1)} collective-permute-done((bf16[512,512]{1,0:T(8,128)(2,1)}, bf16[512,512]{1,0:T(8,128)(2,1)}, u32[]{:S(2)}, u32[]{:S(2)}) %collective-permute-start.2) | collective-permute-done | bytes 524320 | tf_op jit(solution)/shard_map/ppermute | solution.py:19
  46.5 15.3 %fusion.147 = (bf16[1024,1552]{0,1:T(8,128)(2,1)}, f32[1024,1552]{0,1:T(8,128)}) fusion(s32[]{:T(128)S(6)} %select_n.43, bf16[2048,1552]{1,0:T(8,128)(2,1)} %constant_dynamic-update-slice_fusion, bf16[1024,512]{1,0:T(8,128)(2,1)} %collective-permute-done.1, bf16[512,512]{1,0:T(8,128)(2,1)} %collective-permute-done.3, ...), kind=kOutput, calls=%fused_computation.239 | convolution fusion | flops 6544834560 | bytes 20086788 | tf_op jit(solution)/shard_map/dot_general | solution.py:37
  61.8 2.8 %slice_convert_fusion = (f32[1024,256]{0,1:T(8,128)}, f32[1024,256]{0,1:T(8,128)}) fusion(bf16[1024,1552]{0,1:T(8,128)(2,1)} %get-tuple-element.104), kind=kLoop, calls=%fused_computation.86 | loop fusion | flops 524288 | bytes 3145728 | tf_op jit(solution)/shard_map/reshape | solution.py:102
  64.6 2.3 %slice.456 = bf16[1024,512]{0,1:T(8,128)(2,1)} slice(bf16[1024,1552]{0,1:T(8,128)(2,1)} %get-tuple-element.104), slice={[0:1024], [512:1024]} | slice | bytes 2097152 | tf_op jit(solution)/shard_map/slice | solution.py:40
  66.9 2.0 fusion.30
  69.8 2.9 %copy.45 = f32[1024,256]{1,0:T(8,128)} copy(f32[1024,256]{0,1:T(8,128)} %get-tuple-element.49) | data formatting | bytes 2097152 | tf_op jit(solution)/shard_map/convert_element_type | solution.py:101
  72.7 2.5 %copy.48 = f32[1024,256]{1,0:T(8,128)} copy(f32[1024,256]{0,1:T(8,128)} %get-tuple-element.48) | data formatting | bytes 2097152 | tf_op jit(solution)/shard_map/reshape | solution.py:102
  77.6 5.1 %exponential_multiply_fusion.2 = (f32[16,64,256]{2,0,1:T(8,128)}, f32[16,64,256]{2,0,1:T(8,128)}, f32[16,64,256]{2,0,1:T(8,128)S(1)}, f32[16,64,256]{2,0,1:T(8,128)}, f32[16,64,256]{2,0,1:T(8,128)S(1)}) fusion(f32[16,64,256]{2,0,1:T(8,128)} %copy-done.3, f32[16,64,256]{2,1,0:T(8,128)} %bitcast.312, f32[16,256]{1,0:T(8,128)S(1)} %get-tuple-element.61, ...), kind=kLoop, calls=%fused_computation.73 | loop fusion | flops 2359296 | bytes 8441856 | tf_op jit(solution)/shard_map/mul | solution.py:108
  83.3 5.7 %fusion.31 = f32[16,256,512]{2,1,0:T(8,128)} fusion(bf16[16,64,512]{2,1,0:T(8,128)(2,1)S(1)} %bitcast.307, f32[16,64,256]{2,0,1:T(8,128)S(1)} %get-tuple-element.54), kind=kOutput, calls=%fused_computation.62 | convolution fusion | flops 805306368 | bytes 10485760 | tf_op jit(solution)/shard_map/ncd,ncv->ndv/dot_general | solution.py:117
  89.2 3.7 %multiply_add_fusion.2 = (f32[1,256,512]{2,1,0:T(8,128)S(1)}, f32[1,256,512]{2,1,0:T(8,128)S(1)}, f32[1,256,512]{2,1,0:T(8,128)S(1)}, f32[1,256,512]{2,1,0:T(8,1...) fusion(f32[16,256,512]{2,1,0:T(8,128)} %fusion.31, ...), kind=kLoop, calls=%fused_computation.140 | loop fusion | flops 3538944 | bytes 11024384 | tf_op jit(solution)/shard_map/add | solution.py:125
  92.9 1.8 copy-done.1
  96.3 1.9 collective-permute-start.4
  98.2 5.8 %collective-permute-start.7 = (bf16[258,512]{1,0:T(8,128)(2,1)}, bf16[258,512]{1,0:T(8,128)(2,1)}, u32[]{:S(2)}, u32[]{:S(2)}) collective-permute-start(bf16[258,512]{1,0:T(8,128)(2,1)} %pad_maximum_fusion.2), channel_id=1, source_target_pairs={{0,16},{4,20},{8,24},{12,28},{16,32},{20,36},{24,40},{28,44},{32,4... | collective-permute-start | bytes 792584 | tf_op jit(solution)/shard_map/ppermute | solution.py:14
  104.0 2.5 %collective-permute-start.6 = (bf16[258,512]{1,0:T(8,128)(2,1)}, bf16[258,512]{1,0:T(8,128)(2,1)}, u32[]{:S(2)}, u32[]{:S(2)}) collective-permute-start(bf16[258,512]{1,0:T(8,128)(2,1)} %pad_maximum_fusion.2), channel_id=1, source_target_pairs={{0,12},{4,16},{8,20},{12,24},{16,28},{20,32},{24,36},{28,40},{32,4... | collective-permute-start | bytes 792584 | tf_op jit(solution)/shard_map/ppermute | solution.py:14
  106.5 3.4 %collective-permute-start.5 = (bf16[258,512]{1,0:T(8,128)(2,1)}, bf16[258,512]{1,0:T(8,128)(2,1)}, u32[]{:S(2)}, u32[]{:S(2)}) collective-permute-start(bf16[258,512]{1,0:T(8,128)(2,1)} %pad_maximum_fusion.2), channel_id=1, source_target_pairs={{0,8},{4,12},{8,16},{12,20},{16,24},{20,28},{24,32},{28,36},{32,40... | collective-permute-start | bytes 792584 | tf_op jit(solution)/shard_map/ppermute | solution.py:14
  116.2 1.7 convolution_select_fusion
  117.9 2.2 %multiply_add_fusion.1 = f32[16,64,512]{2,1,0:T(8,128)} fusion(f32[16,64,512]{2,1,0:T(8,128)S(1)} %fusion.13, f32[16,64,64]{2,1,0:T(8,128)S(1)} %convolution_select_fusion, bf16[16,64,512]{2,1,0:T(8,128)(2,1)S(1)} %bitcast.308, f32[16,64]{1,0:T(8,128)S(1)} %compare_convert_fusion.1), kind=kOutput, calls=%fused_computation.18 | convolution fusion | flops 202375168 | bytes 5509120 | tf_op jit(solution)/shard_map/ncs,nsv->ncv/dot_general | solution.py:113
  120.1 1.6 copy.60
  121.7 2.9 %copy.61 = f32[1024,512]{0,1:T(8,128)} copy(f32[1024,512]{1,0:T(8,128)} %bitcast.309) | data formatting | bytes 4194304 | tf_op jit(solution)/shard_map/reshape | solution.py:128
  136.8 2.7 %multiply_reduce_fusion = (f32[1024]{0:T(1024)S(1)}, f32[1024,512]{0,1:T(8,128)S(1)}) fusion(f32[1024,512]{0,1:T(8,128)S(1)} %copy-done.2, f32[1024]{0:T(1024)S(1)} %select_bitcast_fusion, f32[258,512]{1,0:T(8,128)S(1)} %convert_element_type.116, f32[258,512]{1,0:T(8,128)S(1)} %convert_element_type.113, f32[258,512]{1,0:T(8,128)S(1)} %convert_element_type.110, ...), kind=kOutput, calls=%fused_computation.16 | convolution fusion | flops 809237504 | bytes 7875584 | tf_op jit(solution)/shard_map/dot_general | solution.py:147
  139.6 2.3 %multiply_convert_fusion = bf16[1024,512]{0,1:T(8,128)(2,1)S(1)} fusion(f32[1024,1552]{0,1:T(8,128)} %get-tuple-element.105, f32[1024,512]{0,1:T(8,128)S(1)} %get-tuple-element.107, f32[512]{0:T(512)S(1)} %copy-done.14, f32[1024]{0:T(1024)S(1)} %rsqrt_multiply_fusion), kind=kLoop, calls=%fused_computation.15 | loop fusion | flops 4194304 | bytes 5249024 | tf_op jit(solution)/shard_map/convert_element_type | solution.py:152
  144.5 2.1 %collective-permute-start.8 = (bf16[1536,512]{1,0:T(8,128)(2,1)S(1)}, bf16[1536,512]{1,0:T(8,128)(2,1)S(1)}, u32[]{:S(2)}, u32[]{:S(2)}) collective-permute-start(bf16[1536,512]{1,0:T(8,128)(2,1)S(1)} %pad_maximum_fusion), channel_id=1, source_target_pairs={{0,1},{1,2},{2,3},{3,0},{4,5},{5,6},{6,7},{7,4},{8,9},{9,10},{10,1... | collective-permute-start | bytes 4718600 | tf_op jit(solution)/shard_map/ppermute | solution.py:19
  146.6 33.8 %collective-permute-done.9 = bf16[1536,512]{1,0:T(8,128)(2,1)S(1)} collective-permute-done((bf16[1536,512]{1,0:T(8,128)(2,1)S(1)}, bf16[1536,512]{1,0:T(8,128)(2,1)S(1)}, u32[]{:S(2)}, u32[]{:S(2)}) %collective-permute-start.9) | collective-permute-done | bytes 1572896 | tf_op jit(solution)/shard_map/ppermute | solution.py:19
  184.6 10.4 %collective-permute-done.11 = bf16[512,512]{1,0:T(8,128)(2,1)} collective-permute-done((bf16[512,512]{1,0:T(8,128)(2,1)}, bf16[512,512]{1,0:T(8,128)(2,1)}, u32[]{:S(2)}, u32[]{:S(2)}) %collective-permute-start.11) | collective-permute-done | bytes 524320 | tf_op jit(solution)/shard_map/ppermute | solution.py:19
  195.0 4.0 %collective-permute-done.10 = bf16[512,512]{1,0:T(8,128)(2,1)} collective-permute-done((bf16[512,512]{1,0:T(8,128)(2,1)}, bf16[512,512]{1,0:T(8,128)(2,1)}, u32[]{:S(2)}, u32[]{:S(2)}) %collective-permute-start.10) | collective-permute-done | bytes 524320 | tf_op jit(solution)/shard_map/ppermute | solution.py:19
  199.1 3.7 %add_convert_fusion = bf16[1024,512]{1,0:T(8,128)(2,1)} fusion(bf16[1536,512]{1,0:T(8,128)(2,1)} %copy-done.10, bf16[1536,512]{1,0:T(8,128)(2,1)} %copy-done.11, bf16[512,512]{1,0:T(8,128)(2,1)} %collective-permute-done.11, bf16[512,512]{1,0:T(8,128)(2,1)} %collective-permute-done.10, bf16[1024,512]{0,1:T(8,128)(2,1)S(1)} %multiply_convert_fusion, ...), kind=kOutput, calls=%fused_computation.14 | convolution fusion | flops 543162368 | bytes 5767172 | tf_op jit(solution)/shard_map/dot_general | solution.py:54
  (120 shorter events, 35.8 us)
Async XLA Ops:
  0.0 141.8 %copy-start = (bf16[512,2048]{1,0:T(8,128)(2,1)S(1)}, bf16[512,2048]{1,0:T(8,128)(2,1)}, u32[]{:S(2)}) copy-start(bf16[512,2048]{1,0:T(8,128)(2,1)} %param.27) | copy-start | bytes 6291460
  0.0 7.7 %copy-start.9 = (bf16[2048,256]{1,0:T(8,128)(2,1)S(1)}, bf16[2048,256]{1,0:T(8,128)(2,1)}, u32[]{:S(2)}) copy-start(bf16[2048,256]{1,0:T(8,128)(2,1)} %param.20) | copy-start | bytes 3145732
  0.0 30.7 %collective-permute-start.1 = (bf16[1024,512]{1,0:T(8,128)(2,1)}, bf16[1024,512]{1,0:T(8,128)(2,1)}, u32[]{:S(2)}, u32[]{:S(2)}) collective-permute-start(bf16[1024,512]{1,0:T(8,128)(2,1)} %param.17), channel_id=1, source_target_pairs={{0,1},{1,2},{2,3},{3,0},{4,5},{5,6},{6,7},{7,4},{8,9},{9,10},{10,1... | collective-permute-start | bytes 3145736 | tf_op jit(solution)/shard_map/ppermute | solution.py:19
  1.6 24.9 %collective-permute-start = (bf16[1024,512]{1,0:T(8,128)(2,1)}, bf16[1024,512]{1,0:T(8,128)(2,1)}, u32[]{:S(2)}, u32[]{:S(2)}) collective-permute-start(bf16[1024,512]{1,0:T(8,128)(2,1)} %param.17), channel_id=1, source_target_pairs={{0,3},{1,0},{2,1},{3,2},{4,7},{5,4},{6,5},{7,6},{8,11},{9,8},{10,9... | collective-permute-start | bytes 3145736 | tf_op jit(solution)/shard_map/ppermute | solution.py:19
  6.2 1.9 copy-start.8
  8.3 22.4 %copy-start.12 = (bf16[2048,1552]{1,0:T(8,128)(2,1)}, bf16[2048,1552]{1,0:T(8,128)(2,1)S(1)}, u32[]{:S(2)}) copy-start(bf16[2048,1552]{1,0:T(8,128)(2,1)S(1)} %constant_dynamic-update-slice_fusion.2) | copy-start | bytes 19070980
  8.3 25.7 %copy-start.13 = (bf16[2048,16]{0,1:T(8,128)(2,1)S(1)}, bf16[2048,16]{0,1:T(8,128)(2,1)}, u32[]{:S(2)}) copy-start(bf16[2048,16]{0,1:T(8,128)(2,1)} %param.23) | copy-start | bytes 196612
  27.6 13.3 %collective-permute-start.3 = (bf16[512,512]{1,0:T(8,128)(2,1)S(1)}, bf16[512,512]{1,0:T(8,128)(2,1)}, u32[]{:S(2)}, u32[]{:S(2)}) collective-permute-start(bf16[512,512]{1,0:T(8,128)(2,1)S(1)} %slice.451), channel_id=1, source_target_pairs={{0,3},{1,0},{2,1},{3,2},{4,7},{5,4},{6,5},{7,6},{8,11},{9,8},{10,9... | collective-permute-start | bytes 1572872 | tf_op jit(solution)/shard_map/ppermute | solution.py:19
  32.5 13.9 %collective-permute-start.2 = (bf16[512,512]{1,0:T(8,128)(2,1)}, bf16[512,512]{1,0:T(8,128)(2,1)}, u32[]{:S(2)}, u32[]{:S(2)}) collective-permute-start(bf16[512,512]{1,0:T(8,128)(2,1)} %slice.450), channel_id=1, source_target_pairs={{0,1},{1,2},{2,3},{3,0},{4,5},{5,6},{6,7},{7,4},{8,9},{9,10},{10,1... | collective-permute-start | bytes 1572872 | tf_op jit(solution)/shard_map/ppermute | solution.py:19
  61.8 5.1 %copy-start.15 = (bf16[16,256]{1,0:T(8,128)(2,1)S(1)}, bf16[16,256]{1,0:T(8,128)(2,1)}, u32[]{:S(2)}) copy-start(bf16[16,256]{1,0:T(8,128)(2,1)} %param.24) | copy-start | bytes 24580
  61.8 5.1 %copy-start.16 = (f32[256]{0:T(256)S(1)}, f32[256]{0:T(256)}, u32[]{:S(2)}) copy-start(f32[256]{0:T(256)} %param.25) | copy-start | bytes 3076
  69.8 3.0 %copy-start.3 = (f32[16,64,256]{2,0,1:T(8,128)}, f32[16,64,256]{2,0,1:T(8,128)S(1)}, u32[]{:S(2)}) copy-start(f32[16,64,256]{2,0,1:T(8,128)S(1)} %fusion.35) | copy-start | bytes 3145732
  83.3 5.7 %copy-start.4 = (f32[16,64,256]{2,1,0:T(8,128)}, f32[16,64,256]{2,1,0:T(8,128)S(1)}, u32[]{:S(2)}) copy-start(f32[16,64,256]{2,1,0:T(8,128)S(1)} %copy.59) | copy-start | bytes 3145732
  89.2 5.6 %copy-start.1 = (f32[16,256,512]{2,1,0:T(8,128)S(1)}, f32[16,256,512]{2,1,0:T(8,128)}, u32[]{:S(2)}) copy-start(f32[16,256,512]{2,1,0:T(8,128)} %fusion.31) | copy-start | bytes 25165828
  94.7 15.2 %copy-start.7 = (f32[16,64,256]{2,0,1:T(8,128)S(1)}, f32[16,64,256]{2,0,1:T(8,128)}, u32[]{:S(2)}) copy-start(f32[16,64,256]{2,0,1:T(8,128)} %get-tuple-element.51) | copy-start | bytes 3145732
  96.3 28.3 %collective-permute-start.4 = (bf16[258,512]{1,0:T(8,128)(2,1)}, bf16[258,512]{1,0:T(8,128)(2,1)S(1)}, u32[]{:S(2)}, u32[]{:S(2)}) collective-permute-start(bf16[258,512]{1,0:T(8,128)(2,1)} %pad_maximum_fusion.2), channel_id=1, source_target_pairs={{0,4},{4,8},{8,12},{12,16},{16,20},{20,24},{24,28},{28,32},{32,36}... | collective-permute-start | bytes 792584 | tf_op jit(solution)/shard_map/ppermute | solution.py:14
  98.2 28.9 %collective-permute-start.7 = (bf16[258,512]{1,0:T(8,128)(2,1)}, bf16[258,512]{1,0:T(8,128)(2,1)}, u32[]{:S(2)}, u32[]{:S(2)}) collective-permute-start(bf16[258,512]{1,0:T(8,128)(2,1)} %pad_maximum_fusion.2), channel_id=1, source_target_pairs={{0,16},{4,20},{8,24},{12,28},{16,32},{20,36},{24,40},{28,44},{32,4... | collective-permute-start | bytes 792584 | tf_op jit(solution)/shard_map/ppermute | solution.py:14
  104.0 21.2 %collective-permute-start.6 = (bf16[258,512]{1,0:T(8,128)(2,1)}, bf16[258,512]{1,0:T(8,128)(2,1)}, u32[]{:S(2)}, u32[]{:S(2)}) collective-permute-start(bf16[258,512]{1,0:T(8,128)(2,1)} %pad_maximum_fusion.2), channel_id=1, source_target_pairs={{0,12},{4,16},{8,20},{12,24},{16,28},{20,32},{24,36},{28,40},{32,4... | collective-permute-start | bytes 792584 | tf_op jit(solution)/shard_map/ppermute | solution.py:14
  106.5 23.3 %collective-permute-start.5 = (bf16[258,512]{1,0:T(8,128)(2,1)}, bf16[258,512]{1,0:T(8,128)(2,1)}, u32[]{:S(2)}, u32[]{:S(2)}) collective-permute-start(bf16[258,512]{1,0:T(8,128)(2,1)} %pad_maximum_fusion.2), channel_id=1, source_target_pairs={{0,8},{4,12},{8,16},{12,20},{16,24},{20,28},{24,32},{28,36},{32,40... | collective-permute-start | bytes 792584 | tf_op jit(solution)/shard_map/ppermute | solution.py:14
  114.6 1.3 copy-start.5
  114.6 1.5 copy-start.6
  127.1 9.7 %copy-start.2 = (f32[1024,512]{0,1:T(8,128)S(1)}, f32[1024,512]{0,1:T(8,128)}, u32[]{:S(2)}) copy-start(f32[1024,512]{0,1:T(8,128)} %copy.61) | copy-start | bytes 6291460
  136.8 2.8 %copy-start.14 = (f32[512]{0:T(512)S(1)}, f32[512]{0:T(512)}, u32[]{:S(2)}) copy-start(f32[512]{0:T(512)} %param.26) | copy-start | bytes 6148
  143.5 36.8 %collective-permute-start.9 = (bf16[1536,512]{1,0:T(8,128)(2,1)S(1)}, bf16[1536,512]{1,0:T(8,128)(2,1)S(1)}, u32[]{:S(2)}, u32[]{:S(2)}) collective-permute-start(bf16[1536,512]{1,0:T(8,128)(2,1)S(1)} %pad_maximum_fusion.1), channel_id=1, source_target_pairs={{0,3},{1,0},{2,1},{3,2},{4,7},{5,4},{6,5},{7,6},{8,11},{9,8},{10,9... | collective-permute-start | bytes 4718600 | tf_op jit(solution)/shard_map/ppermute | solution.py:19
  144.5 38.3 %collective-permute-start.8 = (bf16[1536,512]{1,0:T(8,128)(2,1)S(1)}, bf16[1536,512]{1,0:T(8,128)(2,1)S(1)}, u32[]{:S(2)}, u32[]{:S(2)}) collective-permute-start(bf16[1536,512]{1,0:T(8,128)(2,1)S(1)} %pad_maximum_fusion), channel_id=1, source_target_pairs={{0,1},{1,2},{2,3},{3,0},{4,5},{5,6},{6,7},{7,4},{8,9},{9,10},{10,1... | collective-permute-start | bytes 4718600 | tf_op jit(solution)/shard_map/ppermute | solution.py:19
  180.4 2.4 %copy-start.10 = (bf16[1536,512]{1,0:T(8,128)(2,1)}, bf16[1536,512]{1,0:T(8,128)(2,1)S(1)}, u32[]{:S(2)}) copy-start(bf16[1536,512]{1,0:T(8,128)(2,1)S(1)} %collective-permute-done.9) | copy-start | bytes 4718596
  181.3 13.7 %collective-permute-start.11 = (bf16[512,512]{1,0:T(8,128)(2,1)}, bf16[512,512]{1,0:T(8,128)(2,1)}, u32[]{:S(2)}, u32[]{:S(2)}) collective-permute-start(bf16[512,512]{1,0:T(8,128)(2,1)} %slice.530), channel_id=1, source_target_pairs={{0,3},{1,0},{2,1},{3,2},{4,7},{5,4},{6,5},{7,6},{8,11},{9,8},{10,9... | collective-permute-start | bytes 1572872 | tf_op jit(solution)/shard_map/ppermute | solution.py:19
  182.8 1.3 copy-start.11
  184.1 15.0 %collective-permute-start.10 = (bf16[512,512]{1,0:T(8,128)(2,1)}, bf16[512,512]{1,0:T(8,128)(2,1)}, u32[]{:S(2)}, u32[]{:S(2)}) collective-permute-start(bf16[512,512]{1,0:T(8,128)(2,1)} %slice.529), channel_id=1, source_target_pairs={{0,1},{1,2},{2,3},{3,0},{4,5},{5,6},{6,7},{7,4},{8,9},{9,10},{10,1... | collective-permute-start | bytes 1572872 | tf_op jit(solution)/shard_map/ppermute | solution.py:19

commit v6 on v5

--- a/solution.py
+++ b/solution.py
@@ -54,11 +54,13 @@
         return jnp.dot(gated, cols, preferred_element_type=jnp.float32).astype(jnp.bfloat16)
 
     far = term(2)
-    from_left = ring(jnp.concatenate([term(1), far[:half]]), 1)
-    from_right = ring(jnp.concatenate([term(-1), far[half:]]), -1)
-    relayed = jnp.concatenate([ring(from_left[rows:], 1), ring(from_right[rows:], -1)])
-    total = term(0).astype(jnp.float32) + from_left[:rows].astype(jnp.float32)
-    total = total + from_right[:rows].astype(jnp.float32) + relayed.astype(jnp.float32)
+    far_from_left = ring(far[:half], 1)
+    far_from_right = ring(far[half:], -1)
+    from_left = ring(term(1), 1)
+    from_right = ring(term(-1), -1)
+    relayed = jnp.concatenate([ring(far_from_left, 1), ring(far_from_right, -1)])
+    total = term(0).astype(jnp.float32) + from_left.astype(jnp.float32)
+    total = total + from_right.astype(jnp.float32) + relayed.astype(jnp.float32)
     return total
 
 

time: 204 us -> 203 us (level)
  local copies, waits for them, and re-layouts: 37.2 us -> 35 us
    ppermute x8 -> x10, starting transfers between devices: 10.5 us -> 12.5 us  [ring(): lax.ppermute(x, 'tensor', [(i, (i + step) % size) for i in range(size)])]
    ppermute x8 -> x10, waiting for transfers between devices: 72.1 us -> 70.2 us  [ring(): lax.ppermute(x, 'tensor', [(i, (i + step) % size) for i in range(size)])]
    unnamed x39 -> x35, local copies, waits for them, and re-layouts: 7.91 us -> 7.5 us
  transfers between devices with their start and end apart: 12 -> 14, of which waited for: 6 -> 7; matrix products, arithmetic and copies ran while one was open for 17% -> 17% of each run, Pallas kernels for 0% -> 0%
where the time goes in v6:
time: 203 us; the launch traced here: 202 us
  waiting for transfers between devices  70.2 us (35%)
  matrix products  42.6 us (21%)
  local copies, waits for them, and re-layouts  35 us (17%)
  starting transfers between devices  26.1 us (13%)
  other arithmetic  21.8 us (11%)
  between operations  6.71 us (3%)
    ppermute x10, waiting for transfers between devices, ring(): lax.ppermute(x, 'tensor', [(i, (i + step) % size) for i in range(size)])  70.2 us
    dot_general x1, matrix products, projected(): out = jnp.dot(full, rolled, preferred_element_type=jnp.float32)  15.3 us
    ppermute x4, starting transfers between devices, shifted(): return lax.ppermute(x, axis, pairs)  13.6 us
    ppermute x10, starting transfers between devices, ring(): lax.ppermute(x, 'tensor', [(i, (i + step) % size) for i in range(size)])  12.5 us
    dot_general x4, matrix products, term(): jnp.dot(gated, cols, preferred_element_type=jnp.float32)  7.92 us
    unnamed x35, local copies, waits for them, and re-layouts  7.5 us
    dot_general x1, matrix products, body(): jnp.einsum('ncd,ncv->ndv', k_decayed, v_float, precision=HIGH)  5.69 us
    mul x1, other arithmetic, body(): q_scaled = q_float * jnp.exp(cumul - centre[:, None, :])  5.06 us
  transfers between devices with their start and end apart: 14, of which 7 were waited for; matrix products, arithmetic and copies ran while one was open for 17% of the time, Pallas kernels for 0%

profile of v6, /device:TPU:2, one launch (start us, length us, event | category | flops | bytes accessed | tf_op | source)
XLA Modules:
  0.0 202.3 jit_solution(2408371067547938732)
XLA Ops:
  1.6 1.7 collective-permute-start
  8.3 18.2 %collective-permute-done = bf16[1024,512]{1,0:T(8,128)(2,1)} collective-permute-done((bf16[1024,512]{1,0:T(8,128)(2,1)}, bf16[1024,512]{1,0:T(8,128)(2,1)}, u32[]{:S(2)}, u32[]{:S(2)}) %collective-permute-start) | collective-permute-done | bytes 1048608 | tf_op jit(solution)/shard_map/ppermute | solution.py:19
  27.6 3.1 %collective-permute-start.3 = (bf16[512,512]{1,0:T(8,128)(2,1)S(1)}, bf16[512,512]{1,0:T(8,128)(2,1)}, u32[]{:S(2)}, u32[]{:S(2)}) collective-permute-start(bf16[512,512]{1,0:T(8,128)(2,1)S(1)} %slice.435), channel_id=1, source_target_pairs={{0,3},{1,0},{2,1},{3,2},{4,7},{5,4},{6,5},{7,6},{8,11},{9,8},{10,9... | collective-permute-start | bytes 1572872 | tf_op jit(solution)/shard_map/ppermute | solution.py:19
  30.7 1.9 slice.434
  36.9 3.1 %constant_dynamic-update-slice_fusion.1 = bf16[2048,1552]{1,0:T(8,128)(2,1)} fusion(bf16[2048,1552]{1,0:T(8,128)(2,1)} %copy-done.10, bf16[2048,512]{1,0:T(8,128)(2,1)} %param.22), kind=kLoop, calls=%fused_computation.194 | loop fusion | bytes 4194304
  40.9 5.6 %collective-permute-done.2 = bf16[512,512]{1,0:T(8,128)(2,1)} collective-permute-done((bf16[512,512]{1,0:T(8,128)(2,1)}, bf16[512,512]{1,0:T(8,128)(2,1)}, u32[]{:S(2)}, u32[]{:S(2)}) %collective-permute-start.2) | collective-permute-done | bytes 524320 | tf_op jit(solution)/shard_map/ppermute | solution.py:19
  46.5 15.3 %fusion.147 = (bf16[1024,1552]{0,1:T(8,128)(2,1)}, f32[1024,1552]{0,1:T(8,128)}) fusion(s32[]{:T(128)S(6)} %select_n.43, bf16[2048,1552]{1,0:T(8,128)(2,1)} %constant_dynamic-update-slice_fusion, bf16[1024,512]{1,0:T(8,128)(2,1)} %collective-permute-done.1, bf16[512,512]{1,0:T(8,128)(2,1)} %collective-permute-done.3, ...), kind=kOutput, calls=%fused_computation.237 | convolution fusion | flops 6544834560 | bytes 20086788 | tf_op jit(solution)/shard_map/dot_general | solution.py:37
  61.8 2.8 %slice_convert_fusion = (f32[1024,256]{0,1:T(8,128)}, f32[1024,256]{0,1:T(8,128)}) fusion(bf16[1024,1552]{0,1:T(8,128)(2,1)} %get-tuple-element.104), kind=kLoop, calls=%fused_computation.84 | loop fusion | flops 524288 | bytes 3145728 | tf_op jit(solution)/shard_map/reshape | solution.py:104
  64.6 2.3 %slice.440 = bf16[1024,512]{0,1:T(8,128)(2,1)} slice(bf16[1024,1552]{0,1:T(8,128)(2,1)} %get-tuple-element.104), slice={[0:1024], [512:1024]} | slice | bytes 2097152 | tf_op jit(solution)/shard_map/slice | solution.py:40
  66.9 2.0 fusion.30
  69.8 2.9 %copy.45 = f32[1024,256]{1,0:T(8,128)} copy(f32[1024,256]{0,1:T(8,128)} %get-tuple-element.49) | data formatting | bytes 2097152 | tf_op jit(solution)/shard_map/convert_element_type | solution.py:103
  72.7 2.5 %copy.48 = f32[1024,256]{1,0:T(8,128)} copy(f32[1024,256]{0,1:T(8,128)} %get-tuple-element.48) | data formatting | bytes 2097152 | tf_op jit(solution)/shard_map/reshape | solution.py:104
  77.6 5.1 %exponential_multiply_fusion.2 = (f32[16,64,256]{2,0,1:T(8,128)}, f32[16,64,256]{2,0,1:T(8,128)}, f32[16,64,256]{2,0,1:T(8,128)S(1)}, f32[16,64,256]{2,0,1:T(8,128)}, f32[16,64,256]{2,0,1:T(8,128)S(1)}) fusion(f32[16,64,256]{2,0,1:T(8,128)} %copy-done.3, f32[16,64,256]{2,1,0:T(8,128)} %bitcast.312, f32[16,256]{1,0:T(8,128)S(1)} %get-tuple-element.61, ...), kind=kLoop, calls=%fused_computation.71 | loop fusion | flops 2359296 | bytes 8441856 | tf_op jit(solution)/shard_map/mul | solution.py:110
  83.3 5.7 %fusion.31 = f32[16,256,512]{2,1,0:T(8,128)} fusion(bf16[16,64,512]{2,1,0:T(8,128)(2,1)S(1)} %bitcast.307, f32[16,64,256]{2,0,1:T(8,128)S(1)} %get-tuple-element.54), kind=kOutput, calls=%fused_computation.60 | convolution fusion | flops 805306368 | bytes 10485760 | tf_op jit(solution)/shard_map/ncd,ncv->ndv/dot_general | solution.py:119
  89.2 3.7 %multiply_add_fusion.2 = (f32[1,256,512]{2,1,0:T(8,128)S(1)}, f32[1,256,512]{2,1,0:T(8,128)S(1)}, f32[1,256,512]{2,1,0:T(8,128)S(1)}, f32[1,256,512]{2,1,0:T(8,1...) fusion(f32[16,256,512]{2,1,0:T(8,128)} %fusion.31, ...), kind=kLoop, calls=%fused_computation.138 | loop fusion | flops 3538944 | bytes 11024384 | tf_op jit(solution)/shard_map/add | solution.py:127
  92.9 1.8 copy-done.1
  96.3 1.9 collective-permute-start.4
  98.2 5.8 %collective-permute-start.7 = (bf16[258,512]{1,0:T(8,128)(2,1)}, bf16[258,512]{1,0:T(8,128)(2,1)}, u32[]{:S(2)}, u32[]{:S(2)}) collective-permute-start(bf16[258,512]{1,0:T(8,128)(2,1)} %pad_maximum_fusion), channel_id=1, source_target_pairs={{0,16},{4,20},{8,24},{12,28},{16,32},{20,36},{24,40},{28,44},{32,4... | collective-permute-start | bytes 792584 | tf_op jit(solution)/shard_map/ppermute | solution.py:14
  104.0 2.5 %collective-permute-start.6 = (bf16[258,512]{1,0:T(8,128)(2,1)}, bf16[258,512]{1,0:T(8,128)(2,1)}, u32[]{:S(2)}, u32[]{:S(2)}) collective-permute-start(bf16[258,512]{1,0:T(8,128)(2,1)} %pad_maximum_fusion), channel_id=1, source_target_pairs={{0,12},{4,16},{8,20},{12,24},{16,28},{20,32},{24,36},{28,40},{32,4... | collective-permute-start | bytes 792584 | tf_op jit(solution)/shard_map/ppermute | solution.py:14
  106.5 3.4 %collective-permute-start.5 = (bf16[258,512]{1,0:T(8,128)(2,1)}, bf16[258,512]{1,0:T(8,128)(2,1)}, u32[]{:S(2)}, u32[]{:S(2)}) collective-permute-start(bf16[258,512]{1,0:T(8,128)(2,1)} %pad_maximum_fusion), channel_id=1, source_target_pairs={{0,8},{4,12},{8,16},{12,20},{16,24},{20,28},{24,32},{28,36},{32,40... | collective-permute-start | bytes 792584 | tf_op jit(solution)/shard_map/ppermute | solution.py:14
  116.2 1.7 convolution_select_fusion
  117.9 2.2 %multiply_add_fusion.1 = f32[16,64,512]{2,1,0:T(8,128)} fusion(f32[16,64,512]{2,1,0:T(8,128)S(1)} %fusion.13, f32[16,64,64]{2,1,0:T(8,128)S(1)} %convolution_select_fusion, bf16[16,64,512]{2,1,0:T(8,128)(2,1)S(1)} %bitcast.308, f32[16,64]{1,0:T(8,128)S(1)} %compare_convert_fusion.1), kind=kOutput, calls=%fused_computation.18 | convolution fusion | flops 202375168 | bytes 5509120 | tf_op jit(solution)/shard_map/ncs,nsv->ncv/dot_general | solution.py:115
  121.7 2.9 %copy.61 = f32[1024,512]{0,1:T(8,128)} copy(f32[1024,512]{1,0:T(8,128)} %bitcast.309) | data formatting | bytes 4194304 | tf_op jit(solution)/shard_map/reshape | solution.py:130
  136.8 2.7 %multiply_reduce_fusion = (f32[1024]{0:T(1024)S(1)}, f32[1024,512]{0,1:T(8,128)S(1)}) fusion(f32[1024,512]{0,1:T(8,128)S(1)} %copy-done.2, f32[1024]{0:T(1024)S(1)} %select_bitcast_fusion, f32[258,512]{1,0:T(8,128)S(1)} %convert_element_type.116, f32[258,512]{1,0:T(8,128)S(1)} %convert_element_type.113, f32[258,512]{1,0:T(8,128)S(1)} %convert_element_type.110, ...), kind=kOutput, calls=%fused_computation.16 | convolution fusion | flops 809237504 | bytes 7875584 | tf_op jit(solution)/shard_map/dot_general | solution.py:149
  139.6 2.3 %multiply_convert_fusion = bf16[1024,512]{0,1:T(8,128)(2,1)S(1)} fusion(f32[1024,1552]{0,1:T(8,128)} %get-tuple-element.105, f32[1024,512]{0,1:T(8,128)S(1)} %get-tuple-element.107, f32[512]{0:T(512)S(1)} %copy-done.12, f32[1024]{0:T(1024)S(1)} %rsqrt_multiply_fusion), kind=kLoop, calls=%fused_computation.15 | loop fusion | flops 4194304 | bytes 5249024 | tf_op jit(solution)/shard_map/convert_element_type | solution.py:154
  141.9 1.7 convolution_convert_fusion.1
  143.6 1.7 convolution_convert_fusion.2
  145.3 2.0 collective-permute-start.8
  150.2 30.4 %collective-permute-done.12 = bf16[512,512]{1,0:T(8,128)(2,1)} collective-permute-done((bf16[512,512]{1,0:T(8,128)(2,1)S(1)}, bf16[512,512]{1,0:T(8,128)(2,1)}, u32[]{:S(2)}, u32[]{:S(2)}) %collective-permute-start.12) | collective-permute-done | bytes 524320 | tf_op jit(solution)/shard_map/ppermute | solution.py:19
  184.1 10.3 %collective-permute-done.13 = bf16[512,512]{1,0:T(8,128)(2,1)} collective-permute-done((bf16[512,512]{1,0:T(8,128)(2,1)}, bf16[512,512]{1,0:T(8,128)(2,1)}, u32[]{:S(2)}, u32[]{:S(2)}) %collective-permute-start.13) | collective-permute-done | bytes 524320 | tf_op jit(solution)/shard_map/ppermute | solution.py:19
  194.4 4.1 %collective-permute-done.11 = bf16[512,512]{1,0:T(8,128)(2,1)} collective-permute-done((bf16[512,512]{1,0:T(8,128)(2,1)}, bf16[512,512]{1,0:T(8,128)(2,1)}, u32[]{:S(2)}, u32[]{:S(2)}) %collective-permute-start.11) | collective-permute-done | bytes 524320 | tf_op jit(solution)/shard_map/ppermute | solution.py:19
  198.6 3.7 %add_convert_fusion = bf16[1024,512]{1,0:T(8,128)(2,1)} fusion(bf16[1024,512]{1,0:T(8,128)(2,1)} %collective-permute-done.9, bf16[1024,512]{1,0:T(8,128)(2,1)} %collective-permute-done.8, bf16[512,512]{1,0:T(8,128)(2,1)} %collective-permute-done.13, bf16[512,512]{1,0:T(8,128)(2,1)} %collective-permute-done.11, ...), kind=kOutput, calls=%fused_computation.14 | convolution fusion | flops 543162368 | bytes 5767172 | tf_op jit(solution)/shard_map/dot_general | solution.py:54
  (116 shorter events, 38.5 us)
Async XLA Ops:
  0.0 141.8 %copy-start = (bf16[512,2048]{1,0:T(8,128)(2,1)S(1)}, bf16[512,2048]{1,0:T(8,128)(2,1)}, u32[]{:S(2)}) copy-start(bf16[512,2048]{1,0:T(8,128)(2,1)} %param.27) | copy-start | bytes 6291460
  0.0 7.7 %copy-start.9 = (bf16[2048,256]{1,0:T(8,128)(2,1)S(1)}, bf16[2048,256]{1,0:T(8,128)(2,1)}, u32[]{:S(2)}) copy-start(bf16[2048,256]{1,0:T(8,128)(2,1)} %param.20) | copy-start | bytes 3145732
  0.0 30.7 %collective-permute-start.1 = (bf16[1024,512]{1,0:T(8,128)(2,1)}, bf16[1024,512]{1,0:T(8,128)(2,1)}, u32[]{:S(2)}, u32[]{:S(2)}) collective-permute-start(bf16[1024,512]{1,0:T(8,128)(2,1)} %param.17), channel_id=1, source_target_pairs={{0,1},{1,2},{2,3},{3,0},{4,5},{5,6},{6,7},{7,4},{8,9},{9,10},{10,1... | collective-permute-start | bytes 3145736 | tf_op jit(solution)/shard_map/ppermute | solution.py:19
  1.6 24.9 %collective-permute-start = (bf16[1024,512]{1,0:T(8,128)(2,1)}, bf16[1024,512]{1,0:T(8,128)(2,1)}, u32[]{:S(2)}, u32[]{:S(2)}) collective-permute-start(bf16[1024,512]{1,0:T(8,128)(2,1)} %param.17), channel_id=1, source_target_pairs={{0,3},{1,0},{2,1},{3,2},{4,7},{5,4},{6,5},{7,6},{8,11},{9,8},{10,9... | collective-permute-start | bytes 3145736 | tf_op jit(solution)/shard_map/ppermute | solution.py:19
  6.2 1.9 copy-start.8
  8.3 22.4 %copy-start.10 = (bf16[2048,1552]{1,0:T(8,128)(2,1)}, bf16[2048,1552]{1,0:T(8,128)(2,1)S(1)}, u32[]{:S(2)}) copy-start(bf16[2048,1552]{1,0:T(8,128)(2,1)S(1)} %constant_dynamic-update-slice_fusion.2) | copy-start | bytes 19070980
  8.3 25.7 %copy-start.11 = (bf16[2048,16]{0,1:T(8,128)(2,1)S(1)}, bf16[2048,16]{0,1:T(8,128)(2,1)}, u32[]{:S(2)}) copy-start(bf16[2048,16]{0,1:T(8,128)(2,1)} %param.23) | copy-start | bytes 196612
  27.6 13.3 %collective-permute-start.3 = (bf16[512,512]{1,0:T(8,128)(2,1)S(1)}, bf16[512,512]{1,0:T(8,128)(2,1)}, u32[]{:S(2)}, u32[]{:S(2)}) collective-permute-start(bf16[512,512]{1,0:T(8,128)(2,1)S(1)} %slice.435), channel_id=1, source_target_pairs={{0,3},{1,0},{2,1},{3,2},{4,7},{5,4},{6,5},{7,6},{8,11},{9,8},{10,9... | collective-permute-start | bytes 1572872 | tf_op jit(solution)/shard_map/ppermute | solution.py:19
  32.5 13.9 %collective-permute-start.2 = (bf16[512,512]{1,0:T(8,128)(2,1)}, bf16[512,512]{1,0:T(8,128)(2,1)}, u32[]{:S(2)}, u32[]{:S(2)}) collective-permute-start(bf16[512,512]{1,0:T(8,128)(2,1)} %slice.434), channel_id=1, source_target_pairs={{0,1},{1,2},{2,3},{3,0},{4,5},{5,6},{6,7},{7,4},{8,9},{9,10},{10,1... | collective-permute-start | bytes 1572872 | tf_op jit(solution)/shard_map/ppermute | solution.py:19
  61.8 5.1 %copy-start.13 = (bf16[16,256]{1,0:T(8,128)(2,1)S(1)}, bf16[16,256]{1,0:T(8,128)(2,1)}, u32[]{:S(2)}) copy-start(bf16[16,256]{1,0:T(8,128)(2,1)} %param.24) | copy-start | bytes 24580
  61.8 5.1 %copy-start.14 = (f32[256]{0:T(256)S(1)}, f32[256]{0:T(256)}, u32[]{:S(2)}) copy-start(f32[256]{0:T(256)} %param.25) | copy-start | bytes 3076
  69.8 3.0 %copy-start.3 = (f32[16,64,256]{2,0,1:T(8,128)}, f32[16,64,256]{2,0,1:T(8,128)S(1)}, u32[]{:S(2)}) copy-start(f32[16,64,256]{2,0,1:T(8,128)S(1)} %fusion.35) | copy-start | bytes 3145732
  83.3 5.7 %copy-start.4 = (f32[16,64,256]{2,1,0:T(8,128)}, f32[16,64,256]{2,1,0:T(8,128)S(1)}, u32[]{:S(2)}) copy-start(f32[16,64,256]{2,1,0:T(8,128)S(1)} %copy.59) | copy-start | bytes 3145732
  89.2 5.6 %copy-start.1 = (f32[16,256,512]{2,1,0:T(8,128)S(1)}, f32[16,256,512]{2,1,0:T(8,128)}, u32[]{:S(2)}) copy-start(f32[16,256,512]{2,1,0:T(8,128)} %fusion.31) | copy-start | bytes 25165828
  94.7 15.2 %copy-start.7 = (f32[16,64,256]{2,0,1:T(8,128)S(1)}, f32[16,64,256]{2,0,1:T(8,128)}, u32[]{:S(2)}) copy-start(f32[16,64,256]{2,0,1:T(8,128)} %get-tuple-element.51) | copy-start | bytes 3145732
  96.3 28.3 %collective-permute-start.4 = (bf16[258,512]{1,0:T(8,128)(2,1)}, bf16[258,512]{1,0:T(8,128)(2,1)S(1)}, u32[]{:S(2)}, u32[]{:S(2)}) collective-permute-start(bf16[258,512]{1,0:T(8,128)(2,1)} %pad_maximum_fusion), channel_id=1, source_target_pairs={{0,4},{4,8},{8,12},{12,16},{16,20},{20,24},{24,28},{28,32},{32,36}... | collective-permute-start | bytes 792584 | tf_op jit(solution)/shard_map/ppermute | solution.py:14
  98.2 28.9 %collective-permute-start.7 = (bf16[258,512]{1,0:T(8,128)(2,1)}, bf16[258,512]{1,0:T(8,128)(2,1)}, u32[]{:S(2)}, u32[]{:S(2)}) collective-permute-start(bf16[258,512]{1,0:T(8,128)(2,1)} %pad_maximum_fusion), channel_id=1, source_target_pairs={{0,16},{4,20},{8,24},{12,28},{16,32},{20,36},{24,40},{28,44},{32,4... | collective-permute-start | bytes 792584 | tf_op jit(solution)/shard_map/ppermute | solution.py:14
  104.0 21.2 %collective-permute-start.6 = (bf16[258,512]{1,0:T(8,128)(2,1)}, bf16[258,512]{1,0:T(8,128)(2,1)}, u32[]{:S(2)}, u32[]{:S(2)}) collective-permute-start(bf16[258,512]{1,0:T(8,128)(2,1)} %pad_maximum_fusion), channel_id=1, source_target_pairs={{0,12},{4,16},{8,20},{12,24},{16,28},{20,32},{24,36},{28,40},{32,4... | collective-permute-start | bytes 792584 | tf_op jit(solution)/shard_map/ppermute | solution.py:14
  106.5 23.3 %collective-permute-start.5 = (bf16[258,512]{1,0:T(8,128)(2,1)}, bf16[258,512]{1,0:T(8,128)(2,1)}, u32[]{:S(2)}, u32[]{:S(2)}) collective-permute-start(bf16[258,512]{1,0:T(8,128)(2,1)} %pad_maximum_fusion), channel_id=1, source_target_pairs={{0,8},{4,12},{8,16},{12,20},{16,24},{20,28},{24,32},{28,36},{32,40... | collective-permute-start | bytes 792584 | tf_op jit(solution)/shard_map/ppermute | solution.py:14
  114.6 1.3 copy-start.5
  114.6 1.5 copy-start.6
  127.1 9.7 %copy-start.2 = (f32[1024,512]{0,1:T(8,128)S(1)}, f32[1024,512]{0,1:T(8,128)}, u32[]{:S(2)}) copy-start(f32[1024,512]{0,1:T(8,128)} %copy.61) | copy-start | bytes 6291460
  136.8 2.8 %copy-start.12 = (f32[512]{0:T(512)S(1)}, f32[512]{0:T(512)}, u32[]{:S(2)}) copy-start(f32[512]{0:T(512)} %param.26) | copy-start | bytes 6148
  143.6 40.5 %collective-permute-start.9 = (bf16[1024,512]{1,0:T(8,128)(2,1)}, bf16[1024,512]{1,0:T(8,128)(2,1)}, u32[]{:S(2)}, u32[]{:S(2)}) collective-permute-start(bf16[1024,512]{1,0:T(8,128)(2,1)} %convolution_convert_fusion.1), channel_id=1, source_target_pairs={{0,3},{1,0},{2,1},{3,2},{4,7},{5,4},{6,5},{7,6},{8,11},{9,8},{10,9... | collective-permute-start | bytes 3145736 | tf_op jit(solution)/shard_map/ppermute | solution.py:19
  145.3 38.8 %collective-permute-start.8 = (bf16[1024,512]{1,0:T(8,128)(2,1)}, bf16[1024,512]{1,0:T(8,128)(2,1)}, u32[]{:S(2)}, u32[]{:S(2)}) collective-permute-start(bf16[1024,512]{1,0:T(8,128)(2,1)} %convolution_convert_fusion.2), channel_id=1, source_target_pairs={{0,1},{1,2},{2,3},{3,0},{4,5},{5,6},{6,7},{7,4},{8,9},{9,10},{10,1... | collective-permute-start | bytes 3145736 | tf_op jit(solution)/shard_map/ppermute | solution.py:19
  148.1 32.5 %collective-permute-start.12 = (bf16[512,512]{1,0:T(8,128)(2,1)S(1)}, bf16[512,512]{1,0:T(8,128)(2,1)}, u32[]{:S(2)}, u32[]{:S(2)}) collective-permute-start(bf16[512,512]{1,0:T(8,128)(2,1)S(1)} %get-tuple-element.57), channel_id=1, source_target_pairs={{0,3},{1,0},{2,1},{3,2},{4,7},{5,4},{6,5},{7,6},{8,11},{9,8},{10,9... | collective-permute-start | bytes 1572872 | tf_op jit(solution)/shard_map/ppermute | solution.py:19
  149.4 34.2 %collective-permute-start.10 = (bf16[512,512]{1,0:T(8,128)(2,1)S(1)}, bf16[512,512]{1,0:T(8,128)(2,1)}, u32[]{:S(2)}, u32[]{:S(2)}) collective-permute-start(bf16[512,512]{1,0:T(8,128)(2,1)S(1)} %get-tuple-element.56), channel_id=1, source_target_pairs={{0,1},{1,2},{2,3},{3,0},{4,5},{5,6},{6,7},{7,4},{8,9},{9,10},{10,1... | collective-permute-start | bytes 1572872 | tf_op jit(solution)/shard_map/ppermute | solution.py:19
  180.7 13.7 %collective-permute-start.13 = (bf16[512,512]{1,0:T(8,128)(2,1)}, bf16[512,512]{1,0:T(8,128)(2,1)}, u32[]{:S(2)}, u32[]{:S(2)}) collective-permute-start(bf16[512,512]{1,0:T(8,128)(2,1)} %collective-permute-done.12), channel_id=1, source_target_pairs={{0,3},{1,0},{2,1},{3,2},{4,7},{5,4},{6,5},{7,6},{8,11},{9,8},{10,9... | collective-permute-start | bytes 1572872 | tf_op jit(solution)/shard_map/ppermute | solution.py:19
  183.6 15.0 %collective-permute-start.11 = (bf16[512,512]{1,0:T(8,128)(2,1)}, bf16[512,512]{1,0:T(8,128)(2,1)}, u32[]{:S(2)}, u32[]{:S(2)}) collective-permute-start(bf16[512,512]{1,0:T(8,128)(2,1)} %collective-permute-done.10), channel_id=1, source_target_pairs={{0,1},{1,2},{2,3},{3,0},{4,5},{5,6},{6,7},{7,4},{8,9},{9,10},{10,1... | collective-permute-start | bytes 1572872 | tf_op jit(solution)/shard_map/ppermute | solution.py:19

commit v7 on v6

--- a/solution.py
+++ b/solution.py
@@ -21,9 +21,14 @@
 
 def gathered(local):
     half = local.shape[0] // 2
-    from_left = ring(local, 1)
-    from_right = ring(local, -1)
-    far = jnp.concatenate([ring(from_left[:half], 1), ring(from_right[half:], -1)])
+    left_a = ring(local[:half], 1)
+    right_a = ring(local[half:], -1)
+    left_a, right_a, rest = lax.optimization_barrier((left_a, right_a, local))
+    left_b = ring(rest[half:], 1)
+    right_b = ring(rest[:half], -1)
+    far = jnp.concatenate([ring(left_a, 1), ring(right_a, -1)])
+    from_left = jnp.concatenate([left_a, left_b])
+    from_right = jnp.concatenate([right_b, right_a])
     return jnp.concatenate([local, from_right, far, from_left], axis=1)
 
 
@@ -56,8 +61,12 @@
     far = term(2)
     far_from_left = ring(far[:half], 1)
     far_from_right = ring(far[half:], -1)
-    from_left = ring(term(1), 1)
-    from_right = ring(term(-1), -1)
+    near_right, near_left = term(1), term(-1)
+    far_from_left, far_from_right, near_right, near_left = lax.optimization_barrier(
+        (far_from_left, far_from_right, near_right, near_left)
+    )
+    from_left = ring(near_right, 1)
+    from_right = ring(near_left, -1)
     relayed = jnp.concatenate([ring(far_from_left, 1), ring(far_from_right, -1)])
     total = term(0).astype(jnp.float32) + from_left.astype(jnp.float32)
     total = total + from_right.astype(jnp.float32) + relayed.astype(jnp.float32)

time: 203 us -> 200 us (0.985)
  waiting for transfers between devices: 70.2 us -> 56.8 us
  starting transfers between devices: 26.1 us -> 32.9 us
  local copies, waits for them, and re-layouts: 35 us -> 38.1 us
  other arithmetic: 21.8 us -> 24.1 us
  matrix products: 42.6 us -> 40.5 us
    ppermute x10 -> x12, waiting for transfers between devices: 70.2 us -> 56.8 us  [ring(): lax.ppermute(x, 'tensor', [(i, (i + step) % size) for i in range(size)])]
    ppermute x10 -> x12, starting transfers between devices: 12.5 us -> 19.3 us  [ring(): lax.ppermute(x, 'tensor', [(i, (i + step) % size) for i in range(size)])]
    unnamed x35 -> x41, local copies, waits for them, and re-layouts: 7.5 us -> 11.3 us
    convert_element_type x0 -> x1, other arithmetic: none -> 3.05 us  [body(): return scattered_sum(gated, w_out).astype(jnp.bfloat16)]
  transfers between devices with their start and end apart: 14 -> 16, of which waited for: 7 -> 7; matrix products, arithmetic and copies ran while one was open for 17% -> 18% of each run, Pallas kernels for 0% -> 0%
where the time goes in v7:
time: 200 us; the launch traced here: 199 us
  waiting for transfers between devices  56.8 us (28%)
  matrix products  40.5 us (20%)
  local copies, waits for them, and re-layouts  38.1 us (19%)
  starting transfers between devices  32.9 us (16%)
  other arithmetic  24.1 us (12%)
  between operations  6.89 us (3%)
    ppermute x12, waiting for transfers between devices, ring(): lax.ppermute(x, 'tensor', [(i, (i + step) % size) for i in range(size)])  56.8 us
    ppermute x12, starting transfers between devices, ring(): lax.ppermute(x, 'tensor', [(i, (i + step) % size) for i in range(size)])  19.3 us
    dot_general x1, matrix products, projected(): out = jnp.dot(full, rolled, preferred_element_type=jnp.float32)  15 us
    ppermute x4, starting transfers between devices, shifted(): return lax.ppermute(x, axis, pairs)  13.7 us
    unnamed x41, local copies, waits for them, and re-layouts  11.3 us
    dot_general x4, matrix products, term(): jnp.dot(gated, cols, preferred_element_type=jnp.float32)  6.2 us
    dot_general x1, matrix products, body(): jnp.einsum('ncd,ncv->ndv', k_decayed, v_float, precision=HIGH)  5.71 us
    mul x1, other arithmetic, body(): q_scaled = q_float * jnp.exp(cumul - centre[:, None, :])  5.06 us
  transfers between devices with their start and end apart: 16, of which 7 were waited for; matrix products, arithmetic and copies ran while one was open for 18% of the time, Pallas kernels for 0%

profile of v7, /device:TPU:2, one launch (start us, length us, event | category | flops | bytes accessed | tf_op | source)
XLA Modules:
  0.0 199.4 jit_solution(3057320570378114117)
XLA Ops:
  0.0 2.4 %fusion.145 = (bf16[512,512]{1,0:T(8,128)(2,1)}, bf16[512,512]{1,0:T(8,128)(2,1)}) fusion(bf16[1024,512]{1,0:T(8,128)(2,1)} %param.17), kind=kLoop, calls=%fused_computation.237 | loop fusion | bytes 2097152 | tf_op jit(solution)/shard_map/slice | solution.py:25
  8.4 2.4 %constant_dynamic-update-slice_fusion.3 = bf16[2048,1552]{1,0:T(8,128)(2,1)} fusion(bf16[2048,1552]{1,0:T(8,128)(2,1)} %constant_dynamic-update-slice_fusion.4, bf16[2048,256]{1,0:T(8,128)(2,1)} %param.20), kind=kLoop, calls=%fused_computation.200 | loop fusion | bytes 2097152
  12.3 5.4 %collective-permute-done = bf16[512,512]{1,0:T(8,128)(2,1)} collective-permute-done((bf16[512,512]{1,0:T(8,128)(2,1)}, bf16[512,512]{1,0:T(8,128)(2,1)}, u32[]{:S(2)}, u32[]{:S(2)}) %collective-permute-start) | collective-permute-done | bytes 524320 | tf_op jit(solution)/shard_map/ppermute | solution.py:19
  22.5 2.9 %collective-permute-start.2 = (bf16[512,512]{1,0:T(8,128)(2,1)}, bf16[512,512]{1,0:T(8,128)(2,1)}, u32[]{:S(2)}, u32[]{:S(2)}) collective-permute-start(bf16[512,512]{1,0:T(8,128)(2,1)} %get-tuple-element.92), channel_id=1, source_target_pairs={{0,3},{1,0},{2,1},{3,2},{4,7},{5,4},{6,5},{7,6},{8,11},{9,8},{10,9... | collective-permute-start | bytes 1572872 | tf_op jit(solution)/shard_map/ppermute | solution.py:19
  29.6 3.2 %constant_dynamic-update-slice_fusion.1 = bf16[2048,1552]{1,0:T(8,128)(2,1)} fusion(bf16[2048,1552]{1,0:T(8,128)(2,1)} %constant_dynamic-update-slice_fusion.2, bf16[2048,512]{1,0:T(8,128)(2,1)} %param.22), kind=kLoop, calls=%fused_computation.198 | loop fusion | bytes 4194304
  35.5 8.9 %collective-permute-done.3 = bf16[512,512]{1,0:T(8,128)(2,1)} collective-permute-done((bf16[512,512]{1,0:T(8,128)(2,1)}, bf16[512,512]{1,0:T(8,128)(2,1)}, u32[]{:S(2)}, u32[]{:S(2)}) %collective-permute-start.3) | collective-permute-done | bytes 524320 | tf_op jit(solution)/shard_map/ppermute | solution.py:19
  44.5 15.0 %fusion.151 = (bf16[1024,1552]{0,1:T(8,128)(2,1)}, f32[1024,1552]{0,1:T(8,128)}) fusion(s32[]{:T(128)S(6)} %select_n.43, bf16[2048,1552]{1,0:T(8,128)(2,1)} %constant_dynamic-update-slice_fusion, bf16[512,512]{1,0:T(8,128)(2,1)} %collective-permute-done.5, bf16[512,512]{1,0:T(8,128)(2,1)} %collective-permute-done, ...), kind=kOutput, calls=%fused_computation.243 | convolution fusion | flops 6553223168 | bytes 20086788 | tf_op jit(solution)/shard_map/dot_general | solution.py:42
  59.5 2.8 %slice_convert_fusion = (f32[1024,256]{0,1:T(8,128)}, f32[1024,256]{0,1:T(8,128)}) fusion(bf16[1024,1552]{0,1:T(8,128)(2,1)} %get-tuple-element.122), kind=kLoop, calls=%fused_computation.88 | loop fusion | flops 524288 | bytes 3145728 | tf_op jit(solution)/shard_map/reshape | solution.py:113
  62.2 2.3 %slice.446 = bf16[1024,512]{0,1:T(8,128)(2,1)} slice(bf16[1024,1552]{0,1:T(8,128)(2,1)} %get-tuple-element.122), slice={[0:1024], [512:1024]} | slice | bytes 2097152 | tf_op jit(solution)/shard_map/slice | solution.py:45
  64.5 2.0 %fusion.34 = f32[1024,256]{1,0:T(8,128)S(1)} fusion(bf16[16,256]{1,0:T(8,128)(2,1)S(1)} %copy-done.16, f32[256]{0:T(256)S(1)} %copy-done.17, f32[1024,1552]{0,1:T(8,128)} %get-tuple-element.123), kind=kOutput, calls=%fused_computation.63 | convolution fusion | flops 52953088 | bytes 1123328 | tf_op jit(solution)/shard_map/dot_general | solution.py:97
  67.4 2.9 %copy.45 = f32[1024,256]{1,0:T(8,128)} copy(f32[1024,256]{0,1:T(8,128)} %get-tuple-element.63) | data formatting | bytes 2097152 | tf_op jit(solution)/shard_map/convert_element_type | solution.py:112
  70.4 2.5 %copy.48 = f32[1024,256]{1,0:T(8,128)} copy(f32[1024,256]{0,1:T(8,128)} %get-tuple-element.62) | data formatting | bytes 2097152 | tf_op jit(solution)/shard_map/reshape | solution.py:113
  75.2 5.1 %exponential_multiply_fusion.2 = (f32[16,64,256]{2,0,1:T(8,128)}, f32[16,64,256]{2,0,1:T(8,128)}, f32[16,64,256]{2,0,1:T(8,128)S(1)}, f32[16,64,256]{2,0,1:T(8,128)}, f32[16,64,256]{2,0,1:T(8,128)S(1)}) fusion(f32[16,64,256]{2,0,1:T(8,128)} %copy-done.3, f32[16,64,256]{2,1,0:T(8,128)} %bitcast.312, f32[16,256]{1,0:T(8,128)S(1)} %get-tuple-element.75, ...), kind=kLoop, calls=%fused_computation.75 | loop fusion | flops 2359296 | bytes 8441856 | tf_op jit(solution)/shard_map/mul | solution.py:119
  80.9 5.7 %fusion.35 = f32[16,256,512]{2,1,0:T(8,128)} fusion(bf16[16,64,512]{2,1,0:T(8,128)(2,1)S(1)} %bitcast.307, f32[16,64,256]{2,0,1:T(8,128)S(1)} %get-tuple-element.68), kind=kOutput, calls=%fused_computation.64 | convolution fusion | flops 805306368 | bytes 10485760 | tf_op jit(solution)/shard_map/ncd,ncv->ndv/dot_general | solution.py:128
  86.8 3.7 %multiply_add_fusion.2 = (f32[1,256,512]{2,1,0:T(8,128)S(1)}, f32[1,256,512]{2,1,0:T(8,128)S(1)}, f32[1,256,512]{2,1,0:T(8,128)S(1)}, f32[1,256,512]{2,1,0:T(8,1...) fusion(f32[16,256,512]{2,1,0:T(8,128)} %fusion.35, ...), kind=kLoop, calls=%fused_computation.142 | loop fusion | flops 3538944 | bytes 11024384 | tf_op jit(solution)/shard_map/add | solution.py:136
  90.5 1.8 copy-done.1
  94.0 1.9 collective-permute-start.6
  95.9 5.8 %collective-permute-start.9 = (bf16[258,512]{1,0:T(8,128)(2,1)}, bf16[258,512]{1,0:T(8,128)(2,1)}, u32[]{:S(2)}, u32[]{:S(2)}) collective-permute-start(bf16[258,512]{1,0:T(8,128)(2,1)} %pad_maximum_fusion), channel_id=1, source_target_pairs={{0,16},{4,20},{8,24},{12,28},{16,32},{20,36},{24,40},{28,44},{32,4... | collective-permute-start | bytes 792584 | tf_op jit(solution)/shard_map/ppermute | solution.py:14
  101.7 2.5 %collective-permute-start.8 = (bf16[258,512]{1,0:T(8,128)(2,1)}, bf16[258,512]{1,0:T(8,128)(2,1)}, u32[]{:S(2)}, u32[]{:S(2)}) collective-permute-start(bf16[258,512]{1,0:T(8,128)(2,1)} %pad_maximum_fusion), channel_id=1, source_target_pairs={{0,12},{4,16},{8,20},{12,24},{16,28},{20,32},{24,36},{28,40},{32,4... | collective-permute-start | bytes 792584 | tf_op jit(solution)/shard_map/ppermute | solution.py:14
  104.2 3.5 %collective-permute-start.7 = (bf16[258,512]{1,0:T(8,128)(2,1)}, bf16[258,512]{1,0:T(8,128)(2,1)}, u32[]{:S(2)}, u32[]{:S(2)}) collective-permute-start(bf16[258,512]{1,0:T(8,128)(2,1)} %pad_maximum_fusion), channel_id=1, source_target_pairs={{0,8},{4,12},{8,16},{12,20},{16,24},{20,28},{24,32},{28,36},{32,40... | collective-permute-start | bytes 792584 | tf_op jit(solution)/shard_map/ppermute | solution.py:14
  115.6 2.2 %multiply_add_fusion.1 = f32[16,64,512]{2,1,0:T(8,128)} fusion(f32[16,64,512]{2,1,0:T(8,128)S(1)} %fusion.17, f32[16,64,64]{2,1,0:T(8,128)S(1)} %convolution_select_fusion, bf16[16,64,512]{2,1,0:T(8,128)(2,1)S(1)} %bitcast.308, f32[16,64]{1,0:T(8,128)S(1)} %compare_convert_fusion.1), kind=kOutput, calls=%fused_computation.22 | convolution fusion | flops 202375168 | bytes 5509120 | tf_op jit(solution)/shard_map/ncs,nsv->ncv/dot_general | solution.py:124
  119.4 2.9 %copy.61 = f32[1024,512]{0,1:T(8,128)} copy(f32[1024,512]{1,0:T(8,128)} %bitcast.309) | data formatting | bytes 4194304 | tf_op jit(solution)/shard_map/reshape | solution.py:139
  134.8 2.7 %multiply_reduce_fusion = (f32[1024]{0:T(1024)S(1)}, f32[1024,512]{0,1:T(8,128)S(1)}) fusion(f32[1024,512]{0,1:T(8,128)S(1)} %copy-done.2, f32[1024]{0:T(1024)S(1)} %select_bitcast_fusion, f32[258,512]{1,0:T(8,128)S(1)} %convert_element_type.116, f32[258,512]{1,0:T(8,128)S(1)} %convert_element_type.113, f32[258,512]{1,0:T(8,128)S(1)} %convert_element_type.110, ...), kind=kOutput, calls=%fused_computation.20 | convolution fusion | flops 809237504 | bytes 7875584 | tf_op jit(solution)/shard_map/dot_general | solution.py:158
  137.6 2.3 %multiply_convert_fusion = bf16[1024,512]{0,1:T(8,128)(2,1)S(1)} fusion(f32[1024,1552]{0,1:T(8,128)} %get-tuple-element.123, f32[1024,512]{0,1:T(8,128)S(1)} %get-tuple-element.125, f32[512]{0:T(512)S(1)} %copy-done.15, f32[1024]{0:T(1024)S(1)} %rsqrt_multiply_fusion), kind=kLoop, calls=%fused_computation.19 | loop fusion | flops 4194304 | bytes 5249024 | tf_op jit(solution)/shard_map/convert_element_type | solution.py:163
  141.8 2.2 %collective-permute-start.11 = (bf16[512,512]{1,0:T(8,128)(2,1)S(1)}, bf16[512,512]{1,0:T(8,128)(2,1)}, u32[]{:S(2)}, u32[]{:S(2)}) collective-permute-start(bf16[512,512]{1,0:T(8,128)(2,1)S(1)} %get-tuple-element.70), channel_id=1, source_target_pairs={{0,3},{1,0},{2,1},{3,2},{4,7},{5,4},{6,5},{7,6},{8,11},{9,8},{10,9... | collective-permute-start | bytes 1572872 | tf_op jit(solution)/shard_map/ppermute | solution.py:19
  147.5 8.9 %collective-permute-done.10 = bf16[512,512]{1,0:T(8,128)(2,1)} collective-permute-done((bf16[512,512]{1,0:T(8,128)(2,1)S(1)}, bf16[512,512]{1,0:T(8,128)(2,1)}, u32[]{:S(2)}, u32[]{:S(2)}) %collective-permute-start.10) | collective-permute-done | bytes 524320 | tf_op jit(solution)/shard_map/ppermute | solution.py:19
  156.4 3.0 %collective-permute-start.13 = (bf16[1024,512]{1,0:T(8,128)(2,1)}, bf16[1024,512]{1,0:T(8,128)(2,1)S(1)}, u32[]{:S(2)}, u32[]{:S(2)}) collective-permute-start(bf16[1024,512]{1,0:T(8,128)(2,1)} %convolution_convert_fusion), channel_id=1, source_target_pairs={{0,3},{1,0},{2,1},{3,2},{4,7},{5,4},{6,5},{7,6},{8,11},{9,8},{10,9... | collective-permute-start | bytes 3145736 | tf_op jit(solution)/shard_map/ppermute | solution.py:19
  159.4 3.2 %collective-permute-start.15 = (bf16[512,512]{1,0:T(8,128)(2,1)}, bf16[512,512]{1,0:T(8,128)(2,1)}, u32[]{:S(2)}, u32[]{:S(2)}) collective-permute-start(bf16[512,512]{1,0:T(8,128)(2,1)} %collective-permute-done.11), channel_id=1, source_target_pairs={{0,3},{1,0},{2,1},{3,2},{4,7},{5,4},{6,5},{7,6},{8,11},{9,8},{10,9... | collective-permute-start | bytes 1572872 | tf_op jit(solution)/shard_map/ppermute | solution.py:19
  162.7 2.0 convolution_convert_fusion.3
  164.6 28.3 %collective-permute-done.15 = bf16[512,512]{1,0:T(8,128)(2,1)} collective-permute-done((bf16[512,512]{1,0:T(8,128)(2,1)}, bf16[512,512]{1,0:T(8,128)(2,1)}, u32[]{:S(2)}, u32[]{:S(2)}) %collective-permute-start.15) | collective-permute-done | bytes 524320 | tf_op jit(solution)/shard_map/ppermute | solution.py:19
  193.0 3.4 %collective-permute-done.14 = bf16[512,512]{1,0:T(8,128)(2,1)} collective-permute-done((bf16[512,512]{1,0:T(8,128)(2,1)}, bf16[512,512]{1,0:T(8,128)(2,1)}, u32[]{:S(2)}, u32[]{:S(2)}) %collective-permute-start.14) | collective-permute-done | bytes 524320 | tf_op jit(solution)/shard_map/ppermute | solution.py:19
  196.4 3.0 %add_convert_fusion = bf16[1024,512]{1,0:T(8,128)(2,1)} fusion(bf16[1024,512]{1,0:T(8,128)(2,1)S(1)} %collective-permute-done.13, bf16[1024,512]{1,0:T(8,128)(2,1)} %collective-permute-done.12, bf16[1024,512]{1,0:T(8,128)(2,1)S(1)} %convolution_convert_fusion.3, bf16[512,512]{1,0:T(8,128)(2,1)} %collective-permute-done.15, ...), kind=kLoop, calls=%fused_computation.18 | loop fusion | flops 5767168 | bytes 5242880 | tf_op jit(solution)/shard_map/convert_element_type | solution.py:164
  (127 shorter events, 45.7 us)
Async XLA Ops:
  0.0 139.8 %copy-start = (bf16[512,2048]{1,0:T(8,128)(2,1)S(1)}, bf16[512,2048]{1,0:T(8,128)(2,1)}, u32[]{:S(2)}) copy-start(bf16[512,2048]{1,0:T(8,128)(2,1)} %param.27) | copy-start | bytes 6291460
  0.0 5.7 %copy-start.14 = (s32[1024]{0:T(1024)S(1)}, s32[1024]{0:T(1024)}, u32[]{:S(2)}) copy-start(s32[1024]{0:T(1024)} %param.18) | copy-start | bytes 12292
  0.0 5.8 %copy-start.11 = (bf16[2048,256]{1,0:T(8,128)(2,1)S(1)}, bf16[2048,256]{1,0:T(8,128)(2,1)}, u32[]{:S(2)}) copy-start(bf16[2048,256]{1,0:T(8,128)(2,1)} %param.19) | copy-start | bytes 3145732
  2.4 15.3 %collective-permute-start = (bf16[512,512]{1,0:T(8,128)(2,1)}, bf16[512,512]{1,0:T(8,128)(2,1)}, u32[]{:S(2)}, u32[]{:S(2)}) collective-permute-start(bf16[512,512]{1,0:T(8,128)(2,1)} %get-tuple-element.95), channel_id=1, source_target_pairs={{0,1},{1,2},{2,3},{3,0},{4,5},{5,6},{6,7},{7,4},{8,9},{9,10},{10,1... | collective-permute-start | bytes 1572872 | tf_op jit(solution)/shard_map/ppermute | solution.py:19
  4.0 13.7 %collective-permute-start.1 = (bf16[512,512]{1,0:T(8,128)(2,1)}, bf16[512,512]{1,0:T(8,128)(2,1)}, u32[]{:S(2)}, u32[]{:S(2)}) collective-permute-start(bf16[512,512]{1,0:T(8,128)(2,1)} %get-tuple-element.94), channel_id=1, source_target_pairs={{0,3},{1,0},{2,1},{3,2},{4,7},{5,4},{6,5},{7,6},{8,11},{9,8},{10,9... | collective-permute-start | bytes 1572872 | tf_op jit(solution)/shard_map/ppermute | solution.py:19
  8.2 2.6 %copy-start.9 = (bf16[2048,512]{1,0:T(8,128)(2,1)S(1)}, bf16[2048,512]{1,0:T(8,128)(2,1)}, u32[]{:S(2)}) copy-start(bf16[2048,512]{1,0:T(8,128)(2,1)} %param.21) | copy-start | bytes 6291460
  10.8 6.9 %copy-start.5 = (bf16[1024,512]{1,0:T(8,128)(2,1)S(1)}, bf16[1024,512]{1,0:T(8,128)(2,1)}, u32[]{:S(2)}) copy-start(bf16[1024,512]{1,0:T(8,128)(2,1)} %param.17) | copy-start | bytes 3145732
  12.3 13.7 %copy-start.13 = (bf16[2048,16]{0,1:T(8,128)(2,1)S(1)}, bf16[2048,16]{0,1:T(8,128)(2,1)}, u32[]{:S(2)}) copy-start(bf16[2048,16]{0,1:T(8,128)(2,1)} %param.23) | copy-start | bytes 196612
  18.8 16.3 %collective-permute-start.5 = (bf16[512,512]{1,0:T(8,128)(2,1)}, bf16[512,512]{1,0:T(8,128)(2,1)}, u32[]{:S(2)}, u32[]{:S(2)}) collective-permute-start(bf16[512,512]{1,0:T(8,128)(2,1)} %get-tuple-element.93), channel_id=1, source_target_pairs={{0,1},{1,2},{2,3},{3,0},{4,5},{5,6},{6,7},{7,4},{8,9},{9,10},{10,1... | collective-permute-start | bytes 1572872 | tf_op jit(solution)/shard_map/ppermute | solution.py:19
  20.4 15.1 %collective-permute-start.4 = (bf16[512,512]{1,0:T(8,128)(2,1)}, bf16[512,512]{1,0:T(8,128)(2,1)}, u32[]{:S(2)}, u32[]{:S(2)}) collective-permute-start(bf16[512,512]{1,0:T(8,128)(2,1)} %collective-permute-done.1), channel_id=1, source_target_pairs={{0,3},{1,0},{2,1},{3,2},{4,7},{5,4},{6,5},{7,6},{8,11},{9,8},{10,9... | collective-permute-start | bytes 1572872 | tf_op jit(solution)/shard_map/ppermute | solution.py:19
  22.1 22.4 %collective-permute-start.3 = (bf16[512,512]{1,0:T(8,128)(2,1)}, bf16[512,512]{1,0:T(8,128)(2,1)}, u32[]{:S(2)}, u32[]{:S(2)}) collective-permute-start(bf16[512,512]{1,0:T(8,128)(2,1)} %collective-permute-done), channel_id=1, source_target_pairs={{0,1},{1,2},{2,3},{3,0},{4,5},{5,6},{6,7},{7,4},{8,9},{9,10},{10,1... | collective-permute-start | bytes 1572872 | tf_op jit(solution)/shard_map/ppermute | solution.py:19
  22.5 22.0 %collective-permute-start.2 = (bf16[512,512]{1,0:T(8,128)(2,1)}, bf16[512,512]{1,0:T(8,128)(2,1)}, u32[]{:S(2)}, u32[]{:S(2)}) collective-permute-start(bf16[512,512]{1,0:T(8,128)(2,1)} %get-tuple-element.92), channel_id=1, source_target_pairs={{0,3},{1,0},{2,1},{3,2},{4,7},{5,4},{6,5},{7,6},{8,11},{9,8},{10,9... | collective-permute-start | bytes 1572872 | tf_op jit(solution)/shard_map/ppermute | solution.py:19
  29.6 3.2 %copy-start.10 = (bf16[2048,16]{1,0:T(8,128)(2,1)S(1)}, bf16[2048,16]{1,0:T(8,128)(2,1)}, u32[]{:S(2)}) copy-start(bf16[2048,16]{1,0:T(8,128)(2,1)} %copy.44) | copy-start | bytes 196612
  59.5 5.0 %copy-start.16 = (bf16[16,256]{1,0:T(8,128)(2,1)S(1)}, bf16[16,256]{1,0:T(8,128)(2,1)}, u32[]{:S(2)}) copy-start(bf16[16,256]{1,0:T(8,128)(2,1)} %param.24) | copy-start | bytes 24580
  59.5 5.0 %copy-start.17 = (f32[256]{0:T(256)S(1)}, f32[256]{0:T(256)}, u32[]{:S(2)}) copy-start(f32[256]{0:T(256)} %param.25) | copy-start | bytes 3076
  67.4 3.0 %copy-start.3 = (f32[16,64,256]{2,0,1:T(8,128)}, f32[16,64,256]{2,0,1:T(8,128)S(1)}, u32[]{:S(2)}) copy-start(f32[16,64,256]{2,0,1:T(8,128)S(1)} %fusion.39) | copy-start | bytes 3145732
  80.9 5.7 %copy-start.4 = (f32[16,64,256]{2,1,0:T(8,128)}, f32[16,64,256]{2,1,0:T(8,128)S(1)}, u32[]{:S(2)}) copy-start(f32[16,64,256]{2,1,0:T(8,128)S(1)} %copy.59) | copy-start | bytes 3145732
  86.8 5.6 %copy-start.1 = (f32[16,256,512]{2,1,0:T(8,128)S(1)}, f32[16,256,512]{2,1,0:T(8,128)}, u32[]{:S(2)}) copy-start(f32[16,256,512]{2,1,0:T(8,128)} %fusion.35) | copy-start | bytes 25165828
  92.4 15.3 %copy-start.8 = (f32[16,64,256]{2,0,1:T(8,128)S(1)}, f32[16,64,256]{2,0,1:T(8,128)}, u32[]{:S(2)}) copy-start(f32[16,64,256]{2,0,1:T(8,128)} %get-tuple-element.65) | copy-start | bytes 3145732
  94.0 28.3 %collective-permute-start.6 = (bf16[258,512]{1,0:T(8,128)(2,1)}, bf16[258,512]{1,0:T(8,128)(2,1)S(1)}, u32[]{:S(2)}, u32[]{:S(2)}) collective-permute-start(bf16[258,512]{1,0:T(8,128)(2,1)} %pad_maximum_fusion), channel_id=1, source_target_pairs={{0,4},{4,8},{8,12},{12,16},{16,20},{20,24},{24,28},{28,32},{32,36}... | collective-permute-start | bytes 792584 | tf_op jit(solution)/shard_map/ppermute | solution.py:14
  95.9 29.0 %collective-permute-start.9 = (bf16[258,512]{1,0:T(8,128)(2,1)}, bf16[258,512]{1,0:T(8,128)(2,1)}, u32[]{:S(2)}, u32[]{:S(2)}) collective-permute-start(bf16[258,512]{1,0:T(8,128)(2,1)} %pad_maximum_fusion), channel_id=1, source_target_pairs={{0,16},{4,20},{8,24},{12,28},{16,32},{20,36},{24,40},{28,44},{32,4... | collective-permute-start | bytes 792584 | tf_op jit(solution)/shard_map/ppermute | solution.py:14
  101.7 21.2 %collective-permute-start.8 = (bf16[258,512]{1,0:T(8,128)(2,1)}, bf16[258,512]{1,0:T(8,128)(2,1)}, u32[]{:S(2)}, u32[]{:S(2)}) collective-permute-start(bf16[258,512]{1,0:T(8,128)(2,1)} %pad_maximum_fusion), channel_id=1, source_target_pairs={{0,12},{4,16},{8,20},{12,24},{16,28},{20,32},{24,36},{28,40},{32,4... | collective-permute-start | bytes 792584 | tf_op jit(solution)/shard_map/ppermute | solution.py:14
  104.2 23.6 %collective-permute-start.7 = (bf16[258,512]{1,0:T(8,128)(2,1)}, bf16[258,512]{1,0:T(8,128)(2,1)}, u32[]{:S(2)}, u32[]{:S(2)}) collective-permute-start(bf16[258,512]{1,0:T(8,128)(2,1)} %pad_maximum_fusion), channel_id=1, source_target_pairs={{0,8},{4,12},{8,16},{12,20},{16,24},{20,28},{24,32},{28,36},{32,40... | collective-permute-start | bytes 792584 | tf_op jit(solution)/shard_map/ppermute | solution.py:14
  124.9 9.9 %copy-start.2 = (f32[1024,512]{0,1:T(8,128)S(1)}, f32[1024,512]{0,1:T(8,128)}, u32[]{:S(2)}) copy-start(f32[1024,512]{0,1:T(8,128)} %copy.61) | copy-start | bytes 6291460
  134.8 2.8 %copy-start.15 = (f32[512]{0:T(512)S(1)}, f32[512]{0:T(512)}, u32[]{:S(2)}) copy-start(f32[512]{0:T(512)} %param.26) | copy-start | bytes 6148
  139.9 5.9 %copy-start.12 = (bf16[1024,512]{0,1:T(8,128)(2,1)}, bf16[1024,512]{0,1:T(8,128)(2,1)S(1)}, u32[]{:S(2)}) copy-start(bf16[1024,512]{0,1:T(8,128)(2,1)S(1)} %multiply_convert_fusion) | copy-start | bytes 3145732
  140.7 15.7 %collective-permute-start.10 = (bf16[512,512]{1,0:T(8,128)(2,1)S(1)}, bf16[512,512]{1,0:T(8,128)(2,1)}, u32[]{:S(2)}, u32[]{:S(2)}) collective-permute-start(bf16[512,512]{1,0:T(8,128)(2,1)S(1)} %get-tuple-element.71), channel_id=1, source_target_pairs={{0,1},{1,2},{2,3},{3,0},{4,5},{5,6},{6,7},{7,4},{8,9},{9,10},{10,1... | collective-permute-start | bytes 1572872 | tf_op jit(solution)/shard_map/ppermute | solution.py:19
  141.8 14.6 %collective-permute-start.11 = (bf16[512,512]{1,0:T(8,128)(2,1)S(1)}, bf16[512,512]{1,0:T(8,128)(2,1)}, u32[]{:S(2)}, u32[]{:S(2)}) collective-permute-start(bf16[512,512]{1,0:T(8,128)(2,1)S(1)} %get-tuple-element.70), channel_id=1, source_target_pairs={{0,3},{1,0},{2,1},{3,2},{4,7},{5,4},{6,5},{7,6},{8,11},{9,8},{10,9... | collective-permute-start | bytes 1572872 | tf_op jit(solution)/shard_map/ppermute | solution.py:19
  156.4 40.0 %collective-permute-start.13 = (bf16[1024,512]{1,0:T(8,128)(2,1)}, bf16[1024,512]{1,0:T(8,128)(2,1)S(1)}, u32[]{:S(2)}, u32[]{:S(2)}) collective-permute-start(bf16[1024,512]{1,0:T(8,128)(2,1)} %convolution_convert_fusion), channel_id=1, source_target_pairs={{0,3},{1,0},{2,1},{3,2},{4,7},{5,4},{6,5},{7,6},{8,11},{9,8},{10,9... | collective-permute-start | bytes 3145736 | tf_op jit(solution)/shard_map/ppermute | solution.py:19
  159.4 37.0 %collective-permute-start.12 = (bf16[1024,512]{1,0:T(8,128)(2,1)}, bf16[1024,512]{1,0:T(8,128)(2,1)}, u32[]{:S(2)}, u32[]{:S(2)}) collective-permute-start(bf16[1024,512]{1,0:T(8,128)(2,1)} %convolution_convert_fusion.1), channel_id=1, source_target_pairs={{0,1},{1,2},{2,3},{3,0},{4,5},{5,6},{6,7},{7,4},{8,9},{9,10},{10,1... | collective-permute-start | bytes 3145736 | tf_op jit(solution)/shard_map/ppermute | solution.py:19
  159.4 33.5 %collective-permute-start.15 = (bf16[512,512]{1,0:T(8,128)(2,1)}, bf16[512,512]{1,0:T(8,128)(2,1)}, u32[]{:S(2)}, u32[]{:S(2)}) collective-permute-start(bf16[512,512]{1,0:T(8,128)(2,1)} %collective-permute-done.11), channel_id=1, source_target_pairs={{0,3},{1,0},{2,1},{3,2},{4,7},{5,4},{6,5},{7,6},{8,11},{9,8},{10,9... | collective-permute-start | bytes 1572872 | tf_op jit(solution)/shard_map/ppermute | solution.py:19
  162.7 33.7 %collective-permute-start.14 = (bf16[512,512]{1,0:T(8,128)(2,1)}, bf16[512,512]{1,0:T(8,128)(2,1)}, u32[]{:S(2)}, u32[]{:S(2)}) collective-permute-start(bf16[512,512]{1,0:T(8,128)(2,1)} %collective-permute-done.10), channel_id=1, source_target_pairs={{0,1},{1,2},{2,3},{3,0},{4,5},{5,6},{6,7},{7,4},{8,9},{9,10},{10,1... | collective-permute-start | bytes 1572872 | tf_op jit(solution)/shard_map/ppermute | solution.py:19
  (2 other events, 2.8 us)

commit v8 on v7

--- a/solution.py
+++ b/solution.py
@@ -29,17 +29,21 @@
     far = jnp.concatenate([ring(left_a, 1), ring(right_a, -1)])
     from_left = jnp.concatenate([left_a, left_b])
     from_right = jnp.concatenate([right_b, right_a])
-    return jnp.concatenate([local, from_right, far, from_left], axis=1)
+    return jnp.concatenate([local, from_right, from_left], axis=1), far
 
 
-def projected(full, weights):
+def projected(near, far, weights):
     size = lax.axis_size("tensor")
     index = lax.axis_index("tensor")
-    width = full.shape[1] // size
+    width = far.shape[1]
     joined = jnp.concatenate(weights, axis=1)
-    doubled = jnp.concatenate([joined, joined], axis=0)
-    rolled = lax.dynamic_slice_in_dim(doubled, index * width, joined.shape[0], 0)
-    out = jnp.dot(full, rolled, preferred_element_type=jnp.float32)
+
+    def rows(offset):
+        return lax.dynamic_slice_in_dim(joined, ((index + offset) % size) * width, width, 0)
+
+    near_rows = jnp.concatenate([rows(0), rows(1), rows(size - 1)])
+    out = jnp.dot(near, near_rows, preferred_element_type=jnp.float32)
+    out = out + jnp.dot(far, rows(2), preferred_element_type=jnp.float32)
     parts, at = [], 0
     for weight in weights:
         parts.append(out[:, at : at + weight.shape[1]])
@@ -61,12 +65,8 @@
     far = term(2)
     far_from_left = ring(far[:half], 1)
     far_from_right = ring(far[half:], -1)
-    near_right, near_left = term(1), term(-1)
-    far_from_left, far_from_right, near_right, near_left = lax.optimization_barrier(
-        (far_from_left, far_from_right, near_right, near_left)
-    )
-    from_left = ring(near_right, 1)
-    from_right = ring(near_left, -1)
+    from_left = ring(term(1), 1)
+    from_right = ring(term(-1), -1)
     relayed = jnp.concatenate([ring(far_from_left, 1), ring(far_from_right, -1)])
     total = term(0).astype(jnp.float32) + from_left.astype(jnp.float32)
     total = total + from_right.astype(jnp.float32) + relayed.astype(jnp.float32)
@@ -90,7 +90,7 @@
     key_width = w_query.shape[1]
     value_width = w_value.shape[1]
     weights = (w_query, w_key, w_value, w_outgate, w_gate_down)
-    query_sum, key_sum, value_sum, outgate, low = projected(gathered(hidden_in), weights)
+    query_sum, key_sum, value_sum, outgate, low = projected(*gathered(hidden_in), weights)
     query = query_sum.astype(jnp.bfloat16)
     key = key_sum.astype(jnp.bfloat16)
     value = value_sum.astype(jnp.bfloat16)

time: 200 us -> 201 us (level)
  local copies, waits for them, and re-layouts: 38.1 us -> 42.5 us
  starting transfers between devices: 32.9 us -> 28.5 us
  other arithmetic: 24.1 us -> 21.1 us
  matrix products: 40.5 us -> 42.9 us
    dynamic_slice x0 -> x1, local copies, waits for them, and re-layouts: none -> 4.57 us  [rows(): lax.dynamic_slice_in_dim(joined, (index + offset) % size * width, width, 0)]
    ppermute x12, starting transfers between devices: 19.3 us -> 14.8 us  [ring(): lax.ppermute(x, 'tensor', [(i, (i + step) % size) for i in range(size)])]
    dot_general x1 -> x2, matrix products: 15 us -> 19.4 us  [the longest x1 13.3 us: projected(): out = jnp.dot(near, near_rows, preferred_element_type=jnp.float32)]
    convert_element_type x1 -> x0, other arithmetic: 3.05 us -> none  [body(): return scattered_sum(gated, w_out).astype(jnp.bfloat16)]
  transfers between devices with their start and end apart: 16 -> 16, of which waited for: 7 -> 6; matrix products, arithmetic and copies ran while one was open for 18% -> 20% of each run, Pallas kernels for 0% -> 0%
where the time goes in v8:
time: 201 us; the launch traced here: 200 us
  waiting for transfers between devices  57.9 us (29%)
  matrix products  42.9 us (21%)
  local copies, waits for them, and re-layouts  42.5 us (21%)
  starting transfers between devices  28.5 us (14%)
  other arithmetic  21.1 us (10%)
  between operations  6.83 us (3%)
    ppermute x12, waiting for transfers between devices, ring(): lax.ppermute(x, 'tensor', [(i, (i + step) % size) for i in range(size)])  57.9 us
    ppermute x12, starting transfers between devices, ring(): lax.ppermute(x, 'tensor', [(i, (i + step) % size) for i in range(size)])  14.8 us
    ppermute x4, starting transfers between devices, shifted(): return lax.ppermute(x, axis, pairs)  13.7 us
    dot_general x1, matrix products, projected(): out = jnp.dot(near, near_rows, preferred_element_type=jnp.float32)  13.3 us
    unnamed x41, local copies, waits for them, and re-layouts  12.3 us
    dot_general x1, matrix products, projected(): out = out + jnp.dot(far, rows(2), preferred_element_type=jnp.float32)  6.03 us
    dot_general x1, matrix products, body(): jnp.einsum('ncd,ncv->ndv', k_decayed, v_float, precision=HIGH)  5.7 us
    mul x1, other arithmetic, body(): q_scaled = q_float * jnp.exp(cumul - centre[:, None, :])  5.06 us
  transfers between devices with their start and end apart: 16, of which 6 were waited for; matrix products, arithmetic and copies ran while one was open for 20% of the time, Pallas kernels for 0%

profile of v8, /device:TPU:2, one launch (start us, length us, event | category | flops | bytes accessed | tf_op | source)
XLA Modules:
  0.0 199.7 jit_solution(15304569654716999067)
XLA Ops:
  0.0 2.4 %fusion.155 = (bf16[512,512]{1,0:T(8,128)(2,1)}, bf16[512,512]{1,0:T(8,128)(2,1)}) fusion(bf16[1024,512]{1,0:T(8,128)(2,1)} %param.17), kind=kLoop, calls=%fused_computation.245 | loop fusion | bytes 2097152 | tf_op jit(solution)/shard_map/slice | solution.py:25
  8.4 2.5 %constant_dynamic-update-slice_fusion.3 = bf16[2048,1552]{1,0:T(8,128)(2,1)} fusion(bf16[2048,1552]{1,0:T(8,128)(2,1)} %constant_dynamic-update-slice_fusion.4, bf16[2048,256]{1,0:T(8,128)(2,1)} %param.20), kind=kLoop, calls=%fused_computation.204 | loop fusion | bytes 2097152
  15.8 3.2 %constant_dynamic-update-slice_fusion.1 = bf16[2048,1552]{1,0:T(8,128)(2,1)} fusion(bf16[2048,1552]{1,0:T(8,128)(2,1)} %constant_dynamic-update-slice_fusion.2, bf16[2048,512]{1,0:T(8,128)(2,1)} %param.22), kind=kLoop, calls=%fused_computation.202 | loop fusion | bytes 4194304
  22.4 2.9 %collective-permute-start.2 = (bf16[512,512]{1,0:T(8,128)(2,1)S(1)}, bf16[512,512]{1,0:T(8,128)(2,1)S(1)}, u32[]{:S(2)}, u32[]{:S(2)}) collective-permute-start(bf16[512,512]{1,0:T(8,128)(2,1)S(1)} %get-tuple-element.87), channel_id=1, source_target_pairs={{0,3},{1,0},{2,1},{3,2},{4,7},{5,4},{6,5},{7,6},{8,11},{9,8},{10,9... | collective-permute-start | bytes 1572872 | tf_op jit(solution)/shard_map/ppermute | solution.py:19
  25.3 4.6 %constant_dynamic-slice_fusion.2 = (bf16[512,1552]{1,0:T(8,128)(2,1)S(1)}, bf16[512,1552]{1,0:T(8,128)(2,1)}, bf16[512,1552]{1,0:T(8,128)(2,1)}) fusion(bf16[2048,1552]{1,0:T(8,128)(2,1)} %constant_dynamic-update-slice_fusion, s32[]{:T(128)S(6)} %select_n.57, s32[]{:T(128)S(6)} %select_n.61, s32[]{:T(128)S(6)} %select_n.59), kind=kLoop, calls=%fused_computation.230 | loop fusion | bytes 9535500 | tf_op jit(solution)/shard_map/dynamic_slice | solution.py:42
  29.9 5.0 %collective-permute-done.5 = bf16[512,512]{1,0:T(8,128)(2,1)S(1)} collective-permute-done((bf16[512,512]{1,0:T(8,128)(2,1)}, bf16[512,512]{1,0:T(8,128)(2,1)S(1)}, u32[]{:S(2)}, u32[]{:S(2)}) %collective-permute-start.5) | collective-permute-done | bytes 524320 | tf_op jit(solution)/shard_map/ppermute | solution.py:19
  34.9 3.0 %collective-permute-done.4 = bf16[512,512]{1,0:T(8,128)(2,1)S(1)} collective-permute-done((bf16[512,512]{1,0:T(8,128)(2,1)}, bf16[512,512]{1,0:T(8,128)(2,1)S(1)}, u32[]{:S(2)}, u32[]{:S(2)}) %collective-permute-start.4) | collective-permute-done | bytes 524320 | tf_op jit(solution)/shard_map/ppermute | solution.py:19
  37.9 6.0 %fusion.18 = f32[1024,1552]{0,1:T(8,128)} fusion(bf16[2048,1552]{1,0:T(8,128)(2,1)} %constant_dynamic-update-slice_fusion, s32[]{:T(128)S(6)} %select_n.63, bf16[512,512]{1,0:T(8,128)(2,1)S(1)} %collective-permute-done.5, bf16[512,512]{1,0:T(8,128)(2,1)S(1)} %collective-permute-done.4), kind=kOutput, calls=%fused_computation.22 | convolution fusion | flops 1629487104 | bytes 9109508 | tf_op jit(solution)/shard_map/dot_general | solution.py:46
  43.9 3.2 %collective-permute-done.3 = bf16[512,512]{1,0:T(8,128)(2,1)S(1)} collective-permute-done((bf16[512,512]{1,0:T(8,128)(2,1)S(1)}, bf16[512,512]{1,0:T(8,128)(2,1)S(1)}, u32[]{:S(2)}, u32[]{:S(2)}) %collective-permute-start.3) | collective-permute-done | bytes 524320 | tf_op jit(solution)/shard_map/ppermute | solution.py:19
  48.8 13.3 %fusion.161 = (bf16[1024,1552]{0,1:T(8,128)(2,1)}, f32[1024,1552]{0,1:T(8,128)}) fusion(f32[1024,1552]{0,1:T(8,128)} %fusion.18, bf16[512,1552]{1,0:T(8,128)(2,1)} %get-tuple-element.55, bf16[512,1552]{1,0:T(8,128)(2,1)} %get-tuple-element.56, bf16[512,1552]{1,0:T(8,128)(2,1)S(1)} %get-tuple-element.54, bf16[512,512]{1,0:T(8,128)(2,1)} %copy-done.14, ...), kind=kOutput, calls=%fused_computation.251 | convolution fusion | flops 4915380224 | bytes 23805952 | tf_op jit(solution)/shard_map/dot_general | solution.py:45
  62.1 2.8 %slice_convert_fusion = (f32[1024,256]{0,1:T(8,128)}, f32[1024,256]{0,1:T(8,128)}) fusion(bf16[1024,1552]{0,1:T(8,128)(2,1)} %get-tuple-element.117), kind=kLoop, calls=%fused_computation.92 | loop fusion | flops 524288 | bytes 3145728 | tf_op jit(solution)/shard_map/reshape | solution.py:113
  64.9 2.3 %slice.446 = bf16[1024,512]{0,1:T(8,128)(2,1)} slice(bf16[1024,1552]{0,1:T(8,128)(2,1)} %get-tuple-element.117), slice={[0:1024], [512:1024]} | slice | bytes 2097152 | tf_op jit(solution)/shard_map/slice | solution.py:49
  67.2 2.0 fusion.38
  70.1 2.9 %copy.45 = f32[1024,256]{1,0:T(8,128)} copy(f32[1024,256]{0,1:T(8,128)} %get-tuple-element.58) | data formatting | bytes 2097152 | tf_op jit(solution)/shard_map/convert_element_type | solution.py:112
  73.1 2.5 %copy.48 = f32[1024,256]{1,0:T(8,128)} copy(f32[1024,256]{0,1:T(8,128)} %get-tuple-element.57) | data formatting | bytes 2097152 | tf_op jit(solution)/shard_map/reshape | solution.py:113
  77.9 5.1 %exponential_multiply_fusion.2 = (f32[16,64,256]{2,0,1:T(8,128)}, f32[16,64,256]{2,0,1:T(8,128)}, f32[16,64,256]{2,0,1:T(8,128)S(1)}, f32[16,64,256]{2,0,1:T(8,128)}, f32[16,64,256]{2,0,1:T(8,128)S(1)}) fusion(f32[16,64,256]{2,0,1:T(8,128)} %copy-done.3, f32[16,64,256]{2,1,0:T(8,128)} %bitcast.312, f32[16,256]{1,0:T(8,128)S(1)} %get-tuple-element.70, ...), kind=kLoop, calls=%fused_computation.79 | loop fusion | flops 2359296 | bytes 8441856 | tf_op jit(solution)/shard_map/mul | solution.py:119
  83.6 5.7 %fusion.42 = f32[16,256,512]{2,1,0:T(8,128)} fusion(bf16[16,64,512]{2,1,0:T(8,128)(2,1)S(1)} %bitcast.307, f32[16,64,256]{2,0,1:T(8,128)S(1)} %get-tuple-element.63), kind=kOutput, calls=%fused_computation.68 | convolution fusion | flops 805306368 | bytes 10485760 | tf_op jit(solution)/shard_map/ncd,ncv->ndv/dot_general | solution.py:128
  89.5 3.7 %multiply_add_fusion.2 = (f32[1,256,512]{2,1,0:T(8,128)S(1)}, f32[1,256,512]{2,1,0:T(8,128)S(1)}, f32[1,256,512]{2,1,0:T(8,128)S(1)}, f32[1,256,512]{2,1,0:T(8,1...) fusion(f32[16,256,512]{2,1,0:T(8,128)} %fusion.42, ...), kind=kLoop, calls=%fused_computation.146 | loop fusion | flops 3538944 | bytes 11024384 | tf_op jit(solution)/shard_map/add | solution.py:136
  93.2 1.8 copy-done.1
  96.6 1.9 collective-permute-start.6
  98.5 5.8 %collective-permute-start.9 = (bf16[258,512]{1,0:T(8,128)(2,1)}, bf16[258,512]{1,0:T(8,128)(2,1)}, u32[]{:S(2)}, u32[]{:S(2)}) collective-permute-start(bf16[258,512]{1,0:T(8,128)(2,1)} %pad_maximum_fusion), channel_id=1, source_target_pairs={{0,16},{4,20},{8,24},{12,28},{16,32},{20,36},{24,40},{28,44},{32,4... | collective-permute-start | bytes 792584 | tf_op jit(solution)/shard_map/ppermute | solution.py:14
  104.3 2.5 %collective-permute-start.8 = (bf16[258,512]{1,0:T(8,128)(2,1)}, bf16[258,512]{1,0:T(8,128)(2,1)}, u32[]{:S(2)}, u32[]{:S(2)}) collective-permute-start(bf16[258,512]{1,0:T(8,128)(2,1)} %pad_maximum_fusion), channel_id=1, source_target_pairs={{0,12},{4,16},{8,20},{12,24},{16,28},{20,32},{24,36},{28,40},{32,4... | collective-permute-start | bytes 792584 | tf_op jit(solution)/shard_map/ppermute | solution.py:14
  106.8 3.5 %collective-permute-start.7 = (bf16[258,512]{1,0:T(8,128)(2,1)}, bf16[258,512]{1,0:T(8,128)(2,1)}, u32[]{:S(2)}, u32[]{:S(2)}) collective-permute-start(bf16[258,512]{1,0:T(8,128)(2,1)} %pad_maximum_fusion), channel_id=1, source_target_pairs={{0,8},{4,12},{8,16},{12,20},{16,24},{20,28},{24,32},{28,36},{32,40... | collective-permute-start | bytes 792584 | tf_op jit(solution)/shard_map/ppermute | solution.py:14
  118.3 2.2 %multiply_add_fusion.1 = f32[16,64,512]{2,1,0:T(8,128)} fusion(f32[16,64,512]{2,1,0:T(8,128)S(1)} %fusion.21, f32[16,64,64]{2,1,0:T(8,128)S(1)} %convolution_select_fusion, bf16[16,64,512]{2,1,0:T(8,128)(2,1)S(1)} %bitcast.308, f32[16,64]{1,0:T(8,128)S(1)} %compare_convert_fusion.1), kind=kOutput, calls=%fused_computation.21 | convolution fusion | flops 202375168 | bytes 5509120 | tf_op jit(solution)/shard_map/ncs,nsv->ncv/dot_general | solution.py:124
  122.0 2.9 %copy.61 = f32[1024,512]{0,1:T(8,128)} copy(f32[1024,512]{1,0:T(8,128)} %bitcast.309) | data formatting | bytes 4194304 | tf_op jit(solution)/shard_map/reshape | solution.py:139
  137.5 2.7 %multiply_reduce_fusion = (f32[1024]{0:T(1024)S(1)}, f32[1024,512]{0,1:T(8,128)S(1)}) fusion(f32[1024,512]{0,1:T(8,128)S(1)} %copy-done.2, f32[1024]{0:T(1024)S(1)} %select_bitcast_fusion, f32[258,512]{1,0:T(8,128)S(1)} %convert_element_type.116, f32[258,512]{1,0:T(8,128)S(1)} %convert_element_type.113, f32[258,512]{1,0:T(8,128)S(1)} %convert_element_type.110, ...), kind=kOutput, calls=%fused_computation.19 | convolution fusion | flops 809237504 | bytes 7875584 | tf_op jit(solution)/shard_map/dot_general | solution.py:158
  140.3 2.3 %multiply_convert_fusion = bf16[1024,512]{0,1:T(8,128)(2,1)S(1)} fusion(f32[1024,1552]{0,1:T(8,128)} %get-tuple-element.118, f32[1024,512]{0,1:T(8,128)S(1)} %get-tuple-element.120, f32[512]{0:T(512)S(1)} %copy-done.13, f32[1024]{0:T(1024)S(1)} %rsqrt_multiply_fusion), kind=kLoop, calls=%fused_computation.18 | loop fusion | flops 4194304 | bytes 5249024 | tf_op jit(solution)/shard_map/convert_element_type | solution.py:163
  144.9 2.0 %collective-permute-start.10 = (bf16[1024,512]{1,0:T(8,128)(2,1)S(1)}, bf16[1024,512]{1,0:T(8,128)(2,1)S(1)}, u32[]{:S(2)}, u32[]{:S(2)}) collective-permute-start(bf16[1024,512]{1,0:T(8,128)(2,1)S(1)} %convolution_convert_fusion.2), channel_id=1, source_target_pairs={{0,1},{1,2},{2,3},{3,0},{4,5},{5,6},{6,7},{7,4},{8,9},{9,10},{10,1... | collective-permute-start | bytes 3145736 | tf_op jit(solution)/shard_map/ppermute | solution.py:19
  149.1 32.6 %collective-permute-done.14 = bf16[512,512]{1,0:T(8,128)(2,1)S(1)} collective-permute-done((bf16[512,512]{1,0:T(8,128)(2,1)S(1)}, bf16[512,512]{1,0:T(8,128)(2,1)S(1)}, u32[]{:S(2)}, u32[]{:S(2)}) %collective-permute-start.14) | collective-permute-done | bytes 524320 | tf_op jit(solution)/shard_map/ppermute | solution.py:19
  183.7 11.4 %collective-permute-done.15 = bf16[512,512]{1,0:T(8,128)(2,1)S(1)} collective-permute-done((bf16[512,512]{1,0:T(8,128)(2,1)S(1)}, bf16[512,512]{1,0:T(8,128)(2,1)S(1)}, u32[]{:S(2)}, u32[]{:S(2)}) %collective-permute-start.15) | collective-permute-done | bytes 524320 | tf_op jit(solution)/shard_map/ppermute | solution.py:19
  195.1 2.7 %collective-permute-done.13 = bf16[512,512]{1,0:T(8,128)(2,1)S(1)} collective-permute-done((bf16[512,512]{1,0:T(8,128)(2,1)S(1)}, bf16[512,512]{1,0:T(8,128)(2,1)S(1)}, u32[]{:S(2)}, u32[]{:S(2)}) %collective-permute-start.13) | collective-permute-done | bytes 524320 | tf_op jit(solution)/shard_map/ppermute | solution.py:19
  197.8 2.0 add_convert_fusion
  (128 shorter events, 43.6 us)
Async XLA Ops:
  0.0 142.5 %copy-start = (bf16[512,2048]{1,0:T(8,128)(2,1)S(1)}, bf16[512,2048]{1,0:T(8,128)(2,1)}, u32[]{:S(2)}) copy-start(bf16[512,2048]{1,0:T(8,128)(2,1)} %param.27) | copy-start | bytes 6291460
  0.0 5.7 %copy-start.12 = (s32[1024]{0:T(1024)S(1)}, s32[1024]{0:T(1024)}, u32[]{:S(2)}) copy-start(s32[1024]{0:T(1024)} %param.18) | copy-start | bytes 12292
  0.0 5.8 %copy-start.10 = (bf16[2048,256]{1,0:T(8,128)(2,1)S(1)}, bf16[2048,256]{1,0:T(8,128)(2,1)}, u32[]{:S(2)}) copy-start(bf16[2048,256]{1,0:T(8,128)(2,1)} %param.19) | copy-start | bytes 3145732
  2.4 17.4 %collective-permute-start = (bf16[512,512]{1,0:T(8,128)(2,1)}, bf16[512,512]{1,0:T(8,128)(2,1)}, u32[]{:S(2)}, u32[]{:S(2)}) collective-permute-start(bf16[512,512]{1,0:T(8,128)(2,1)} %get-tuple-element.90), channel_id=1, source_target_pairs={{0,1},{1,2},{2,3},{3,0},{4,5},{5,6},{6,7},{7,4},{8,9},{9,10},{10,1... | collective-permute-start | bytes 1572872 | tf_op jit(solution)/shard_map/ppermute | solution.py:19
  4.0 15.9 %collective-permute-start.1 = (bf16[512,512]{1,0:T(8,128)(2,1)}, bf16[512,512]{1,0:T(8,128)(2,1)}, u32[]{:S(2)}, u32[]{:S(2)}) collective-permute-start(bf16[512,512]{1,0:T(8,128)(2,1)} %get-tuple-element.89), channel_id=1, source_target_pairs={{0,3},{1,0},{2,1},{3,2},{4,7},{5,4},{6,5},{7,6},{8,11},{9,8},{10,9... | collective-permute-start | bytes 1572872 | tf_op jit(solution)/shard_map/ppermute | solution.py:19
  8.2 2.7 %copy-start.9 = (bf16[2048,512]{1,0:T(8,128)(2,1)S(1)}, bf16[2048,512]{1,0:T(8,128)(2,1)}, u32[]{:S(2)}) copy-start(bf16[2048,512]{1,0:T(8,128)(2,1)} %param.21) | copy-start | bytes 6291460
  10.8 2.1 %copy-start.11 = (bf16[2048,16]{0,1:T(8,128)(2,1)S(1)}, bf16[2048,16]{0,1:T(8,128)(2,1)}, u32[]{:S(2)}) copy-start(bf16[2048,16]{0,1:T(8,128)(2,1)} %param.23) | copy-start | bytes 196612
  15.8 6.1 %copy-start.5 = (bf16[1024,512]{1,0:T(8,128)(2,1)S(1)}, bf16[1024,512]{1,0:T(8,128)(2,1)}, u32[]{:S(2)}) copy-start(bf16[1024,512]{1,0:T(8,128)(2,1)} %param.17) | copy-start | bytes 3145732
  19.9 15.0 %collective-permute-start.5 = (bf16[512,512]{1,0:T(8,128)(2,1)}, bf16[512,512]{1,0:T(8,128)(2,1)S(1)}, u32[]{:S(2)}, u32[]{:S(2)}) collective-permute-start(bf16[512,512]{1,0:T(8,128)(2,1)} %collective-permute-done.1), channel_id=1, source_target_pairs={{0,3},{1,0},{2,1},{3,2},{4,7},{5,4},{6,5},{7,6},{8,11},{9,8},{10,9... | collective-permute-start | bytes 1572872 | tf_op jit(solution)/shard_map/ppermute | solution.py:19
  21.7 16.2 %collective-permute-start.4 = (bf16[512,512]{1,0:T(8,128)(2,1)}, bf16[512,512]{1,0:T(8,128)(2,1)S(1)}, u32[]{:S(2)}, u32[]{:S(2)}) collective-permute-start(bf16[512,512]{1,0:T(8,128)(2,1)} %collective-permute-done), channel_id=1, source_target_pairs={{0,1},{1,2},{2,3},{3,0},{4,5},{5,6},{6,7},{7,4},{8,9},{9,10},{10,1... | collective-permute-start | bytes 1572872 | tf_op jit(solution)/shard_map/ppermute | solution.py:19
  22.0 25.2 %collective-permute-start.3 = (bf16[512,512]{1,0:T(8,128)(2,1)S(1)}, bf16[512,512]{1,0:T(8,128)(2,1)S(1)}, u32[]{:S(2)}, u32[]{:S(2)}) collective-permute-start(bf16[512,512]{1,0:T(8,128)(2,1)S(1)} %get-tuple-element.88), channel_id=1, source_target_pairs={{0,1},{1,2},{2,3},{3,0},{4,5},{5,6},{6,7},{7,4},{8,9},{9,10},{10,1... | collective-permute-start | bytes 1572872 | tf_op jit(solution)/shard_map/ppermute | solution.py:19
  22.4 24.8 %collective-permute-start.2 = (bf16[512,512]{1,0:T(8,128)(2,1)S(1)}, bf16[512,512]{1,0:T(8,128)(2,1)S(1)}, u32[]{:S(2)}, u32[]{:S(2)}) collective-permute-start(bf16[512,512]{1,0:T(8,128)(2,1)S(1)} %get-tuple-element.87), channel_id=1, source_target_pairs={{0,3},{1,0},{2,1},{3,2},{4,7},{5,4},{6,5},{7,6},{8,11},{9,8},{10,9... | collective-permute-start | bytes 1572872 | tf_op jit(solution)/shard_map/ppermute | solution.py:19
  62.1 5.1 %copy-start.16 = (bf16[16,256]{1,0:T(8,128)(2,1)S(1)}, bf16[16,256]{1,0:T(8,128)(2,1)}, u32[]{:S(2)}) copy-start(bf16[16,256]{1,0:T(8,128)(2,1)} %param.24) | copy-start | bytes 24580
  62.1 5.1 %copy-start.17 = (f32[256]{0:T(256)S(1)}, f32[256]{0:T(256)}, u32[]{:S(2)}) copy-start(f32[256]{0:T(256)} %param.25) | copy-start | bytes 3076
  70.1 3.0 %copy-start.3 = (f32[16,64,256]{2,0,1:T(8,128)}, f32[16,64,256]{2,0,1:T(8,128)S(1)}, u32[]{:S(2)}) copy-start(f32[16,64,256]{2,0,1:T(8,128)S(1)} %fusion.46) | copy-start | bytes 3145732
  83.6 5.7 %copy-start.4 = (f32[16,64,256]{2,1,0:T(8,128)}, f32[16,64,256]{2,1,0:T(8,128)S(1)}, u32[]{:S(2)}) copy-start(f32[16,64,256]{2,1,0:T(8,128)S(1)} %copy.59) | copy-start | bytes 3145732
  89.5 5.6 %copy-start.1 = (f32[16,256,512]{2,1,0:T(8,128)S(1)}, f32[16,256,512]{2,1,0:T(8,128)}, u32[]{:S(2)}) copy-start(f32[16,256,512]{2,1,0:T(8,128)} %fusion.42) | copy-start | bytes 25165828
  95.0 15.3 %copy-start.8 = (f32[16,64,256]{2,0,1:T(8,128)S(1)}, f32[16,64,256]{2,0,1:T(8,128)}, u32[]{:S(2)}) copy-start(f32[16,64,256]{2,0,1:T(8,128)} %get-tuple-element.60) | copy-start | bytes 3145732
  96.6 28.3 %collective-permute-start.6 = (bf16[258,512]{1,0:T(8,128)(2,1)}, bf16[258,512]{1,0:T(8,128)(2,1)S(1)}, u32[]{:S(2)}, u32[]{:S(2)}) collective-permute-start(bf16[258,512]{1,0:T(8,128)(2,1)} %pad_maximum_fusion), channel_id=1, source_target_pairs={{0,4},{4,8},{8,12},{12,16},{16,20},{20,24},{24,28},{28,32},{32,36}... | collective-permute-start | bytes 792584 | tf_op jit(solution)/shard_map/ppermute | solution.py:14
  98.5 29.1 %collective-permute-start.9 = (bf16[258,512]{1,0:T(8,128)(2,1)}, bf16[258,512]{1,0:T(8,128)(2,1)}, u32[]{:S(2)}, u32[]{:S(2)}) collective-permute-start(bf16[258,512]{1,0:T(8,128)(2,1)} %pad_maximum_fusion), channel_id=1, source_target_pairs={{0,16},{4,20},{8,24},{12,28},{16,32},{20,36},{24,40},{28,44},{32,4... | collective-permute-start | bytes 792584 | tf_op jit(solution)/shard_map/ppermute | solution.py:14
  104.3 21.2 %collective-permute-start.8 = (bf16[258,512]{1,0:T(8,128)(2,1)}, bf16[258,512]{1,0:T(8,128)(2,1)}, u32[]{:S(2)}, u32[]{:S(2)}) collective-permute-start(bf16[258,512]{1,0:T(8,128)(2,1)} %pad_maximum_fusion), channel_id=1, source_target_pairs={{0,12},{4,16},{8,20},{12,24},{16,28},{20,32},{24,36},{28,40},{32,4... | collective-permute-start | bytes 792584 | tf_op jit(solution)/shard_map/ppermute | solution.py:14
  106.8 23.6 %collective-permute-start.7 = (bf16[258,512]{1,0:T(8,128)(2,1)}, bf16[258,512]{1,0:T(8,128)(2,1)}, u32[]{:S(2)}, u32[]{:S(2)}) collective-permute-start(bf16[258,512]{1,0:T(8,128)(2,1)} %pad_maximum_fusion), channel_id=1, source_target_pairs={{0,8},{4,12},{8,16},{12,20},{16,24},{20,28},{24,32},{28,36},{32,40... | collective-permute-start | bytes 792584 | tf_op jit(solution)/shard_map/ppermute | solution.py:14
  115.0 1.3 copy-start.6
  115.0 1.5 copy-start.7
  127.6 9.9 %copy-start.2 = (f32[1024,512]{0,1:T(8,128)S(1)}, f32[1024,512]{0,1:T(8,128)}, u32[]{:S(2)}) copy-start(f32[1024,512]{0,1:T(8,128)} %copy.61) | copy-start | bytes 6291460
  137.5 2.8 %copy-start.13 = (f32[512]{0:T(512)S(1)}, f32[512]{0:T(512)}, u32[]{:S(2)}) copy-start(f32[512]{0:T(512)} %param.26) | copy-start | bytes 6148
  144.8 38.9 %collective-permute-start.11 = (bf16[1024,512]{1,0:T(8,128)(2,1)S(1)}, bf16[1024,512]{1,0:T(8,128)(2,1)S(1)}, u32[]{:S(2)}, u32[]{:S(2)}) collective-permute-start(bf16[1024,512]{1,0:T(8,128)(2,1)S(1)} %convolution_convert_fusion.1), channel_id=1, source_target_pairs={{0,3},{1,0},{2,1},{3,2},{4,7},{5,4},{6,5},{7,6},{8,11},{9,8},{10,9... | collective-permute-start | bytes 3145736 | tf_op jit(solution)/shard_map/ppermute | solution.py:19
  144.9 38.8 %collective-permute-start.10 = (bf16[1024,512]{1,0:T(8,128)(2,1)S(1)}, bf16[1024,512]{1,0:T(8,128)(2,1)S(1)}, u32[]{:S(2)}, u32[]{:S(2)}) collective-permute-start(bf16[1024,512]{1,0:T(8,128)(2,1)S(1)} %convolution_convert_fusion.2), channel_id=1, source_target_pairs={{0,1},{1,2},{2,3},{3,0},{4,5},{5,6},{6,7},{7,4},{8,9},{9,10},{10,1... | collective-permute-start | bytes 3145736 | tf_op jit(solution)/shard_map/ppermute | solution.py:19
  147.0 34.7 %collective-permute-start.14 = (bf16[512,512]{1,0:T(8,128)(2,1)S(1)}, bf16[512,512]{1,0:T(8,128)(2,1)S(1)}, u32[]{:S(2)}, u32[]{:S(2)}) collective-permute-start(bf16[512,512]{1,0:T(8,128)(2,1)S(1)} %get-tuple-element.66), channel_id=1, source_target_pairs={{0,3},{1,0},{2,1},{3,2},{4,7},{5,4},{6,5},{7,6},{8,11},{9,8},{10,9... | collective-permute-start | bytes 1572872 | tf_op jit(solution)/shard_map/ppermute | solution.py:19
  148.4 34.8 %collective-permute-start.12 = (bf16[512,512]{1,0:T(8,128)(2,1)S(1)}, bf16[512,512]{1,0:T(8,128)(2,1)S(1)}, u32[]{:S(2)}, u32[]{:S(2)}) collective-permute-start(bf16[512,512]{1,0:T(8,128)(2,1)S(1)} %get-tuple-element.65), channel_id=1, source_target_pairs={{0,1},{1,2},{2,3},{3,0},{4,5},{5,6},{6,7},{7,4},{8,9},{9,10},{10,1... | collective-permute-start | bytes 1572872 | tf_op jit(solution)/shard_map/ppermute | solution.py:19
  181.7 13.4 %collective-permute-start.15 = (bf16[512,512]{1,0:T(8,128)(2,1)S(1)}, bf16[512,512]{1,0:T(8,128)(2,1)S(1)}, u32[]{:S(2)}, u32[]{:S(2)}) collective-permute-start(bf16[512,512]{1,0:T(8,128)(2,1)S(1)} %collective-permute-done.14), channel_id=1, source_target_pairs={{0,3},{1,0},{2,1},{3,2},{4,7},{5,4},{6,5},{7,6},{8,11},{9,8},{10,9... | collective-permute-start | bytes 1572872 | tf_op jit(solution)/shard_map/ppermute | solution.py:19
  183.2 14.6 %collective-permute-start.13 = (bf16[512,512]{1,0:T(8,128)(2,1)S(1)}, bf16[512,512]{1,0:T(8,128)(2,1)S(1)}, u32[]{:S(2)}, u32[]{:S(2)}) collective-permute-start(bf16[512,512]{1,0:T(8,128)(2,1)S(1)} %collective-permute-done.12), channel_id=1, source_target_pairs={{0,1},{1,2},{2,3},{3,0},{4,5},{5,6},{6,7},{7,4},{8,9},{9,10},{10,1... | collective-permute-start | bytes 1572872 | tf_op jit(solution)/shard_map/ppermute | solution.py:19
  (2 other events, 1.6 us)

commit v9 on v8

--- a/solution.py
+++ b/solution.py
@@ -36,18 +36,15 @@
     size = lax.axis_size("tensor")
     index = lax.axis_index("tensor")
     width = far.shape[1]
-    joined = jnp.concatenate(weights, axis=1)
+    parts = []
+    for weight in weights:
 
-    def rows(offset):
-        return lax.dynamic_slice_in_dim(joined, ((index + offset) % size) * width, width, 0)
+        def rows(offset):
+            return lax.dynamic_slice_in_dim(weight, ((index + offset) % size) * width, width, 0)
 
-    near_rows = jnp.concatenate([rows(0), rows(1), rows(size - 1)])
-    out = jnp.dot(near, near_rows, preferred_element_type=jnp.float32)
-    out = out + jnp.dot(far, rows(2), preferred_element_type=jnp.float32)
-    parts, at = [], 0
-    for weight in weights:
-        parts.append(out[:, at : at + weight.shape[1]])
-        at += weight.shape[1]
+        near_rows = jnp.concatenate([rows(0), rows(1), rows(size - 1)])
+        out = jnp.dot(near, near_rows, preferred_element_type=jnp.float32)
+        parts.append(out + jnp.dot(far, rows(2), preferred_element_type=jnp.float32))
     return parts
 
 

time: 201 us -> 177 us (0.88)
  local copies, waits for them, and re-layouts: 42.5 us -> 19.6 us
  other arithmetic: 21.1 us -> 13.3 us
  waiting for transfers between devices: 57.9 us -> 62.7 us
  starting transfers between devices: 28.5 us -> 33.2 us
  matrix products: 42.9 us -> 40.1 us
    unnamed x41 -> x57, local copies, waits for them, and re-layouts: 12.3 us -> 3.36 us
    ppermute x12, starting transfers between devices: 14.8 us -> 19.8 us  [ring(): lax.ppermute(x, 'tensor', [(i, (i + step) % size) for i in range(size)])]
    ppermute x12, waiting for transfers between devices: 57.9 us -> 62.7 us  [ring(): lax.ppermute(x, 'tensor', [(i, (i + step) % size) for i in range(size)])]
    slice x2 -> x0, local copies, waits for them, and re-layouts: 3.76 us -> none  [projected(): parts.append(out[:, at:at + weight.shape[1]])]
    convert_element_type x1 -> x0, local copies, waits for them, and re-layouts: 2.93 us -> none  [body(): q_float = query.astype(jnp.float32).reshape(blocks, GROUP, key_width)]
    reshape x1, other arithmetic: 2.78 us -> 0.1 us  [body(): k_float = key.astype(jnp.float32).reshape(blocks, GROUP, key_width)]
    reshape x1 -> x0, local copies, waits for them, and re-layouts: 2.53 us -> none  [body(): k_float = key.astype(jnp.float32).reshape(blocks, GROUP, key_width)]
    convert_element_type x1 -> x0, other arithmetic: 2.26 us -> none  [body(): gated = (normed * jax.nn.silu(outgate)).astype(jnp.bfloat16)]
  transfers between devices with their start and end apart: 16 -> 16, of which waited for: 6 -> 7; matrix products, arithmetic and copies ran while one was open for 20% -> 16% of each run, Pallas kernels for 0% -> 0%
where the time goes in v9:
time: 177 us; the launch traced here: 176 us
  waiting for transfers between devices  62.7 us (35%)
  matrix products  40.1 us (23%)
  starting transfers between devices  33.2 us (19%)
  local copies, waits for them, and re-layouts  19.6 us (11%)
  other arithmetic  13.3 us (8%)
  between operations  7.16 us (4%)
    ppermute x12, waiting for transfers between devices, ring(): lax.ppermute(x, 'tensor', [(i, (i + step) % size) for i in range(size)])  62.7 us
    ppermute x12, starting transfers between devices, ring(): lax.ppermute(x, 'tensor', [(i, (i + step) % size) for i in range(size)])  19.8 us
    ppermute x4, starting transfers between devices, shifted(): return lax.ppermute(x, axis, pairs)  13.4 us
    dot_general x5, matrix products, projected(): out = jnp.dot(near, near_rows, preferred_element_type=jnp.float32)  13.3 us
    dot_general x1, matrix products, body(): jnp.einsum('ncd,ncv->ndv', k_decayed, v_float, precision=HIGH)  5.74 us
    dot_general x5, matrix products, projected(): jnp.dot(far, rows(2), preferred_element_type=jnp.float32)  5.14 us
    dot_general x16, matrix products, body(): inters.append(jnp.dot(q_decayed[n], entering, precision=HIGH))  5.02 us
    dot_general x4, matrix products, term(): jnp.dot(gated, cols, preferred_element_type=jnp.float32)  4.24 us
  transfers between devices with their start and end apart: 16, of which 7 were waited for; matrix products, arithmetic and copies ran while one was open for 16% of the time, Pallas kernels for 0%

profile of v9, /device:TPU:2, one launch (start us, length us, event | category | flops | bytes accessed | tf_op | source)
XLA Modules:
  0.0 176.2 jit_solution(13411581105650269514)
XLA Ops:
  1.4 1.6 collective-permute-start
  3.1 1.7 collective-permute-start.1
  12.5 4.0 %collective-permute-done = bf16[512,512]{1,0:T(8,128)(2,1)} collective-permute-done((bf16[512,512]{1,0:T(8,128)(2,1)S(1)}, bf16[512,512]{1,0:T(8,128)(2,1)}, u32[]{:S(2)}, u32[]{:S(2)}) %collective-permute-start) | collective-permute-done | bytes 524320 | tf_op jit(solution)/shard_map/ppermute | solution.py:19
  18.2 1.7 collective-permute-start.5
  20.5 2.9 %collective-permute-start.2 = (bf16[512,512]{1,0:T(8,128)(2,1)S(1)}, bf16[512,512]{1,0:T(8,128)(2,1)S(1)}, u32[]{:S(2)}, u32[]{:S(2)}) collective-permute-start(bf16[512,512]{1,0:T(8,128)(2,1)S(1)} %get-tuple-element.94), channel_id=1, source_target_pairs={{0,3},{1,0},{2,1},{3,2},{4,7},{5,4},{6,5},{7,6},{8,11},{9,8},{10,9... | collective-permute-start | bytes 1572872 | tf_op jit(solution)/shard_map/ppermute | solution.py:19
  23.4 9.4 %collective-permute-done.4 = bf16[512,512]{1,0:T(8,128)(2,1)S(1)} collective-permute-done((bf16[512,512]{1,0:T(8,128)(2,1)}, bf16[512,512]{1,0:T(8,128)(2,1)S(1)}, u32[]{:S(2)}, u32[]{:S(2)}) %collective-permute-start.4) | collective-permute-done | bytes 524320 | tf_op jit(solution)/shard_map/ppermute | solution.py:19
  33.3 2.1 %fusion.103 = f32[1024,512]{0,1:T(8,128)} fusion(bf16[1024,512]{1,0:T(8,128)(2,1)S(1)} %constant_dynamic-update-slice_fusion, bf16[2048,512]{1,0:T(8,128)(2,1)S(1)} %copy-done.12, s32[]{:T(128)S(6)} %select_n.111), kind=kOutput, calls=%fused_computation.150 | convolution fusion | flops 536870912 | bytes 3670020 | tf_op jit(solution)/shard_map/dot_general | solution.py:47
  36.7 1.8 fusion.107
  38.4 3.7 %collective-permute-done.3 = bf16[512,512]{1,0:T(8,128)(2,1)S(1)} collective-permute-done((bf16[512,512]{1,0:T(8,128)(2,1)S(1)}, bf16[512,512]{1,0:T(8,128)(2,1)S(1)}, u32[]{:S(2)}, u32[]{:S(2)}) %collective-permute-start.3) | collective-permute-done | bytes 524320 | tf_op jit(solution)/shard_map/ppermute | solution.py:19
  42.1 2.5 %convolution_add_fusion.3 = f32[1024,16]{0,1:T(8,128)S(1)} fusion(f32[1024,16]{0,1:T(8,128)S(1)} %fusion.160, bf16[512,16]{0,1:T(8,128)(2,1)S(1)} %get-tuple-element.106, bf16[512,16]{0,1:T(8,128)(2,1)S(1)} %get-tuple-element.105, bf16[512,16]{0,1:T(8,128)(2,1)S(1)} %get-tuple-element.104, bf16[512,512]{1,0:T(8,128)(2,1)S(1)} %collective-permute-done.3, ...), kind=kOutput, calls=%fused_computation.64 | convolution fusion | flops 66224128 | bytes 3325952 | tf_op jit(solution)/shard_map/dot_general | solution.py:46
  46.5 2.2 %fusion.17 = bf16[1024,256]{1,0:T(8,128)(2,1)S(1)} fusion(f32[1024,256]{1,0:T(8,128)S(1)} %fusion.116, bf16[512,256]{1,0:T(8,128)(2,1)S(1)} %get-tuple-element.90, bf16[512,256]{1,0:T(8,128)(2,1)S(1)} %get-tuple-element.89, bf16[512,256]{1,0:T(8,128)(2,1)S(1)} %get-tuple-element.88, bf16[512,512]{1,0:T(8,128)(2,1)S(1)} %collective-permute-done.3, ...), kind=kOutput, calls=%fused_computation.30 | convolution fusion | flops 823918592 | bytes 5505024 | tf_op jit(solution)/shard_map/dot_general | solution.py:46
  48.9 2.2 %fusion.16 = f32[1024,256]{1,0:T(8,128)S(1)} fusion(f32[1024,256]{1,0:T(8,128)S(1)} %fusion.118, bf16[512,256]{1,0:T(8,128)(2,1)S(1)} %get-tuple-element.129, bf16[512,256]{1,0:T(8,128)(2,1)S(1)} %get-tuple-element.130, bf16[512,256]{1,0:T(8,128)(2,1)S(1)} %get-tuple-element.131, bf16[512,512]{1,0:T(8,128)(2,1)S(1)} %collective-permute-done.3, ...), kind=kOutput, calls=%fused_computation.29 | convolution fusion | flops 824180736 | bytes 6029312 | tf_op jit(solution)/shard_map/dot_general | solution.py:46
  51.1 3.2 %exponential_multiply_fusion.2 = (f32[16,64,256]{2,0,1:T(8,128)}, f32[16,64,256]{2,0,1:T(8,128)}, f32[16,64,256]{2,0,1:T(8,128)S(1)}, f32[16,64,256]{2,0,1:T(8,128)}, f32[16,64,256]{2,0,1:T(8,128)S(1)}) fusion(f32[16,64,256]{2,0,1:T(8,128)S(1)} %fusion.42, f32[16,64,256]{2,1,0:T(8,128)S(1)} %bitcast.319, f32[16,256]{1,0:T(8,128)S(1)} %get-tuple-element.71, ...), kind=kLoop, calls=%fused_computation.78 | loop fusion | flops 2359296 | bytes 8441856 | tf_op jit(solution)/shard_map/mul | solution.py:116
  55.0 3.0 %add_convert_fusion.1 = bf16[1024,512]{1,0:T(8,128)(2,1)S(1)} fusion(f32[1024,512]{1,0:T(8,128)S(1)} %fusion.107, bf16[512,512]{1,0:T(8,128)(2,1)S(1)} %get-tuple-element.63, bf16[512,512]{1,0:T(8,128)(2,1)S(1)} %get-tuple-element.62, bf16[512,512]{1,0:T(8,128)(2,1)S(1)} %get-tuple-element.61, bf16[512,512]{1,0:T(8,128)(2,1)S(1)} %collective-permute-done.3, ...), kind=kOutput, calls=%fused_computation.7 | convolution fusion | flops 1632108544 | bytes 7864320 | tf_op jit(solution)/shard_map/dot_general | solution.py:46
  58.0 5.7 %fusion.38 = f32[16,256,512]{2,1,0:T(8,128)} fusion(bf16[16,64,512]{2,1,0:T(8,128)(2,1)S(1)} %bitcast.317, f32[16,64,256]{2,0,1:T(8,128)S(1)} %get-tuple-element.64), kind=kOutput, calls=%fused_computation.67 | convolution fusion | flops 805306368 | bytes 10485760 | tf_op jit(solution)/shard_map/ncd,ncv->ndv/dot_general | solution.py:125
  64.2 3.7 %multiply_add_fusion.2 = (f32[1,256,512]{2,1,0:T(8,128)S(1)}, f32[1,256,512]{2,1,0:T(8,128)S(1)}, f32[1,256,512]{2,1,0:T(8,128)S(1)}, f32[1,256,512]{2,1,0:T(8,1...) fusion(f32[16,256,512]{2,1,0:T(8,128)} %fusion.38, ...), kind=kLoop, calls=%fused_computation.155 | loop fusion | flops 3538944 | bytes 11024384 | tf_op jit(solution)/shard_map/add | solution.py:133
  67.9 1.8 %copy-done.1 = f32[16,256,512]{2,1,0:T(8,128)S(1)} copy-done((f32[16,256,512]{2,1,0:T(8,128)S(1)}, f32[16,256,512]{2,1,0:T(8,128)}, u32[]{:S(2)}) %copy-start.1) | copy-done | bytes 8388632
  71.3 1.9 %collective-permute-start.6 = (bf16[258,512]{1,0:T(8,128)(2,1)}, bf16[258,512]{1,0:T(8,128)(2,1)S(1)}, u32[]{:S(2)}, u32[]{:S(2)}) collective-permute-start(bf16[258,512]{1,0:T(8,128)(2,1)} %pad_maximum_fusion), channel_id=1, source_target_pairs={{0,4},{4,8},{8,12},{12,16},{16,20},{20,24},{24,28},{28,32},{32,36}... | collective-permute-start | bytes 792584 | tf_op jit(solution)/shard_map/ppermute | solution.py:14
  73.2 5.8 %collective-permute-start.9 = (bf16[258,512]{1,0:T(8,128)(2,1)}, bf16[258,512]{1,0:T(8,128)(2,1)}, u32[]{:S(2)}, u32[]{:S(2)}) collective-permute-start(bf16[258,512]{1,0:T(8,128)(2,1)} %pad_maximum_fusion), channel_id=1, source_target_pairs={{0,16},{4,20},{8,24},{12,28},{16,32},{20,36},{24,40},{28,44},{32,4... | collective-permute-start | bytes 792584 | tf_op jit(solution)/shard_map/ppermute | solution.py:14
  79.0 2.5 %collective-permute-start.8 = (bf16[258,512]{1,0:T(8,128)(2,1)}, bf16[258,512]{1,0:T(8,128)(2,1)}, u32[]{:S(2)}, u32[]{:S(2)}) collective-permute-start(bf16[258,512]{1,0:T(8,128)(2,1)} %pad_maximum_fusion), channel_id=1, source_target_pairs={{0,12},{4,16},{8,20},{12,24},{16,28},{20,32},{24,36},{28,40},{32,4... | collective-permute-start | bytes 792584 | tf_op jit(solution)/shard_map/ppermute | solution.py:14
  81.5 3.2 %collective-permute-start.7 = (bf16[258,512]{1,0:T(8,128)(2,1)}, bf16[258,512]{1,0:T(8,128)(2,1)}, u32[]{:S(2)}, u32[]{:S(2)}) collective-permute-start(bf16[258,512]{1,0:T(8,128)(2,1)} %pad_maximum_fusion), channel_id=1, source_target_pairs={{0,8},{4,12},{8,16},{12,20},{16,24},{20,28},{24,32},{28,36},{32,40... | collective-permute-start | bytes 792584 | tf_op jit(solution)/shard_map/ppermute | solution.py:14
  91.0 1.7 convolution_select_fusion
  92.7 2.2 %multiply_add_fusion.1 = f32[16,64,512]{2,1,0:T(8,128)} fusion(f32[16,64,512]{2,1,0:T(8,128)S(1)} %fusion.18, f32[16,64,64]{2,1,0:T(8,128)S(1)} %convolution_select_fusion, bf16[16,64,512]{2,1,0:T(8,128)(2,1)S(1)} %bitcast.318, f32[16,64]{1,0:T(8,128)S(1)} %compare_convert_fusion.1), kind=kOutput, calls=%fused_computation.6 | convolution fusion | flops 202375168 | bytes 5509120 | tf_op jit(solution)/shard_map/ncs,nsv->ncv/dot_general | solution.py:121
  94.9 2.9 %copy.51 = f32[1024,512]{0,1:T(8,128)} copy(f32[1024,512]{1,0:T(8,128)} %bitcast.314) | data formatting | bytes 4194304 | tf_op jit(solution)/shard_map/reshape | solution.py:136
  113.3 3.4 %multiply_convert_fusion = bf16[1024,512]{0,1:T(8,128)(2,1)S(1)} fusion(f32[1024,512]{0,1:T(8,128)S(1)} %copy-done.13, f32[1024,512]{0,1:T(8,128)S(1)} %get-tuple-element.128, bf16[512,512]{1,0:T(8,128)(2,1)S(1)} %copy-done.18, bf16[512,512]{1,0:T(8,128)(2,1)S(1)} %copy-done.17, bf16[512,512]{1,0:T(8,128)(2,1)S(1)} %copy-done.16, f32[512]{0:T(512)S(1)} %copy-done.26, ...), kind=kOutput, calls=%fused_computation.3 | convolution fusion | flops 1635778560 | bytes 9967616 | tf_op jit(solution)/shard_map/dot_general | solution.py:46
  119.0 2.9 %collective-permute-start.11 = (bf16[1024,512]{1,0:T(8,128)(2,1)S(1)}, bf16[1024,512]{1,0:T(8,128)(2,1)S(1)}, u32[]{:S(2)}, u32[]{:S(2)}) collective-permute-start(bf16[1024,512]{1,0:T(8,128)(2,1)S(1)} %convolution_convert_fusion.1), channel_id=1, source_target_pairs={{0,3},{1,0},{2,1},{3,2},{4,7},{5,4},{6,5},{7,6},{8,11},{9,8},{10,9... | collective-permute-start | bytes 3145736 | tf_op jit(solution)/shard_map/ppermute | solution.py:19
  122.0 3.3 %collective-permute-start.14 = (bf16[512,512]{1,0:T(8,128)(2,1)S(1)}, bf16[512,512]{1,0:T(8,128)(2,1)S(1)}, u32[]{:S(2)}, u32[]{:S(2)}) collective-permute-start(bf16[512,512]{1,0:T(8,128)(2,1)S(1)} %get-tuple-element.67), channel_id=1, source_target_pairs={{0,3},{1,0},{2,1},{3,2},{4,7},{5,4},{6,5},{7,6},{8,11},{9,8},{10,9... | collective-permute-start | bytes 1572872 | tf_op jit(solution)/shard_map/ppermute | solution.py:19
  125.3 30.9 %collective-permute-done.14 = bf16[512,512]{1,0:T(8,128)(2,1)S(1)} collective-permute-done((bf16[512,512]{1,0:T(8,128)(2,1)S(1)}, bf16[512,512]{1,0:T(8,128)(2,1)S(1)}, u32[]{:S(2)}, u32[]{:S(2)}) %collective-permute-start.14) | collective-permute-done | bytes 524320 | tf_op jit(solution)/shard_map/ppermute | solution.py:19
  156.2 3.7 %collective-permute-start.15 = (bf16[512,512]{1,0:T(8,128)(2,1)S(1)}, bf16[512,512]{1,0:T(8,128)(2,1)S(1)}, u32[]{:S(2)}, u32[]{:S(2)}) collective-permute-start(bf16[512,512]{1,0:T(8,128)(2,1)S(1)} %collective-permute-done.14), channel_id=1, source_target_pairs={{0,3},{1,0},{2,1},{3,2},{4,7},{5,4},{6,5},{7,6},{8,11},{9,8},{10,9... | collective-permute-start | bytes 1572872 | tf_op jit(solution)/shard_map/ppermute | solution.py:19
  159.9 10.9 %collective-permute-done.15 = bf16[512,512]{1,0:T(8,128)(2,1)S(1)} collective-permute-done((bf16[512,512]{1,0:T(8,128)(2,1)S(1)}, bf16[512,512]{1,0:T(8,128)(2,1)S(1)}, u32[]{:S(2)}, u32[]{:S(2)}) %collective-permute-start.15) | collective-permute-done | bytes 524320 | tf_op jit(solution)/shard_map/ppermute | solution.py:19
  170.8 3.4 %collective-permute-done.13 = bf16[512,512]{1,0:T(8,128)(2,1)S(1)} collective-permute-done((bf16[512,512]{1,0:T(8,128)(2,1)S(1)}, bf16[512,512]{1,0:T(8,128)(2,1)S(1)}, u32[]{:S(2)}, u32[]{:S(2)}) %collective-permute-start.13) | collective-permute-done | bytes 524320 | tf_op jit(solution)/shard_map/ppermute | solution.py:19
  174.2 2.0 %add_convert_fusion = bf16[1024,512]{1,0:T(8,128)(2,1)} fusion(bf16[1024,512]{1,0:T(8,128)(2,1)S(1)} %collective-permute-done.11, bf16[1024,512]{1,0:T(8,128)(2,1)S(1)} %collective-permute-done.10, bf16[512,512]{1,0:T(8,128)(2,1)S(1)} %collective-permute-done.15, bf16[512,512]{1,0:T(8,128)(2,1)S(1)} %collective-permute-done.13, ...), kind=kOutput, calls=%fused_computation.2 | convolution fusion | flops 543162368 | bytes 5767172 | tf_op jit(solution)/shard_map/dot_general | solution.py:60
  (149 shorter events, 35.1 us)
Async XLA Ops:
  0.0 116.7 %copy-start = (bf16[512,2048]{1,0:T(8,128)(2,1)S(1)}, bf16[512,2048]{1,0:T(8,128)(2,1)}, u32[]{:S(2)}) copy-start(bf16[512,2048]{1,0:T(8,128)(2,1)} %param.27) | copy-start | bytes 6291460
  0.0 4.7 %copy-start.20 = (s32[1024]{0:T(1024)S(1)}, s32[1024]{0:T(1024)}, u32[]{:S(2)}) copy-start(s32[1024]{0:T(1024)} %param.18) | copy-start | bytes 12292
  0.0 9.4 %copy-start.19 = (bf16[2048,16]{0,1:T(8,128)(2,1)S(1)}, bf16[2048,16]{0,1:T(8,128)(2,1)}, u32[]{:S(2)}) copy-start(bf16[2048,16]{0,1:T(8,128)(2,1)} %param.23) | copy-start | bytes 196612
  1.4 15.1 %collective-permute-start = (bf16[512,512]{1,0:T(8,128)(2,1)S(1)}, bf16[512,512]{1,0:T(8,128)(2,1)}, u32[]{:S(2)}, u32[]{:S(2)}) collective-permute-start(bf16[512,512]{1,0:T(8,128)(2,1)S(1)} %get-tuple-element.97), channel_id=1, source_target_pairs={{0,1},{1,2},{2,3},{3,0},{4,5},{5,6},{6,7},{7,4},{8,9},{9,10},{10,1... | collective-permute-start | bytes 1572872 | tf_op jit(solution)/shard_map/ppermute | solution.py:19
  3.1 13.5 %collective-permute-start.1 = (bf16[512,512]{1,0:T(8,128)(2,1)S(1)}, bf16[512,512]{1,0:T(8,128)(2,1)}, u32[]{:S(2)}, u32[]{:S(2)}) collective-permute-start(bf16[512,512]{1,0:T(8,128)(2,1)S(1)} %get-tuple-element.96), channel_id=1, source_target_pairs={{0,3},{1,0},{2,1},{3,2},{4,7},{5,4},{6,5},{7,6},{8,11},{9,8},{10,9... | collective-permute-start | bytes 1572872 | tf_op jit(solution)/shard_map/ppermute | solution.py:19
  11.3 8.6 %copy-start.14 = (bf16[2048,256]{1,0:T(8,128)(2,1)S(1)}, bf16[2048,256]{1,0:T(8,128)(2,1)}, u32[]{:S(2)}) copy-start(bf16[2048,256]{1,0:T(8,128)(2,1)} %param.19) | copy-start | bytes 3145732
  11.3 8.6 %copy-start.15 = (bf16[2048,256]{1,0:T(8,128)(2,1)S(1)}, bf16[2048,256]{1,0:T(8,128)(2,1)}, u32[]{:S(2)}) copy-start(bf16[2048,256]{1,0:T(8,128)(2,1)} %param.20) | copy-start | bytes 3145732
  12.5 7.5 %copy-start.3 = (bf16[1024,512]{1,0:T(8,128)(2,1)S(1)}, bf16[1024,512]{1,0:T(8,128)(2,1)}, u32[]{:S(2)}) copy-start(bf16[1024,512]{1,0:T(8,128)(2,1)} %param.17) | copy-start | bytes 3145732
  16.6 16.2 %collective-permute-start.4 = (bf16[512,512]{1,0:T(8,128)(2,1)}, bf16[512,512]{1,0:T(8,128)(2,1)S(1)}, u32[]{:S(2)}, u32[]{:S(2)}) collective-permute-start(bf16[512,512]{1,0:T(8,128)(2,1)} %collective-permute-done), channel_id=1, source_target_pairs={{0,1},{1,2},{2,3},{3,0},{4,5},{5,6},{6,7},{7,4},{8,9},{9,10},{10,1... | collective-permute-start | bytes 1572872 | tf_op jit(solution)/shard_map/ppermute | solution.py:19
  18.2 15.1 %collective-permute-start.5 = (bf16[512,512]{1,0:T(8,128)(2,1)}, bf16[512,512]{1,0:T(8,128)(2,1)S(1)}, u32[]{:S(2)}, u32[]{:S(2)}) collective-permute-start(bf16[512,512]{1,0:T(8,128)(2,1)} %collective-permute-done.1), channel_id=1, source_target_pairs={{0,3},{1,0},{2,1},{3,2},{4,7},{5,4},{6,5},{7,6},{8,11},{9,8},{10,9... | collective-permute-start | bytes 1572872 | tf_op jit(solution)/shard_map/ppermute | solution.py:19
  20.1 22.0 %collective-permute-start.3 = (bf16[512,512]{1,0:T(8,128)(2,1)S(1)}, bf16[512,512]{1,0:T(8,128)(2,1)S(1)}, u32[]{:S(2)}, u32[]{:S(2)}) collective-permute-start(bf16[512,512]{1,0:T(8,128)(2,1)S(1)} %get-tuple-element.95), channel_id=1, source_target_pairs={{0,1},{1,2},{2,3},{3,0},{4,5},{5,6},{6,7},{7,4},{8,9},{9,10},{10,1... | collective-permute-start | bytes 1572872 | tf_op jit(solution)/shard_map/ppermute | solution.py:19
  20.5 21.6 %collective-permute-start.2 = (bf16[512,512]{1,0:T(8,128)(2,1)S(1)}, bf16[512,512]{1,0:T(8,128)(2,1)S(1)}, u32[]{:S(2)}, u32[]{:S(2)}) collective-permute-start(bf16[512,512]{1,0:T(8,128)(2,1)S(1)} %get-tuple-element.94), channel_id=1, source_target_pairs={{0,3},{1,0},{2,1},{3,2},{4,7},{5,4},{6,5},{7,6},{8,11},{9,8},{10,9... | collective-permute-start | bytes 1572872 | tf_op jit(solution)/shard_map/ppermute | solution.py:19
  42.1 12.9 %copy-start.21 = (bf16[512,512]{1,0:T(8,128)(2,1)}, bf16[512,512]{1,0:T(8,128)(2,1)S(1)}, u32[]{:S(2)}) copy-start(bf16[512,512]{1,0:T(8,128)(2,1)S(1)} %collective-permute-done.3) | copy-start | bytes 1572868
  42.1 12.9 %copy-start.23 = (bf16[512,512]{1,0:T(8,128)(2,1)}, bf16[512,512]{1,0:T(8,128)(2,1)S(1)}, u32[]{:S(2)}) copy-start(bf16[512,512]{1,0:T(8,128)(2,1)S(1)} %collective-permute-done.2) | copy-start | bytes 1572868
  51.1 3.2 %copy-start.10 = (f32[1024,256]{1,0:T(8,128)}, f32[1024,256]{1,0:T(8,128)S(1)}, u32[]{:S(2)}) copy-start(f32[1024,256]{1,0:T(8,128)S(1)} %fusion.16) | copy-start | bytes 3145732
  58.0 5.8 %copy-start.5 = (bf16[1024,512]{1,0:T(8,128)(2,1)}, bf16[1024,512]{1,0:T(8,128)(2,1)S(1)}, u32[]{:S(2)}) copy-start(bf16[1024,512]{1,0:T(8,128)(2,1)S(1)} %add_convert_fusion.1) | copy-start | bytes 3145732
  64.2 5.6 %copy-start.1 = (f32[16,256,512]{2,1,0:T(8,128)S(1)}, f32[16,256,512]{2,1,0:T(8,128)}, u32[]{:S(2)}) copy-start(f32[16,256,512]{2,1,0:T(8,128)} %fusion.38) | copy-start | bytes 25165828
  69.7 15.0 %copy-start.9 = (f32[16,64,256]{2,0,1:T(8,128)S(1)}, f32[16,64,256]{2,0,1:T(8,128)}, u32[]{:S(2)}) copy-start(f32[16,64,256]{2,0,1:T(8,128)} %get-tuple-element.58) | copy-start | bytes 3145732
  71.3 26.6 %collective-permute-start.6 = (bf16[258,512]{1,0:T(8,128)(2,1)}, bf16[258,512]{1,0:T(8,128)(2,1)S(1)}, u32[]{:S(2)}, u32[]{:S(2)}) collective-permute-start(bf16[258,512]{1,0:T(8,128)(2,1)} %pad_maximum_fusion), channel_id=1, source_target_pairs={{0,4},{4,8},{8,12},{12,16},{16,20},{20,24},{24,28},{28,32},{32,36}... | collective-permute-start | bytes 792584 | tf_op jit(solution)/shard_map/ppermute | solution.py:14
  73.2 27.4 %collective-permute-start.9 = (bf16[258,512]{1,0:T(8,128)(2,1)}, bf16[258,512]{1,0:T(8,128)(2,1)}, u32[]{:S(2)}, u32[]{:S(2)}) collective-permute-start(bf16[258,512]{1,0:T(8,128)(2,1)} %pad_maximum_fusion), channel_id=1, source_target_pairs={{0,16},{4,20},{8,24},{12,28},{16,32},{20,36},{24,40},{28,44},{32,4... | collective-permute-start | bytes 792584 | tf_op jit(solution)/shard_map/ppermute | solution.py:14
  79.0 19.5 %collective-permute-start.8 = (bf16[258,512]{1,0:T(8,128)(2,1)}, bf16[258,512]{1,0:T(8,128)(2,1)}, u32[]{:S(2)}, u32[]{:S(2)}) collective-permute-start(bf16[258,512]{1,0:T(8,128)(2,1)} %pad_maximum_fusion), channel_id=1, source_target_pairs={{0,12},{4,16},{8,20},{12,24},{16,28},{20,32},{24,36},{28,40},{32,4... | collective-permute-start | bytes 792584 | tf_op jit(solution)/shard_map/ppermute | solution.py:14
  81.5 22.0 %collective-permute-start.7 = (bf16[258,512]{1,0:T(8,128)(2,1)}, bf16[258,512]{1,0:T(8,128)(2,1)}, u32[]{:S(2)}, u32[]{:S(2)}) collective-permute-start(bf16[258,512]{1,0:T(8,128)(2,1)} %pad_maximum_fusion), channel_id=1, source_target_pairs={{0,8},{4,12},{8,16},{12,20},{16,24},{20,28},{24,32},{28,36},{32,40... | collective-permute-start | bytes 792584 | tf_op jit(solution)/shard_map/ppermute | solution.py:14
  100.5 10.1 %copy-start.2 = (f32[1024,512]{0,1:T(8,128)S(1)}, f32[1024,512]{0,1:T(8,128)}, u32[]{:S(2)}) copy-start(f32[1024,512]{0,1:T(8,128)} %copy.51) | copy-start | bytes 6291460
  100.5 10.1 %copy-start.11 = (f32[1024,256]{1,0:T(8,128)S(1)}, f32[1024,256]{1,0:T(8,128)}, u32[]{:S(2)}) copy-start(f32[1024,256]{1,0:T(8,128)} %copy-done.10) | copy-start | bytes 3145732
  110.7 2.6 %copy-start.24 = (bf16[512,512]{1,0:T(8,128)(2,1)S(1)}, bf16[512,512]{1,0:T(8,128)(2,1)}, u32[]{:S(2)}) copy-start(bf16[512,512]{1,0:T(8,128)(2,1)} %copy-done.23) | copy-start | bytes 1572868
  110.7 2.6 %copy-start.26 = (f32[512]{0:T(512)S(1)}, f32[512]{0:T(512)}, u32[]{:S(2)}) copy-start(f32[512]{0:T(512)} %param.26) | copy-start | bytes 6148
  119.0 40.9 %collective-permute-start.11 = (bf16[1024,512]{1,0:T(8,128)(2,1)S(1)}, bf16[1024,512]{1,0:T(8,128)(2,1)S(1)}, u32[]{:S(2)}, u32[]{:S(2)}) collective-permute-start(bf16[1024,512]{1,0:T(8,128)(2,1)S(1)} %convolution_convert_fusion.1), channel_id=1, source_target_pairs={{0,3},{1,0},{2,1},{3,2},{4,7},{5,4},{6,5},{7,6},{8,11},{9,8},{10,9... | collective-permute-start | bytes 3145736 | tf_op jit(solution)/shard_map/ppermute | solution.py:19
  121.9 38.0 %collective-permute-start.10 = (bf16[1024,512]{1,0:T(8,128)(2,1)S(1)}, bf16[1024,512]{1,0:T(8,128)(2,1)S(1)}, u32[]{:S(2)}, u32[]{:S(2)}) collective-permute-start(bf16[1024,512]{1,0:T(8,128)(2,1)S(1)} %convolution_convert_fusion.2), channel_id=1, source_target_pairs={{0,1},{1,2},{2,3},{3,0},{4,5},{5,6},{6,7},{7,4},{8,9},{9,10},{10,1... | collective-permute-start | bytes 3145736 | tf_op jit(solution)/shard_map/ppermute | solution.py:19
  122.0 34.2 %collective-permute-start.14 = (bf16[512,512]{1,0:T(8,128)(2,1)S(1)}, bf16[512,512]{1,0:T(8,128)(2,1)S(1)}, u32[]{:S(2)}, u32[]{:S(2)}) collective-permute-start(bf16[512,512]{1,0:T(8,128)(2,1)S(1)} %get-tuple-element.67), channel_id=1, source_target_pairs={{0,3},{1,0},{2,1},{3,2},{4,7},{5,4},{6,5},{7,6},{8,11},{9,8},{10,9... | collective-permute-start | bytes 1572872 | tf_op jit(solution)/shard_map/ppermute | solution.py:19
  125.3 34.6 %collective-permute-start.12 = (bf16[512,512]{1,0:T(8,128)(2,1)S(1)}, bf16[512,512]{1,0:T(8,128)(2,1)S(1)}, u32[]{:S(2)}, u32[]{:S(2)}) collective-permute-start(bf16[512,512]{1,0:T(8,128)(2,1)S(1)} %get-tuple-element.66), channel_id=1, source_target_pairs={{0,1},{1,2},{2,3},{3,0},{4,5},{5,6},{6,7},{7,4},{8,9},{9,10},{10,1... | collective-permute-start | bytes 1572872 | tf_op jit(solution)/shard_map/ppermute | solution.py:19
  156.2 14.6 %collective-permute-start.15 = (bf16[512,512]{1,0:T(8,128)(2,1)S(1)}, bf16[512,512]{1,0:T(8,128)(2,1)S(1)}, u32[]{:S(2)}, u32[]{:S(2)}) collective-permute-start(bf16[512,512]{1,0:T(8,128)(2,1)S(1)} %collective-permute-done.14), channel_id=1, source_target_pairs={{0,3},{1,0},{2,1},{3,2},{4,7},{5,4},{6,5},{7,6},{8,11},{9,8},{10,9... | collective-permute-start | bytes 1572872 | tf_op jit(solution)/shard_map/ppermute | solution.py:19
  159.9 14.3 %collective-permute-start.13 = (bf16[512,512]{1,0:T(8,128)(2,1)S(1)}, bf16[512,512]{1,0:T(8,128)(2,1)S(1)}, u32[]{:S(2)}, u32[]{:S(2)}) collective-permute-start(bf16[512,512]{1,0:T(8,128)(2,1)S(1)} %collective-permute-done.12), channel_id=1, source_target_pairs={{0,1},{1,2},{2,3},{3,0},{4,5},{5,6},{6,7},{7,4},{8,9},{9,10},{10,1... | collective-permute-start | bytes 1572872 | tf_op jit(solution)/shard_map/ppermute | solution.py:19
  (12 other events, 24.7 us)

commit v10 on v9

--- a/solution.py
+++ b/solution.py
@@ -60,13 +60,19 @@
         return jnp.dot(gated, cols, preferred_element_type=jnp.float32).astype(jnp.bfloat16)
 
     far = term(2)
-    far_from_left = ring(far[:half], 1)
-    far_from_right = ring(far[half:], -1)
-    from_left = ring(term(1), 1)
-    from_right = ring(term(-1), -1)
-    relayed = jnp.concatenate([ring(far_from_left, 1), ring(far_from_right, -1)])
+    far_from_left = ring(far[:half], 1).astype(jnp.float32)
+    far_from_right = ring(far[half:], -1).astype(jnp.float32)
+    near_right, near_left = term(1), term(-1)
+    to_right = jnp.concatenate(
+        [(near_right[:half].astype(jnp.float32) + far_from_left).astype(jnp.bfloat16), near_right[half:]]
+    )
+    to_left = jnp.concatenate(
+        [near_left[:half], (near_left[half:].astype(jnp.float32) + far_from_right).astype(jnp.bfloat16)]
+    )
+    from_left = ring(to_right, 1)
+    from_right = ring(to_left, -1)
     total = term(0).astype(jnp.float32) + from_left.astype(jnp.float32)
-    total = total + from_right.astype(jnp.float32) + relayed.astype(jnp.float32)
+    total = total + from_right.astype(jnp.float32)
     return total
 
 

time: 177 us -> 165 us (0.932)
  waiting for transfers between devices: 62.7 us -> 53.2 us
  starting transfers between devices: 33.2 us -> 30.3 us
    ppermute x12 -> x10, waiting for transfers between devices: 62.7 us -> 53.2 us  [ring(): lax.ppermute(x, 'tensor', [(i, (i + step) % size) for i in range(size)])]
    ppermute x12 -> x10, starting transfers between devices: 19.8 us -> 16.7 us  [ring(): lax.ppermute(x, 'tensor', [(i, (i + step) % size) for i in range(size)])]
  transfers between devices with their start and end apart: 16 -> 14, of which waited for: 7 -> 7; matrix products, arithmetic and copies ran while one was open for 16% -> 18% of each run, Pallas kernels for 0% -> 0%
where the time goes in v10:
time: 165 us; the launch traced here: 164 us
  waiting for transfers between devices  53.2 us (32%)
  matrix products  40 us (24%)
  starting transfers between devices  30.3 us (18%)
  local copies, waits for them, and re-layouts  19.4 us (12%)
  other arithmetic  13.7 us (8%)
  between operations  7.33 us (4%)
    ppermute x10, waiting for transfers between devices, ring(): lax.ppermute(x, 'tensor', [(i, (i + step) % size) for i in range(size)])  53.2 us
    ppermute x10, starting transfers between devices, ring(): lax.ppermute(x, 'tensor', [(i, (i + step) % size) for i in range(size)])  16.7 us
    ppermute x4, starting transfers between devices, shifted(): return lax.ppermute(x, axis, pairs)  13.6 us
    dot_general x5, matrix products, projected(): out = jnp.dot(near, near_rows, preferred_element_type=jnp.float32)  13.3 us
    dot_general x1, matrix products, body(): jnp.einsum('ncd,ncv->ndv', k_decayed, v_float, precision=HIGH)  5.75 us
    dot_general x5, matrix products, projected(): jnp.dot(far, rows(2), preferred_element_type=jnp.float32)  5.13 us
    dot_general x16, matrix products, body(): inters.append(jnp.dot(q_decayed[n], entering, precision=HIGH))  5.01 us
    dot_general x4, matrix products, term(): jnp.dot(gated, cols, preferred_element_type=jnp.float32)  4.09 us
  transfers between devices with their start and end apart: 14, of which 7 were waited for; matrix products, arithmetic and copies ran while one was open for 18% of the time, Pallas kernels for 0%

profile of v10, /device:TPU:2, one launch (start us, length us, event | category | flops | bytes accessed | tf_op | source)
XLA Modules:
  0.0 164.0 jit_solution(5707550375647596705)
XLA Ops:
  1.4 1.6 %collective-permute-start = (bf16[512,512]{1,0:T(8,128)(2,1)S(1)}, bf16[512,512]{1,0:T(8,128)(2,1)}, u32[]{:S(2)}, u32[]{:S(2)}) collective-permute-start(bf16[512,512]{1,0:T(8,128)(2,1)S(1)} %get-tuple-element.97), channel_id=1, source_target_pairs={{0,1},{1,2},{2,3},{3,0},{4,5},{5,6},{6,7},{7,4},{8,9},{9,10},{10,1... | collective-permute-start | bytes 1572872 | tf_op jit(solution)/shard_map/ppermute | solution.py:19
  3.1 1.7 %collective-permute-start.1 = (bf16[512,512]{1,0:T(8,128)(2,1)S(1)}, bf16[512,512]{1,0:T(8,128)(2,1)}, u32[]{:S(2)}, u32[]{:S(2)}) collective-permute-start(bf16[512,512]{1,0:T(8,128)(2,1)S(1)} %get-tuple-element.96), channel_id=1, source_target_pairs={{0,3},{1,0},{2,1},{3,2},{4,7},{5,4},{6,5},{7,6},{8,11},{9,8},{10,9... | collective-permute-start | bytes 1572872 | tf_op jit(solution)/shard_map/ppermute | solution.py:19
  12.6 3.9 %collective-permute-done = bf16[512,512]{1,0:T(8,128)(2,1)} collective-permute-done((bf16[512,512]{1,0:T(8,128)(2,1)S(1)}, bf16[512,512]{1,0:T(8,128)(2,1)}, u32[]{:S(2)}, u32[]{:S(2)}) %collective-permute-start) | collective-permute-done | bytes 524320 | tf_op jit(solution)/shard_map/ppermute | solution.py:19
  18.2 1.7 %collective-permute-start.5 = (bf16[512,512]{1,0:T(8,128)(2,1)}, bf16[512,512]{1,0:T(8,128)(2,1)S(1)}, u32[]{:S(2)}, u32[]{:S(2)}) collective-permute-start(bf16[512,512]{1,0:T(8,128)(2,1)} %collective-permute-done.1), channel_id=1, source_target_pairs={{0,3},{1,0},{2,1},{3,2},{4,7},{5,4},{6,5},{7,6},{8,11},{9,8},{10,9... | collective-permute-start | bytes 1572872 | tf_op jit(solution)/shard_map/ppermute | solution.py:19
  20.5 2.9 %collective-permute-start.2 = (bf16[512,512]{1,0:T(8,128)(2,1)S(1)}, bf16[512,512]{1,0:T(8,128)(2,1)S(1)}, u32[]{:S(2)}, u32[]{:S(2)}) collective-permute-start(bf16[512,512]{1,0:T(8,128)(2,1)S(1)} %get-tuple-element.94), channel_id=1, source_target_pairs={{0,3},{1,0},{2,1},{3,2},{4,7},{5,4},{6,5},{7,6},{8,11},{9,8},{10,9... | collective-permute-start | bytes 1572872 | tf_op jit(solution)/shard_map/ppermute | solution.py:19
  23.4 9.4 %collective-permute-done.4 = bf16[512,512]{1,0:T(8,128)(2,1)S(1)} collective-permute-done((bf16[512,512]{1,0:T(8,128)(2,1)}, bf16[512,512]{1,0:T(8,128)(2,1)S(1)}, u32[]{:S(2)}, u32[]{:S(2)}) %collective-permute-start.4) | collective-permute-done | bytes 524320 | tf_op jit(solution)/shard_map/ppermute | solution.py:19
  33.3 2.1 %fusion.101 = f32[1024,512]{0,1:T(8,128)} fusion(bf16[1024,512]{1,0:T(8,128)(2,1)S(1)} %constant_dynamic-update-slice_fusion, bf16[2048,512]{1,0:T(8,128)(2,1)S(1)} %copy-done.12, s32[]{:T(128)S(6)} %select_n.111), kind=kOutput, calls=%fused_computation.154 | convolution fusion | flops 536870912 | bytes 3670020 | tf_op jit(solution)/shard_map/dot_general | solution.py:47
  36.7 1.8 %fusion.105 = f32[1024,512]{1,0:T(8,128)S(1)} fusion(bf16[1024,512]{1,0:T(8,128)(2,1)S(1)} %constant_dynamic-update-slice_fusion, bf16[2048,512]{1,0:T(8,128)(2,1)} %param.21, s32[]{:T(128)S(6)} %select_n.111), kind=kOutput, calls=%fused_computation.172 | convolution fusion | flops 536870912 | bytes 3670020 | tf_op jit(solution)/shard_map/dot_general | solution.py:47
  38.4 3.7 %collective-permute-done.3 = bf16[512,512]{1,0:T(8,128)(2,1)S(1)} collective-permute-done((bf16[512,512]{1,0:T(8,128)(2,1)S(1)}, bf16[512,512]{1,0:T(8,128)(2,1)S(1)}, u32[]{:S(2)}, u32[]{:S(2)}) %collective-permute-start.3) | collective-permute-done | bytes 524320 | tf_op jit(solution)/shard_map/ppermute | solution.py:19
  42.1 2.5 %convolution_add_fusion.3 = f32[1024,16]{0,1:T(8,128)S(1)} fusion(f32[1024,16]{0,1:T(8,128)S(1)} %fusion.158, bf16[512,16]{0,1:T(8,128)(2,1)S(1)} %get-tuple-element.106, bf16[512,16]{0,1:T(8,128)(2,1)S(1)} %get-tuple-element.105, bf16[512,16]{0,1:T(8,128)(2,1)S(1)} %get-tuple-element.104, bf16[512,512]{1,0:T(8,128)(2,1)S(1)} %collective-permute-done.3, ...), kind=kOutput, calls=%fused_computation.64 | convolution fusion | flops 66224128 | bytes 3325952 | tf_op jit(solution)/shard_map/dot_general | solution.py:46
  46.5 2.2 %fusion.17 = bf16[1024,256]{1,0:T(8,128)(2,1)S(1)} fusion(f32[1024,256]{1,0:T(8,128)S(1)} %fusion.114, bf16[512,256]{1,0:T(8,128)(2,1)S(1)} %get-tuple-element.90, bf16[512,256]{1,0:T(8,128)(2,1)S(1)} %get-tuple-element.89, bf16[512,256]{1,0:T(8,128)(2,1)S(1)} %get-tuple-element.88, bf16[512,512]{1,0:T(8,128)(2,1)S(1)} %collective-permute-done.3, ...), kind=kOutput, calls=%fused_computation.30 | convolution fusion | flops 823918592 | bytes 5505024 | tf_op jit(solution)/shard_map/dot_general | solution.py:46
  48.9 2.2 %fusion.16 = f32[1024,256]{1,0:T(8,128)S(1)} fusion(f32[1024,256]{1,0:T(8,128)S(1)} %fusion.116, bf16[512,256]{1,0:T(8,128)(2,1)S(1)} %get-tuple-element.129, bf16[512,256]{1,0:T(8,128)(2,1)S(1)} %get-tuple-element.130, bf16[512,256]{1,0:T(8,128)(2,1)S(1)} %get-tuple-element.131, bf16[512,512]{1,0:T(8,128)(2,1)S(1)} %collective-permute-done.3, ...), kind=kOutput, calls=%fused_computation.29 | convolution fusion | flops 824180736 | bytes 6029312 | tf_op jit(solution)/shard_map/dot_general | solution.py:46
  51.1 3.2 %exponential_multiply_fusion.2 = (f32[16,64,256]{2,0,1:T(8,128)}, f32[16,64,256]{2,0,1:T(8,128)}, f32[16,64,256]{2,0,1:T(8,128)S(1)}, f32[16,64,256]{2,0,1:T(8,128)}, f32[16,64,256]{2,0,1:T(8,128)S(1)}) fusion(f32[16,64,256]{2,0,1:T(8,128)S(1)} %fusion.42, f32[16,64,256]{2,1,0:T(8,128)S(1)} %bitcast.319, f32[16,256]{1,0:T(8,128)S(1)} %get-tuple-element.71, ...), kind=kLoop, calls=%fused_computation.82 | loop fusion | flops 2359296 | bytes 8441856 | tf_op jit(solution)/shard_map/mul | solution.py:122
  55.0 3.0 %add_convert_fusion.1 = bf16[1024,512]{1,0:T(8,128)(2,1)S(1)} fusion(f32[1024,512]{1,0:T(8,128)S(1)} %fusion.105, bf16[512,512]{1,0:T(8,128)(2,1)S(1)} %get-tuple-element.63, bf16[512,512]{1,0:T(8,128)(2,1)S(1)} %get-tuple-element.62, bf16[512,512]{1,0:T(8,128)(2,1)S(1)} %get-tuple-element.61, bf16[512,512]{1,0:T(8,128)(2,1)S(1)} %collective-permute-done.3, ...), kind=kOutput, calls=%fused_computation.7 | convolution fusion | flops 1632108544 | bytes 7864320 | tf_op jit(solution)/shard_map/dot_general | solution.py:46
  58.0 5.8 %fusion.38 = f32[16,256,512]{2,1,0:T(8,128)} fusion(bf16[16,64,512]{2,1,0:T(8,128)(2,1)S(1)} %bitcast.317, f32[16,64,256]{2,0,1:T(8,128)S(1)} %get-tuple-element.64), kind=kOutput, calls=%fused_computation.69 | convolution fusion | flops 805306368 | bytes 10485760 | tf_op jit(solution)/shard_map/ncd,ncv->ndv/dot_general | solution.py:131
  63.9 3.7 %multiply_add_fusion.2 = (f32[1,256,512]{2,1,0:T(8,128)S(1)}, f32[1,256,512]{2,1,0:T(8,128)S(1)}, f32[1,256,512]{2,1,0:T(8,128)S(1)}, f32[1,256,512]{2,1,0:T(8,1...) fusion(f32[16,256,512]{2,1,0:T(8,128)} %fusion.38, ...), kind=kLoop, calls=%fused_computation.159 | loop fusion | flops 3538944 | bytes 11024384 | tf_op jit(solution)/shard_map/add | solution.py:139
  67.7 1.8 %copy-done.1 = f32[16,256,512]{2,1,0:T(8,128)S(1)} copy-done((f32[16,256,512]{2,1,0:T(8,128)S(1)}, f32[16,256,512]{2,1,0:T(8,128)}, u32[]{:S(2)}) %copy-start.1) | copy-done | bytes 8388632
  71.1 1.9 %collective-permute-start.6 = (bf16[258,512]{1,0:T(8,128)(2,1)}, bf16[258,512]{1,0:T(8,128)(2,1)S(1)}, u32[]{:S(2)}, u32[]{:S(2)}) collective-permute-start(bf16[258,512]{1,0:T(8,128)(2,1)} %pad_maximum_fusion.2), channel_id=1, source_target_pairs={{0,4},{4,8},{8,12},{12,16},{16,20},{20,24},{24,28},{28,32},{32,36}... | collective-permute-start | bytes 792584 | tf_op jit(solution)/shard_map/ppermute | solution.py:14
  73.0 5.8 %collective-permute-start.9 = (bf16[258,512]{1,0:T(8,128)(2,1)}, bf16[258,512]{1,0:T(8,128)(2,1)}, u32[]{:S(2)}, u32[]{:S(2)}) collective-permute-start(bf16[258,512]{1,0:T(8,128)(2,1)} %pad_maximum_fusion.2), channel_id=1, source_target_pairs={{0,16},{4,20},{8,24},{12,28},{16,32},{20,36},{24,40},{28,44},{32,4... | collective-permute-start | bytes 792584 | tf_op jit(solution)/shard_map/ppermute | solution.py:14
  78.8 2.5 %collective-permute-start.8 = (bf16[258,512]{1,0:T(8,128)(2,1)}, bf16[258,512]{1,0:T(8,128)(2,1)}, u32[]{:S(2)}, u32[]{:S(2)}) collective-permute-start(bf16[258,512]{1,0:T(8,128)(2,1)} %pad_maximum_fusion.2), channel_id=1, source_target_pairs={{0,12},{4,16},{8,20},{12,24},{16,28},{20,32},{24,36},{28,40},{32,4... | collective-permute-start | bytes 792584 | tf_op jit(solution)/shard_map/ppermute | solution.py:14
  81.2 3.4 %collective-permute-start.7 = (bf16[258,512]{1,0:T(8,128)(2,1)}, bf16[258,512]{1,0:T(8,128)(2,1)}, u32[]{:S(2)}, u32[]{:S(2)}) collective-permute-start(bf16[258,512]{1,0:T(8,128)(2,1)} %pad_maximum_fusion.2), channel_id=1, source_target_pairs={{0,8},{4,12},{8,16},{12,20},{16,24},{20,28},{24,32},{28,36},{32,40... | collective-permute-start | bytes 792584 | tf_op jit(solution)/shard_map/ppermute | solution.py:14
  91.0 1.7 %convolution_select_fusion = f32[16,64,64]{2,1,0:T(8,128)S(1)} fusion(f32[16,64,256]{2,0,1:T(8,128)S(1)} %copy-done.8, f32[16,64,256]{2,0,1:T(8,128)S(1)} %copy-done.7, s32[16,64]{1,0:T(8,128)S(1)} %eq.88, pred[64,64]{1,0:T(8,128)(4,1)S(1)} %iota_compare_fusion), kind=kOutput, calls=%fused_computation.31 | convolution fusion | flops 100859904 | bytes 2367488 | tf_op jit(solution)/shard_map/ncd,nsd->ncs/dot_general | solution.py:124
  92.7 2.2 %multiply_add_fusion.1 = f32[16,64,512]{2,1,0:T(8,128)} fusion(f32[16,64,512]{2,1,0:T(8,128)S(1)} %fusion.18, f32[16,64,64]{2,1,0:T(8,128)S(1)} %convolution_select_fusion, bf16[16,64,512]{2,1,0:T(8,128)(2,1)S(1)} %bitcast.318, f32[16,64]{1,0:T(8,128)S(1)} %compare_convert_fusion.1), kind=kOutput, calls=%fused_computation.6 | convolution fusion | flops 202375168 | bytes 5509120 | tf_op jit(solution)/shard_map/ncs,nsv->ncv/dot_general | solution.py:127
  94.9 2.9 %copy.51 = f32[1024,512]{0,1:T(8,128)} copy(f32[1024,512]{1,0:T(8,128)} %bitcast.314) | data formatting | bytes 4194304 | tf_op jit(solution)/shard_map/reshape | solution.py:142
  110.8 1.6 multiply_reduce_fusion
  113.3 3.4 %multiply_convert_fusion = bf16[1024,512]{0,1:T(8,128)(2,1)S(1)} fusion(f32[1024,512]{0,1:T(8,128)S(1)} %copy-done.13, f32[1024,512]{0,1:T(8,128)S(1)} %get-tuple-element.128, bf16[512,512]{1,0:T(8,128)(2,1)S(1)} %copy-done.18, bf16[512,512]{1,0:T(8,128)(2,1)S(1)} %copy-done.17, bf16[512,512]{1,0:T(8,128)(2,1)S(1)} %copy-done.16, f32[512]{0:T(512)S(1)} %copy-done.26, ...), kind=kOutput, calls=%fused_computation.3 | convolution fusion | flops 1635778560 | bytes 9967616 | tf_op jit(solution)/shard_map/dot_general | solution.py:46
  117.6 2.9 %collective-permute-start.12 = (bf16[512,512]{1,0:T(8,128)(2,1)S(1)}, bf16[512,512]{1,0:T(8,128)(2,1)S(1)}, u32[]{:S(2)}, u32[]{:S(2)}) collective-permute-start(bf16[512,512]{1,0:T(8,128)(2,1)S(1)} %get-tuple-element.67), channel_id=1, source_target_pairs={{0,3},{1,0},{2,1},{3,2},{4,7},{5,4},{6,5},{7,6},{8,11},{9,8},{10,9... | collective-permute-start | bytes 1572872 | tf_op jit(solution)/shard_map/ppermute | solution.py:19
  122.1 10.2 %collective-permute-done.12 = bf16[512,512]{1,0:T(8,128)(2,1)S(1)} collective-permute-done((bf16[512,512]{1,0:T(8,128)(2,1)S(1)}, bf16[512,512]{1,0:T(8,128)(2,1)S(1)}, u32[]{:S(2)}, u32[]{:S(2)}) %collective-permute-start.12) | collective-permute-done | bytes 524320 | tf_op jit(solution)/shard_map/ppermute | solution.py:19
  132.5 3.8 %collective-permute-start.13 = (bf16[1024,512]{1,0:T(8,128)(2,1)S(1)}, bf16[1024,512]{1,0:T(8,128)(2,1)S(1)}, u32[]{:S(2)}, u32[]{:S(2)}) collective-permute-start(bf16[1024,512]{1,0:T(8,128)(2,1)S(1)} %pad_maximum_fusion.1), channel_id=1, source_target_pairs={{0,3},{1,0},{2,1},{3,2},{4,7},{5,4},{6,5},{7,6},{8,11},{9,8},{10,9... | collective-permute-start | bytes 3145736 | tf_op jit(solution)/shard_map/ppermute | solution.py:19
  136.6 21.9 %collective-permute-done.13 = bf16[1024,512]{1,0:T(8,128)(2,1)S(1)} collective-permute-done((bf16[1024,512]{1,0:T(8,128)(2,1)S(1)}, bf16[1024,512]{1,0:T(8,128)(2,1)S(1)}, u32[]{:S(2)}, u32[]{:S(2)}) %collective-permute-start.13) | collective-permute-done | bytes 1048608 | tf_op jit(solution)/shard_map/ppermute | solution.py:19
  158.4 3.7 %collective-permute-done.11 = bf16[1024,512]{1,0:T(8,128)(2,1)S(1)} collective-permute-done((bf16[1024,512]{1,0:T(8,128)(2,1)S(1)}, bf16[1024,512]{1,0:T(8,128)(2,1)S(1)}, u32[]{:S(2)}, u32[]{:S(2)}) %collective-permute-start.11) | collective-permute-done | bytes 1048608 | tf_op jit(solution)/shard_map/ppermute | solution.py:19
  162.1 1.8 %add_convert_fusion = bf16[1024,512]{1,0:T(8,128)(2,1)} fusion(bf16[1024,512]{1,0:T(8,128)(2,1)S(1)} %collective-permute-done.13, bf16[1024,512]{1,0:T(8,128)(2,1)S(1)} %collective-permute-done.11, bf16[1024,512]{0,1:T(8,128)(2,1)S(1)} %multiply_convert_fusion, bf16[512,2048]{1,0:T(8,128)(2,1)S(1)} %copy-done, s32[]{:T(128)S(6)} %select_n.105), kind=kOutput, calls=%fused_computation.2 | convolution fusion | flops 540540928 | bytes 4718596 | tf_op jit(solution)/shard_map/dot_general | solution.py:60
  (151 shorter events, 33.7 us)
Async XLA Ops:
  0.0 116.7 %copy-start = (bf16[512,2048]{1,0:T(8,128)(2,1)S(1)}, bf16[512,2048]{1,0:T(8,128)(2,1)}, u32[]{:S(2)}) copy-start(bf16[512,2048]{1,0:T(8,128)(2,1)} %param.27) | copy-start | bytes 6291460
  0.0 4.7 %copy-start.20 = (s32[1024]{0:T(1024)S(1)}, s32[1024]{0:T(1024)}, u32[]{:S(2)}) copy-start(s32[1024]{0:T(1024)} %param.18) | copy-start | bytes 12292
  0.0 9.5 %copy-start.19 = (bf16[2048,16]{0,1:T(8,128)(2,1)S(1)}, bf16[2048,16]{0,1:T(8,128)(2,1)}, u32[]{:S(2)}) copy-start(bf16[2048,16]{0,1:T(8,128)(2,1)} %param.23) | copy-start | bytes 196612
  1.4 15.1 %collective-permute-start = (bf16[512,512]{1,0:T(8,128)(2,1)S(1)}, bf16[512,512]{1,0:T(8,128)(2,1)}, u32[]{:S(2)}, u32[]{:S(2)}) collective-permute-start(bf16[512,512]{1,0:T(8,128)(2,1)S(1)} %get-tuple-element.97), channel_id=1, source_target_pairs={{0,1},{1,2},{2,3},{3,0},{4,5},{5,6},{6,7},{7,4},{8,9},{9,10},{10,1... | collective-permute-start | bytes 1572872 | tf_op jit(solution)/shard_map/ppermute | solution.py:19
  3.1 13.5 %collective-permute-start.1 = (bf16[512,512]{1,0:T(8,128)(2,1)S(1)}, bf16[512,512]{1,0:T(8,128)(2,1)}, u32[]{:S(2)}, u32[]{:S(2)}) collective-permute-start(bf16[512,512]{1,0:T(8,128)(2,1)S(1)} %get-tuple-element.96), channel_id=1, source_target_pairs={{0,3},{1,0},{2,1},{3,2},{4,7},{5,4},{6,5},{7,6},{8,11},{9,8},{10,9... | collective-permute-start | bytes 1572872 | tf_op jit(solution)/shard_map/ppermute | solution.py:19
  11.4 8.5 %copy-start.14 = (bf16[2048,256]{1,0:T(8,128)(2,1)S(1)}, bf16[2048,256]{1,0:T(8,128)(2,1)}, u32[]{:S(2)}) copy-start(bf16[2048,256]{1,0:T(8,128)(2,1)} %param.19) | copy-start | bytes 3145732
  11.4 8.5 %copy-start.15 = (bf16[2048,256]{1,0:T(8,128)(2,1)S(1)}, bf16[2048,256]{1,0:T(8,128)(2,1)}, u32[]{:S(2)}) copy-start(bf16[2048,256]{1,0:T(8,128)(2,1)} %param.20) | copy-start | bytes 3145732
  12.6 7.4 %copy-start.3 = (bf16[1024,512]{1,0:T(8,128)(2,1)S(1)}, bf16[1024,512]{1,0:T(8,128)(2,1)}, u32[]{:S(2)}) copy-start(bf16[1024,512]{1,0:T(8,128)(2,1)} %param.17) | copy-start | bytes 3145732
  16.6 16.2 %collective-permute-start.4 = (bf16[512,512]{1,0:T(8,128)(2,1)}, bf16[512,512]{1,0:T(8,128)(2,1)S(1)}, u32[]{:S(2)}, u32[]{:S(2)}) collective-permute-start(bf16[512,512]{1,0:T(8,128)(2,1)} %collective-permute-done), channel_id=1, source_target_pairs={{0,1},{1,2},{2,3},{3,0},{4,5},{5,6},{6,7},{7,4},{8,9},{9,10},{10,1... | collective-permute-start | bytes 1572872 | tf_op jit(solution)/shard_map/ppermute | solution.py:19
  18.2 15.1 %collective-permute-start.5 = (bf16[512,512]{1,0:T(8,128)(2,1)}, bf16[512,512]{1,0:T(8,128)(2,1)S(1)}, u32[]{:S(2)}, u32[]{:S(2)}) collective-permute-start(bf16[512,512]{1,0:T(8,128)(2,1)} %collective-permute-done.1), channel_id=1, source_target_pairs={{0,3},{1,0},{2,1},{3,2},{4,7},{5,4},{6,5},{7,6},{8,11},{9,8},{10,9... | collective-permute-start | bytes 1572872 | tf_op jit(solution)/shard_map/ppermute | solution.py:19
  20.1 22.0 %collective-permute-start.3 = (bf16[512,512]{1,0:T(8,128)(2,1)S(1)}, bf16[512,512]{1,0:T(8,128)(2,1)S(1)}, u32[]{:S(2)}, u32[]{:S(2)}) collective-permute-start(bf16[512,512]{1,0:T(8,128)(2,1)S(1)} %get-tuple-element.95), channel_id=1, source_target_pairs={{0,1},{1,2},{2,3},{3,0},{4,5},{5,6},{6,7},{7,4},{8,9},{9,10},{10,1... | collective-permute-start | bytes 1572872 | tf_op jit(solution)/shard_map/ppermute | solution.py:19
  20.5 21.6 %collective-permute-start.2 = (bf16[512,512]{1,0:T(8,128)(2,1)S(1)}, bf16[512,512]{1,0:T(8,128)(2,1)S(1)}, u32[]{:S(2)}, u32[]{:S(2)}) collective-permute-start(bf16[512,512]{1,0:T(8,128)(2,1)S(1)} %get-tuple-element.94), channel_id=1, source_target_pairs={{0,3},{1,0},{2,1},{3,2},{4,7},{5,4},{6,5},{7,6},{8,11},{9,8},{10,9... | collective-permute-start | bytes 1572872 | tf_op jit(solution)/shard_map/ppermute | solution.py:19
  42.1 12.9 %copy-start.21 = (bf16[512,512]{1,0:T(8,128)(2,1)}, bf16[512,512]{1,0:T(8,128)(2,1)S(1)}, u32[]{:S(2)}) copy-start(bf16[512,512]{1,0:T(8,128)(2,1)S(1)} %collective-permute-done.3) | copy-start | bytes 1572868
  42.1 12.9 %copy-start.23 = (bf16[512,512]{1,0:T(8,128)(2,1)}, bf16[512,512]{1,0:T(8,128)(2,1)S(1)}, u32[]{:S(2)}) copy-start(bf16[512,512]{1,0:T(8,128)(2,1)S(1)} %collective-permute-done.2) | copy-start | bytes 1572868
  42.1 2.5 %copy-start.25 = (bf16[16,256]{1,0:T(8,128)(2,1)S(1)}, bf16[16,256]{1,0:T(8,128)(2,1)}, u32[]{:S(2)}) copy-start(bf16[16,256]{1,0:T(8,128)(2,1)} %param.24) | copy-start | bytes 24580
  42.1 2.5 %copy-start.27 = (f32[256]{0:T(256)S(1)}, f32[256]{0:T(256)}, u32[]{:S(2)}) copy-start(f32[256]{0:T(256)} %param.25) | copy-start | bytes 3076
  51.1 3.2 %copy-start.10 = (f32[1024,256]{1,0:T(8,128)}, f32[1024,256]{1,0:T(8,128)S(1)}, u32[]{:S(2)}) copy-start(f32[1024,256]{1,0:T(8,128)S(1)} %fusion.16) | copy-start | bytes 3145732
  58.0 5.8 %copy-start.5 = (bf16[1024,512]{1,0:T(8,128)(2,1)}, bf16[1024,512]{1,0:T(8,128)(2,1)S(1)}, u32[]{:S(2)}) copy-start(bf16[1024,512]{1,0:T(8,128)(2,1)S(1)} %add_convert_fusion.1) | copy-start | bytes 3145732
  63.9 5.6 %copy-start.1 = (f32[16,256,512]{2,1,0:T(8,128)S(1)}, f32[16,256,512]{2,1,0:T(8,128)}, u32[]{:S(2)}) copy-start(f32[16,256,512]{2,1,0:T(8,128)} %fusion.38) | copy-start | bytes 25165828
  69.5 15.2 %copy-start.9 = (f32[16,64,256]{2,0,1:T(8,128)S(1)}, f32[16,64,256]{2,0,1:T(8,128)}, u32[]{:S(2)}) copy-start(f32[16,64,256]{2,0,1:T(8,128)} %get-tuple-element.58) | copy-start | bytes 3145732
  71.1 26.8 %collective-permute-start.6 = (bf16[258,512]{1,0:T(8,128)(2,1)}, bf16[258,512]{1,0:T(8,128)(2,1)S(1)}, u32[]{:S(2)}, u32[]{:S(2)}) collective-permute-start(bf16[258,512]{1,0:T(8,128)(2,1)} %pad_maximum_fusion.2), channel_id=1, source_target_pairs={{0,4},{4,8},{8,12},{12,16},{16,20},{20,24},{24,28},{28,32},{32,36}... | collective-permute-start | bytes 792584 | tf_op jit(solution)/shard_map/ppermute | solution.py:14
  73.0 27.6 %collective-permute-start.9 = (bf16[258,512]{1,0:T(8,128)(2,1)}, bf16[258,512]{1,0:T(8,128)(2,1)}, u32[]{:S(2)}, u32[]{:S(2)}) collective-permute-start(bf16[258,512]{1,0:T(8,128)(2,1)} %pad_maximum_fusion.2), channel_id=1, source_target_pairs={{0,16},{4,20},{8,24},{12,28},{16,32},{20,36},{24,40},{28,44},{32,4... | collective-permute-start | bytes 792584 | tf_op jit(solution)/shard_map/ppermute | solution.py:14
  78.8 19.7 %collective-permute-start.8 = (bf16[258,512]{1,0:T(8,128)(2,1)}, bf16[258,512]{1,0:T(8,128)(2,1)}, u32[]{:S(2)}, u32[]{:S(2)}) collective-permute-start(bf16[258,512]{1,0:T(8,128)(2,1)} %pad_maximum_fusion.2), channel_id=1, source_target_pairs={{0,12},{4,16},{8,20},{12,24},{16,28},{20,32},{24,36},{28,40},{32,4... | collective-permute-start | bytes 792584 | tf_op jit(solution)/shard_map/ppermute | solution.py:14
  81.2 22.2 %collective-permute-start.7 = (bf16[258,512]{1,0:T(8,128)(2,1)}, bf16[258,512]{1,0:T(8,128)(2,1)}, u32[]{:S(2)}, u32[]{:S(2)}) collective-permute-start(bf16[258,512]{1,0:T(8,128)(2,1)} %pad_maximum_fusion.2), channel_id=1, source_target_pairs={{0,8},{4,12},{8,16},{12,20},{16,24},{20,28},{24,32},{28,36},{32,40... | collective-permute-start | bytes 792584 | tf_op jit(solution)/shard_map/ppermute | solution.py:14
  100.5 10.1 %copy-start.2 = (f32[1024,512]{0,1:T(8,128)S(1)}, f32[1024,512]{0,1:T(8,128)}, u32[]{:S(2)}) copy-start(f32[1024,512]{0,1:T(8,128)} %copy.51) | copy-start | bytes 6291460
  100.5 10.1 %copy-start.11 = (f32[1024,256]{1,0:T(8,128)S(1)}, f32[1024,256]{1,0:T(8,128)}, u32[]{:S(2)}) copy-start(f32[1024,256]{1,0:T(8,128)} %copy-done.10) | copy-start | bytes 3145732
  110.7 2.6 %copy-start.24 = (bf16[512,512]{1,0:T(8,128)(2,1)S(1)}, bf16[512,512]{1,0:T(8,128)(2,1)}, u32[]{:S(2)}) copy-start(bf16[512,512]{1,0:T(8,128)(2,1)} %copy-done.23) | copy-start | bytes 1572868
  110.7 2.6 %copy-start.26 = (f32[512]{0:T(512)S(1)}, f32[512]{0:T(512)}, u32[]{:S(2)}) copy-start(f32[512]{0:T(512)} %param.26) | copy-start | bytes 6148
  117.6 14.7 %collective-permute-start.12 = (bf16[512,512]{1,0:T(8,128)(2,1)S(1)}, bf16[512,512]{1,0:T(8,128)(2,1)S(1)}, u32[]{:S(2)}, u32[]{:S(2)}) collective-permute-start(bf16[512,512]{1,0:T(8,128)(2,1)S(1)} %get-tuple-element.67), channel_id=1, source_target_pairs={{0,3},{1,0},{2,1},{3,2},{4,7},{5,4},{6,5},{7,6},{8,11},{9,8},{10,9... | collective-permute-start | bytes 1572872 | tf_op jit(solution)/shard_map/ppermute | solution.py:19
  120.5 15.8 %collective-permute-start.10 = (bf16[512,512]{1,0:T(8,128)(2,1)S(1)}, bf16[512,512]{1,0:T(8,128)(2,1)S(1)}, u32[]{:S(2)}, u32[]{:S(2)}) collective-permute-start(bf16[512,512]{1,0:T(8,128)(2,1)S(1)} %get-tuple-element.66), channel_id=1, source_target_pairs={{0,1},{1,2},{2,3},{3,0},{4,5},{5,6},{6,7},{7,4},{8,9},{9,10},{10,1... | collective-permute-start | bytes 1572872 | tf_op jit(solution)/shard_map/ppermute | solution.py:19
  132.5 25.9 %collective-permute-start.13 = (bf16[1024,512]{1,0:T(8,128)(2,1)S(1)}, bf16[1024,512]{1,0:T(8,128)(2,1)S(1)}, u32[]{:S(2)}, u32[]{:S(2)}) collective-permute-start(bf16[1024,512]{1,0:T(8,128)(2,1)S(1)} %pad_maximum_fusion.1), channel_id=1, source_target_pairs={{0,3},{1,0},{2,1},{3,2},{4,7},{5,4},{6,5},{7,6},{8,11},{9,8},{10,9... | collective-permute-start | bytes 3145736 | tf_op jit(solution)/shard_map/ppermute | solution.py:19
  136.5 25.7 %collective-permute-start.11 = (bf16[1024,512]{1,0:T(8,128)(2,1)S(1)}, bf16[1024,512]{1,0:T(8,128)(2,1)S(1)}, u32[]{:S(2)}, u32[]{:S(2)}) collective-permute-start(bf16[1024,512]{1,0:T(8,128)(2,1)S(1)} %pad_maximum_fusion), channel_id=1, source_target_pairs={{0,1},{1,2},{2,3},{3,0},{4,5},{5,6},{6,7},{7,4},{8,9},{9,10},{10,1... | collective-permute-start | bytes 3145736 | tf_op jit(solution)/shard_map/ppermute | solution.py:19
  (10 other events, 19.7 us)

commit v11 on v10

--- a/solution.py
+++ b/solution.py
@@ -149,14 +149,27 @@
     tail = jnp.zeros((2, value_width), jnp.float32)
     tail = tail.at[0, :key_width].set(decay_device).at[1, 0].set(first_id).at[1, 1].set(last_id)
     message = jnp.concatenate([final_state, tail]).astype(jnp.bfloat16)
-    got = [shifted(message, "req", j, devices).astype(jnp.float32) for j in range(1, window + 1)]
-    state_in = got[-1][:key_width]
-    last_far = got[-1][key_width + 1, 1]
-    for j in range(window - 1, 0, -1):
-        msg = got[j - 1]
-        link = (msg[key_width + 1, 0] == last_far).astype(jnp.float32)
-        state_in = msg[:key_width] + (link * msg[key_width, :key_width])[:, None] * state_in
-        last_far = msg[key_width + 1, 1]
+    def unpack(msg):
+        return msg[:key_width], msg[key_width, :key_width], msg[key_width + 1, 0], msg[key_width + 1, 1]
+
+    def joined(earlier, later):
+        state_a, decay_a, first_a, last_a = earlier
+        state_b, decay_b, first_b, last_b = later
+        link = (first_b == last_a).astype(jnp.float32)
+        return (state_b + (link * decay_b)[:, None] * state_a, decay_a * decay_b * link, first_a, last_b)
+
+    assert window == 4
+    pair = joined(
+        unpack(shifted(message, "req", 2, devices).astype(jnp.float32)),
+        unpack(shifted(message, "req", 1, devices).astype(jnp.float32)),
+    )
+    pair_state, pair_decay, pair_first, pair_last = pair
+    pair_tail = jnp.zeros((2, value_width), jnp.float32)
+    pair_tail = pair_tail.at[0, :key_width].set(pair_decay).at[1, 0].set(pair_first)
+    pair_tail = pair_tail.at[1, 1].set(pair_last)
+    pair_message = jnp.concatenate([pair_state, pair_tail]).astype(jnp.bfloat16)
+    earlier_pair = unpack(shifted(pair_message, "req", 2, devices).astype(jnp.float32))
+    state_in, _, _, last_far = joined(earlier_pair, pair)
     linked = (first_id == last_far).astype(jnp.float32)
     carried = jnp.dot(
         query.astype(jnp.float32) * jnp.exp(device_cumul), state_in, precision=HIGH

time: 165 us -> 163 us (0.988)
  waiting for transfers between devices: 53.2 us -> 57.5 us
  matrix products: 40 us -> 43.6 us
  starting transfers between devices: 30.3 us -> 26.7 us
  other arithmetic: 13.7 us -> 11.1 us
    ppermute x4 -> x3, starting transfers between devices: 13.6 us -> 10 us  [shifted(): return lax.ppermute(x, axis, pairs)]
    slice x4 -> x3, local copies, waits for them, and re-layouts: 4.9 us -> 1.83 us  [the longest x2 1.23 us: unpack(): msg[key_width + 1, 0]]
    convert_element_type x4 -> x3, other arithmetic: 3.07 us -> 0.16 us  [the longest x1 0.05 us: body(): shifted(pair_message, 'req', 2, devices).astype(jnp.float32)]
    ppermute x10, waiting for transfers between devices: 53.2 us -> 55.7 us  [ring(): lax.ppermute(x, 'tensor', [(i, (i + step) % size) for i in range(size)])]
    dot_general x1, matrix products: 1.62 us -> 3.84 us  [body(): jnp.dot(query.astype(jnp.float32) * jnp.exp(device_cumul), state_in, prec...]
    ppermute x4 -> x3, waiting for transfers between devices: 0.01 us -> 1.81 us  [shifted(): return lax.ppermute(x, axis, pairs)]
    unnamed x57 -> x63, local copies, waits for them, and re-layouts: 3.36 us -> 3.27 us
  transfers between devices with their start and end apart: 14 -> 13, of which waited for: 7 -> 8; matrix products, arithmetic and copies ran while one was open for 18% -> 17% of each run, Pallas kernels for 0% -> 0%
where the time goes in v11:
time: 163 us; the launch traced here: 162 us
  waiting for transfers between devices  57.5 us (35%)
  matrix products  43.6 us (27%)
  starting transfers between devices  26.7 us (16%)
  local copies, waits for them, and re-layouts  17.8 us (11%)
  other arithmetic  11.1 us (7%)
  between operations  5.75 us (4%)
    ppermute x10, waiting for transfers between devices, ring(): lax.ppermute(x, 'tensor', [(i, (i + step) % size) for i in range(size)])  55.7 us
    ppermute x10, starting transfers between devices, ring(): lax.ppermute(x, 'tensor', [(i, (i + step) % size) for i in range(size)])  16.7 us
    dot_general x5, matrix products, projected(): out = jnp.dot(near, near_rows, preferred_element_type=jnp.float32)  13.7 us
    ppermute x3, starting transfers between devices, shifted(): return lax.ppermute(x, axis, pairs)  10 us
    dot_general x5, matrix products, projected(): jnp.dot(far, rows(2), preferred_element_type=jnp.float32)  6.16 us
    dot_general x1, matrix products, body(): jnp.einsum('ncd,ncv->ndv', k_decayed, v_float, precision=HIGH)  5.74 us
    dot_general x16, matrix products, body(): inters.append(jnp.dot(q_decayed[n], entering, precision=HIGH))  4.97 us
    dot_general x4, matrix products, term(): jnp.dot(gated, cols, preferred_element_type=jnp.float32)  4.05 us
  transfers between devices with their start and end apart: 13, of which 8 were waited for; matrix products, arithmetic and copies ran while one was open for 17% of the time, Pallas kernels for 0%

profile of v11, /device:TPU:2, one launch (start us, length us, event | category | flops | bytes accessed | tf_op | source)
XLA Modules:
  0.0 162.3 jit_solution(8250059119348920942)
XLA Ops:
  1.4 1.6 %collective-permute-start = (bf16[512,512]{1,0:T(8,128)(2,1)S(1)}, bf16[512,512]{1,0:T(8,128)(2,1)}, u32[]{:S(2)}, u32[]{:S(2)}) collective-permute-start(bf16[512,512]{1,0:T(8,128)(2,1)S(1)} %get-tuple-element.133), channel_id=1, source_target_pairs={{0,1},{1,2},{2,3},{3,0},{4,5},{5,6},{6,7},{7,4},{8,9},{9,10},{10,1... | collective-permute-start | bytes 1572872 | tf_op jit(solution)/shard_map/ppermute | solution.py:19
  3.1 1.7 %collective-permute-start.1 = (bf16[512,512]{1,0:T(8,128)(2,1)S(1)}, bf16[512,512]{1,0:T(8,128)(2,1)}, u32[]{:S(2)}, u32[]{:S(2)}) collective-permute-start(bf16[512,512]{1,0:T(8,128)(2,1)S(1)} %get-tuple-element.132), channel_id=1, source_target_pairs={{0,3},{1,0},{2,1},{3,2},{4,7},{5,4},{6,5},{7,6},{8,11},{9,8},{10,9... | collective-permute-start | bytes 1572872 | tf_op jit(solution)/shard_map/ppermute | solution.py:19
  12.5 4.0 %collective-permute-done = bf16[512,512]{1,0:T(8,128)(2,1)} collective-permute-done((bf16[512,512]{1,0:T(8,128)(2,1)S(1)}, bf16[512,512]{1,0:T(8,128)(2,1)}, u32[]{:S(2)}, u32[]{:S(2)}) %collective-permute-start) | collective-permute-done | bytes 524320 | tf_op jit(solution)/shard_map/ppermute | solution.py:19
  18.2 1.7 %collective-permute-start.5 = (bf16[512,512]{1,0:T(8,128)(2,1)}, bf16[512,512]{1,0:T(8,128)(2,1)S(1)}, u32[]{:S(2)}, u32[]{:S(2)}) collective-permute-start(bf16[512,512]{1,0:T(8,128)(2,1)} %collective-permute-done.1), channel_id=1, source_target_pairs={{0,3},{1,0},{2,1},{3,2},{4,7},{5,4},{6,5},{7,6},{8,11},{9,8},{10,9... | collective-permute-start | bytes 1572872 | tf_op jit(solution)/shard_map/ppermute | solution.py:19
  20.5 2.9 %collective-permute-start.2 = (bf16[512,512]{1,0:T(8,128)(2,1)S(1)}, bf16[512,512]{1,0:T(8,128)(2,1)S(1)}, u32[]{:S(2)}, u32[]{:S(2)}) collective-permute-start(bf16[512,512]{1,0:T(8,128)(2,1)S(1)} %get-tuple-element.130), channel_id=1, source_target_pairs={{0,3},{1,0},{2,1},{3,2},{4,7},{5,4},{6,5},{7,6},{8,11},{9,8},{10,9... | collective-permute-start | bytes 1572872 | tf_op jit(solution)/shard_map/ppermute | solution.py:19
  23.4 9.4 %collective-permute-done.4 = bf16[512,512]{1,0:T(8,128)(2,1)S(1)} collective-permute-done((bf16[512,512]{1,0:T(8,128)(2,1)}, bf16[512,512]{1,0:T(8,128)(2,1)S(1)}, u32[]{:S(2)}, u32[]{:S(2)}) %collective-permute-start.4) | collective-permute-done | bytes 524320 | tf_op jit(solution)/shard_map/ppermute | solution.py:19
  34.5 1.8 %fusion.99 = f32[1024,512]{1,0:T(8,128)S(1)} fusion(bf16[1024,512]{1,0:T(8,128)(2,1)S(1)} %constant_dynamic-update-slice_fusion, bf16[2048,512]{1,0:T(8,128)(2,1)} %param.27, s32[]{:T(128)S(6)} %select_n.111), kind=kOutput, calls=%fused_computation.167 | convolution fusion | flops 536870912 | bytes 3670020 | tf_op jit(solution)/shard_map/dot_general | solution.py:47
  36.3 5.8 %collective-permute-done.3 = bf16[512,512]{1,0:T(8,128)(2,1)S(1)} collective-permute-done((bf16[512,512]{1,0:T(8,128)(2,1)S(1)}, bf16[512,512]{1,0:T(8,128)(2,1)S(1)}, u32[]{:S(2)}, u32[]{:S(2)}) %collective-permute-start.3) | collective-permute-done | bytes 524320 | tf_op jit(solution)/shard_map/ppermute | solution.py:19
  42.1 2.5 %convolution_add_fusion.3 = f32[1024,16]{0,1:T(8,128)S(1)} fusion(f32[1024,16]{0,1:T(8,128)S(1)} %fusion.150, bf16[512,16]{0,1:T(8,128)(2,1)S(1)} %get-tuple-element.142, bf16[512,16]{0,1:T(8,128)(2,1)S(1)} %get-tuple-element.141, bf16[512,16]{0,1:T(8,128)(2,1)S(1)} %get-tuple-element.140, bf16[512,512]{1,0:T(8,128)(2,1)S(1)} %collective-permute-done.3, ...), kind=kOutput, calls=%fused_computation.64 | convolution fusion | flops 66224128 | bytes 3325952 | tf_op jit(solution)/shard_map/dot_general | solution.py:46
  46.5 2.2 %fusion.17 = bf16[1024,256]{1,0:T(8,128)(2,1)S(1)} fusion(f32[1024,256]{1,0:T(8,128)S(1)} %fusion.106, bf16[512,256]{1,0:T(8,128)(2,1)S(1)} %get-tuple-element.126, bf16[512,256]{1,0:T(8,128)(2,1)S(1)} %get-tuple-element.125, bf16[512,256]{1,0:T(8,128)(2,1)S(1)} %get-tuple-element.124, bf16[512,512]{1,0:T(8,128)(2,1)S(1)} %collective-permute-done.3, ...), kind=kOutput, calls=%fused_computation.30 | convolution fusion | flops 823918592 | bytes 5505024 | tf_op jit(solution)/shard_map/dot_general | solution.py:46
  48.9 2.2 %fusion.16 = f32[1024,256]{1,0:T(8,128)S(1)} fusion(f32[1024,256]{1,0:T(8,128)S(1)} %fusion.108, bf16[512,256]{1,0:T(8,128)(2,1)S(1)} %get-tuple-element.165, bf16[512,256]{1,0:T(8,128)(2,1)S(1)} %get-tuple-element.166, bf16[512,256]{1,0:T(8,128)(2,1)S(1)} %get-tuple-element.167, bf16[512,512]{1,0:T(8,128)(2,1)S(1)} %collective-permute-done.3, ...), kind=kOutput, calls=%fused_computation.29 | convolution fusion | flops 824180736 | bytes 6029312 | tf_op jit(solution)/shard_map/dot_general | solution.py:46
  51.1 3.3 %exponential_multiply_fusion.2 = (f32[16,64,256]{2,0,1:T(8,128)}, f32[16,64,256]{2,0,1:T(8,128)}, f32[16,64,256]{2,0,1:T(8,128)S(1)}, f32[16,64,256]{2,0,1:T(8,128)}, f32[16,64,256]{2,0,1:T(8,128)S(1)}) fusion(f32[16,64,256]{2,0,1:T(8,128)S(1)} %fusion.42, f32[16,64,256]{2,1,0:T(8,128)S(1)} %bitcast.317, f32[16,256]{1,0:T(8,128)S(1)} %get-tuple-element.107, ...), kind=kLoop, calls=%fused_computation.82 | loop fusion | flops 2359296 | bytes 8441856 | tf_op jit(solution)/shard_map/mul | solution.py:122
  55.1 3.4 %add_convert_fusion.1 = bf16[1024,512]{1,0:T(8,128)(2,1)S(1)} fusion(f32[1024,512]{1,0:T(8,128)S(1)} %fusion.99, bf16[512,512]{1,0:T(8,128)(2,1)S(1)} %get-tuple-element.99, bf16[512,512]{1,0:T(8,128)(2,1)S(1)} %get-tuple-element.98, bf16[512,512]{1,0:T(8,128)(2,1)S(1)} %get-tuple-element.97, bf16[512,512]{1,0:T(8,128)(2,1)S(1)} %collective-permute-done.3, ...), kind=kOutput, calls=%fused_computation.7 | convolution fusion | flops 1632108544 | bytes 7864320 | tf_op jit(solution)/shard_map/dot_general | solution.py:46
  58.5 5.7 %fusion.38 = f32[16,256,512]{2,1,0:T(8,128)} fusion(bf16[16,64,512]{2,1,0:T(8,128)(2,1)S(1)} %bitcast.315, f32[16,64,256]{2,0,1:T(8,128)S(1)} %get-tuple-element.100), kind=kOutput, calls=%fused_computation.69 | convolution fusion | flops 805306368 | bytes 10485760 | tf_op jit(solution)/shard_map/ncd,ncv->ndv/dot_general | solution.py:131
  64.4 3.7 %multiply_add_fusion.2 = (f32[1,256,512]{2,1,0:T(8,128)S(1)}, f32[1,256,512]{2,1,0:T(8,128)S(1)}, f32[1,256,512]{2,1,0:T(8,128)S(1)}, f32[1,256,512]{2,1,0:T(8,1...) fusion(f32[16,256,512]{2,1,0:T(8,128)} %fusion.38, ...), kind=kLoop, calls=%fused_computation.154 | loop fusion | flops 3538944 | bytes 11024384 | tf_op jit(solution)/shard_map/add | solution.py:139
  68.1 1.8 %copy-done.1 = f32[16,256,512]{2,1,0:T(8,128)S(1)} copy-done((f32[16,256,512]{2,1,0:T(8,128)S(1)}, f32[16,256,512]{2,1,0:T(8,128)}, u32[]{:S(2)}) %copy-start.1) | copy-done | bytes 8388632
  70.9 1.9 %collective-permute-start.6 = (bf16[258,512]{1,0:T(8,128)(2,1)S(1)}, bf16[258,512]{1,0:T(8,128)(2,1)S(1)}, u32[]{:S(2)}, u32[]{:S(2)}) collective-permute-start(bf16[258,512]{1,0:T(8,128)(2,1)S(1)} %pad_maximum_fusion.2), channel_id=1, source_target_pairs={{0,4},{4,8},{8,12},{12,16},{16,20},{20,24},{24,28},{28,32},{32,36}... | collective-permute-start | bytes 792584 | tf_op jit(solution)/shard_map/ppermute | solution.py:14
  72.8 4.0 %collective-permute-start.7 = (bf16[258,512]{1,0:T(8,128)(2,1)S(1)}, bf16[258,512]{1,0:T(8,128)(2,1)S(1)}, u32[]{:S(2)}, u32[]{:S(2)}) collective-permute-start(bf16[258,512]{1,0:T(8,128)(2,1)S(1)} %pad_maximum_fusion.2), channel_id=1, source_target_pairs={{0,8},{4,12},{8,16},{12,20},{16,24},{20,28},{24,32},{28,36},{32,40... | collective-permute-start | bytes 792584 | tf_op jit(solution)/shard_map/ppermute | solution.py:14
  83.1 1.7 %convolution_select_fusion = f32[16,64,64]{2,1,0:T(8,128)S(1)} fusion(f32[16,64,256]{2,0,1:T(8,128)S(1)} %copy-done.13, f32[16,64,256]{2,0,1:T(8,128)S(1)} %copy-done.12, s32[16,64]{1,0:T(8,128)S(1)} %eq.84, pred[64,64]{1,0:T(8,128)(4,1)S(1)} %iota_compare_fusion), kind=kOutput, calls=%fused_computation.31 | convolution fusion | flops 100859904 | bytes 2367488 | tf_op jit(solution)/shard_map/ncd,nsd->ncs/dot_general | solution.py:124
  84.8 2.3 %multiply_add_fusion.1 = f32[16,64,512]{2,1,0:T(8,128)} fusion(f32[16,64,512]{2,1,0:T(8,128)S(1)} %fusion.18, f32[16,64,64]{2,1,0:T(8,128)S(1)} %convolution_select_fusion, bf16[16,64,512]{2,1,0:T(8,128)(2,1)S(1)} %bitcast.316, f32[16,64]{1,0:T(8,128)S(1)} %compare_convert_fusion.1), kind=kOutput, calls=%fused_computation.6 | convolution fusion | flops 202375168 | bytes 5509120 | tf_op jit(solution)/shard_map/ncs,nsv->ncv/dot_general | solution.py:127
  92.7 4.1 %collective-permute-start.8 = (bf16[258,512]{1,0:T(8,128)(2,1)}, bf16[258,512]{1,0:T(8,128)(2,1)S(1)}, u32[]{:S(2)}, u32[]{:S(2)}) collective-permute-start(bf16[258,512]{1,0:T(8,128)(2,1)} %pad_maximum_fusion.3), channel_id=1, source_target_pairs={{0,8},{4,12},{8,16},{12,20},{16,24},{20,28},{24,32},{28,36},{32,40... | collective-permute-start | bytes 792584 | tf_op jit(solution)/shard_map/ppermute | solution.py:14
  96.8 3.1 %fusion.95 = f32[1024,512]{0,1:T(8,128)} fusion(bf16[1024,512]{1,0:T(8,128)(2,1)S(1)} %constant_dynamic-update-slice_fusion, bf16[2048,512]{1,0:T(8,128)(2,1)} %param.28, s32[]{:T(128)S(6)} %select_n.111), kind=kOutput, calls=%fused_computation.149 | convolution fusion | flops 536870912 | bytes 3670020 | tf_op jit(solution)/shard_map/dot_general | solution.py:47
  99.9 3.0 %copy.51 = f32[1024,512]{0,1:T(8,128)} copy(f32[1024,512]{1,0:T(8,128)} %bitcast.312) | data formatting | bytes 4194304 | tf_op jit(solution)/shard_map/reshape | solution.py:142
  103.7 1.8 %collective-permute-done.8 = bf16[258,512]{1,0:T(8,128)(2,1)S(1)} collective-permute-done((bf16[258,512]{1,0:T(8,128)(2,1)}, bf16[258,512]{1,0:T(8,128)(2,1)S(1)}, u32[]{:S(2)}, u32[]{:S(2)}) %collective-permute-start.8) | collective-permute-done | bytes 264224 | tf_op jit(solution)/shard_map/ppermute | solution.py:14
  107.5 3.8 %multiply_reduce_fusion = (f32[1024]{0:T(1024)S(1)}, f32[1024,512]{0,1:T(8,128)S(1)}) fusion(f32[1024,512]{0,1:T(8,128)} %copy.51, f32[1024]{0:T(1024)S(1)} %select_bitcast_fusion, f32[258,512]{1,0:T(8,128)S(1)} %convert_element_type.129, f32[256]{0:T(256)S(1)} %bitcast.360, f32[258,512]{1,0:T(8,128)S(1)} %copy-done.5, f32[256]{0:T(256)S(1)} %bitcast.358, ...), kind=kOutput, calls=%fused_computation.4 | convolution fusion | flops 808713216 | bytes 7874560 | tf_op jit(solution)/shard_map/dot_general | solution.py:174
  111.4 3.4 %multiply_convert_fusion = bf16[1024,512]{0,1:T(8,128)(2,1)S(1)} fusion(f32[1024,512]{0,1:T(8,128)S(1)} %copy-done.16, f32[1024,512]{0,1:T(8,128)S(1)} %get-tuple-element.164, bf16[512,512]{1,0:T(8,128)(2,1)S(1)} %copy-done.21, bf16[512,512]{1,0:T(8,128)(2,1)S(1)} %copy-done.20, bf16[512,512]{1,0:T(8,128)(2,1)S(1)} %copy-done.19, f32[512]{0:T(512)S(1)} %copy-done.29, ...), kind=kOutput, calls=%fused_computation.3 | convolution fusion | flops 1635778560 | bytes 9967616 | tf_op jit(solution)/shard_map/dot_general | solution.py:46
  115.7 2.9 %collective-permute-start.11 = (bf16[512,512]{1,0:T(8,128)(2,1)S(1)}, bf16[512,512]{1,0:T(8,128)(2,1)S(1)}, u32[]{:S(2)}, u32[]{:S(2)}) collective-permute-start(bf16[512,512]{1,0:T(8,128)(2,1)S(1)} %get-tuple-element.103), channel_id=1, source_target_pairs={{0,3},{1,0},{2,1},{3,2},{4,7},{5,4},{6,5},{7,6},{8,11},{9,8},{10,9... | collective-permute-start | bytes 1572872 | tf_op jit(solution)/shard_map/ppermute | solution.py:19
  120.2 10.4 %collective-permute-done.11 = bf16[512,512]{1,0:T(8,128)(2,1)S(1)} collective-permute-done((bf16[512,512]{1,0:T(8,128)(2,1)S(1)}, bf16[512,512]{1,0:T(8,128)(2,1)S(1)}, u32[]{:S(2)}, u32[]{:S(2)}) %collective-permute-start.11) | collective-permute-done | bytes 524320 | tf_op jit(solution)/shard_map/ppermute | solution.py:19
  130.7 3.8 %collective-permute-start.12 = (bf16[1024,512]{1,0:T(8,128)(2,1)S(1)}, bf16[1024,512]{1,0:T(8,128)(2,1)S(1)}, u32[]{:S(2)}, u32[]{:S(2)}) collective-permute-start(bf16[1024,512]{1,0:T(8,128)(2,1)S(1)} %pad_maximum_fusion.1), channel_id=1, source_target_pairs={{0,3},{1,0},{2,1},{3,2},{4,7},{5,4},{6,5},{7,6},{8,11},{9,8},{10,9... | collective-permute-start | bytes 3145736 | tf_op jit(solution)/shard_map/ppermute | solution.py:19
  134.8 22.0 %collective-permute-done.12 = bf16[1024,512]{1,0:T(8,128)(2,1)S(1)} collective-permute-done((bf16[1024,512]{1,0:T(8,128)(2,1)S(1)}, bf16[1024,512]{1,0:T(8,128)(2,1)S(1)}, u32[]{:S(2)}, u32[]{:S(2)}) %collective-permute-start.12) | collective-permute-done | bytes 1048608 | tf_op jit(solution)/shard_map/ppermute | solution.py:19
  156.8 3.7 %collective-permute-done.10 = bf16[1024,512]{1,0:T(8,128)(2,1)S(1)} collective-permute-done((bf16[1024,512]{1,0:T(8,128)(2,1)S(1)}, bf16[1024,512]{1,0:T(8,128)(2,1)S(1)}, u32[]{:S(2)}, u32[]{:S(2)}) %collective-permute-start.10) | collective-permute-done | bytes 1048608 | tf_op jit(solution)/shard_map/ppermute | solution.py:19
  160.5 1.8 %add_convert_fusion = bf16[1024,512]{1,0:T(8,128)(2,1)} fusion(bf16[1024,512]{1,0:T(8,128)(2,1)S(1)} %collective-permute-done.12, bf16[1024,512]{1,0:T(8,128)(2,1)S(1)} %collective-permute-done.10, bf16[1024,512]{0,1:T(8,128)(2,1)S(1)} %multiply_convert_fusion, bf16[512,2048]{1,0:T(8,128)(2,1)S(1)} %copy-done, s32[]{:T(128)S(6)} %select_n.105), kind=kOutput, calls=%fused_computation.2 | convolution fusion | flops 540540928 | bytes 4718596 | tf_op jit(solution)/shard_map/dot_general | solution.py:60
  (157 shorter events, 29.2 us)
Async XLA Ops:
  0.0 114.8 %copy-start = (bf16[512,2048]{1,0:T(8,128)(2,1)S(1)}, bf16[512,2048]{1,0:T(8,128)(2,1)}, u32[]{:S(2)}) copy-start(bf16[512,2048]{1,0:T(8,128)(2,1)} %param.33) | copy-start | bytes 6291460
  0.0 4.7 %copy-start.23 = (s32[1024]{0:T(1024)S(1)}, s32[1024]{0:T(1024)}, u32[]{:S(2)}) copy-start(s32[1024]{0:T(1024)} %param.24) | copy-start | bytes 12292
  0.0 9.5 %copy-start.22 = (bf16[2048,16]{0,1:T(8,128)(2,1)S(1)}, bf16[2048,16]{0,1:T(8,128)(2,1)}, u32[]{:S(2)}) copy-start(bf16[2048,16]{0,1:T(8,128)(2,1)} %param.29) | copy-start | bytes 196612
  1.4 15.1 %collective-permute-start = (bf16[512,512]{1,0:T(8,128)(2,1)S(1)}, bf16[512,512]{1,0:T(8,128)(2,1)}, u32[]{:S(2)}, u32[]{:S(2)}) collective-permute-start(bf16[512,512]{1,0:T(8,128)(2,1)S(1)} %get-tuple-element.133), channel_id=1, source_target_pairs={{0,1},{1,2},{2,3},{3,0},{4,5},{5,6},{6,7},{7,4},{8,9},{9,10},{10,1... | collective-permute-start | bytes 1572872 | tf_op jit(solution)/shard_map/ppermute | solution.py:19
  3.1 13.5 %collective-permute-start.1 = (bf16[512,512]{1,0:T(8,128)(2,1)S(1)}, bf16[512,512]{1,0:T(8,128)(2,1)}, u32[]{:S(2)}, u32[]{:S(2)}) collective-permute-start(bf16[512,512]{1,0:T(8,128)(2,1)S(1)} %get-tuple-element.132), channel_id=1, source_target_pairs={{0,3},{1,0},{2,1},{3,2},{4,7},{5,4},{6,5},{7,6},{8,11},{9,8},{10,9... | collective-permute-start | bytes 1572872 | tf_op jit(solution)/shard_map/ppermute | solution.py:19
  11.4 8.5 %copy-start.17 = (bf16[2048,256]{1,0:T(8,128)(2,1)S(1)}, bf16[2048,256]{1,0:T(8,128)(2,1)}, u32[]{:S(2)}) copy-start(bf16[2048,256]{1,0:T(8,128)(2,1)} %param.25) | copy-start | bytes 3145732
  11.4 8.5 %copy-start.18 = (bf16[2048,256]{1,0:T(8,128)(2,1)S(1)}, bf16[2048,256]{1,0:T(8,128)(2,1)}, u32[]{:S(2)}) copy-start(bf16[2048,256]{1,0:T(8,128)(2,1)} %param.26) | copy-start | bytes 3145732
  12.5 7.5 %copy-start.7 = (bf16[1024,512]{1,0:T(8,128)(2,1)S(1)}, bf16[1024,512]{1,0:T(8,128)(2,1)}, u32[]{:S(2)}) copy-start(bf16[1024,512]{1,0:T(8,128)(2,1)} %param.23) | copy-start | bytes 3145732
  16.6 16.2 %collective-permute-start.4 = (bf16[512,512]{1,0:T(8,128)(2,1)}, bf16[512,512]{1,0:T(8,128)(2,1)S(1)}, u32[]{:S(2)}, u32[]{:S(2)}) collective-permute-start(bf16[512,512]{1,0:T(8,128)(2,1)} %collective-permute-done), channel_id=1, source_target_pairs={{0,1},{1,2},{2,3},{3,0},{4,5},{5,6},{6,7},{7,4},{8,9},{9,10},{10,1... | collective-permute-start | bytes 1572872 | tf_op jit(solution)/shard_map/ppermute | solution.py:19
  18.2 15.1 %collective-permute-start.5 = (bf16[512,512]{1,0:T(8,128)(2,1)}, bf16[512,512]{1,0:T(8,128)(2,1)S(1)}, u32[]{:S(2)}, u32[]{:S(2)}) collective-permute-start(bf16[512,512]{1,0:T(8,128)(2,1)} %collective-permute-done.1), channel_id=1, source_target_pairs={{0,3},{1,0},{2,1},{3,2},{4,7},{5,4},{6,5},{7,6},{8,11},{9,8},{10,9... | collective-permute-start | bytes 1572872 | tf_op jit(solution)/shard_map/ppermute | solution.py:19
  20.1 22.0 %collective-permute-start.3 = (bf16[512,512]{1,0:T(8,128)(2,1)S(1)}, bf16[512,512]{1,0:T(8,128)(2,1)S(1)}, u32[]{:S(2)}, u32[]{:S(2)}) collective-permute-start(bf16[512,512]{1,0:T(8,128)(2,1)S(1)} %get-tuple-element.131), channel_id=1, source_target_pairs={{0,1},{1,2},{2,3},{3,0},{4,5},{5,6},{6,7},{7,4},{8,9},{9,10},{10,1... | collective-permute-start | bytes 1572872 | tf_op jit(solution)/shard_map/ppermute | solution.py:19
  20.5 21.5 %collective-permute-start.2 = (bf16[512,512]{1,0:T(8,128)(2,1)S(1)}, bf16[512,512]{1,0:T(8,128)(2,1)S(1)}, u32[]{:S(2)}, u32[]{:S(2)}) collective-permute-start(bf16[512,512]{1,0:T(8,128)(2,1)S(1)} %get-tuple-element.130), channel_id=1, source_target_pairs={{0,3},{1,0},{2,1},{3,2},{4,7},{5,4},{6,5},{7,6},{8,11},{9,8},{10,9... | collective-permute-start | bytes 1572872 | tf_op jit(solution)/shard_map/ppermute | solution.py:19
  42.1 13.0 %copy-start.24 = (bf16[512,512]{1,0:T(8,128)(2,1)}, bf16[512,512]{1,0:T(8,128)(2,1)S(1)}, u32[]{:S(2)}) copy-start(bf16[512,512]{1,0:T(8,128)(2,1)S(1)} %collective-permute-done.3) | copy-start | bytes 1572868
  42.1 13.0 %copy-start.26 = (bf16[512,512]{1,0:T(8,128)(2,1)}, bf16[512,512]{1,0:T(8,128)(2,1)S(1)}, u32[]{:S(2)}) copy-start(bf16[512,512]{1,0:T(8,128)(2,1)S(1)} %collective-permute-done.2) | copy-start | bytes 1572868
  55.1 9.1 %copy-start.6 = (f32[16,64,256]{2,1,0:T(8,128)}, f32[16,64,256]{2,1,0:T(8,128)S(1)}, u32[]{:S(2)}) copy-start(f32[16,64,256]{2,1,0:T(8,128)S(1)} %copy.50) | copy-start | bytes 3145732
  58.5 5.8 %copy-start.9 = (bf16[1024,512]{1,0:T(8,128)(2,1)}, bf16[1024,512]{1,0:T(8,128)(2,1)S(1)}, u32[]{:S(2)}) copy-start(bf16[1024,512]{1,0:T(8,128)(2,1)S(1)} %add_convert_fusion.1) | copy-start | bytes 3145732
  64.4 5.6 %copy-start.1 = (f32[16,256,512]{2,1,0:T(8,128)S(1)}, f32[16,256,512]{2,1,0:T(8,128)}, u32[]{:S(2)}) copy-start(f32[16,256,512]{2,1,0:T(8,128)} %fusion.38) | copy-start | bytes 25165828
  70.0 6.9 %copy-start.14 = (f32[16,64,256]{2,0,1:T(8,128)S(1)}, f32[16,64,256]{2,0,1:T(8,128)}, u32[]{:S(2)}) copy-start(f32[16,64,256]{2,0,1:T(8,128)} %get-tuple-element.94) | copy-start | bytes 3145732
  70.9 16.2 %collective-permute-start.6 = (bf16[258,512]{1,0:T(8,128)(2,1)S(1)}, bf16[258,512]{1,0:T(8,128)(2,1)S(1)}, u32[]{:S(2)}, u32[]{:S(2)}) collective-permute-start(bf16[258,512]{1,0:T(8,128)(2,1)S(1)} %pad_maximum_fusion.2), channel_id=1, source_target_pairs={{0,4},{4,8},{8,12},{12,16},{16,20},{20,24},{24,28},{28,32},{32,36}... | collective-permute-start | bytes 792584 | tf_op jit(solution)/shard_map/ppermute | solution.py:14
  72.8 14.9 %collective-permute-start.7 = (bf16[258,512]{1,0:T(8,128)(2,1)S(1)}, bf16[258,512]{1,0:T(8,128)(2,1)S(1)}, u32[]{:S(2)}, u32[]{:S(2)}) collective-permute-start(bf16[258,512]{1,0:T(8,128)(2,1)S(1)} %pad_maximum_fusion.2), channel_id=1, source_target_pairs={{0,8},{4,12},{8,16},{12,20},{16,24},{20,28},{24,32},{28,36},{32,40... | collective-permute-start | bytes 792584 | tf_op jit(solution)/shard_map/ppermute | solution.py:14
  92.7 12.8 %collective-permute-start.8 = (bf16[258,512]{1,0:T(8,128)(2,1)}, bf16[258,512]{1,0:T(8,128)(2,1)S(1)}, u32[]{:S(2)}, u32[]{:S(2)}) collective-permute-start(bf16[258,512]{1,0:T(8,128)(2,1)} %pad_maximum_fusion.3), channel_id=1, source_target_pairs={{0,8},{4,12},{8,16},{12,20},{16,24},{20,28},{24,32},{28,36},{32,40... | collective-permute-start | bytes 792584 | tf_op jit(solution)/shard_map/ppermute | solution.py:14
  99.9 7.4 %copy-start.3 = (f32[258,512]{1,0:T(8,128)S(1)}, f32[258,512]{1,0:T(8,128)}, u32[]{:S(2)}) copy-start(f32[258,512]{1,0:T(8,128)} %copy-done.2) | copy-start | bytes 1585156
  99.9 7.4 %copy-start.5 = (f32[258,512]{1,0:T(8,128)S(1)}, f32[258,512]{1,0:T(8,128)}, u32[]{:S(2)}) copy-start(f32[258,512]{1,0:T(8,128)} %copy-done.4) | copy-start | bytes 1585156
  107.4 3.9 %copy-start.8 = (bf16[1024,512]{1,0:T(8,128)(2,1)S(1)}, bf16[1024,512]{1,0:T(8,128)(2,1)}, u32[]{:S(2)}) copy-start(bf16[1024,512]{1,0:T(8,128)(2,1)} %param.23) | copy-start | bytes 3145732
  107.4 3.9 %copy-start.16 = (f32[1024,512]{0,1:T(8,128)S(1)}, f32[1024,512]{0,1:T(8,128)}, u32[]{:S(2)}) copy-start(f32[1024,512]{0,1:T(8,128)} %fusion.95) | copy-start | bytes 6291460
  107.4 3.9 %copy-start.19 = (bf16[512,512]{1,0:T(8,128)(2,1)S(1)}, bf16[512,512]{1,0:T(8,128)(2,1)}, u32[]{:S(2)}) copy-start(bf16[512,512]{1,0:T(8,128)(2,1)} %get-tuple-element.90) | copy-start | bytes 1572868
  107.4 3.9 %copy-start.20 = (bf16[512,512]{1,0:T(8,128)(2,1)S(1)}, bf16[512,512]{1,0:T(8,128)(2,1)}, u32[]{:S(2)}) copy-start(bf16[512,512]{1,0:T(8,128)(2,1)} %get-tuple-element.91) | copy-start | bytes 1572868
  107.4 3.9 %copy-start.21 = (bf16[512,512]{1,0:T(8,128)(2,1)S(1)}, bf16[512,512]{1,0:T(8,128)(2,1)}, u32[]{:S(2)}) copy-start(bf16[512,512]{1,0:T(8,128)(2,1)} %get-tuple-element.92) | copy-start | bytes 1572868
  115.7 14.8 %collective-permute-start.11 = (bf16[512,512]{1,0:T(8,128)(2,1)S(1)}, bf16[512,512]{1,0:T(8,128)(2,1)S(1)}, u32[]{:S(2)}, u32[]{:S(2)}) collective-permute-start(bf16[512,512]{1,0:T(8,128)(2,1)S(1)} %get-tuple-element.103), channel_id=1, source_target_pairs={{0,3},{1,0},{2,1},{3,2},{4,7},{5,4},{6,5},{7,6},{8,11},{9,8},{10,9... | collective-permute-start | bytes 1572872 | tf_op jit(solution)/shard_map/ppermute | solution.py:19
  118.6 15.9 %collective-permute-start.9 = (bf16[512,512]{1,0:T(8,128)(2,1)S(1)}, bf16[512,512]{1,0:T(8,128)(2,1)S(1)}, u32[]{:S(2)}, u32[]{:S(2)}) collective-permute-start(bf16[512,512]{1,0:T(8,128)(2,1)S(1)} %get-tuple-element.102), channel_id=1, source_target_pairs={{0,1},{1,2},{2,3},{3,0},{4,5},{5,6},{6,7},{7,4},{8,9},{9,10},{10,1... | collective-permute-start | bytes 1572872 | tf_op jit(solution)/shard_map/ppermute | solution.py:19
  130.7 26.1 %collective-permute-start.12 = (bf16[1024,512]{1,0:T(8,128)(2,1)S(1)}, bf16[1024,512]{1,0:T(8,128)(2,1)S(1)}, u32[]{:S(2)}, u32[]{:S(2)}) collective-permute-start(bf16[1024,512]{1,0:T(8,128)(2,1)S(1)} %pad_maximum_fusion.1), channel_id=1, source_target_pairs={{0,3},{1,0},{2,1},{3,2},{4,7},{5,4},{6,5},{7,6},{8,11},{9,8},{10,9... | collective-permute-start | bytes 3145736 | tf_op jit(solution)/shard_map/ppermute | solution.py:19
  134.7 25.8 %collective-permute-start.10 = (bf16[1024,512]{1,0:T(8,128)(2,1)S(1)}, bf16[1024,512]{1,0:T(8,128)(2,1)S(1)}, u32[]{:S(2)}, u32[]{:S(2)}) collective-permute-start(bf16[1024,512]{1,0:T(8,128)(2,1)S(1)} %pad_maximum_fusion), channel_id=1, source_target_pairs={{0,1},{1,2},{2,3},{3,0},{4,5},{5,6},{6,7},{7,4},{8,9},{9,10},{10,1... | collective-permute-start | bytes 3145736 | tf_op jit(solution)/shard_map/ppermute | solution.py:19
  (12 other events, 29.2 us)

commit v12 on v11

--- a/solution.py
+++ b/solution.py
@@ -12,6 +12,13 @@
 def shifted(x, axis, shift, devices):
     pairs = [(i, i + shift) for i in range(devices - shift)]
     return lax.ppermute(x, axis, pairs)
+
+
+def split_dot(spec, a, b):
+    high = a.astype(jnp.bfloat16)
+    low = (a - high.astype(jnp.float32)).astype(jnp.bfloat16)
+    first = jnp.einsum(spec, high, b, preferred_element_type=jnp.float32)
+    return first + jnp.einsum(spec, low, b, preferred_element_type=jnp.float32)
 
 
 def ring(x, step):
@@ -114,7 +121,7 @@
 
     q_float = query.astype(jnp.float32).reshape(blocks, GROUP, key_width)
     k_float = key.astype(jnp.float32).reshape(blocks, GROUP, key_width)
-    v_float = value.astype(jnp.float32).reshape(blocks, GROUP, value_width)
+    v_blocks = value.reshape(blocks, GROUP, value_width)
 
     positions = jnp.arange(GROUP)
     causal = positions[None, :] <= positions[:, None]
@@ -124,11 +131,11 @@
     raw_scores = jnp.einsum("ncd,nsd->ncs", q_scaled, k_scaled, precision=HIGH)
     allowed = causal[None] & (seg_blocks[:, :, None] == seg_blocks[:, None, :])
     scores = jnp.where(allowed, raw_scores, 0.0)
-    intra = jnp.einsum("ncs,nsv->ncv", scores, v_float, precision=HIGH)
+    intra = split_dot("ncs,nsv->ncv", scores, v_blocks)
 
     same_last = (seg_blocks == seg_blocks[:, -1:]).astype(jnp.float32)
     k_decayed = k_float * jnp.exp(block_totals[:, None, :] - cumul) * same_last[:, :, None]
-    chunk_states = jnp.einsum("ncd,ncv->ndv", k_decayed, v_float, precision=HIGH)
+    chunk_states = split_dot("ncd,ncv->ndv", k_decayed, v_blocks)
     chunk_decay = jnp.exp(block_totals) * live_blocks[:, -1:]
 
     q_decayed = q_float * jnp.exp(cumul)

time: 163 us -> 163 us (level)
    convert_element_type x0 -> x1, other arithmetic: none -> 3.34 us  [split_dot(): low = (a - high.astype(jnp.float32)).astype(jnp.bfloat16)]
    mul x1 -> x0, other arithmetic: 3.32 us -> none  [body(): q_scaled = q_float * jnp.exp(cumul - centre[:, None, :])]
    dot_general x2 -> x4, matrix products: 8 us -> 8.09 us  [the longest x2 6.38 us: split_dot(): return first + jnp.einsum(spec, low, b, preferred_element_type=jnp.float32)]
where the time goes in v12:
time: 163 us; the launch traced here: 162 us
  waiting for transfers between devices  57.5 us (35%)
  matrix products  43.7 us (27%)
  starting transfers between devices  26.8 us (16%)
  local copies, waits for them, and re-layouts  17.5 us (11%)
  other arithmetic  11.1 us (7%)
  between operations  5.77 us (4%)
    ppermute x10, waiting for transfers between devices, ring(): lax.ppermute(x, 'tensor', [(i, (i + step) % size) for i in range(size)])  55.7 us
    ppermute x10, starting transfers between devices, ring(): lax.ppermute(x, 'tensor', [(i, (i + step) % size) for i in range(size)])  16.7 us
    dot_general x5, matrix products, projected(): out = jnp.dot(near, near_rows, preferred_element_type=jnp.float32)  13.7 us
    ppermute x3, starting transfers between devices, shifted(): return lax.ppermute(x, axis, pairs)  10.2 us
    dot_general x2, matrix products, split_dot(): return first + jnp.einsum(spec, low, b, preferred_element_type=jnp.float32)  6.38 us
    dot_general x5, matrix products, projected(): jnp.dot(far, rows(2), preferred_element_type=jnp.float32)  6.16 us
    dot_general x16, matrix products, body(): inters.append(jnp.dot(q_decayed[n], entering, precision=HIGH))  4.98 us
    dot_general x4, matrix products, term(): jnp.dot(gated, cols, preferred_element_type=jnp.float32)  4.05 us
  transfers between devices with their start and end apart: 13, of which 8 were waited for; matrix products, arithmetic and copies ran while one was open for 17% of the time, Pallas kernels for 0%

profile of v12, /device:TPU:2, one launch (start us, length us, event | category | flops | bytes accessed | tf_op | source)
XLA Modules:
  0.0 162.4 jit_solution(2100860802738506627)
XLA Ops:
  1.4 1.6 %collective-permute-start = (bf16[512,512]{1,0:T(8,128)(2,1)S(1)}, bf16[512,512]{1,0:T(8,128)(2,1)}, u32[]{:S(2)}, u32[]{:S(2)}) collective-permute-start(bf16[512,512]{1,0:T(8,128)(2,1)S(1)} %get-tuple-element.134), channel_id=1, source_target_pairs={{0,1},{1,2},{2,3},{3,0},{4,5},{5,6},{6,7},{7,4},{8,9},{9,10},{10,1... | collective-permute-start | bytes 1572872 | tf_op jit(solution)/shard_map/ppermute | solution.py:26
  3.1 1.7 %collective-permute-start.1 = (bf16[512,512]{1,0:T(8,128)(2,1)S(1)}, bf16[512,512]{1,0:T(8,128)(2,1)}, u32[]{:S(2)}, u32[]{:S(2)}) collective-permute-start(bf16[512,512]{1,0:T(8,128)(2,1)S(1)} %get-tuple-element.133), channel_id=1, source_target_pairs={{0,3},{1,0},{2,1},{3,2},{4,7},{5,4},{6,5},{7,6},{8,11},{9,8},{10,9... | collective-permute-start | bytes 1572872 | tf_op jit(solution)/shard_map/ppermute | solution.py:26
  12.5 4.0 %collective-permute-done = bf16[512,512]{1,0:T(8,128)(2,1)} collective-permute-done((bf16[512,512]{1,0:T(8,128)(2,1)S(1)}, bf16[512,512]{1,0:T(8,128)(2,1)}, u32[]{:S(2)}, u32[]{:S(2)}) %collective-permute-start) | collective-permute-done | bytes 524320 | tf_op jit(solution)/shard_map/ppermute | solution.py:26
  18.2 1.7 %collective-permute-start.5 = (bf16[512,512]{1,0:T(8,128)(2,1)}, bf16[512,512]{1,0:T(8,128)(2,1)S(1)}, u32[]{:S(2)}, u32[]{:S(2)}) collective-permute-start(bf16[512,512]{1,0:T(8,128)(2,1)} %collective-permute-done.1), channel_id=1, source_target_pairs={{0,3},{1,0},{2,1},{3,2},{4,7},{5,4},{6,5},{7,6},{8,11},{9,8},{10,9... | collective-permute-start | bytes 1572872 | tf_op jit(solution)/shard_map/ppermute | solution.py:26
  20.5 2.9 %collective-permute-start.2 = (bf16[512,512]{1,0:T(8,128)(2,1)S(1)}, bf16[512,512]{1,0:T(8,128)(2,1)S(1)}, u32[]{:S(2)}, u32[]{:S(2)}) collective-permute-start(bf16[512,512]{1,0:T(8,128)(2,1)S(1)} %get-tuple-element.131), channel_id=1, source_target_pairs={{0,3},{1,0},{2,1},{3,2},{4,7},{5,4},{6,5},{7,6},{8,11},{9,8},{10,9... | collective-permute-start | bytes 1572872 | tf_op jit(solution)/shard_map/ppermute | solution.py:26
  23.4 9.4 %collective-permute-done.4 = bf16[512,512]{1,0:T(8,128)(2,1)S(1)} collective-permute-done((bf16[512,512]{1,0:T(8,128)(2,1)}, bf16[512,512]{1,0:T(8,128)(2,1)S(1)}, u32[]{:S(2)}, u32[]{:S(2)}) %collective-permute-start.4) | collective-permute-done | bytes 524320 | tf_op jit(solution)/shard_map/ppermute | solution.py:26
  34.5 1.8 %fusion.100 = f32[1024,512]{1,0:T(8,128)S(1)} fusion(bf16[1024,512]{1,0:T(8,128)(2,1)S(1)} %constant_dynamic-update-slice_fusion, bf16[2048,512]{1,0:T(8,128)(2,1)} %param.27, s32[]{:T(128)S(6)} %select_n.111), kind=kOutput, calls=%fused_computation.171 | convolution fusion | flops 536870912 | bytes 3670020 | tf_op jit(solution)/shard_map/dot_general | solution.py:54
  36.3 5.8 %collective-permute-done.3 = bf16[512,512]{1,0:T(8,128)(2,1)S(1)} collective-permute-done((bf16[512,512]{1,0:T(8,128)(2,1)S(1)}, bf16[512,512]{1,0:T(8,128)(2,1)S(1)}, u32[]{:S(2)}, u32[]{:S(2)}) %collective-permute-start.3) | collective-permute-done | bytes 524320 | tf_op jit(solution)/shard_map/ppermute | solution.py:26
  42.1 2.5 %convolution_add_fusion.4 = f32[1024,16]{0,1:T(8,128)S(1)} fusion(f32[1024,16]{0,1:T(8,128)S(1)} %fusion.155, bf16[512,16]{0,1:T(8,128)(2,1)S(1)} %get-tuple-element.143, bf16[512,16]{0,1:T(8,128)(2,1)S(1)} %get-tuple-element.142, bf16[512,16]{0,1:T(8,128)(2,1)S(1)} %get-tuple-element.141, bf16[512,512]{1,0:T(8,128)(2,1)S(1)} %collective-permute-done.3, ...), kind=kOutput, calls=%fused_computation.65 | convolution fusion | flops 66224128 | bytes 3325952 | tf_op jit(solution)/shard_map/dot_general | solution.py:53
  46.5 2.2 %fusion.17 = bf16[1024,256]{1,0:T(8,128)(2,1)S(1)} fusion(f32[1024,256]{1,0:T(8,128)S(1)} %fusion.107, bf16[512,256]{1,0:T(8,128)(2,1)S(1)} %get-tuple-element.127, bf16[512,256]{1,0:T(8,128)(2,1)S(1)} %get-tuple-element.126, bf16[512,256]{1,0:T(8,128)(2,1)S(1)} %get-tuple-element.125, bf16[512,512]{1,0:T(8,128)(2,1)S(1)} %collective-permute-done.3, ...), kind=kOutput, calls=%fused_computation.31 | convolution fusion | flops 823918592 | bytes 5505024 | tf_op jit(solution)/shard_map/dot_general | solution.py:53
  48.9 2.2 %fusion.16 = f32[1024,256]{1,0:T(8,128)S(1)} fusion(f32[1024,256]{1,0:T(8,128)S(1)} %fusion.109, bf16[512,256]{1,0:T(8,128)(2,1)S(1)} %get-tuple-element.166, bf16[512,256]{1,0:T(8,128)(2,1)S(1)} %get-tuple-element.167, bf16[512,256]{1,0:T(8,128)(2,1)S(1)} %get-tuple-element.168, bf16[512,512]{1,0:T(8,128)(2,1)S(1)} %collective-permute-done.3, ...), kind=kOutput, calls=%fused_computation.30 | convolution fusion | flops 824180736 | bytes 6029312 | tf_op jit(solution)/shard_map/dot_general | solution.py:53
  51.2 3.3 %subtract_convert_fusion = (bf16[16,64,256]{2,0,1:T(8,128)(2,1)S(1)}, bf16[16,64,256]{2,0,1:T(8,128)(2,1)S(1)}, f32[16,64,256]{2,0,1:T(8,128)}, f32[16,64,256]{2...) fusion(f32[16,64]{0,1:T(8,128)S(1)} %copy.52, f32[16,64,256]{2,0,1:T(8,128)S(1)} %fusion.40, ...), kind=kLoop, calls=%fused_computation.78 | loop fusion | flops 3407872 | bytes 8441856 | tf_op jit(solution)/shard_map/convert_element_type | solution.py:19
  55.1 3.3 %add_convert_fusion.1 = bf16[1024,512]{1,0:T(8,128)(2,1)S(1)} fusion(f32[1024,512]{1,0:T(8,128)S(1)} %fusion.100, bf16[512,512]{1,0:T(8,128)(2,1)S(1)} %get-tuple-element.100, bf16[512,512]{1,0:T(8,128)(2,1)S(1)} %get-tuple-element.99, bf16[512,512]{1,0:T(8,128)(2,1)S(1)} %get-tuple-element.98, bf16[512,512]{1,0:T(8,128)(2,1)S(1)} %collective-permute-done.3, ...), kind=kOutput, calls=%fused_computation.8 | convolution fusion | flops 1632108544 | bytes 7864320 | tf_op jit(solution)/shard_map/dot_general | solution.py:53
  59.8 4.6 %convolution_add_fusion = f32[16,256,512]{2,1,0:T(8,128)} fusion(f32[16,256,512]{2,1,0:T(8,128)S(1)} %fusion.90, bf16[16,64,512]{2,1,0:T(8,128)(2,1)S(1)} %bitcast.314, bf16[16,64,256]{2,0,1:T(8,128)(2,1)S(1)} %get-tuple-element.90), kind=kOutput, calls=%fused_computation | convolution fusion | flops 270532608 | bytes 18350080 | tf_op jit(solution)/shard_map/ncd,ncv->ndv/dot_general | solution.py:21
  64.6 3.7 %multiply_add_fusion.2 = (f32[1,256,512]{2,1,0:T(8,128)S(1)}, f32[1,256,512]{2,1,0:T(8,128)S(1)}, f32[1,256,512]{2,1,0:T(8,128)S(1)}, f32[1,256,512]{2,1,0:T(8,1...) fusion(f32[16,256,512]{2,1,0:T(8,128)} %convolution_add_fusion, ...), kind=kLoop, calls=%fused_computation.157 | loop fusion | flops 3538944 | bytes 11024384 | tf_op jit(solution)/shard_map/add | solution.py:146
  68.3 1.8 %copy-done.1 = f32[16,256,512]{2,1,0:T(8,128)S(1)} copy-done((f32[16,256,512]{2,1,0:T(8,128)S(1)}, f32[16,256,512]{2,1,0:T(8,128)}, u32[]{:S(2)}) %copy-start.1) | copy-done | bytes 8388632
  71.0 2.1 %collective-permute-start.6 = (bf16[258,512]{1,0:T(8,128)(2,1)S(1)}, bf16[258,512]{1,0:T(8,128)(2,1)S(1)}, u32[]{:S(2)}, u32[]{:S(2)}) collective-permute-start(bf16[258,512]{1,0:T(8,128)(2,1)S(1)} %pad_maximum_fusion.2), channel_id=1, source_target_pairs={{0,4},{4,8},{8,12},{12,16},{16,20},{20,24},{24,28},{28,32},{32,36}... | collective-permute-start | bytes 792584 | tf_op jit(solution)/shard_map/ppermute | solution.py:14
  73.1 4.0 %collective-permute-start.7 = (bf16[258,512]{1,0:T(8,128)(2,1)S(1)}, bf16[258,512]{1,0:T(8,128)(2,1)S(1)}, u32[]{:S(2)}, u32[]{:S(2)}) collective-permute-start(bf16[258,512]{1,0:T(8,128)(2,1)S(1)} %pad_maximum_fusion.2), channel_id=1, source_target_pairs={{0,8},{4,12},{8,16},{12,20},{16,24},{20,28},{24,32},{28,36},{32,40... | collective-permute-start | bytes 792584 | tf_op jit(solution)/shard_map/ppermute | solution.py:14
  78.3 1.7 %convolution_select_fusion = f32[16,64,64]{2,1,0:T(8,128)S(1)} fusion(f32[16,64,256]{2,0,1:T(8,128)S(1)} %copy-done.12, f32[16,64,256]{2,0,1:T(8,128)S(1)} %copy-done.13, s32[16,64]{1,0:T(8,128)S(1)} %eq.84, pred[64,64]{1,0:T(8,128)(4,1)S(1)} %iota_compare_fusion), kind=kOutput, calls=%fused_computation.32 | convolution fusion | flops 100859904 | bytes 2367488 | tf_op jit(solution)/shard_map/ncd,nsd->ncs/dot_general | solution.py:131
  85.3 1.8 %multiply_add_fusion.1 = f32[16,64,512]{2,1,0:T(8,128)} fusion(f32[16,64,512]{2,1,0:T(8,128)S(1)} %fusion.18, f32[16,64,512]{2,1,0:T(8,128)S(1)} %fusion.113, bf16[16,64,512]{2,1,0:T(8,128)(2,1)S(1)} %bitcast.316, f32[16,64]{1,0:T(8,128)S(1)} %compare_convert_fusion.1, f32[16,64,64]{2,1,0:T(8,128)S(1)} %convolution_select_fusion), kind=kOutput, calls=%fused_computation.7 | convolution fusion | flops 68943872 | bytes 7606272 | tf_op jit(solution)/shard_map/ncs,nsv->ncv/dot_general | solution.py:21
  92.7 4.1 %collective-permute-start.8 = (bf16[258,512]{1,0:T(8,128)(2,1)}, bf16[258,512]{1,0:T(8,128)(2,1)S(1)}, u32[]{:S(2)}, u32[]{:S(2)}) collective-permute-start(bf16[258,512]{1,0:T(8,128)(2,1)} %pad_maximum_fusion.3), channel_id=1, source_target_pairs={{0,8},{4,12},{8,16},{12,20},{16,24},{20,28},{24,32},{28,36},{32,40... | collective-permute-start | bytes 792584 | tf_op jit(solution)/shard_map/ppermute | solution.py:14
  96.8 3.1 %fusion.96 = f32[1024,512]{0,1:T(8,128)} fusion(bf16[1024,512]{1,0:T(8,128)(2,1)S(1)} %constant_dynamic-update-slice_fusion, bf16[2048,512]{1,0:T(8,128)(2,1)} %param.28, s32[]{:T(128)S(6)} %select_n.111), kind=kOutput, calls=%fused_computation.152 | convolution fusion | flops 536870912 | bytes 3670020 | tf_op jit(solution)/shard_map/dot_general | solution.py:54
  100.0 3.0 %copy.58 = f32[1024,512]{0,1:T(8,128)} copy(f32[1024,512]{1,0:T(8,128)} %bitcast.317) | data formatting | bytes 4194304 | tf_op jit(solution)/shard_map/reshape | solution.py:149
  103.7 1.8 %collective-permute-done.8 = bf16[258,512]{1,0:T(8,128)(2,1)S(1)} collective-permute-done((bf16[258,512]{1,0:T(8,128)(2,1)}, bf16[258,512]{1,0:T(8,128)(2,1)S(1)}, u32[]{:S(2)}, u32[]{:S(2)}) %collective-permute-start.8) | collective-permute-done | bytes 264224 | tf_op jit(solution)/shard_map/ppermute | solution.py:14
  107.5 3.8 %multiply_reduce_fusion = (f32[1024]{0:T(1024)S(1)}, f32[1024,512]{0,1:T(8,128)S(1)}) fusion(f32[1024,512]{0,1:T(8,128)} %copy.58, f32[1024]{0:T(1024)S(1)} %select_bitcast_fusion, f32[258,512]{1,0:T(8,128)S(1)} %convert_element_type.152, f32[256]{0:T(256)S(1)} %bitcast.363, f32[258,512]{1,0:T(8,128)S(1)} %copy-done.7, f32[256]{0:T(256)S(1)} %bitcast.361, ...), kind=kOutput, calls=%fused_computation.5 | convolution fusion | flops 808713216 | bytes 7874560 | tf_op jit(solution)/shard_map/dot_general | solution.py:181
  111.5 3.4 %multiply_convert_fusion = bf16[1024,512]{0,1:T(8,128)(2,1)S(1)} fusion(f32[1024,512]{0,1:T(8,128)S(1)} %copy-done.16, f32[1024,512]{0,1:T(8,128)S(1)} %get-tuple-element.165, bf16[512,512]{1,0:T(8,128)(2,1)S(1)} %copy-done.21, bf16[512,512]{1,0:T(8,128)(2,1)S(1)} %copy-done.20, bf16[512,512]{1,0:T(8,128)(2,1)S(1)} %copy-done.19, f32[512]{0:T(512)S(1)} %copy-done.29, ...), kind=kOutput, calls=%fused_computation.4 | convolution fusion | flops 1635778560 | bytes 9967616 | tf_op jit(solution)/shard_map/dot_general | solution.py:53
  115.7 2.9 %collective-permute-start.11 = (bf16[512,512]{1,0:T(8,128)(2,1)S(1)}, bf16[512,512]{1,0:T(8,128)(2,1)S(1)}, u32[]{:S(2)}, u32[]{:S(2)}) collective-permute-start(bf16[512,512]{1,0:T(8,128)(2,1)S(1)} %get-tuple-element.102), channel_id=1, source_target_pairs={{0,3},{1,0},{2,1},{3,2},{4,7},{5,4},{6,5},{7,6},{8,11},{9,8},{10,9... | collective-permute-start | bytes 1572872 | tf_op jit(solution)/shard_map/ppermute | solution.py:26
  120.2 10.4 %collective-permute-done.11 = bf16[512,512]{1,0:T(8,128)(2,1)S(1)} collective-permute-done((bf16[512,512]{1,0:T(8,128)(2,1)S(1)}, bf16[512,512]{1,0:T(8,128)(2,1)S(1)}, u32[]{:S(2)}, u32[]{:S(2)}) %collective-permute-start.11) | collective-permute-done | bytes 524320 | tf_op jit(solution)/shard_map/ppermute | solution.py:26
  130.8 3.8 %collective-permute-start.12 = (bf16[1024,512]{1,0:T(8,128)(2,1)S(1)}, bf16[1024,512]{1,0:T(8,128)(2,1)S(1)}, u32[]{:S(2)}, u32[]{:S(2)}) collective-permute-start(bf16[1024,512]{1,0:T(8,128)(2,1)S(1)} %pad_maximum_fusion.1), channel_id=1, source_target_pairs={{0,3},{1,0},{2,1},{3,2},{4,7},{5,4},{6,5},{7,6},{8,11},{9,8},{10,9... | collective-permute-start | bytes 3145736 | tf_op jit(solution)/shard_map/ppermute | solution.py:26
  134.9 22.0 %collective-permute-done.12 = bf16[1024,512]{1,0:T(8,128)(2,1)S(1)} collective-permute-done((bf16[1024,512]{1,0:T(8,128)(2,1)S(1)}, bf16[1024,512]{1,0:T(8,128)(2,1)S(1)}, u32[]{:S(2)}, u32[]{:S(2)}) %collective-permute-start.12) | collective-permute-done | bytes 1048608 | tf_op jit(solution)/shard_map/ppermute | solution.py:26
  156.9 3.7 %collective-permute-done.10 = bf16[1024,512]{1,0:T(8,128)(2,1)S(1)} collective-permute-done((bf16[1024,512]{1,0:T(8,128)(2,1)S(1)}, bf16[1024,512]{1,0:T(8,128)(2,1)S(1)}, u32[]{:S(2)}, u32[]{:S(2)}) %collective-permute-start.10) | collective-permute-done | bytes 1048608 | tf_op jit(solution)/shard_map/ppermute | solution.py:26
  160.6 1.8 %add_convert_fusion = bf16[1024,512]{1,0:T(8,128)(2,1)} fusion(bf16[1024,512]{1,0:T(8,128)(2,1)S(1)} %collective-permute-done.12, bf16[1024,512]{1,0:T(8,128)(2,1)S(1)} %collective-permute-done.10, bf16[1024,512]{0,1:T(8,128)(2,1)S(1)} %multiply_convert_fusion, bf16[512,2048]{1,0:T(8,128)(2,1)S(1)} %copy-done, s32[]{:T(128)S(6)} %select_n.105), kind=kOutput, calls=%fused_computation.3 | convolution fusion | flops 540540928 | bytes 4718596 | tf_op jit(solution)/shard_map/dot_general | solution.py:67
  (159 shorter events, 30.7 us)
Async XLA Ops:
  0.0 114.9 %copy-start = (bf16[512,2048]{1,0:T(8,128)(2,1)S(1)}, bf16[512,2048]{1,0:T(8,128)(2,1)}, u32[]{:S(2)}) copy-start(bf16[512,2048]{1,0:T(8,128)(2,1)} %param.33) | copy-start | bytes 6291460
  0.0 4.7 %copy-start.23 = (s32[1024]{0:T(1024)S(1)}, s32[1024]{0:T(1024)}, u32[]{:S(2)}) copy-start(s32[1024]{0:T(1024)} %param.24) | copy-start | bytes 12292
  0.0 9.5 %copy-start.22 = (bf16[2048,16]{0,1:T(8,128)(2,1)S(1)}, bf16[2048,16]{0,1:T(8,128)(2,1)}, u32[]{:S(2)}) copy-start(bf16[2048,16]{0,1:T(8,128)(2,1)} %param.29) | copy-start | bytes 196612
  1.4 15.1 %collective-permute-start = (bf16[512,512]{1,0:T(8,128)(2,1)S(1)}, bf16[512,512]{1,0:T(8,128)(2,1)}, u32[]{:S(2)}, u32[]{:S(2)}) collective-permute-start(bf16[512,512]{1,0:T(8,128)(2,1)S(1)} %get-tuple-element.134), channel_id=1, source_target_pairs={{0,1},{1,2},{2,3},{3,0},{4,5},{5,6},{6,7},{7,4},{8,9},{9,10},{10,1... | collective-permute-start | bytes 1572872 | tf_op jit(solution)/shard_map/ppermute | solution.py:26
  3.1 13.5 %collective-permute-start.1 = (bf16[512,512]{1,0:T(8,128)(2,1)S(1)}, bf16[512,512]{1,0:T(8,128)(2,1)}, u32[]{:S(2)}, u32[]{:S(2)}) collective-permute-start(bf16[512,512]{1,0:T(8,128)(2,1)S(1)} %get-tuple-element.133), channel_id=1, source_target_pairs={{0,3},{1,0},{2,1},{3,2},{4,7},{5,4},{6,5},{7,6},{8,11},{9,8},{10,9... | collective-permute-start | bytes 1572872 | tf_op jit(solution)/shard_map/ppermute | solution.py:26
  11.4 8.5 %copy-start.17 = (bf16[2048,256]{1,0:T(8,128)(2,1)S(1)}, bf16[2048,256]{1,0:T(8,128)(2,1)}, u32[]{:S(2)}) copy-start(bf16[2048,256]{1,0:T(8,128)(2,1)} %param.26) | copy-start | bytes 3145732
  11.4 8.5 %copy-start.18 = (bf16[2048,256]{1,0:T(8,128)(2,1)S(1)}, bf16[2048,256]{1,0:T(8,128)(2,1)}, u32[]{:S(2)}) copy-start(bf16[2048,256]{1,0:T(8,128)(2,1)} %param.25) | copy-start | bytes 3145732
  12.5 7.5 %copy-start.9 = (bf16[1024,512]{1,0:T(8,128)(2,1)S(1)}, bf16[1024,512]{1,0:T(8,128)(2,1)}, u32[]{:S(2)}) copy-start(bf16[1024,512]{1,0:T(8,128)(2,1)} %param.23) | copy-start | bytes 3145732
  16.6 16.2 %collective-permute-start.4 = (bf16[512,512]{1,0:T(8,128)(2,1)}, bf16[512,512]{1,0:T(8,128)(2,1)S(1)}, u32[]{:S(2)}, u32[]{:S(2)}) collective-permute-start(bf16[512,512]{1,0:T(8,128)(2,1)} %collective-permute-done), channel_id=1, source_target_pairs={{0,1},{1,2},{2,3},{3,0},{4,5},{5,6},{6,7},{7,4},{8,9},{9,10},{10,1... | collective-permute-start | bytes 1572872 | tf_op jit(solution)/shard_map/ppermute | solution.py:26
  18.2 15.1 %collective-permute-start.5 = (bf16[512,512]{1,0:T(8,128)(2,1)}, bf16[512,512]{1,0:T(8,128)(2,1)S(1)}, u32[]{:S(2)}, u32[]{:S(2)}) collective-permute-start(bf16[512,512]{1,0:T(8,128)(2,1)} %collective-permute-done.1), channel_id=1, source_target_pairs={{0,3},{1,0},{2,1},{3,2},{4,7},{5,4},{6,5},{7,6},{8,11},{9,8},{10,9... | collective-permute-start | bytes 1572872 | tf_op jit(solution)/shard_map/ppermute | solution.py:26
  20.1 22.0 %collective-permute-start.3 = (bf16[512,512]{1,0:T(8,128)(2,1)S(1)}, bf16[512,512]{1,0:T(8,128)(2,1)S(1)}, u32[]{:S(2)}, u32[]{:S(2)}) collective-permute-start(bf16[512,512]{1,0:T(8,128)(2,1)S(1)} %get-tuple-element.132), channel_id=1, source_target_pairs={{0,1},{1,2},{2,3},{3,0},{4,5},{5,6},{6,7},{7,4},{8,9},{9,10},{10,1... | collective-permute-start | bytes 1572872 | tf_op jit(solution)/shard_map/ppermute | solution.py:26
  20.5 21.5 %collective-permute-start.2 = (bf16[512,512]{1,0:T(8,128)(2,1)S(1)}, bf16[512,512]{1,0:T(8,128)(2,1)S(1)}, u32[]{:S(2)}, u32[]{:S(2)}) collective-permute-start(bf16[512,512]{1,0:T(8,128)(2,1)S(1)} %get-tuple-element.131), channel_id=1, source_target_pairs={{0,3},{1,0},{2,1},{3,2},{4,7},{5,4},{6,5},{7,6},{8,11},{9,8},{10,9... | collective-permute-start | bytes 1572872 | tf_op jit(solution)/shard_map/ppermute | solution.py:26
  42.1 13.0 %copy-start.24 = (bf16[512,512]{1,0:T(8,128)(2,1)}, bf16[512,512]{1,0:T(8,128)(2,1)S(1)}, u32[]{:S(2)}) copy-start(bf16[512,512]{1,0:T(8,128)(2,1)S(1)} %collective-permute-done.3) | copy-start | bytes 1572868
  42.1 13.0 %copy-start.26 = (bf16[512,512]{1,0:T(8,128)(2,1)}, bf16[512,512]{1,0:T(8,128)(2,1)S(1)}, u32[]{:S(2)}) copy-start(bf16[512,512]{1,0:T(8,128)(2,1)S(1)} %collective-permute-done.2) | copy-start | bytes 1572868
  55.1 9.3 %copy-start.8 = (f32[16,64,256]{2,1,0:T(8,128)}, f32[16,64,256]{2,1,0:T(8,128)S(1)}, u32[]{:S(2)}) copy-start(f32[16,64,256]{2,1,0:T(8,128)S(1)} %copy.57) | copy-start | bytes 3145732
  64.6 5.6 %copy-start.1 = (f32[16,256,512]{2,1,0:T(8,128)S(1)}, f32[16,256,512]{2,1,0:T(8,128)}, u32[]{:S(2)}) copy-start(f32[16,256,512]{2,1,0:T(8,128)} %convolution_add_fusion) | copy-start | bytes 25165828
  70.1 7.0 %copy-start.14 = (f32[16,64,256]{2,0,1:T(8,128)S(1)}, f32[16,64,256]{2,0,1:T(8,128)}, u32[]{:S(2)}) copy-start(f32[16,64,256]{2,0,1:T(8,128)} %get-tuple-element.104) | copy-start | bytes 3145732
  71.0 7.3 %copy-start.12 = (f32[16,64,256]{2,0,1:T(8,128)S(1)}, f32[16,64,256]{2,0,1:T(8,128)}, u32[]{:S(2)}) copy-start(f32[16,64,256]{2,0,1:T(8,128)} %get-tuple-element.97) | copy-start | bytes 3145732
  71.0 7.3 %copy-start.13 = (f32[16,64,256]{2,0,1:T(8,128)S(1)}, f32[16,64,256]{2,0,1:T(8,128)}, u32[]{:S(2)}) copy-start(f32[16,64,256]{2,0,1:T(8,128)} %get-tuple-element.105) | copy-start | bytes 3145732
  71.0 16.1 %collective-permute-start.6 = (bf16[258,512]{1,0:T(8,128)(2,1)S(1)}, bf16[258,512]{1,0:T(8,128)(2,1)S(1)}, u32[]{:S(2)}, u32[]{:S(2)}) collective-permute-start(bf16[258,512]{1,0:T(8,128)(2,1)S(1)} %pad_maximum_fusion.2), channel_id=1, source_target_pairs={{0,4},{4,8},{8,12},{12,16},{16,20},{20,24},{24,28},{28,32},{32,36}... | collective-permute-start | bytes 792584 | tf_op jit(solution)/shard_map/ppermute | solution.py:14
  73.1 14.7 %collective-permute-start.7 = (bf16[258,512]{1,0:T(8,128)(2,1)S(1)}, bf16[258,512]{1,0:T(8,128)(2,1)S(1)}, u32[]{:S(2)}, u32[]{:S(2)}) collective-permute-start(bf16[258,512]{1,0:T(8,128)(2,1)S(1)} %pad_maximum_fusion.2), channel_id=1, source_target_pairs={{0,8},{4,12},{8,16},{12,20},{16,24},{20,28},{24,32},{28,36},{32,40... | collective-permute-start | bytes 792584 | tf_op jit(solution)/shard_map/ppermute | solution.py:14
  92.7 12.8 %collective-permute-start.8 = (bf16[258,512]{1,0:T(8,128)(2,1)}, bf16[258,512]{1,0:T(8,128)(2,1)S(1)}, u32[]{:S(2)}, u32[]{:S(2)}) collective-permute-start(bf16[258,512]{1,0:T(8,128)(2,1)} %pad_maximum_fusion.3), channel_id=1, source_target_pairs={{0,8},{4,12},{8,16},{12,20},{16,24},{20,28},{24,32},{28,36},{32,40... | collective-permute-start | bytes 792584 | tf_op jit(solution)/shard_map/ppermute | solution.py:14
  100.0 7.4 %copy-start.5 = (f32[258,512]{1,0:T(8,128)S(1)}, f32[258,512]{1,0:T(8,128)}, u32[]{:S(2)}) copy-start(f32[258,512]{1,0:T(8,128)} %copy-done.4) | copy-start | bytes 1585156
  100.0 7.4 %copy-start.7 = (f32[258,512]{1,0:T(8,128)S(1)}, f32[258,512]{1,0:T(8,128)}, u32[]{:S(2)}) copy-start(f32[258,512]{1,0:T(8,128)} %copy-done.6) | copy-start | bytes 1585156
  107.4 4.0 %copy-start.10 = (bf16[1024,512]{1,0:T(8,128)(2,1)S(1)}, bf16[1024,512]{1,0:T(8,128)(2,1)}, u32[]{:S(2)}) copy-start(bf16[1024,512]{1,0:T(8,128)(2,1)} %param.23) | copy-start | bytes 3145732
  107.4 4.0 %copy-start.16 = (f32[1024,512]{0,1:T(8,128)S(1)}, f32[1024,512]{0,1:T(8,128)}, u32[]{:S(2)}) copy-start(f32[1024,512]{0,1:T(8,128)} %fusion.96) | copy-start | bytes 6291460
  107.4 4.0 %copy-start.19 = (bf16[512,512]{1,0:T(8,128)(2,1)S(1)}, bf16[512,512]{1,0:T(8,128)(2,1)}, u32[]{:S(2)}) copy-start(bf16[512,512]{1,0:T(8,128)(2,1)} %get-tuple-element.92) | copy-start | bytes 1572868
  107.5 4.0 %copy-start.20 = (bf16[512,512]{1,0:T(8,128)(2,1)S(1)}, bf16[512,512]{1,0:T(8,128)(2,1)}, u32[]{:S(2)}) copy-start(bf16[512,512]{1,0:T(8,128)(2,1)} %get-tuple-element.93) | copy-start | bytes 1572868
  115.7 14.9 %collective-permute-start.11 = (bf16[512,512]{1,0:T(8,128)(2,1)S(1)}, bf16[512,512]{1,0:T(8,128)(2,1)S(1)}, u32[]{:S(2)}, u32[]{:S(2)}) collective-permute-start(bf16[512,512]{1,0:T(8,128)(2,1)S(1)} %get-tuple-element.102), channel_id=1, source_target_pairs={{0,3},{1,0},{2,1},{3,2},{4,7},{5,4},{6,5},{7,6},{8,11},{9,8},{10,9... | collective-permute-start | bytes 1572872 | tf_op jit(solution)/shard_map/ppermute | solution.py:26
  118.6 15.9 %collective-permute-start.9 = (bf16[512,512]{1,0:T(8,128)(2,1)S(1)}, bf16[512,512]{1,0:T(8,128)(2,1)S(1)}, u32[]{:S(2)}, u32[]{:S(2)}) collective-permute-start(bf16[512,512]{1,0:T(8,128)(2,1)S(1)} %get-tuple-element.101), channel_id=1, source_target_pairs={{0,1},{1,2},{2,3},{3,0},{4,5},{5,6},{6,7},{7,4},{8,9},{9,10},{10,1... | collective-permute-start | bytes 1572872 | tf_op jit(solution)/shard_map/ppermute | solution.py:26
  130.8 26.1 %collective-permute-start.12 = (bf16[1024,512]{1,0:T(8,128)(2,1)S(1)}, bf16[1024,512]{1,0:T(8,128)(2,1)S(1)}, u32[]{:S(2)}, u32[]{:S(2)}) collective-permute-start(bf16[1024,512]{1,0:T(8,128)(2,1)S(1)} %pad_maximum_fusion.1), channel_id=1, source_target_pairs={{0,3},{1,0},{2,1},{3,2},{4,7},{5,4},{6,5},{7,6},{8,11},{9,8},{10,9... | collective-permute-start | bytes 3145736 | tf_op jit(solution)/shard_map/ppermute | solution.py:26
  134.8 25.8 %collective-permute-start.10 = (bf16[1024,512]{1,0:T(8,128)(2,1)S(1)}, bf16[1024,512]{1,0:T(8,128)(2,1)S(1)}, u32[]{:S(2)}, u32[]{:S(2)}) collective-permute-start(bf16[1024,512]{1,0:T(8,128)(2,1)S(1)} %pad_maximum_fusion), channel_id=1, source_target_pairs={{0,1},{1,2},{2,3},{3,0},{4,5},{5,6},{6,7},{7,4},{8,9},{9,10},{10,1... | collective-permute-start | bytes 3145736 | tf_op jit(solution)/shard_map/ppermute | solution.py:26
  (12 other events, 32.2 us)

commit v13 on v11

--- a/solution.py
+++ b/solution.py
@@ -135,7 +135,13 @@
     entering = jnp.zeros((key_width, value_width), jnp.float32)
     inters = []
     for n in range(blocks):
-        inters.append(jnp.dot(q_decayed[n], entering, precision=HIGH))
+        inters.append(
+            jnp.dot(
+                q_decayed[n].astype(jnp.bfloat16),
+                entering.astype(jnp.bfloat16),
+                preferred_element_type=jnp.float32,
+            )
+        )
         entering = chunk_decay[n][:, None] * entering + chunk_states[n]
     final_state = entering
     inter = jnp.stack(inters) * live_blocks[:, :, None]

time: 163 us -> 162 us (level)
  matrix products: 43.6 us -> 41.9 us
    dot_general x16, matrix products: 4.97 us -> 3.34 us  [body(): jnp.dot(q_decayed[n].astype(jnp.bfloat16), entering.astype(jnp.bfloat16),...]
  transfers between devices with their start and end apart: 13 -> 13, of which waited for: 8 -> 8; matrix products, arithmetic and copies ran while one was open for 17% -> 16% of each run, Pallas kernels for 0% -> 0%
where the time goes in v13:
time: 162 us; the launch traced here: 161 us
  waiting for transfers between devices  57.8 us (36%)
  matrix products  41.9 us (26%)
  starting transfers between devices  26.5 us (16%)
  local copies, waits for them, and re-layouts  18.3 us (11%)
  other arithmetic  10.9 us (7%)
  between operations  5.84 us (4%)
    ppermute x10, waiting for transfers between devices, ring(): lax.ppermute(x, 'tensor', [(i, (i + step) % size) for i in range(size)])  55.7 us
    ppermute x10, starting transfers between devices, ring(): lax.ppermute(x, 'tensor', [(i, (i + step) % size) for i in range(size)])  16.7 us
    dot_general x5, matrix products, projected(): out = jnp.dot(near, near_rows, preferred_element_type=jnp.float32)  13.7 us
    ppermute x3, starting transfers between devices, shifted(): return lax.ppermute(x, axis, pairs)  9.78 us
    dot_general x5, matrix products, projected(): jnp.dot(far, rows(2), preferred_element_type=jnp.float32)  6.16 us
    dot_general x1, matrix products, body(): jnp.einsum('ncd,ncv->ndv', k_decayed, v_float, precision=HIGH)  5.75 us
    dot_general x4, matrix products, term(): jnp.dot(gated, cols, preferred_element_type=jnp.float32)  4.05 us
    dot_general x1, matrix products, body(): jnp.dot(query.astype(jnp.float32) * jnp.exp(device_cumul), state_in, prec...  3.84 us
  transfers between devices with their start and end apart: 13, of which 8 were waited for; matrix products, arithmetic and copies ran while one was open for 16% of the time, Pallas kernels for 0%

profile of v13, /device:TPU:2, one launch (start us, length us, event | category | flops | bytes accessed | tf_op | source)
XLA Modules:
  0.0 161.2 jit_solution(246913387079070791)
XLA Ops:
  1.4 1.6 %collective-permute-start = (bf16[512,512]{1,0:T(8,128)(2,1)S(1)}, bf16[512,512]{1,0:T(8,128)(2,1)}, u32[]{:S(2)}, u32[]{:S(2)}) collective-permute-start(bf16[512,512]{1,0:T(8,128)(2,1)S(1)} %get-tuple-element.117), channel_id=1, source_target_pairs={{0,1},{1,2},{2,3},{3,0},{4,5},{5,6},{6,7},{7,4},{8,9},{9,10},{10,1... | collective-permute-start | bytes 1572872 | tf_op jit(solution)/shard_map/ppermute | solution.py:19
  3.1 1.7 %collective-permute-start.1 = (bf16[512,512]{1,0:T(8,128)(2,1)S(1)}, bf16[512,512]{1,0:T(8,128)(2,1)}, u32[]{:S(2)}, u32[]{:S(2)}) collective-permute-start(bf16[512,512]{1,0:T(8,128)(2,1)S(1)} %get-tuple-element.116), channel_id=1, source_target_pairs={{0,3},{1,0},{2,1},{3,2},{4,7},{5,4},{6,5},{7,6},{8,11},{9,8},{10,9... | collective-permute-start | bytes 1572872 | tf_op jit(solution)/shard_map/ppermute | solution.py:19
  12.5 4.0 %collective-permute-done = bf16[512,512]{1,0:T(8,128)(2,1)} collective-permute-done((bf16[512,512]{1,0:T(8,128)(2,1)S(1)}, bf16[512,512]{1,0:T(8,128)(2,1)}, u32[]{:S(2)}, u32[]{:S(2)}) %collective-permute-start) | collective-permute-done | bytes 524320 | tf_op jit(solution)/shard_map/ppermute | solution.py:19
  18.2 1.7 %collective-permute-start.5 = (bf16[512,512]{1,0:T(8,128)(2,1)}, bf16[512,512]{1,0:T(8,128)(2,1)S(1)}, u32[]{:S(2)}, u32[]{:S(2)}) collective-permute-start(bf16[512,512]{1,0:T(8,128)(2,1)} %collective-permute-done.1), channel_id=1, source_target_pairs={{0,3},{1,0},{2,1},{3,2},{4,7},{5,4},{6,5},{7,6},{8,11},{9,8},{10,9... | collective-permute-start | bytes 1572872 | tf_op jit(solution)/shard_map/ppermute | solution.py:19
  20.5 2.9 %collective-permute-start.2 = (bf16[512,512]{1,0:T(8,128)(2,1)S(1)}, bf16[512,512]{1,0:T(8,128)(2,1)S(1)}, u32[]{:S(2)}, u32[]{:S(2)}) collective-permute-start(bf16[512,512]{1,0:T(8,128)(2,1)S(1)} %get-tuple-element.114), channel_id=1, source_target_pairs={{0,3},{1,0},{2,1},{3,2},{4,7},{5,4},{6,5},{7,6},{8,11},{9,8},{10,9... | collective-permute-start | bytes 1572872 | tf_op jit(solution)/shard_map/ppermute | solution.py:19
  23.4 9.4 %collective-permute-done.4 = bf16[512,512]{1,0:T(8,128)(2,1)S(1)} collective-permute-done((bf16[512,512]{1,0:T(8,128)(2,1)}, bf16[512,512]{1,0:T(8,128)(2,1)S(1)}, u32[]{:S(2)}, u32[]{:S(2)}) %collective-permute-start.4) | collective-permute-done | bytes 524320 | tf_op jit(solution)/shard_map/ppermute | solution.py:19
  34.5 1.8 %fusion.82 = f32[1024,512]{1,0:T(8,128)S(1)} fusion(bf16[1024,512]{1,0:T(8,128)(2,1)S(1)} %constant_dynamic-update-slice_fusion, bf16[2048,512]{1,0:T(8,128)(2,1)} %param.27, s32[]{:T(128)S(6)} %select_n.111), kind=kOutput, calls=%fused_computation.151 | convolution fusion | flops 536870912 | bytes 3670020 | tf_op jit(solution)/shard_map/dot_general | solution.py:47
  36.3 5.8 %collective-permute-done.3 = bf16[512,512]{1,0:T(8,128)(2,1)S(1)} collective-permute-done((bf16[512,512]{1,0:T(8,128)(2,1)S(1)}, bf16[512,512]{1,0:T(8,128)(2,1)S(1)}, u32[]{:S(2)}, u32[]{:S(2)}) %collective-permute-start.3) | collective-permute-done | bytes 524320 | tf_op jit(solution)/shard_map/ppermute | solution.py:19
  42.1 2.5 %convolution_add_fusion.3 = f32[1024,16]{0,1:T(8,128)S(1)} fusion(f32[1024,16]{0,1:T(8,128)S(1)} %fusion.161, bf16[512,16]{0,1:T(8,128)(2,1)S(1)} %get-tuple-element.142, bf16[512,16]{0,1:T(8,128)(2,1)S(1)} %get-tuple-element.141, bf16[512,16]{0,1:T(8,128)(2,1)S(1)} %get-tuple-element.140, bf16[512,512]{1,0:T(8,128)(2,1)S(1)} %collective-permute-done.3, ...), kind=kOutput, calls=%fused_computation.64 | convolution fusion | flops 66224128 | bytes 3325952 | tf_op jit(solution)/shard_map/dot_general | solution.py:46
  46.5 2.2 %fusion.17 = bf16[1024,256]{1,0:T(8,128)(2,1)S(1)} fusion(f32[1024,256]{1,0:T(8,128)S(1)} %fusion.118, bf16[512,256]{1,0:T(8,128)(2,1)S(1)} %get-tuple-element.110, bf16[512,256]{1,0:T(8,128)(2,1)S(1)} %get-tuple-element.109, bf16[512,256]{1,0:T(8,128)(2,1)S(1)} %get-tuple-element.108, bf16[512,512]{1,0:T(8,128)(2,1)S(1)} %collective-permute-done.3, ...), kind=kOutput, calls=%fused_computation.30 | convolution fusion | flops 823918592 | bytes 5505024 | tf_op jit(solution)/shard_map/dot_general | solution.py:46
  48.9 2.2 %fusion.16 = f32[1024,256]{1,0:T(8,128)S(1)} fusion(f32[1024,256]{1,0:T(8,128)S(1)} %fusion.120, bf16[512,256]{1,0:T(8,128)(2,1)S(1)} %get-tuple-element.165, bf16[512,256]{1,0:T(8,128)(2,1)S(1)} %get-tuple-element.166, bf16[512,256]{1,0:T(8,128)(2,1)S(1)} %get-tuple-element.167, bf16[512,512]{1,0:T(8,128)(2,1)S(1)} %collective-permute-done.3, ...), kind=kOutput, calls=%fused_computation.29 | convolution fusion | flops 824180736 | bytes 6029312 | tf_op jit(solution)/shard_map/dot_general | solution.py:46
  51.2 3.1 %exponential_multiply_fusion.1 = (f32[16,64,256]{2,0,1:T(8,128)}, bf16[16,64,256]{2,0,1:T(8,128)(2,1)}, f32[16,64,256]{2,0,1:T(8,128)S(1)}, f32[16,64,256]{2,0,1:T(8,128)}, f32[16,64,256]{2,0,1:T(8,128)S(1)}) fusion(f32[16,64,256]{2,0,1:T(8,128)S(1)} %fusion.42, f32[16,64,256]{2,1,0:T(8,128)S(1)} %bitcast.315, f32[16,256]{1,0:T(8,128)S(1)} %get-tuple-element.107, ...), kind=kLoop, calls=%fused_computation.82 | loop fusion | flops 2621440 | bytes 7917568 | tf_op jit(solution)/shard_map/mul | solution.py:122
  54.9 3.3 %add_convert_fusion.1 = bf16[1024,512]{1,0:T(8,128)(2,1)S(1)} fusion(f32[1024,512]{1,0:T(8,128)S(1)} %fusion.82, bf16[512,512]{1,0:T(8,128)(2,1)S(1)} %get-tuple-element.99, bf16[512,512]{1,0:T(8,128)(2,1)S(1)} %get-tuple-element.98, bf16[512,512]{1,0:T(8,128)(2,1)S(1)} %get-tuple-element.97, bf16[512,512]{1,0:T(8,128)(2,1)S(1)} %collective-permute-done.3, ...), kind=kOutput, calls=%fused_computation.7 | convolution fusion | flops 1632108544 | bytes 7864320 | tf_op jit(solution)/shard_map/dot_general | solution.py:46
  58.2 5.7 %fusion.38 = f32[16,256,512]{2,1,0:T(8,128)} fusion(bf16[16,64,512]{2,1,0:T(8,128)(2,1)S(1)} %bitcast.316, f32[16,64,256]{2,0,1:T(8,128)S(1)} %get-tuple-element.100), kind=kOutput, calls=%fused_computation.69 | convolution fusion | flops 805306368 | bytes 10485760 | tf_op jit(solution)/shard_map/ncd,ncv->ndv/dot_general | solution.py:131
  64.2 3.7 %multiply_add_fusion.2 = (f32[1,256,512]{2,1,0:T(8,128)S(1)}, f32[1,256,512]{2,1,0:T(8,128)S(1)}, f32[1,256,512]{2,1,0:T(8,128)S(1)}, f32[1,256,512]{2,1,0:T(8,1...) fusion(f32[16,256,512]{2,1,0:T(8,128)} %fusion.38, ...), kind=kLoop, calls=%fused_computation.138 | loop fusion | flops 3538944 | bytes 11024384 | tf_op jit(solution)/shard_map/add | solution.py:145
  67.9 1.8 %copy-done.1 = f32[16,256,512]{2,1,0:T(8,128)S(1)} copy-done((f32[16,256,512]{2,1,0:T(8,128)S(1)}, f32[16,256,512]{2,1,0:T(8,128)}, u32[]{:S(2)}) %copy-start.1) | copy-done | bytes 8388632
  70.6 1.9 %collective-permute-start.6 = (bf16[258,512]{1,0:T(8,128)(2,1)S(1)}, bf16[258,512]{1,0:T(8,128)(2,1)S(1)}, u32[]{:S(2)}, u32[]{:S(2)}) collective-permute-start(bf16[258,512]{1,0:T(8,128)(2,1)S(1)} %pad_maximum_fusion.2), channel_id=1, source_target_pairs={{0,4},{4,8},{8,12},{12,16},{16,20},{20,24},{24,28},{28,32},{32,36}... | collective-permute-start | bytes 792584 | tf_op jit(solution)/shard_map/ppermute | solution.py:14
  72.5 4.0 %collective-permute-start.7 = (bf16[258,512]{1,0:T(8,128)(2,1)S(1)}, bf16[258,512]{1,0:T(8,128)(2,1)S(1)}, u32[]{:S(2)}, u32[]{:S(2)}) collective-permute-start(bf16[258,512]{1,0:T(8,128)(2,1)S(1)} %pad_maximum_fusion.2), channel_id=1, source_target_pairs={{0,8},{4,12},{8,16},{12,20},{16,24},{20,28},{24,32},{28,36},{32,40... | collective-permute-start | bytes 792584 | tf_op jit(solution)/shard_map/ppermute | solution.py:14
  81.7 1.7 %convolution_select_fusion = f32[16,64,64]{2,1,0:T(8,128)S(1)} fusion(f32[16,64,256]{2,0,1:T(8,128)S(1)} %copy-done.10, f32[16,64,256]{2,0,1:T(8,128)S(1)} %copy-done.9, s32[16,64]{1,0:T(8,128)S(1)} %eq.84, pred[64,64]{1,0:T(8,128)(4,1)S(1)} %iota_compare_fusion), kind=kOutput, calls=%fused_computation.31 | convolution fusion | flops 100859904 | bytes 2367488 | tf_op jit(solution)/shard_map/ncd,nsd->ncs/dot_general | solution.py:124
  83.4 2.2 %multiply_add_fusion.1 = f32[16,64,512]{2,1,0:T(8,128)} fusion(f32[16,64,512]{2,1,0:T(8,128)S(1)} %fusion.18, f32[16,64,64]{2,1,0:T(8,128)S(1)} %convolution_select_fusion, bf16[16,64,512]{2,1,0:T(8,128)(2,1)S(1)} %bitcast.317, f32[16,64]{1,0:T(8,128)S(1)} %compare_convert_fusion.1), kind=kOutput, calls=%fused_computation.6 | convolution fusion | flops 202375168 | bytes 5509120 | tf_op jit(solution)/shard_map/ncs,nsv->ncv/dot_general | solution.py:127
  91.5 3.8 %collective-permute-start.8 = (bf16[258,512]{1,0:T(8,128)(2,1)}, bf16[258,512]{1,0:T(8,128)(2,1)S(1)}, u32[]{:S(2)}, u32[]{:S(2)}) collective-permute-start(bf16[258,512]{1,0:T(8,128)(2,1)} %pad_maximum_fusion.3), channel_id=1, source_target_pairs={{0,8},{4,12},{8,16},{12,20},{16,24},{20,28},{24,32},{28,36},{32,40... | collective-permute-start | bytes 792584 | tf_op jit(solution)/shard_map/ppermute | solution.py:14
  95.3 3.1 %fusion.80 = f32[1024,512]{0,1:T(8,128)} fusion(bf16[1024,512]{1,0:T(8,128)(2,1)S(1)} %constant_dynamic-update-slice_fusion, bf16[2048,512]{1,0:T(8,128)(2,1)} %param.28, s32[]{:T(128)S(6)} %select_n.111), kind=kOutput, calls=%fused_computation.134 | convolution fusion | flops 536870912 | bytes 3670020 | tf_op jit(solution)/shard_map/dot_general | solution.py:47
  98.4 3.0 %copy.51 = f32[1024,512]{0,1:T(8,128)} copy(f32[1024,512]{1,0:T(8,128)} %bitcast.312) | data formatting | bytes 4194304 | tf_op jit(solution)/shard_map/reshape | solution.py:148
  102.1 2.1 %collective-permute-done.8 = bf16[258,512]{1,0:T(8,128)(2,1)S(1)} collective-permute-done((bf16[258,512]{1,0:T(8,128)(2,1)}, bf16[258,512]{1,0:T(8,128)(2,1)S(1)}, u32[]{:S(2)}, u32[]{:S(2)}) %collective-permute-start.8) | collective-permute-done | bytes 264224 | tf_op jit(solution)/shard_map/ppermute | solution.py:14
  106.3 3.8 %multiply_reduce_fusion = (f32[1024]{0:T(1024)S(1)}, f32[1024,512]{0,1:T(8,128)S(1)}) fusion(f32[1024,512]{0,1:T(8,128)} %copy.51, f32[1024]{0:T(1024)S(1)} %select_bitcast_fusion, f32[258,512]{1,0:T(8,128)S(1)} %convert_element_type.331, f32[256]{0:T(256)S(1)} %bitcast.360, f32[258,512]{1,0:T(8,128)S(1)} %copy-done.6, f32[256]{0:T(256)S(1)} %bitcast.358, ...), kind=kOutput, calls=%fused_computation.4 | convolution fusion | flops 808713216 | bytes 7874560 | tf_op jit(solution)/shard_map/dot_general | solution.py:180
  110.2 3.4 %multiply_convert_fusion = bf16[1024,512]{0,1:T(8,128)(2,1)S(1)} fusion(f32[1024,512]{0,1:T(8,128)S(1)} %copy-done.16, f32[1024,512]{0,1:T(8,128)S(1)} %get-tuple-element.164, bf16[512,512]{1,0:T(8,128)(2,1)S(1)} %copy-done.21, bf16[512,512]{1,0:T(8,128)(2,1)S(1)} %copy-done.20, bf16[512,512]{1,0:T(8,128)(2,1)S(1)} %copy-done.19, f32[512]{0:T(512)S(1)} %copy-done.29, ...), kind=kOutput, calls=%fused_computation.3 | convolution fusion | flops 1635778560 | bytes 9967616 | tf_op jit(solution)/shard_map/dot_general | solution.py:46
  114.5 2.9 %collective-permute-start.11 = (bf16[512,512]{1,0:T(8,128)(2,1)S(1)}, bf16[512,512]{1,0:T(8,128)(2,1)S(1)}, u32[]{:S(2)}, u32[]{:S(2)}) collective-permute-start(bf16[512,512]{1,0:T(8,128)(2,1)S(1)} %get-tuple-element.103), channel_id=1, source_target_pairs={{0,3},{1,0},{2,1},{3,2},{4,7},{5,4},{6,5},{7,6},{8,11},{9,8},{10,9... | collective-permute-start | bytes 1572872 | tf_op jit(solution)/shard_map/ppermute | solution.py:19
  119.0 10.3 %collective-permute-done.11 = bf16[512,512]{1,0:T(8,128)(2,1)S(1)} collective-permute-done((bf16[512,512]{1,0:T(8,128)(2,1)S(1)}, bf16[512,512]{1,0:T(8,128)(2,1)S(1)}, u32[]{:S(2)}, u32[]{:S(2)}) %collective-permute-start.11) | collective-permute-done | bytes 524320 | tf_op jit(solution)/shard_map/ppermute | solution.py:19
  129.6 3.8 %collective-permute-start.12 = (bf16[1024,512]{1,0:T(8,128)(2,1)S(1)}, bf16[1024,512]{1,0:T(8,128)(2,1)S(1)}, u32[]{:S(2)}, u32[]{:S(2)}) collective-permute-start(bf16[1024,512]{1,0:T(8,128)(2,1)S(1)} %pad_maximum_fusion.1), channel_id=1, source_target_pairs={{0,3},{1,0},{2,1},{3,2},{4,7},{5,4},{6,5},{7,6},{8,11},{9,8},{10,9... | collective-permute-start | bytes 3145736 | tf_op jit(solution)/shard_map/ppermute | solution.py:19
  133.6 22.0 %collective-permute-done.12 = bf16[1024,512]{1,0:T(8,128)(2,1)S(1)} collective-permute-done((bf16[1024,512]{1,0:T(8,128)(2,1)S(1)}, bf16[1024,512]{1,0:T(8,128)(2,1)S(1)}, u32[]{:S(2)}, u32[]{:S(2)}) %collective-permute-start.12) | collective-permute-done | bytes 1048608 | tf_op jit(solution)/shard_map/ppermute | solution.py:19
  155.6 3.7 %collective-permute-done.10 = bf16[1024,512]{1,0:T(8,128)(2,1)S(1)} collective-permute-done((bf16[1024,512]{1,0:T(8,128)(2,1)S(1)}, bf16[1024,512]{1,0:T(8,128)(2,1)S(1)}, u32[]{:S(2)}, u32[]{:S(2)}) %collective-permute-start.10) | collective-permute-done | bytes 1048608 | tf_op jit(solution)/shard_map/ppermute | solution.py:19
  159.3 1.8 %add_convert_fusion = bf16[1024,512]{1,0:T(8,128)(2,1)} fusion(bf16[1024,512]{1,0:T(8,128)(2,1)S(1)} %collective-permute-done.12, bf16[1024,512]{1,0:T(8,128)(2,1)S(1)} %collective-permute-done.10, bf16[1024,512]{0,1:T(8,128)(2,1)S(1)} %multiply_convert_fusion, bf16[512,2048]{1,0:T(8,128)(2,1)S(1)} %copy-done, s32[]{:T(128)S(6)} %select_n.105), kind=kOutput, calls=%fused_computation.2 | convolution fusion | flops 540540928 | bytes 4718596 | tf_op jit(solution)/shard_map/dot_general | solution.py:60
  (157 shorter events, 28.0 us)
Async XLA Ops:
  0.0 113.7 %copy-start = (bf16[512,2048]{1,0:T(8,128)(2,1)S(1)}, bf16[512,2048]{1,0:T(8,128)(2,1)}, u32[]{:S(2)}) copy-start(bf16[512,2048]{1,0:T(8,128)(2,1)} %param.33) | copy-start | bytes 6291460
  0.0 4.7 %copy-start.23 = (s32[1024]{0:T(1024)S(1)}, s32[1024]{0:T(1024)}, u32[]{:S(2)}) copy-start(s32[1024]{0:T(1024)} %param.24) | copy-start | bytes 12292
  0.0 9.5 %copy-start.22 = (bf16[2048,16]{0,1:T(8,128)(2,1)S(1)}, bf16[2048,16]{0,1:T(8,128)(2,1)}, u32[]{:S(2)}) copy-start(bf16[2048,16]{0,1:T(8,128)(2,1)} %param.29) | copy-start | bytes 196612
  1.4 15.1 %collective-permute-start = (bf16[512,512]{1,0:T(8,128)(2,1)S(1)}, bf16[512,512]{1,0:T(8,128)(2,1)}, u32[]{:S(2)}, u32[]{:S(2)}) collective-permute-start(bf16[512,512]{1,0:T(8,128)(2,1)S(1)} %get-tuple-element.117), channel_id=1, source_target_pairs={{0,1},{1,2},{2,3},{3,0},{4,5},{5,6},{6,7},{7,4},{8,9},{9,10},{10,1... | collective-permute-start | bytes 1572872 | tf_op jit(solution)/shard_map/ppermute | solution.py:19
  3.1 13.5 %collective-permute-start.1 = (bf16[512,512]{1,0:T(8,128)(2,1)S(1)}, bf16[512,512]{1,0:T(8,128)(2,1)}, u32[]{:S(2)}, u32[]{:S(2)}) collective-permute-start(bf16[512,512]{1,0:T(8,128)(2,1)S(1)} %get-tuple-element.116), channel_id=1, source_target_pairs={{0,3},{1,0},{2,1},{3,2},{4,7},{5,4},{6,5},{7,6},{8,11},{9,8},{10,9... | collective-permute-start | bytes 1572872 | tf_op jit(solution)/shard_map/ppermute | solution.py:19
  11.3 8.5 %copy-start.17 = (bf16[2048,256]{1,0:T(8,128)(2,1)S(1)}, bf16[2048,256]{1,0:T(8,128)(2,1)}, u32[]{:S(2)}) copy-start(bf16[2048,256]{1,0:T(8,128)(2,1)} %param.25) | copy-start | bytes 3145732
  11.3 8.5 %copy-start.18 = (bf16[2048,256]{1,0:T(8,128)(2,1)S(1)}, bf16[2048,256]{1,0:T(8,128)(2,1)}, u32[]{:S(2)}) copy-start(bf16[2048,256]{1,0:T(8,128)(2,1)} %param.26) | copy-start | bytes 3145732
  12.5 7.5 %copy-start.11 = (bf16[1024,512]{1,0:T(8,128)(2,1)S(1)}, bf16[1024,512]{1,0:T(8,128)(2,1)}, u32[]{:S(2)}) copy-start(bf16[1024,512]{1,0:T(8,128)(2,1)} %param.23) | copy-start | bytes 3145732
  16.6 16.2 %collective-permute-start.4 = (bf16[512,512]{1,0:T(8,128)(2,1)}, bf16[512,512]{1,0:T(8,128)(2,1)S(1)}, u32[]{:S(2)}, u32[]{:S(2)}) collective-permute-start(bf16[512,512]{1,0:T(8,128)(2,1)} %collective-permute-done), channel_id=1, source_target_pairs={{0,1},{1,2},{2,3},{3,0},{4,5},{5,6},{6,7},{7,4},{8,9},{9,10},{10,1... | collective-permute-start | bytes 1572872 | tf_op jit(solution)/shard_map/ppermute | solution.py:19
  18.2 15.1 %collective-permute-start.5 = (bf16[512,512]{1,0:T(8,128)(2,1)}, bf16[512,512]{1,0:T(8,128)(2,1)S(1)}, u32[]{:S(2)}, u32[]{:S(2)}) collective-permute-start(bf16[512,512]{1,0:T(8,128)(2,1)} %collective-permute-done.1), channel_id=1, source_target_pairs={{0,3},{1,0},{2,1},{3,2},{4,7},{5,4},{6,5},{7,6},{8,11},{9,8},{10,9... | collective-permute-start | bytes 1572872 | tf_op jit(solution)/shard_map/ppermute | solution.py:19
  20.1 22.0 %collective-permute-start.3 = (bf16[512,512]{1,0:T(8,128)(2,1)S(1)}, bf16[512,512]{1,0:T(8,128)(2,1)S(1)}, u32[]{:S(2)}, u32[]{:S(2)}) collective-permute-start(bf16[512,512]{1,0:T(8,128)(2,1)S(1)} %get-tuple-element.115), channel_id=1, source_target_pairs={{0,1},{1,2},{2,3},{3,0},{4,5},{5,6},{6,7},{7,4},{8,9},{9,10},{10,1... | collective-permute-start | bytes 1572872 | tf_op jit(solution)/shard_map/ppermute | solution.py:19
  20.5 21.6 %collective-permute-start.2 = (bf16[512,512]{1,0:T(8,128)(2,1)S(1)}, bf16[512,512]{1,0:T(8,128)(2,1)S(1)}, u32[]{:S(2)}, u32[]{:S(2)}) collective-permute-start(bf16[512,512]{1,0:T(8,128)(2,1)S(1)} %get-tuple-element.114), channel_id=1, source_target_pairs={{0,3},{1,0},{2,1},{3,2},{4,7},{5,4},{6,5},{7,6},{8,11},{9,8},{10,9... | collective-permute-start | bytes 1572872 | tf_op jit(solution)/shard_map/ppermute | solution.py:19
  42.1 12.8 %copy-start.24 = (bf16[512,512]{1,0:T(8,128)(2,1)}, bf16[512,512]{1,0:T(8,128)(2,1)S(1)}, u32[]{:S(2)}) copy-start(bf16[512,512]{1,0:T(8,128)(2,1)S(1)} %collective-permute-done.3) | copy-start | bytes 1572868
  42.1 12.8 %copy-start.26 = (bf16[512,512]{1,0:T(8,128)(2,1)}, bf16[512,512]{1,0:T(8,128)(2,1)S(1)}, u32[]{:S(2)}) copy-start(bf16[512,512]{1,0:T(8,128)(2,1)S(1)} %collective-permute-done.2) | copy-start | bytes 1572868
  54.9 9.1 %copy-start.7 = (f32[16,64,256]{2,1,0:T(8,128)}, f32[16,64,256]{2,1,0:T(8,128)S(1)}, u32[]{:S(2)}) copy-start(f32[16,64,256]{2,1,0:T(8,128)S(1)} %copy.50) | copy-start | bytes 3145732
  58.2 5.8 %copy-start.13 = (bf16[1024,512]{1,0:T(8,128)(2,1)}, bf16[1024,512]{1,0:T(8,128)(2,1)S(1)}, u32[]{:S(2)}) copy-start(bf16[1024,512]{1,0:T(8,128)(2,1)S(1)} %add_convert_fusion.1) | copy-start | bytes 3145732
  64.2 5.6 %copy-start.1 = (f32[16,256,512]{2,1,0:T(8,128)S(1)}, f32[16,256,512]{2,1,0:T(8,128)}, u32[]{:S(2)}) copy-start(f32[16,256,512]{2,1,0:T(8,128)} %fusion.38) | copy-start | bytes 25165828
  69.8 6.8 %copy-start.2 = (bf16[16,64,256]{2,0,1:T(8,128)(2,1)S(1)}, bf16[16,64,256]{2,0,1:T(8,128)(2,1)}, u32[]{:S(2)}) copy-start(bf16[16,64,256]{2,0,1:T(8,128)(2,1)} %get-tuple-element.94) | copy-start | bytes 1572868
  70.6 15.1 %collective-permute-start.6 = (bf16[258,512]{1,0:T(8,128)(2,1)S(1)}, bf16[258,512]{1,0:T(8,128)(2,1)S(1)}, u32[]{:S(2)}, u32[]{:S(2)}) collective-permute-start(bf16[258,512]{1,0:T(8,128)(2,1)S(1)} %pad_maximum_fusion.2), channel_id=1, source_target_pairs={{0,4},{4,8},{8,12},{12,16},{16,20},{20,24},{24,28},{28,32},{32,36}... | collective-permute-start | bytes 792584 | tf_op jit(solution)/shard_map/ppermute | solution.py:14
  72.5 13.7 %collective-permute-start.7 = (bf16[258,512]{1,0:T(8,128)(2,1)S(1)}, bf16[258,512]{1,0:T(8,128)(2,1)S(1)}, u32[]{:S(2)}, u32[]{:S(2)}) collective-permute-start(bf16[258,512]{1,0:T(8,128)(2,1)S(1)} %pad_maximum_fusion.2), channel_id=1, source_target_pairs={{0,8},{4,12},{8,16},{12,20},{16,24},{20,28},{24,32},{28,36},{32,40... | collective-permute-start | bytes 792584 | tf_op jit(solution)/shard_map/ppermute | solution.py:14
  91.5 12.8 %collective-permute-start.8 = (bf16[258,512]{1,0:T(8,128)(2,1)}, bf16[258,512]{1,0:T(8,128)(2,1)S(1)}, u32[]{:S(2)}, u32[]{:S(2)}) collective-permute-start(bf16[258,512]{1,0:T(8,128)(2,1)} %pad_maximum_fusion.3), channel_id=1, source_target_pairs={{0,8},{4,12},{8,16},{12,20},{16,24},{20,28},{24,32},{28,36},{32,40... | collective-permute-start | bytes 792584 | tf_op jit(solution)/shard_map/ppermute | solution.py:14
  98.4 7.8 %copy-start.4 = (f32[258,512]{1,0:T(8,128)S(1)}, f32[258,512]{1,0:T(8,128)}, u32[]{:S(2)}) copy-start(f32[258,512]{1,0:T(8,128)} %copy-done.3) | copy-start | bytes 1585156
  98.4 7.8 %copy-start.6 = (f32[258,512]{1,0:T(8,128)S(1)}, f32[258,512]{1,0:T(8,128)}, u32[]{:S(2)}) copy-start(f32[258,512]{1,0:T(8,128)} %copy-done.5) | copy-start | bytes 1585156
  106.2 4.0 %copy-start.12 = (bf16[1024,512]{1,0:T(8,128)(2,1)S(1)}, bf16[1024,512]{1,0:T(8,128)(2,1)}, u32[]{:S(2)}) copy-start(bf16[1024,512]{1,0:T(8,128)(2,1)} %param.23) | copy-start | bytes 3145732
  106.2 3.9 %copy-start.16 = (f32[1024,512]{0,1:T(8,128)S(1)}, f32[1024,512]{0,1:T(8,128)}, u32[]{:S(2)}) copy-start(f32[1024,512]{0,1:T(8,128)} %fusion.80) | copy-start | bytes 6291460
  106.2 3.9 %copy-start.19 = (bf16[512,512]{1,0:T(8,128)(2,1)S(1)}, bf16[512,512]{1,0:T(8,128)(2,1)}, u32[]{:S(2)}) copy-start(bf16[512,512]{1,0:T(8,128)(2,1)} %get-tuple-element.90) | copy-start | bytes 1572868
  106.2 3.9 %copy-start.20 = (bf16[512,512]{1,0:T(8,128)(2,1)S(1)}, bf16[512,512]{1,0:T(8,128)(2,1)}, u32[]{:S(2)}) copy-start(bf16[512,512]{1,0:T(8,128)(2,1)} %get-tuple-element.91) | copy-start | bytes 1572868
  106.2 3.9 %copy-start.21 = (bf16[512,512]{1,0:T(8,128)(2,1)S(1)}, bf16[512,512]{1,0:T(8,128)(2,1)}, u32[]{:S(2)}) copy-start(bf16[512,512]{1,0:T(8,128)(2,1)} %get-tuple-element.92) | copy-start | bytes 1572868
  114.5 14.9 %collective-permute-start.11 = (bf16[512,512]{1,0:T(8,128)(2,1)S(1)}, bf16[512,512]{1,0:T(8,128)(2,1)S(1)}, u32[]{:S(2)}, u32[]{:S(2)}) collective-permute-start(bf16[512,512]{1,0:T(8,128)(2,1)S(1)} %get-tuple-element.103), channel_id=1, source_target_pairs={{0,3},{1,0},{2,1},{3,2},{4,7},{5,4},{6,5},{7,6},{8,11},{9,8},{10,9... | collective-permute-start | bytes 1572872 | tf_op jit(solution)/shard_map/ppermute | solution.py:19
  117.4 15.9 %collective-permute-start.9 = (bf16[512,512]{1,0:T(8,128)(2,1)S(1)}, bf16[512,512]{1,0:T(8,128)(2,1)S(1)}, u32[]{:S(2)}, u32[]{:S(2)}) collective-permute-start(bf16[512,512]{1,0:T(8,128)(2,1)S(1)} %get-tuple-element.102), channel_id=1, source_target_pairs={{0,1},{1,2},{2,3},{3,0},{4,5},{5,6},{6,7},{7,4},{8,9},{9,10},{10,1... | collective-permute-start | bytes 1572872 | tf_op jit(solution)/shard_map/ppermute | solution.py:19
  129.6 26.1 %collective-permute-start.12 = (bf16[1024,512]{1,0:T(8,128)(2,1)S(1)}, bf16[1024,512]{1,0:T(8,128)(2,1)S(1)}, u32[]{:S(2)}, u32[]{:S(2)}) collective-permute-start(bf16[1024,512]{1,0:T(8,128)(2,1)S(1)} %pad_maximum_fusion.1), channel_id=1, source_target_pairs={{0,3},{1,0},{2,1},{3,2},{4,7},{5,4},{6,5},{7,6},{8,11},{9,8},{10,9... | collective-permute-start | bytes 3145736 | tf_op jit(solution)/shard_map/ppermute | solution.py:19
  133.6 25.8 %collective-permute-start.10 = (bf16[1024,512]{1,0:T(8,128)(2,1)S(1)}, bf16[1024,512]{1,0:T(8,128)(2,1)S(1)}, u32[]{:S(2)}, u32[]{:S(2)}) collective-permute-start(bf16[1024,512]{1,0:T(8,128)(2,1)S(1)} %pad_maximum_fusion), channel_id=1, source_target_pairs={{0,1},{1,2},{2,3},{3,0},{4,5},{5,6},{6,7},{7,4},{8,9},{9,10},{10,1... | collective-permute-start | bytes 3145736 | tf_op jit(solution)/shard_map/ppermute | solution.py:19
  (12 other events, 29.2 us)

commit v14 on v13

--- a/solution.py
+++ b/solution.py
@@ -121,7 +121,12 @@
     centre = cumul[:, GROUP // 2, :]
     q_scaled = q_float * jnp.exp(cumul - centre[:, None, :])
     k_scaled = k_float * jnp.exp(centre[:, None, :] - cumul)
-    raw_scores = jnp.einsum("ncd,nsd->ncs", q_scaled, k_scaled, precision=HIGH)
+    raw_scores = jnp.einsum(
+        "ncd,nsd->ncs",
+        q_scaled.astype(jnp.bfloat16),
+        k_scaled.astype(jnp.bfloat16),
+        preferred_element_type=jnp.float32,
+    )
     allowed = causal[None] & (seg_blocks[:, :, None] == seg_blocks[:, None, :])
     scores = jnp.where(allowed, raw_scores, 0.0)
     intra = jnp.einsum("ncs,nsv->ncv", scores, v_float, precision=HIGH)
@@ -178,7 +183,9 @@
     state_in, _, _, last_far = joined(earlier_pair, pair)
     linked = (first_id == last_far).astype(jnp.float32)
     carried = jnp.dot(
-        query.astype(jnp.float32) * jnp.exp(device_cumul), state_in, precision=HIGH
+        (query.astype(jnp.float32) * jnp.exp(device_cumul)).astype(jnp.bfloat16),
+        state_in.astype(jnp.bfloat16),
+        preferred_element_type=jnp.float32,
     )
     attn = (local_out + carried * (live_device * linked)[:, None]) * key_width ** (-0.5)
     normed = attn * lax.rsqrt(jnp.mean(attn * attn, axis=-1, keepdims=True) + 1e-05) * norm_gain

time: 162 us -> 159 us (0.981)
  matrix products: 41.9 us -> 39.9 us
    mul x1 -> x0, other arithmetic: 3.09 us -> none  [body(): q_scaled = q_float * jnp.exp(cumul - centre[:, None, :])]
    convert_element_type x0 -> x1, other arithmetic: none -> 2.76 us  [body(): q_scaled.astype(jnp.bfloat16)]
    ppermute x3, waiting for transfers between devices: 2.14 us -> 4.62 us  [shifted(): return lax.ppermute(x, axis, pairs)]
    dot_general x2, matrix products: 5.56 us -> 3.52 us  [the longest x1 3.09 us: body(): jnp.dot((query.astype(jnp.float32) * jnp.exp(device_cumul)).astype(jnp.bf...]
  transfers between devices with their start and end apart: 13 -> 13, of which waited for: 8 -> 9; matrix products, arithmetic and copies ran while one was open for 16% -> 15% of each run, Pallas kernels for 0% -> 0%
where the time goes in v14:
time: 159 us
  waiting for transfers between devices  59 us (37%)
  matrix products  39.9 us (25%)
  starting transfers between devices  25.4 us (16%)
  local copies, waits for them, and re-layouts  18.6 us (12%)
  other arithmetic  10.5 us (7%)
  between operations  5.61 us (4%)
    ppermute x10, waiting for transfers between devices, ring(): lax.ppermute(x, 'tensor', [(i, (i + step) % size) for i in range(size)])  54.3 us
    ppermute x10, starting transfers between devices, ring(): lax.ppermute(x, 'tensor', [(i, (i + step) % size) for i in range(size)])  16.7 us
    dot_general x5, matrix products, projected(): out = jnp.dot(near, near_rows, preferred_element_type=jnp.float32)  13.6 us
    ppermute x3, starting transfers between devices, shifted(): return lax.ppermute(x, axis, pairs)  8.79 us
    dot_general x5, matrix products, projected(): jnp.dot(far, rows(2), preferred_element_type=jnp.float32)  6.15 us
    dot_general x1, matrix products, body(): jnp.einsum('ncd,ncv->ndv', k_decayed, v_float, precision=HIGH)  5.74 us
    ppermute x3, waiting for transfers between devices, shifted(): return lax.ppermute(x, axis, pairs)  4.62 us
    unnamed x63, local copies, waits for them, and re-layouts  4.14 us
  transfers between devices with their start and end apart: 13, of which 9 were waited for; matrix products, arithmetic and copies ran while one was open for 15% of the time, Pallas kernels for 0%

profile of v14, /device:TPU:2, one launch (start us, length us, event | category | flops | bytes accessed | tf_op | source)
XLA Modules:
  0.0 159.0 jit_solution(205394460233914207)
XLA Ops:
  1.4 1.6 %collective-permute-start = (bf16[512,512]{1,0:T(8,128)(2,1)S(1)}, bf16[512,512]{1,0:T(8,128)(2,1)}, u32[]{:S(2)}, u32[]{:S(2)}) collective-permute-start(bf16[512,512]{1,0:T(8,128)(2,1)S(1)} %get-tuple-element.117), channel_id=1, source_target_pairs={{0,1},{1,2},{2,3},{3,0},{4,5},{5,6},{6,7},{7,4},{8,9},{9,10},{10,1... | collective-permute-start | bytes 1572872 | tf_op jit(solution)/shard_map/ppermute | solution.py:19
  3.1 1.7 %collective-permute-start.1 = (bf16[512,512]{1,0:T(8,128)(2,1)S(1)}, bf16[512,512]{1,0:T(8,128)(2,1)}, u32[]{:S(2)}, u32[]{:S(2)}) collective-permute-start(bf16[512,512]{1,0:T(8,128)(2,1)S(1)} %get-tuple-element.116), channel_id=1, source_target_pairs={{0,3},{1,0},{2,1},{3,2},{4,7},{5,4},{6,5},{7,6},{8,11},{9,8},{10,9... | collective-permute-start | bytes 1572872 | tf_op jit(solution)/shard_map/ppermute | solution.py:19
  9.4 1.6 constant_dynamic-slice_fusion.5
  12.5 4.0 %collective-permute-done = bf16[512,512]{1,0:T(8,128)(2,1)} collective-permute-done((bf16[512,512]{1,0:T(8,128)(2,1)S(1)}, bf16[512,512]{1,0:T(8,128)(2,1)}, u32[]{:S(2)}, u32[]{:S(2)}) %collective-permute-start) | collective-permute-done | bytes 524320 | tf_op jit(solution)/shard_map/ppermute | solution.py:19
  18.2 1.7 %collective-permute-start.5 = (bf16[512,512]{1,0:T(8,128)(2,1)}, bf16[512,512]{1,0:T(8,128)(2,1)S(1)}, u32[]{:S(2)}, u32[]{:S(2)}) collective-permute-start(bf16[512,512]{1,0:T(8,128)(2,1)} %collective-permute-done.1), channel_id=1, source_target_pairs={{0,3},{1,0},{2,1},{3,2},{4,7},{5,4},{6,5},{7,6},{8,11},{9,8},{10,9... | collective-permute-start | bytes 1572872 | tf_op jit(solution)/shard_map/ppermute | solution.py:19
  20.5 2.9 %collective-permute-start.2 = (bf16[512,512]{1,0:T(8,128)(2,1)S(1)}, bf16[512,512]{1,0:T(8,128)(2,1)S(1)}, u32[]{:S(2)}, u32[]{:S(2)}) collective-permute-start(bf16[512,512]{1,0:T(8,128)(2,1)S(1)} %get-tuple-element.114), channel_id=1, source_target_pairs={{0,3},{1,0},{2,1},{3,2},{4,7},{5,4},{6,5},{7,6},{8,11},{9,8},{10,9... | collective-permute-start | bytes 1572872 | tf_op jit(solution)/shard_map/ppermute | solution.py:19
  23.4 9.4 %collective-permute-done.4 = bf16[512,512]{1,0:T(8,128)(2,1)S(1)} collective-permute-done((bf16[512,512]{1,0:T(8,128)(2,1)}, bf16[512,512]{1,0:T(8,128)(2,1)S(1)}, u32[]{:S(2)}, u32[]{:S(2)}) %collective-permute-start.4) | collective-permute-done | bytes 524320 | tf_op jit(solution)/shard_map/ppermute | solution.py:19
  34.5 1.8 %fusion.80 = f32[1024,512]{1,0:T(8,128)S(1)} fusion(bf16[1024,512]{1,0:T(8,128)(2,1)S(1)} %constant_dynamic-update-slice_fusion, bf16[2048,512]{1,0:T(8,128)(2,1)} %param.27, s32[]{:T(128)S(6)} %select_n.111), kind=kOutput, calls=%fused_computation.151 | convolution fusion | flops 536870912 | bytes 3670020 | tf_op jit(solution)/shard_map/dot_general | solution.py:47
  36.3 5.8 %collective-permute-done.3 = bf16[512,512]{1,0:T(8,128)(2,1)S(1)} collective-permute-done((bf16[512,512]{1,0:T(8,128)(2,1)S(1)}, bf16[512,512]{1,0:T(8,128)(2,1)S(1)}, u32[]{:S(2)}, u32[]{:S(2)}) %collective-permute-start.3) | collective-permute-done | bytes 524320 | tf_op jit(solution)/shard_map/ppermute | solution.py:19
  42.1 2.5 %convolution_add_fusion.3 = f32[1024,16]{0,1:T(8,128)S(1)} fusion(f32[1024,16]{0,1:T(8,128)S(1)} %fusion.160, bf16[512,16]{0,1:T(8,128)(2,1)S(1)} %get-tuple-element.142, bf16[512,16]{0,1:T(8,128)(2,1)S(1)} %get-tuple-element.141, bf16[512,16]{0,1:T(8,128)(2,1)S(1)} %get-tuple-element.140, bf16[512,512]{1,0:T(8,128)(2,1)S(1)} %collective-permute-done.3, ...), kind=kOutput, calls=%fused_computation.64 | convolution fusion | flops 66224128 | bytes 3325952 | tf_op jit(solution)/shard_map/dot_general | solution.py:46
  46.5 2.2 %fusion.17 = bf16[1024,256]{1,0:T(8,128)(2,1)S(1)} fusion(f32[1024,256]{1,0:T(8,128)S(1)} %fusion.117, bf16[512,256]{1,0:T(8,128)(2,1)S(1)} %get-tuple-element.110, bf16[512,256]{1,0:T(8,128)(2,1)S(1)} %get-tuple-element.109, bf16[512,256]{1,0:T(8,128)(2,1)S(1)} %get-tuple-element.108, bf16[512,512]{1,0:T(8,128)(2,1)S(1)} %collective-permute-done.3, ...), kind=kOutput, calls=%fused_computation.30 | convolution fusion | flops 823918592 | bytes 5505024 | tf_op jit(solution)/shard_map/dot_general | solution.py:46
  48.9 2.2 %fusion.16 = f32[1024,256]{1,0:T(8,128)S(1)} fusion(f32[1024,256]{1,0:T(8,128)S(1)} %fusion.119, bf16[512,256]{1,0:T(8,128)(2,1)S(1)} %get-tuple-element.165, bf16[512,256]{1,0:T(8,128)(2,1)S(1)} %get-tuple-element.166, bf16[512,256]{1,0:T(8,128)(2,1)S(1)} %get-tuple-element.167, bf16[512,512]{1,0:T(8,128)(2,1)S(1)} %collective-permute-done.3, ...), kind=kOutput, calls=%fused_computation.29 | convolution fusion | flops 824180736 | bytes 6029312 | tf_op jit(solution)/shard_map/dot_general | solution.py:46
  51.1 2.8 %multiply_convert_fusion.4 = (bf16[16,64,256]{2,0,1:T(8,128)(2,1)}, bf16[16,64,256]{2,0,1:T(8,128)(2,1)}, f32[16,64,256]{2,0,1:T(8,128)S(1)}, bf16[16,64,256]{2,0,1:T(8,128)(2,1)}, f32[16,64,256]{2,0,1:T(8,128)S(1)}) fusion(f32[16,64,256]{2,0,1:T(8,128)S(1)} %fusion.40, f32[16,64,256]{2,1,0:T(8,128)S(1)} %bitcast.315, f32[16,256]{1,0:T(8,128)S(1)} %get-tuple-element.107, ...), kind=kLoop, calls=%fused_computation.79 | loop fusion | flops 3145728 | bytes 6868992 | tf_op jit(solution)/shard_map/convert_element_type | solution.py:126
  54.5 3.3 %add_convert_fusion.1 = bf16[1024,512]{1,0:T(8,128)(2,1)S(1)} fusion(f32[1024,512]{1,0:T(8,128)S(1)} %fusion.80, bf16[512,512]{1,0:T(8,128)(2,1)S(1)} %get-tuple-element.99, bf16[512,512]{1,0:T(8,128)(2,1)S(1)} %get-tuple-element.98, bf16[512,512]{1,0:T(8,128)(2,1)S(1)} %get-tuple-element.97, bf16[512,512]{1,0:T(8,128)(2,1)S(1)} %collective-permute-done.3, ...), kind=kOutput, calls=%fused_computation.7 | convolution fusion | flops 1632108544 | bytes 7864320 | tf_op jit(solution)/shard_map/dot_general | solution.py:46
  57.9 5.7 %fusion.38 = f32[16,256,512]{2,1,0:T(8,128)} fusion(bf16[16,64,512]{2,1,0:T(8,128)(2,1)S(1)} %bitcast.316, f32[16,64,256]{2,0,1:T(8,128)S(1)} %get-tuple-element.100), kind=kOutput, calls=%fused_computation.69 | convolution fusion | flops 805306368 | bytes 10485760 | tf_op jit(solution)/shard_map/ncd,ncv->ndv/dot_general | solution.py:136
  63.9 3.7 %multiply_add_fusion.2 = (f32[1,256,512]{2,1,0:T(8,128)S(1)}, f32[1,256,512]{2,1,0:T(8,128)S(1)}, f32[1,256,512]{2,1,0:T(8,128)S(1)}, f32[1,256,512]{2,1,0:T(8,1...) fusion(f32[16,256,512]{2,1,0:T(8,128)} %fusion.38, ...), kind=kLoop, calls=%fused_computation.138 | loop fusion | flops 3538944 | bytes 11024384 | tf_op jit(solution)/shard_map/add | solution.py:150
  67.6 1.8 %copy-done.1 = f32[16,256,512]{2,1,0:T(8,128)S(1)} copy-done((f32[16,256,512]{2,1,0:T(8,128)S(1)}, f32[16,256,512]{2,1,0:T(8,128)}, u32[]{:S(2)}) %copy-start.1) | copy-done | bytes 8388632
  70.3 1.9 %collective-permute-start.6 = (bf16[258,512]{1,0:T(8,128)(2,1)S(1)}, bf16[258,512]{1,0:T(8,128)(2,1)S(1)}, u32[]{:S(2)}, u32[]{:S(2)}) collective-permute-start(bf16[258,512]{1,0:T(8,128)(2,1)S(1)} %pad_maximum_fusion.2), channel_id=1, source_target_pairs={{0,4},{4,8},{8,12},{12,16},{16,20},{20,24},{24,28},{28,32},{32,36}... | collective-permute-start | bytes 792584 | tf_op jit(solution)/shard_map/ppermute | solution.py:14
  72.2 4.0 %collective-permute-start.7 = (bf16[258,512]{1,0:T(8,128)(2,1)S(1)}, bf16[258,512]{1,0:T(8,128)(2,1)S(1)}, u32[]{:S(2)}, u32[]{:S(2)}) collective-permute-start(bf16[258,512]{1,0:T(8,128)(2,1)S(1)} %pad_maximum_fusion.2), channel_id=1, source_target_pairs={{0,8},{4,12},{8,16},{12,20},{16,24},{20,28},{24,32},{28,36},{32,40... | collective-permute-start | bytes 792584 | tf_op jit(solution)/shard_map/ppermute | solution.py:14
  81.4 2.3 %multiply_add_fusion.1 = f32[16,64,512]{2,1,0:T(8,128)} fusion(f32[16,64,512]{2,1,0:T(8,128)S(1)} %fusion.18, f32[16,64,64]{2,1,0:T(8,128)S(1)} %convolution_select_fusion, bf16[16,64,512]{2,1,0:T(8,128)(2,1)S(1)} %bitcast.317, f32[16,64]{1,0:T(8,128)S(1)} %compare_convert_fusion.1), kind=kOutput, calls=%fused_computation.6 | convolution fusion | flops 202375168 | bytes 5509120 | tf_op jit(solution)/shard_map/ncs,nsv->ncv/dot_general | solution.py:132
  90.3 2.8 %collective-permute-start.8 = (bf16[258,512]{1,0:T(8,128)(2,1)}, bf16[258,512]{1,0:T(8,128)(2,1)S(1)}, u32[]{:S(2)}, u32[]{:S(2)}) collective-permute-start(bf16[258,512]{1,0:T(8,128)(2,1)} %pad_maximum_fusion.3), channel_id=1, source_target_pairs={{0,8},{4,12},{8,16},{12,20},{16,24},{20,28},{24,32},{28,36},{32,40... | collective-permute-start | bytes 792584 | tf_op jit(solution)/shard_map/ppermute | solution.py:14
  93.1 3.1 %fusion.78 = f32[1024,512]{0,1:T(8,128)} fusion(bf16[1024,512]{1,0:T(8,128)(2,1)S(1)} %constant_dynamic-update-slice_fusion, bf16[2048,512]{1,0:T(8,128)(2,1)} %param.28, s32[]{:T(128)S(6)} %select_n.111), kind=kOutput, calls=%fused_computation.134 | convolution fusion | flops 536870912 | bytes 3670020 | tf_op jit(solution)/shard_map/dot_general | solution.py:47
  96.2 3.0 %copy.51 = f32[1024,512]{0,1:T(8,128)} copy(f32[1024,512]{1,0:T(8,128)} %bitcast.312) | data formatting | bytes 4194304 | tf_op jit(solution)/shard_map/reshape | solution.py:153
  100.0 3.6 %collective-permute-done.8 = bf16[258,512]{1,0:T(8,128)(2,1)S(1)} collective-permute-done((bf16[258,512]{1,0:T(8,128)(2,1)}, bf16[258,512]{1,0:T(8,128)(2,1)S(1)}, u32[]{:S(2)}, u32[]{:S(2)}) %collective-permute-start.8) | collective-permute-done | bytes 264224 | tf_op jit(solution)/shard_map/ppermute | solution.py:14
  105.6 3.1 %multiply_reduce_fusion = (f32[1024]{0:T(1024)S(1)}, f32[1024,512]{0,1:T(8,128)S(1)}) fusion(f32[1024,512]{0,1:T(8,128)} %copy.51, f32[1024]{0:T(1024)S(1)} %select_bitcast_fusion, f32[258,512]{1,0:T(8,128)S(1)} %convert_element_type.346, f32[256]{0:T(256)S(1)} %bitcast.360, f32[258,512]{1,0:T(8,128)S(1)} %copy-done.6, f32[256]{0:T(256)S(1)} %bitcast.358, ...), kind=kOutput, calls=%fused_computation.4 | convolution fusion | flops 272235520 | bytes 7874560 | tf_op jit(solution)/shard_map/dot_general | solution.py:185
  109.4 3.4 %multiply_convert_fusion = bf16[1024,512]{0,1:T(8,128)(2,1)S(1)} fusion(f32[1024,512]{0,1:T(8,128)S(1)} %copy-done.14, f32[1024,512]{0,1:T(8,128)S(1)} %get-tuple-element.164, bf16[512,512]{1,0:T(8,128)(2,1)S(1)} %copy-done.19, bf16[512,512]{1,0:T(8,128)(2,1)S(1)} %copy-done.18, bf16[512,512]{1,0:T(8,128)(2,1)S(1)} %copy-done.17, f32[512]{0:T(512)S(1)} %copy-done.29, ...), kind=kOutput, calls=%fused_computation.3 | convolution fusion | flops 1635778560 | bytes 9967616 | tf_op jit(solution)/shard_map/dot_general | solution.py:46
  113.7 2.9 %collective-permute-start.11 = (bf16[512,512]{1,0:T(8,128)(2,1)S(1)}, bf16[512,512]{1,0:T(8,128)(2,1)S(1)}, u32[]{:S(2)}, u32[]{:S(2)}) collective-permute-start(bf16[512,512]{1,0:T(8,128)(2,1)S(1)} %get-tuple-element.103), channel_id=1, source_target_pairs={{0,3},{1,0},{2,1},{3,2},{4,7},{5,4},{6,5},{7,6},{8,11},{9,8},{10,9... | collective-permute-start | bytes 1572872 | tf_op jit(solution)/shard_map/ppermute | solution.py:19
  118.1 9.7 %collective-permute-done.11 = bf16[512,512]{1,0:T(8,128)(2,1)S(1)} collective-permute-done((bf16[512,512]{1,0:T(8,128)(2,1)S(1)}, bf16[512,512]{1,0:T(8,128)(2,1)S(1)}, u32[]{:S(2)}, u32[]{:S(2)}) %collective-permute-start.11) | collective-permute-done | bytes 524320 | tf_op jit(solution)/shard_map/ppermute | solution.py:19
  128.0 3.8 %collective-permute-start.12 = (bf16[1024,512]{1,0:T(8,128)(2,1)S(1)}, bf16[1024,512]{1,0:T(8,128)(2,1)S(1)}, u32[]{:S(2)}, u32[]{:S(2)}) collective-permute-start(bf16[1024,512]{1,0:T(8,128)(2,1)S(1)} %pad_maximum_fusion.1), channel_id=1, source_target_pairs={{0,3},{1,0},{2,1},{3,2},{4,7},{5,4},{6,5},{7,6},{8,11},{9,8},{10,9... | collective-permute-start | bytes 3145736 | tf_op jit(solution)/shard_map/ppermute | solution.py:19
  132.1 21.3 %collective-permute-done.12 = bf16[1024,512]{1,0:T(8,128)(2,1)S(1)} collective-permute-done((bf16[1024,512]{1,0:T(8,128)(2,1)S(1)}, bf16[1024,512]{1,0:T(8,128)(2,1)S(1)}, u32[]{:S(2)}, u32[]{:S(2)}) %collective-permute-start.12) | collective-permute-done | bytes 1048608 | tf_op jit(solution)/shard_map/ppermute | solution.py:19
  153.4 3.7 %collective-permute-done.10 = bf16[1024,512]{1,0:T(8,128)(2,1)S(1)} collective-permute-done((bf16[1024,512]{1,0:T(8,128)(2,1)S(1)}, bf16[1024,512]{1,0:T(8,128)(2,1)S(1)}, u32[]{:S(2)}, u32[]{:S(2)}) %collective-permute-start.10) | collective-permute-done | bytes 1048608 | tf_op jit(solution)/shard_map/ppermute | solution.py:19
  157.1 1.8 %add_convert_fusion = bf16[1024,512]{1,0:T(8,128)(2,1)} fusion(bf16[1024,512]{1,0:T(8,128)(2,1)S(1)} %collective-permute-done.12, bf16[1024,512]{1,0:T(8,128)(2,1)S(1)} %collective-permute-done.10, bf16[1024,512]{0,1:T(8,128)(2,1)S(1)} %multiply_convert_fusion, bf16[512,2048]{1,0:T(8,128)(2,1)S(1)} %copy-done, s32[]{:T(128)S(6)} %select_n.105), kind=kOutput, calls=%fused_computation.2 | convolution fusion | flops 540540928 | bytes 4718596 | tf_op jit(solution)/shard_map/dot_general | solution.py:60
  (157 shorter events, 28.1 us)
Async XLA Ops:
  0.0 112.8 %copy-start = (bf16[512,2048]{1,0:T(8,128)(2,1)S(1)}, bf16[512,2048]{1,0:T(8,128)(2,1)}, u32[]{:S(2)}) copy-start(bf16[512,2048]{1,0:T(8,128)(2,1)} %param.33) | copy-start | bytes 6291460
  0.0 4.7 %copy-start.23 = (s32[1024]{0:T(1024)S(1)}, s32[1024]{0:T(1024)}, u32[]{:S(2)}) copy-start(s32[1024]{0:T(1024)} %param.24) | copy-start | bytes 12292
  0.0 9.4 %copy-start.22 = (bf16[2048,16]{0,1:T(8,128)(2,1)S(1)}, bf16[2048,16]{0,1:T(8,128)(2,1)}, u32[]{:S(2)}) copy-start(bf16[2048,16]{0,1:T(8,128)(2,1)} %param.29) | copy-start | bytes 196612
  1.4 15.1 %collective-permute-start = (bf16[512,512]{1,0:T(8,128)(2,1)S(1)}, bf16[512,512]{1,0:T(8,128)(2,1)}, u32[]{:S(2)}, u32[]{:S(2)}) collective-permute-start(bf16[512,512]{1,0:T(8,128)(2,1)S(1)} %get-tuple-element.117), channel_id=1, source_target_pairs={{0,1},{1,2},{2,3},{3,0},{4,5},{5,6},{6,7},{7,4},{8,9},{9,10},{10,1... | collective-permute-start | bytes 1572872 | tf_op jit(solution)/shard_map/ppermute | solution.py:19
  3.1 13.5 %collective-permute-start.1 = (bf16[512,512]{1,0:T(8,128)(2,1)S(1)}, bf16[512,512]{1,0:T(8,128)(2,1)}, u32[]{:S(2)}, u32[]{:S(2)}) collective-permute-start(bf16[512,512]{1,0:T(8,128)(2,1)S(1)} %get-tuple-element.116), channel_id=1, source_target_pairs={{0,3},{1,0},{2,1},{3,2},{4,7},{5,4},{6,5},{7,6},{8,11},{9,8},{10,9... | collective-permute-start | bytes 1572872 | tf_op jit(solution)/shard_map/ppermute | solution.py:19
  11.2 8.6 %copy-start.15 = (bf16[2048,256]{1,0:T(8,128)(2,1)S(1)}, bf16[2048,256]{1,0:T(8,128)(2,1)}, u32[]{:S(2)}) copy-start(bf16[2048,256]{1,0:T(8,128)(2,1)} %param.25) | copy-start | bytes 3145732
  11.2 8.6 %copy-start.16 = (bf16[2048,256]{1,0:T(8,128)(2,1)S(1)}, bf16[2048,256]{1,0:T(8,128)(2,1)}, u32[]{:S(2)}) copy-start(bf16[2048,256]{1,0:T(8,128)(2,1)} %param.26) | copy-start | bytes 3145732
  12.5 7.5 %copy-start.8 = (bf16[1024,512]{1,0:T(8,128)(2,1)S(1)}, bf16[1024,512]{1,0:T(8,128)(2,1)}, u32[]{:S(2)}) copy-start(bf16[1024,512]{1,0:T(8,128)(2,1)} %param.23) | copy-start | bytes 3145732
  16.6 16.2 %collective-permute-start.4 = (bf16[512,512]{1,0:T(8,128)(2,1)}, bf16[512,512]{1,0:T(8,128)(2,1)S(1)}, u32[]{:S(2)}, u32[]{:S(2)}) collective-permute-start(bf16[512,512]{1,0:T(8,128)(2,1)} %collective-permute-done), channel_id=1, source_target_pairs={{0,1},{1,2},{2,3},{3,0},{4,5},{5,6},{6,7},{7,4},{8,9},{9,10},{10,1... | collective-permute-start | bytes 1572872 | tf_op jit(solution)/shard_map/ppermute | solution.py:19
  18.2 15.1 %collective-permute-start.5 = (bf16[512,512]{1,0:T(8,128)(2,1)}, bf16[512,512]{1,0:T(8,128)(2,1)S(1)}, u32[]{:S(2)}, u32[]{:S(2)}) collective-permute-start(bf16[512,512]{1,0:T(8,128)(2,1)} %collective-permute-done.1), channel_id=1, source_target_pairs={{0,3},{1,0},{2,1},{3,2},{4,7},{5,4},{6,5},{7,6},{8,11},{9,8},{10,9... | collective-permute-start | bytes 1572872 | tf_op jit(solution)/shard_map/ppermute | solution.py:19
  20.1 22.0 %collective-permute-start.3 = (bf16[512,512]{1,0:T(8,128)(2,1)S(1)}, bf16[512,512]{1,0:T(8,128)(2,1)S(1)}, u32[]{:S(2)}, u32[]{:S(2)}) collective-permute-start(bf16[512,512]{1,0:T(8,128)(2,1)S(1)} %get-tuple-element.115), channel_id=1, source_target_pairs={{0,1},{1,2},{2,3},{3,0},{4,5},{5,6},{6,7},{7,4},{8,9},{9,10},{10,1... | collective-permute-start | bytes 1572872 | tf_op jit(solution)/shard_map/ppermute | solution.py:19
  20.5 21.5 %collective-permute-start.2 = (bf16[512,512]{1,0:T(8,128)(2,1)S(1)}, bf16[512,512]{1,0:T(8,128)(2,1)S(1)}, u32[]{:S(2)}, u32[]{:S(2)}) collective-permute-start(bf16[512,512]{1,0:T(8,128)(2,1)S(1)} %get-tuple-element.114), channel_id=1, source_target_pairs={{0,3},{1,0},{2,1},{3,2},{4,7},{5,4},{6,5},{7,6},{8,11},{9,8},{10,9... | collective-permute-start | bytes 1572872 | tf_op jit(solution)/shard_map/ppermute | solution.py:19
  42.1 12.4 %copy-start.24 = (bf16[512,512]{1,0:T(8,128)(2,1)}, bf16[512,512]{1,0:T(8,128)(2,1)S(1)}, u32[]{:S(2)}) copy-start(bf16[512,512]{1,0:T(8,128)(2,1)S(1)} %collective-permute-done.3) | copy-start | bytes 1572868
  42.1 12.4 %copy-start.26 = (bf16[512,512]{1,0:T(8,128)(2,1)}, bf16[512,512]{1,0:T(8,128)(2,1)S(1)}, u32[]{:S(2)}) copy-start(bf16[512,512]{1,0:T(8,128)(2,1)S(1)} %collective-permute-done.2) | copy-start | bytes 1572868
  54.5 9.1 %copy-start.7 = (f32[16,64,256]{2,1,0:T(8,128)}, f32[16,64,256]{2,1,0:T(8,128)S(1)}, u32[]{:S(2)}) copy-start(f32[16,64,256]{2,1,0:T(8,128)S(1)} %copy.50) | copy-start | bytes 3145732
  57.9 5.8 %copy-start.11 = (bf16[1024,512]{1,0:T(8,128)(2,1)}, bf16[1024,512]{1,0:T(8,128)(2,1)S(1)}, u32[]{:S(2)}) copy-start(bf16[1024,512]{1,0:T(8,128)(2,1)S(1)} %add_convert_fusion.1) | copy-start | bytes 3145732
  63.9 5.6 %copy-start.1 = (f32[16,256,512]{2,1,0:T(8,128)S(1)}, f32[16,256,512]{2,1,0:T(8,128)}, u32[]{:S(2)}) copy-start(f32[16,256,512]{2,1,0:T(8,128)} %fusion.38) | copy-start | bytes 25165828
  69.4 6.8 %copy-start.2 = (bf16[16,64,256]{2,0,1:T(8,128)(2,1)S(1)}, bf16[16,64,256]{2,0,1:T(8,128)(2,1)}, u32[]{:S(2)}) copy-start(bf16[16,64,256]{2,0,1:T(8,128)(2,1)} %get-tuple-element.94) | copy-start | bytes 1572868
  70.3 13.4 %collective-permute-start.6 = (bf16[258,512]{1,0:T(8,128)(2,1)S(1)}, bf16[258,512]{1,0:T(8,128)(2,1)S(1)}, u32[]{:S(2)}, u32[]{:S(2)}) collective-permute-start(bf16[258,512]{1,0:T(8,128)(2,1)S(1)} %pad_maximum_fusion.2), channel_id=1, source_target_pairs={{0,4},{4,8},{8,12},{12,16},{16,20},{20,24},{24,28},{28,32},{32,36}... | collective-permute-start | bytes 792584 | tf_op jit(solution)/shard_map/ppermute | solution.py:14
  72.2 13.1 %collective-permute-start.7 = (bf16[258,512]{1,0:T(8,128)(2,1)S(1)}, bf16[258,512]{1,0:T(8,128)(2,1)S(1)}, u32[]{:S(2)}, u32[]{:S(2)}) collective-permute-start(bf16[258,512]{1,0:T(8,128)(2,1)S(1)} %pad_maximum_fusion.2), channel_id=1, source_target_pairs={{0,8},{4,12},{8,16},{12,20},{16,24},{20,28},{24,32},{28,36},{32,40... | collective-permute-start | bytes 792584 | tf_op jit(solution)/shard_map/ppermute | solution.py:14
  90.3 13.3 %collective-permute-start.8 = (bf16[258,512]{1,0:T(8,128)(2,1)}, bf16[258,512]{1,0:T(8,128)(2,1)S(1)}, u32[]{:S(2)}, u32[]{:S(2)}) collective-permute-start(bf16[258,512]{1,0:T(8,128)(2,1)} %pad_maximum_fusion.3), channel_id=1, source_target_pairs={{0,8},{4,12},{8,16},{12,20},{16,24},{20,28},{24,32},{28,36},{32,40... | collective-permute-start | bytes 792584 | tf_op jit(solution)/shard_map/ppermute | solution.py:14
  96.2 9.2 %copy-start.4 = (f32[258,512]{1,0:T(8,128)S(1)}, f32[258,512]{1,0:T(8,128)}, u32[]{:S(2)}) copy-start(f32[258,512]{1,0:T(8,128)} %copy-done.3) | copy-start | bytes 1585156
  96.2 9.3 %copy-start.6 = (f32[258,512]{1,0:T(8,128)S(1)}, f32[258,512]{1,0:T(8,128)}, u32[]{:S(2)}) copy-start(f32[258,512]{1,0:T(8,128)} %copy-done.5) | copy-start | bytes 1585156
  105.5 3.4 %copy-start.18 = (bf16[512,512]{1,0:T(8,128)(2,1)S(1)}, bf16[512,512]{1,0:T(8,128)(2,1)}, u32[]{:S(2)}) copy-start(bf16[512,512]{1,0:T(8,128)(2,1)} %get-tuple-element.91) | copy-start | bytes 1572868
  105.5 3.5 %copy-start.19 = (bf16[512,512]{1,0:T(8,128)(2,1)S(1)}, bf16[512,512]{1,0:T(8,128)(2,1)}, u32[]{:S(2)}) copy-start(bf16[512,512]{1,0:T(8,128)(2,1)} %get-tuple-element.92) | copy-start | bytes 1572868
  105.6 3.7 %copy-start.25 = (bf16[512,512]{1,0:T(8,128)(2,1)S(1)}, bf16[512,512]{1,0:T(8,128)(2,1)}, u32[]{:S(2)}) copy-start(bf16[512,512]{1,0:T(8,128)(2,1)} %copy-done.24) | copy-start | bytes 1572868
  105.6 3.8 %copy-start.27 = (bf16[512,512]{1,0:T(8,128)(2,1)S(1)}, bf16[512,512]{1,0:T(8,128)(2,1)}, u32[]{:S(2)}) copy-start(bf16[512,512]{1,0:T(8,128)(2,1)} %copy-done.26) | copy-start | bytes 1572868
  105.6 3.8 %copy-start.29 = (f32[512]{0:T(512)S(1)}, f32[512]{0:T(512)}, u32[]{:S(2)}) copy-start(f32[512]{0:T(512)} %param.32) | copy-start | bytes 6148
  113.7 14.2 %collective-permute-start.11 = (bf16[512,512]{1,0:T(8,128)(2,1)S(1)}, bf16[512,512]{1,0:T(8,128)(2,1)S(1)}, u32[]{:S(2)}, u32[]{:S(2)}) collective-permute-start(bf16[512,512]{1,0:T(8,128)(2,1)S(1)} %get-tuple-element.103), channel_id=1, source_target_pairs={{0,3},{1,0},{2,1},{3,2},{4,7},{5,4},{6,5},{7,6},{8,11},{9,8},{10,9... | collective-permute-start | bytes 1572872 | tf_op jit(solution)/shard_map/ppermute | solution.py:19
  116.6 15.2 %collective-permute-start.9 = (bf16[512,512]{1,0:T(8,128)(2,1)S(1)}, bf16[512,512]{1,0:T(8,128)(2,1)S(1)}, u32[]{:S(2)}, u32[]{:S(2)}) collective-permute-start(bf16[512,512]{1,0:T(8,128)(2,1)S(1)} %get-tuple-element.102), channel_id=1, source_target_pairs={{0,1},{1,2},{2,3},{3,0},{4,5},{5,6},{6,7},{7,4},{8,9},{9,10},{10,1... | collective-permute-start | bytes 1572872 | tf_op jit(solution)/shard_map/ppermute | solution.py:19
  128.0 25.4 %collective-permute-start.12 = (bf16[1024,512]{1,0:T(8,128)(2,1)S(1)}, bf16[1024,512]{1,0:T(8,128)(2,1)S(1)}, u32[]{:S(2)}, u32[]{:S(2)}) collective-permute-start(bf16[1024,512]{1,0:T(8,128)(2,1)S(1)} %pad_maximum_fusion.1), channel_id=1, source_target_pairs={{0,3},{1,0},{2,1},{3,2},{4,7},{5,4},{6,5},{7,6},{8,11},{9,8},{10,9... | collective-permute-start | bytes 3145736 | tf_op jit(solution)/shard_map/ppermute | solution.py:19
  132.0 25.1 %collective-permute-start.10 = (bf16[1024,512]{1,0:T(8,128)(2,1)S(1)}, bf16[1024,512]{1,0:T(8,128)(2,1)S(1)}, u32[]{:S(2)}, u32[]{:S(2)}) collective-permute-start(bf16[1024,512]{1,0:T(8,128)(2,1)S(1)} %pad_maximum_fusion), channel_id=1, source_target_pairs={{0,1},{1,2},{2,3},{3,0},{4,5},{5,6},{6,7},{7,4},{8,9},{9,10},{10,1... | collective-permute-start | bytes 3145736 | tf_op jit(solution)/shard_map/ppermute | solution.py:19
  (12 other events, 24.8 us)

commit v15 on v14

--- a/solution.py
+++ b/solution.py
@@ -114,7 +114,7 @@
 
     q_float = query.astype(jnp.float32).reshape(blocks, GROUP, key_width)
     k_float = key.astype(jnp.float32).reshape(blocks, GROUP, key_width)
-    v_float = value.astype(jnp.float32).reshape(blocks, GROUP, value_width)
+    v_blocks = value.reshape(blocks, GROUP, value_width)
 
     positions = jnp.arange(GROUP)
     causal = positions[None, :] <= positions[:, None]
@@ -129,11 +129,15 @@
     )
     allowed = causal[None] & (seg_blocks[:, :, None] == seg_blocks[:, None, :])
     scores = jnp.where(allowed, raw_scores, 0.0)
-    intra = jnp.einsum("ncs,nsv->ncv", scores, v_float, precision=HIGH)
+    intra = jnp.einsum(
+        "ncs,nsv->ncv", scores.astype(jnp.bfloat16), v_blocks, preferred_element_type=jnp.float32
+    )
 
     same_last = (seg_blocks == seg_blocks[:, -1:]).astype(jnp.float32)
     k_decayed = k_float * jnp.exp(block_totals[:, None, :] - cumul) * same_last[:, :, None]
-    chunk_states = jnp.einsum("ncd,ncv->ndv", k_decayed, v_float, precision=HIGH)
+    chunk_states = jnp.einsum(
+        "ncd,ncv->ndv", k_decayed.astype(jnp.bfloat16), v_blocks, preferred_element_type=jnp.float32
+    )
     chunk_decay = jnp.exp(block_totals) * live_blocks[:, -1:]
 
     q_decayed = q_float * jnp.exp(cumul)

time: 159 us -> 164 us (1.031)
  local copies, waits for them, and re-layouts: 18.6 us -> 20.5 us
  other arithmetic: 10.5 us -> 12.2 us
    ppermute x3, waiting for transfers between devices: 4.62 us -> 2.09 us  [shifted(): return lax.ppermute(x, axis, pairs)]
    unnamed x63 -> x59, local copies, waits for them, and re-layouts: 4.14 us -> 4.88 us
    dot_general x3 -> x2, matrix products: 8.43 us -> 8.91 us  [the longest x1 4.58 us: body(): jnp.einsum('ncd,ncv->ndv', k_decayed.astype(jnp.bfloat16), v_blocks, pref...]
  transfers between devices with their start and end apart: 13 -> 13, of which waited for: 9 -> 8; matrix products, arithmetic and copies ran while one was open for 15% -> 16% of each run, Pallas kernels for 0% -> 0%
where the time goes in v15:
time: 164 us; the launch traced here: 163 us
  waiting for transfers between devices  57.5 us (35%)
  matrix products  40.4 us (25%)
  starting transfers between devices  26.4 us (16%)
  local copies, waits for them, and re-layouts  20.5 us (12%)
  other arithmetic  12.2 us (7%)
  between operations  5.91 us (4%)
    ppermute x10, waiting for transfers between devices, ring(): lax.ppermute(x, 'tensor', [(i, (i + step) % size) for i in range(size)])  55.4 us
    ppermute x10, starting transfers between devices, ring(): lax.ppermute(x, 'tensor', [(i, (i + step) % size) for i in range(size)])  16.7 us
    dot_general x5, matrix products, projected(): out = jnp.dot(near, near_rows, preferred_element_type=jnp.float32)  13.7 us
    ppermute x3, starting transfers between devices, shifted(): return lax.ppermute(x, axis, pairs)  9.77 us
    dot_general x5, matrix products, projected(): jnp.dot(far, rows(2), preferred_element_type=jnp.float32)  6.13 us
    unnamed x59, local copies, waits for them, and re-layouts  4.88 us
    dot_general x1, matrix products, body(): jnp.einsum('ncd,ncv->ndv', k_decayed.astype(jnp.bfloat16), v_blocks, pref...  4.58 us
    dot_general x1, matrix products, body(): jnp.einsum('ncs,nsv->ncv', scores.astype(jnp.bfloat16), v_blocks, preferr...  4.34 us
  transfers between devices with their start and end apart: 13, of which 8 were waited for; matrix products, arithmetic and copies ran while one was open for 16% of the time, Pallas kernels for 0%

profile of v15, /device:TPU:2, one launch (start us, length us, event | category | flops | bytes accessed | tf_op | source)
XLA Modules:
  0.0 162.9 jit_solution(8268917893856053931)
XLA Ops:
  1.4 1.6 %collective-permute-start = (bf16[512,512]{1,0:T(8,128)(2,1)S(1)}, bf16[512,512]{1,0:T(8,128)(2,1)}, u32[]{:S(2)}, u32[]{:S(2)}) collective-permute-start(bf16[512,512]{1,0:T(8,128)(2,1)S(1)} %get-tuple-element.117), channel_id=1, source_target_pairs={{0,1},{1,2},{2,3},{3,0},{4,5},{5,6},{6,7},{7,4},{8,9},{9,10},{10,1... | collective-permute-start | bytes 1572872 | tf_op jit(solution)/shard_map/ppermute | solution.py:19
  3.1 1.7 %collective-permute-start.1 = (bf16[512,512]{1,0:T(8,128)(2,1)S(1)}, bf16[512,512]{1,0:T(8,128)(2,1)}, u32[]{:S(2)}, u32[]{:S(2)}) collective-permute-start(bf16[512,512]{1,0:T(8,128)(2,1)S(1)} %get-tuple-element.116), channel_id=1, source_target_pairs={{0,3},{1,0},{2,1},{3,2},{4,7},{5,4},{6,5},{7,6},{8,11},{9,8},{10,9... | collective-permute-start | bytes 1572872 | tf_op jit(solution)/shard_map/ppermute | solution.py:19
  9.7 1.6 constant_dynamic-slice_fusion.5
  12.8 3.8 %collective-permute-done = bf16[512,512]{1,0:T(8,128)(2,1)} collective-permute-done((bf16[512,512]{1,0:T(8,128)(2,1)S(1)}, bf16[512,512]{1,0:T(8,128)(2,1)}, u32[]{:S(2)}, u32[]{:S(2)}) %collective-permute-start) | collective-permute-done | bytes 524320 | tf_op jit(solution)/shard_map/ppermute | solution.py:19
  18.2 1.7 %collective-permute-start.5 = (bf16[512,512]{1,0:T(8,128)(2,1)}, bf16[512,512]{1,0:T(8,128)(2,1)S(1)}, u32[]{:S(2)}, u32[]{:S(2)}) collective-permute-start(bf16[512,512]{1,0:T(8,128)(2,1)} %collective-permute-done.1), channel_id=1, source_target_pairs={{0,3},{1,0},{2,1},{3,2},{4,7},{5,4},{6,5},{7,6},{8,11},{9,8},{10,9... | collective-permute-start | bytes 1572872 | tf_op jit(solution)/shard_map/ppermute | solution.py:19
  20.5 2.9 %collective-permute-start.2 = (bf16[512,512]{1,0:T(8,128)(2,1)S(1)}, bf16[512,512]{1,0:T(8,128)(2,1)S(1)}, u32[]{:S(2)}, u32[]{:S(2)}) collective-permute-start(bf16[512,512]{1,0:T(8,128)(2,1)S(1)} %get-tuple-element.114), channel_id=1, source_target_pairs={{0,3},{1,0},{2,1},{3,2},{4,7},{5,4},{6,5},{7,6},{8,11},{9,8},{10,9... | collective-permute-start | bytes 1572872 | tf_op jit(solution)/shard_map/ppermute | solution.py:19
  23.4 9.4 %collective-permute-done.4 = bf16[512,512]{1,0:T(8,128)(2,1)S(1)} collective-permute-done((bf16[512,512]{1,0:T(8,128)(2,1)}, bf16[512,512]{1,0:T(8,128)(2,1)S(1)}, u32[]{:S(2)}, u32[]{:S(2)}) %collective-permute-start.4) | collective-permute-done | bytes 524320 | tf_op jit(solution)/shard_map/ppermute | solution.py:19
  34.5 1.8 %fusion.83 = f32[1024,512]{1,0:T(8,128)S(1)} fusion(bf16[1024,512]{1,0:T(8,128)(2,1)S(1)} %constant_dynamic-update-slice_fusion, bf16[2048,512]{1,0:T(8,128)(2,1)} %param.27, s32[]{:T(128)S(6)} %select_n.111), kind=kOutput, calls=%fused_computation.152 | convolution fusion | flops 536870912 | bytes 3670020 | tf_op jit(solution)/shard_map/dot_general | solution.py:47
  36.3 5.8 %collective-permute-done.3 = bf16[512,512]{1,0:T(8,128)(2,1)S(1)} collective-permute-done((bf16[512,512]{1,0:T(8,128)(2,1)S(1)}, bf16[512,512]{1,0:T(8,128)(2,1)S(1)}, u32[]{:S(2)}, u32[]{:S(2)}) %collective-permute-start.3) | collective-permute-done | bytes 524320 | tf_op jit(solution)/shard_map/ppermute | solution.py:19
  42.1 2.5 %convolution_add_fusion.3 = f32[1024,16]{0,1:T(8,128)S(1)} fusion(f32[1024,16]{0,1:T(8,128)S(1)} %fusion.169, bf16[512,16]{0,1:T(8,128)(2,1)S(1)} %get-tuple-element.142, bf16[512,16]{0,1:T(8,128)(2,1)S(1)} %get-tuple-element.141, bf16[512,16]{0,1:T(8,128)(2,1)S(1)} %get-tuple-element.140, bf16[512,512]{1,0:T(8,128)(2,1)S(1)} %collective-permute-done.3, ...), kind=kOutput, calls=%fused_computation.65 | convolution fusion | flops 66224128 | bytes 3325952 | tf_op jit(solution)/shard_map/dot_general | solution.py:46
  46.5 2.2 %fusion.17 = bf16[1024,256]{1,0:T(8,128)(2,1)S(1)} fusion(f32[1024,256]{1,0:T(8,128)S(1)} %fusion.123, bf16[512,256]{1,0:T(8,128)(2,1)S(1)} %get-tuple-element.110, bf16[512,256]{1,0:T(8,128)(2,1)S(1)} %get-tuple-element.109, bf16[512,256]{1,0:T(8,128)(2,1)S(1)} %get-tuple-element.108, bf16[512,512]{1,0:T(8,128)(2,1)S(1)} %collective-permute-done.3, ...), kind=kOutput, calls=%fused_computation.30 | convolution fusion | flops 823918592 | bytes 5505024 | tf_op jit(solution)/shard_map/dot_general | solution.py:46
  48.9 2.2 %fusion.16 = f32[1024,256]{1,0:T(8,128)S(1)} fusion(f32[1024,256]{1,0:T(8,128)S(1)} %fusion.125, bf16[512,256]{1,0:T(8,128)(2,1)S(1)} %get-tuple-element.165, bf16[512,256]{1,0:T(8,128)(2,1)S(1)} %get-tuple-element.166, bf16[512,256]{1,0:T(8,128)(2,1)S(1)} %get-tuple-element.167, bf16[512,512]{1,0:T(8,128)(2,1)S(1)} %collective-permute-done.3, ...), kind=kOutput, calls=%fused_computation.29 | convolution fusion | flops 824180736 | bytes 6029312 | tf_op jit(solution)/shard_map/dot_general | solution.py:46
  51.2 2.6 %multiply_convert_fusion.5 = (bf16[16,64,256]{2,0,1:T(8,128)(2,1)}, bf16[16,64,256]{2,0,1:T(8,128)(2,1)}, bf16[16,64,256]{2,0,1:T(8,128)(2,1)S(1)}, bf16[16,64,256]{2,0,1:T(8,128)(2,1)}, f32[16,64,256]{2,0,1:T(8,128)S(1)}) fusion(f32[16,64,256]{2,0,1:T(8,128)S(1)} %fusion.39, f32[16,64,256]{2,1,0:T(8,128)S(1)} %bitcast.314, ...), kind=kLoop, calls=%fused_computation.78 | loop fusion | flops 3407872 | bytes 6344704 | tf_op jit(solution)/shard_map/convert_element_type | solution.py:126
  54.5 3.3 %add_convert_fusion.1 = bf16[1024,512]{1,0:T(8,128)(2,1)S(1)} fusion(f32[1024,512]{1,0:T(8,128)S(1)} %fusion.83, bf16[512,512]{1,0:T(8,128)(2,1)S(1)} %get-tuple-element.99, bf16[512,512]{1,0:T(8,128)(2,1)S(1)} %get-tuple-element.98, bf16[512,512]{1,0:T(8,128)(2,1)S(1)} %get-tuple-element.97, bf16[512,512]{1,0:T(8,128)(2,1)S(1)} %collective-permute-done.3, ...), kind=kOutput, calls=%fused_computation.7 | convolution fusion | flops 1632108544 | bytes 7864320 | tf_op jit(solution)/shard_map/dot_general | solution.py:46
  57.8 4.6 %fusion.71 = f32[16,256,512]{2,1,0:T(8,128)} fusion(bf16[16,64,512]{2,1,0:T(8,128)(2,1)S(1)} %bitcast.315, bf16[16,64,256]{2,0,1:T(8,128)(2,1)S(1)} %get-tuple-element.100), kind=kOutput, calls=%fused_computation.127 | convolution fusion | flops 268435456 | bytes 9961472 | tf_op jit(solution)/shard_map/ncd,ncv->ndv/dot_general | solution.py:138
  62.6 3.7 %multiply_add_fusion.2 = (f32[1,256,512]{2,1,0:T(8,128)S(1)}, f32[1,256,512]{2,1,0:T(8,128)S(1)}, f32[1,256,512]{2,1,0:T(8,128)S(1)}, f32[1,256,512]{2,1,0:T(8,1...) fusion(f32[16,256,512]{2,1,0:T(8,128)} %fusion.71, ...), kind=kLoop, calls=%fused_computation.139 | loop fusion | flops 3538944 | bytes 11024384 | tf_op jit(solution)/shard_map/add | solution.py:154
  66.3 1.8 %copy-done.1 = f32[16,256,512]{2,1,0:T(8,128)S(1)} copy-done((f32[16,256,512]{2,1,0:T(8,128)S(1)}, f32[16,256,512]{2,1,0:T(8,128)}, u32[]{:S(2)}) %copy-start.1) | copy-done | bytes 8388632
  69.7 1.9 %collective-permute-start.6 = (bf16[258,512]{1,0:T(8,128)(2,1)}, bf16[258,512]{1,0:T(8,128)(2,1)S(1)}, u32[]{:S(2)}, u32[]{:S(2)}) collective-permute-start(bf16[258,512]{1,0:T(8,128)(2,1)} %pad_maximum_fusion.2), channel_id=1, source_target_pairs={{0,4},{4,8},{8,12},{12,16},{16,20},{20,24},{24,28},{28,32},{32,36}... | collective-permute-start | bytes 792584 | tf_op jit(solution)/shard_map/ppermute | solution.py:14
  71.6 4.0 %collective-permute-start.7 = (bf16[258,512]{1,0:T(8,128)(2,1)}, bf16[258,512]{1,0:T(8,128)(2,1)}, u32[]{:S(2)}, u32[]{:S(2)}) collective-permute-start(bf16[258,512]{1,0:T(8,128)(2,1)} %pad_maximum_fusion.2), channel_id=1, source_target_pairs={{0,8},{4,12},{8,16},{12,20},{16,24},{20,28},{24,32},{28,36},{32,40... | collective-permute-start | bytes 792584 | tf_op jit(solution)/shard_map/ppermute | solution.py:14
  81.5 4.3 %multiply_add_fusion.1 = f32[16,64,512]{2,1,0:T(8,128)} fusion(f32[16,64,512]{2,1,0:T(8,128)} %copy-done.12, bf16[16,64,512]{2,1,0:T(8,128)(2,1)} %bitcast.316, f32[16,64]{1,0:T(8,128)S(1)} %compare_convert_fusion.1, bf16[16,64,256]{2,0,1:T(8,128)(2,1)} %get-tuple-element.101, bf16[16,64,256]{2,0,1:T(8,128)(2,1)} %get-tuple-element.93, ...), kind=kOutput, calls=%fused_computation.6 | convolution fusion | flops 101974016 | bytes 6303744 | tf_op jit(solution)/shard_map/ncs,nsv->ncv/dot_general | solution.py:132
  93.3 3.8 %collective-permute-start.8 = (bf16[258,512]{1,0:T(8,128)(2,1)}, bf16[258,512]{1,0:T(8,128)(2,1)S(1)}, u32[]{:S(2)}, u32[]{:S(2)}) collective-permute-start(bf16[258,512]{1,0:T(8,128)(2,1)} %pad_maximum_fusion.3), channel_id=1, source_target_pairs={{0,8},{4,12},{8,16},{12,20},{16,24},{20,28},{24,32},{28,36},{32,40... | collective-permute-start | bytes 792584 | tf_op jit(solution)/shard_map/ppermute | solution.py:14
  97.1 3.1 %fusion.81 = f32[1024,512]{0,1:T(8,128)} fusion(bf16[1024,512]{1,0:T(8,128)(2,1)S(1)} %constant_dynamic-update-slice_fusion, bf16[2048,512]{1,0:T(8,128)(2,1)} %param.28, s32[]{:T(128)S(6)} %select_n.111), kind=kOutput, calls=%fused_computation.135 | convolution fusion | flops 536870912 | bytes 3670020 | tf_op jit(solution)/shard_map/dot_general | solution.py:47
  100.2 3.0 %copy.51 = f32[1024,512]{0,1:T(8,128)} copy(f32[1024,512]{1,0:T(8,128)} %bitcast.311) | data formatting | bytes 4194304 | tf_op jit(solution)/shard_map/reshape | solution.py:157
  104.0 2.1 %collective-permute-done.8 = bf16[258,512]{1,0:T(8,128)(2,1)S(1)} collective-permute-done((bf16[258,512]{1,0:T(8,128)(2,1)}, bf16[258,512]{1,0:T(8,128)(2,1)S(1)}, u32[]{:S(2)}, u32[]{:S(2)}) %collective-permute-start.8) | collective-permute-done | bytes 264224 | tf_op jit(solution)/shard_map/ppermute | solution.py:14
  108.2 3.1 %multiply_reduce_fusion = (f32[1024]{0:T(1024)S(1)}, f32[1024,512]{0,1:T(8,128)S(1)}) fusion(f32[1024,512]{0,1:T(8,128)} %copy.51, f32[1024]{0:T(1024)S(1)} %select_bitcast_fusion, f32[258,512]{1,0:T(8,128)S(1)} %convert_element_type.353, f32[256]{0:T(256)S(1)} %bitcast.359, f32[258,512]{1,0:T(8,128)S(1)} %copy-done.6, f32[256]{0:T(256)S(1)} %bitcast.357, ...), kind=kOutput, calls=%fused_computation.4 | convolution fusion | flops 272235520 | bytes 7874560 | tf_op jit(solution)/shard_map/dot_general | solution.py:189
  112.0 3.4 %multiply_convert_fusion = bf16[1024,512]{0,1:T(8,128)(2,1)S(1)} fusion(f32[1024,512]{0,1:T(8,128)S(1)} %copy-done.14, f32[1024,512]{0,1:T(8,128)S(1)} %get-tuple-element.164, bf16[512,512]{1,0:T(8,128)(2,1)S(1)} %copy-done.19, bf16[512,512]{1,0:T(8,128)(2,1)S(1)} %copy-done.18, bf16[512,512]{1,0:T(8,128)(2,1)S(1)} %copy-done.17, f32[512]{0:T(512)S(1)} %copy-done.27, ...), kind=kOutput, calls=%fused_computation.3 | convolution fusion | flops 1635778560 | bytes 9967616 | tf_op jit(solution)/shard_map/dot_general | solution.py:46
  116.3 2.9 %collective-permute-start.11 = (bf16[512,512]{1,0:T(8,128)(2,1)S(1)}, bf16[512,512]{1,0:T(8,128)(2,1)S(1)}, u32[]{:S(2)}, u32[]{:S(2)}) collective-permute-start(bf16[512,512]{1,0:T(8,128)(2,1)S(1)} %get-tuple-element.103), channel_id=1, source_target_pairs={{0,3},{1,0},{2,1},{3,2},{4,7},{5,4},{6,5},{7,6},{8,11},{9,8},{10,9... | collective-permute-start | bytes 1572872 | tf_op jit(solution)/shard_map/ppermute | solution.py:19
  120.8 10.4 %collective-permute-done.11 = bf16[512,512]{1,0:T(8,128)(2,1)S(1)} collective-permute-done((bf16[512,512]{1,0:T(8,128)(2,1)S(1)}, bf16[512,512]{1,0:T(8,128)(2,1)S(1)}, u32[]{:S(2)}, u32[]{:S(2)}) %collective-permute-start.11) | collective-permute-done | bytes 524320 | tf_op jit(solution)/shard_map/ppermute | solution.py:19
  131.3 3.8 %collective-permute-start.12 = (bf16[1024,512]{1,0:T(8,128)(2,1)S(1)}, bf16[1024,512]{1,0:T(8,128)(2,1)S(1)}, u32[]{:S(2)}, u32[]{:S(2)}) collective-permute-start(bf16[1024,512]{1,0:T(8,128)(2,1)S(1)} %pad_maximum_fusion.1), channel_id=1, source_target_pairs={{0,3},{1,0},{2,1},{3,2},{4,7},{5,4},{6,5},{7,6},{8,11},{9,8},{10,9... | collective-permute-start | bytes 3145736 | tf_op jit(solution)/shard_map/ppermute | solution.py:19
  135.4 22.0 %collective-permute-done.12 = bf16[1024,512]{1,0:T(8,128)(2,1)S(1)} collective-permute-done((bf16[1024,512]{1,0:T(8,128)(2,1)S(1)}, bf16[1024,512]{1,0:T(8,128)(2,1)S(1)}, u32[]{:S(2)}, u32[]{:S(2)}) %collective-permute-start.12) | collective-permute-done | bytes 1048608 | tf_op jit(solution)/shard_map/ppermute | solution.py:19
  157.4 3.7 %collective-permute-done.10 = bf16[1024,512]{1,0:T(8,128)(2,1)S(1)} collective-permute-done((bf16[1024,512]{1,0:T(8,128)(2,1)S(1)}, bf16[1024,512]{1,0:T(8,128)(2,1)S(1)}, u32[]{:S(2)}, u32[]{:S(2)}) %collective-permute-start.10) | collective-permute-done | bytes 1048608 | tf_op jit(solution)/shard_map/ppermute | solution.py:19
  161.1 1.8 %add_convert_fusion = bf16[1024,512]{1,0:T(8,128)(2,1)} fusion(bf16[1024,512]{1,0:T(8,128)(2,1)S(1)} %collective-permute-done.12, bf16[1024,512]{1,0:T(8,128)(2,1)S(1)} %collective-permute-done.10, bf16[1024,512]{0,1:T(8,128)(2,1)S(1)} %multiply_convert_fusion, bf16[512,2048]{1,0:T(8,128)(2,1)S(1)} %copy-done, s32[]{:T(128)S(6)} %select_n.105), kind=kOutput, calls=%fused_computation.2 | convolution fusion | flops 540540928 | bytes 4718596 | tf_op jit(solution)/shard_map/dot_general | solution.py:60
  (152 shorter events, 30.4 us)
Async XLA Ops:
  0.0 115.4 %copy-start = (bf16[512,2048]{1,0:T(8,128)(2,1)S(1)}, bf16[512,2048]{1,0:T(8,128)(2,1)}, u32[]{:S(2)}) copy-start(bf16[512,2048]{1,0:T(8,128)(2,1)} %param.33) | copy-start | bytes 6291460
  0.0 4.7 %copy-start.21 = (s32[1024]{0:T(1024)S(1)}, s32[1024]{0:T(1024)}, u32[]{:S(2)}) copy-start(s32[1024]{0:T(1024)} %param.24) | copy-start | bytes 12292
  0.0 9.7 %copy-start.20 = (bf16[2048,16]{0,1:T(8,128)(2,1)S(1)}, bf16[2048,16]{0,1:T(8,128)(2,1)}, u32[]{:S(2)}) copy-start(bf16[2048,16]{0,1:T(8,128)(2,1)} %param.29) | copy-start | bytes 196612
  1.4 15.1 %collective-permute-start = (bf16[512,512]{1,0:T(8,128)(2,1)S(1)}, bf16[512,512]{1,0:T(8,128)(2,1)}, u32[]{:S(2)}, u32[]{:S(2)}) collective-permute-start(bf16[512,512]{1,0:T(8,128)(2,1)S(1)} %get-tuple-element.117), channel_id=1, source_target_pairs={{0,1},{1,2},{2,3},{3,0},{4,5},{5,6},{6,7},{7,4},{8,9},{9,10},{10,1... | collective-permute-start | bytes 1572872 | tf_op jit(solution)/shard_map/ppermute | solution.py:19
  3.1 13.5 %collective-permute-start.1 = (bf16[512,512]{1,0:T(8,128)(2,1)S(1)}, bf16[512,512]{1,0:T(8,128)(2,1)}, u32[]{:S(2)}, u32[]{:S(2)}) collective-permute-start(bf16[512,512]{1,0:T(8,128)(2,1)S(1)} %get-tuple-element.116), channel_id=1, source_target_pairs={{0,3},{1,0},{2,1},{3,2},{4,7},{5,4},{6,5},{7,6},{8,11},{9,8},{10,9... | collective-permute-start | bytes 1572872 | tf_op jit(solution)/shard_map/ppermute | solution.py:19
  11.5 8.4 %copy-start.15 = (bf16[2048,256]{1,0:T(8,128)(2,1)S(1)}, bf16[2048,256]{1,0:T(8,128)(2,1)}, u32[]{:S(2)}) copy-start(bf16[2048,256]{1,0:T(8,128)(2,1)} %param.25) | copy-start | bytes 3145732
  11.5 8.4 %copy-start.16 = (bf16[2048,256]{1,0:T(8,128)(2,1)S(1)}, bf16[2048,256]{1,0:T(8,128)(2,1)}, u32[]{:S(2)}) copy-start(bf16[2048,256]{1,0:T(8,128)(2,1)} %param.26) | copy-start | bytes 3145732
  12.8 7.2 %copy-start.9 = (bf16[1024,512]{1,0:T(8,128)(2,1)S(1)}, bf16[1024,512]{1,0:T(8,128)(2,1)}, u32[]{:S(2)}) copy-start(bf16[1024,512]{1,0:T(8,128)(2,1)} %param.23) | copy-start | bytes 3145732
  16.6 16.2 %collective-permute-start.4 = (bf16[512,512]{1,0:T(8,128)(2,1)}, bf16[512,512]{1,0:T(8,128)(2,1)S(1)}, u32[]{:S(2)}, u32[]{:S(2)}) collective-permute-start(bf16[512,512]{1,0:T(8,128)(2,1)} %collective-permute-done), channel_id=1, source_target_pairs={{0,1},{1,2},{2,3},{3,0},{4,5},{5,6},{6,7},{7,4},{8,9},{9,10},{10,1... | collective-permute-start | bytes 1572872 | tf_op jit(solution)/shard_map/ppermute | solution.py:19
  18.2 15.1 %collective-permute-start.5 = (bf16[512,512]{1,0:T(8,128)(2,1)}, bf16[512,512]{1,0:T(8,128)(2,1)S(1)}, u32[]{:S(2)}, u32[]{:S(2)}) collective-permute-start(bf16[512,512]{1,0:T(8,128)(2,1)} %collective-permute-done.1), channel_id=1, source_target_pairs={{0,3},{1,0},{2,1},{3,2},{4,7},{5,4},{6,5},{7,6},{8,11},{9,8},{10,9... | collective-permute-start | bytes 1572872 | tf_op jit(solution)/shard_map/ppermute | solution.py:19
  20.1 22.0 %collective-permute-start.3 = (bf16[512,512]{1,0:T(8,128)(2,1)S(1)}, bf16[512,512]{1,0:T(8,128)(2,1)S(1)}, u32[]{:S(2)}, u32[]{:S(2)}) collective-permute-start(bf16[512,512]{1,0:T(8,128)(2,1)S(1)} %get-tuple-element.115), channel_id=1, source_target_pairs={{0,1},{1,2},{2,3},{3,0},{4,5},{5,6},{6,7},{7,4},{8,9},{9,10},{10,1... | collective-permute-start | bytes 1572872 | tf_op jit(solution)/shard_map/ppermute | solution.py:19
  20.5 21.6 %collective-permute-start.2 = (bf16[512,512]{1,0:T(8,128)(2,1)S(1)}, bf16[512,512]{1,0:T(8,128)(2,1)S(1)}, u32[]{:S(2)}, u32[]{:S(2)}) collective-permute-start(bf16[512,512]{1,0:T(8,128)(2,1)S(1)} %get-tuple-element.114), channel_id=1, source_target_pairs={{0,3},{1,0},{2,1},{3,2},{4,7},{5,4},{6,5},{7,6},{8,11},{9,8},{10,9... | collective-permute-start | bytes 1572872 | tf_op jit(solution)/shard_map/ppermute | solution.py:19
  42.1 12.4 %copy-start.22 = (bf16[512,512]{1,0:T(8,128)(2,1)}, bf16[512,512]{1,0:T(8,128)(2,1)S(1)}, u32[]{:S(2)}) copy-start(bf16[512,512]{1,0:T(8,128)(2,1)S(1)} %collective-permute-done.3) | copy-start | bytes 1572868
  42.1 12.4 %copy-start.24 = (bf16[512,512]{1,0:T(8,128)(2,1)}, bf16[512,512]{1,0:T(8,128)(2,1)S(1)}, u32[]{:S(2)}) copy-start(bf16[512,512]{1,0:T(8,128)(2,1)S(1)} %collective-permute-done.2) | copy-start | bytes 1572868
  54.4 8.0 %copy-start.7 = (f32[16,64,256]{2,1,0:T(8,128)}, f32[16,64,256]{2,1,0:T(8,128)S(1)}, u32[]{:S(2)}) copy-start(f32[16,64,256]{2,1,0:T(8,128)S(1)} %copy.50) | copy-start | bytes 3145732
  57.8 4.6 %copy-start.11 = (bf16[1024,512]{1,0:T(8,128)(2,1)}, bf16[1024,512]{1,0:T(8,128)(2,1)S(1)}, u32[]{:S(2)}) copy-start(bf16[1024,512]{1,0:T(8,128)(2,1)S(1)} %add_convert_fusion.1) | copy-start | bytes 3145732
  62.6 5.6 %copy-start.1 = (f32[16,256,512]{2,1,0:T(8,128)S(1)}, f32[16,256,512]{2,1,0:T(8,128)}, u32[]{:S(2)}) copy-start(f32[16,256,512]{2,1,0:T(8,128)} %fusion.71) | copy-start | bytes 25165828
  68.2 7.5 %copy-start.2 = (bf16[16,64,256]{2,0,1:T(8,128)(2,1)S(1)}, bf16[16,64,256]{2,0,1:T(8,128)(2,1)}, u32[]{:S(2)}) copy-start(bf16[16,64,256]{2,0,1:T(8,128)(2,1)} %get-tuple-element.94) | copy-start | bytes 1572868
  69.7 16.1 %collective-permute-start.6 = (bf16[258,512]{1,0:T(8,128)(2,1)}, bf16[258,512]{1,0:T(8,128)(2,1)S(1)}, u32[]{:S(2)}, u32[]{:S(2)}) collective-permute-start(bf16[258,512]{1,0:T(8,128)(2,1)} %pad_maximum_fusion.2), channel_id=1, source_target_pairs={{0,4},{4,8},{8,12},{12,16},{16,20},{20,24},{24,28},{28,32},{32,36}... | collective-permute-start | bytes 792584 | tf_op jit(solution)/shard_map/ppermute | solution.py:14
  71.6 14.8 %collective-permute-start.7 = (bf16[258,512]{1,0:T(8,128)(2,1)}, bf16[258,512]{1,0:T(8,128)(2,1)}, u32[]{:S(2)}, u32[]{:S(2)}) collective-permute-start(bf16[258,512]{1,0:T(8,128)(2,1)} %pad_maximum_fusion.2), channel_id=1, source_target_pairs={{0,8},{4,12},{8,16},{12,20},{16,24},{20,28},{24,32},{28,36},{32,40... | collective-permute-start | bytes 792584 | tf_op jit(solution)/shard_map/ppermute | solution.py:14
  93.3 12.8 %collective-permute-start.8 = (bf16[258,512]{1,0:T(8,128)(2,1)}, bf16[258,512]{1,0:T(8,128)(2,1)S(1)}, u32[]{:S(2)}, u32[]{:S(2)}) collective-permute-start(bf16[258,512]{1,0:T(8,128)(2,1)} %pad_maximum_fusion.3), channel_id=1, source_target_pairs={{0,8},{4,12},{8,16},{12,20},{16,24},{20,28},{24,32},{28,36},{32,40... | collective-permute-start | bytes 792584 | tf_op jit(solution)/shard_map/ppermute | solution.py:14
  100.2 7.9 %copy-start.4 = (f32[258,512]{1,0:T(8,128)S(1)}, f32[258,512]{1,0:T(8,128)}, u32[]{:S(2)}) copy-start(f32[258,512]{1,0:T(8,128)} %copy-done.3) | copy-start | bytes 1585156
  100.2 7.9 %copy-start.6 = (f32[258,512]{1,0:T(8,128)S(1)}, f32[258,512]{1,0:T(8,128)}, u32[]{:S(2)}) copy-start(f32[258,512]{1,0:T(8,128)} %copy-done.5) | copy-start | bytes 1585156
  108.1 3.4 %copy-start.18 = (bf16[512,512]{1,0:T(8,128)(2,1)S(1)}, bf16[512,512]{1,0:T(8,128)(2,1)}, u32[]{:S(2)}) copy-start(bf16[512,512]{1,0:T(8,128)(2,1)} %get-tuple-element.91) | copy-start | bytes 1572868
  108.2 3.5 %copy-start.19 = (bf16[512,512]{1,0:T(8,128)(2,1)S(1)}, bf16[512,512]{1,0:T(8,128)(2,1)}, u32[]{:S(2)}) copy-start(bf16[512,512]{1,0:T(8,128)(2,1)} %get-tuple-element.92) | copy-start | bytes 1572868
  108.2 3.7 %copy-start.23 = (bf16[512,512]{1,0:T(8,128)(2,1)S(1)}, bf16[512,512]{1,0:T(8,128)(2,1)}, u32[]{:S(2)}) copy-start(bf16[512,512]{1,0:T(8,128)(2,1)} %copy-done.22) | copy-start | bytes 1572868
  108.2 3.8 %copy-start.25 = (bf16[512,512]{1,0:T(8,128)(2,1)S(1)}, bf16[512,512]{1,0:T(8,128)(2,1)}, u32[]{:S(2)}) copy-start(bf16[512,512]{1,0:T(8,128)(2,1)} %copy-done.24) | copy-start | bytes 1572868
  108.2 3.8 %copy-start.27 = (f32[512]{0:T(512)S(1)}, f32[512]{0:T(512)}, u32[]{:S(2)}) copy-start(f32[512]{0:T(512)} %param.32) | copy-start | bytes 6148
  116.3 14.8 %collective-permute-start.11 = (bf16[512,512]{1,0:T(8,128)(2,1)S(1)}, bf16[512,512]{1,0:T(8,128)(2,1)S(1)}, u32[]{:S(2)}, u32[]{:S(2)}) collective-permute-start(bf16[512,512]{1,0:T(8,128)(2,1)S(1)} %get-tuple-element.103), channel_id=1, source_target_pairs={{0,3},{1,0},{2,1},{3,2},{4,7},{5,4},{6,5},{7,6},{8,11},{9,8},{10,9... | collective-permute-start | bytes 1572872 | tf_op jit(solution)/shard_map/ppermute | solution.py:19
  119.2 15.9 %collective-permute-start.9 = (bf16[512,512]{1,0:T(8,128)(2,1)S(1)}, bf16[512,512]{1,0:T(8,128)(2,1)S(1)}, u32[]{:S(2)}, u32[]{:S(2)}) collective-permute-start(bf16[512,512]{1,0:T(8,128)(2,1)S(1)} %get-tuple-element.102), channel_id=1, source_target_pairs={{0,1},{1,2},{2,3},{3,0},{4,5},{5,6},{6,7},{7,4},{8,9},{9,10},{10,1... | collective-permute-start | bytes 1572872 | tf_op jit(solution)/shard_map/ppermute | solution.py:19
  131.3 26.1 %collective-permute-start.12 = (bf16[1024,512]{1,0:T(8,128)(2,1)S(1)}, bf16[1024,512]{1,0:T(8,128)(2,1)S(1)}, u32[]{:S(2)}, u32[]{:S(2)}) collective-permute-start(bf16[1024,512]{1,0:T(8,128)(2,1)S(1)} %pad_maximum_fusion.1), channel_id=1, source_target_pairs={{0,3},{1,0},{2,1},{3,2},{4,7},{5,4},{6,5},{7,6},{8,11},{9,8},{10,9... | collective-permute-start | bytes 3145736 | tf_op jit(solution)/shard_map/ppermute | solution.py:19
  135.3 25.8 %collective-permute-start.10 = (bf16[1024,512]{1,0:T(8,128)(2,1)S(1)}, bf16[1024,512]{1,0:T(8,128)(2,1)S(1)}, u32[]{:S(2)}, u32[]{:S(2)}) collective-permute-start(bf16[1024,512]{1,0:T(8,128)(2,1)S(1)} %pad_maximum_fusion), channel_id=1, source_target_pairs={{0,1},{1,2},{2,3},{3,0},{4,5},{5,6},{6,7},{7,4},{8,9},{9,10},{10,1... | collective-permute-start | bytes 3145736 | tf_op jit(solution)/shard_map/ppermute | solution.py:19
  (10 other events, 22.8 us)

commit v16 on v14

--- a/solution.py
+++ b/solution.py
@@ -59,9 +59,11 @@
         cols = lax.dynamic_slice_in_dim(w_out, ((index + offset) % size) * width, width, 1)
         return jnp.dot(gated, cols, preferred_element_type=jnp.float32).astype(jnp.bfloat16)
 
-    far = term(2)
-    far_from_left = ring(far[:half], 1).astype(jnp.float32)
-    far_from_right = ring(far[half:], -1).astype(jnp.float32)
+    far_cols = lax.dynamic_slice_in_dim(w_out, ((index + 2) % size) * width, width, 1)
+    far_top = jnp.dot(gated[:half], far_cols, preferred_element_type=jnp.float32)
+    far_from_left = ring(far_top.astype(jnp.bfloat16), 1).astype(jnp.float32)
+    far_bottom = jnp.dot(gated[half:], far_cols, preferred_element_type=jnp.float32)
+    far_from_right = ring(far_bottom.astype(jnp.bfloat16), -1).astype(jnp.float32)
     near_right, near_left = term(1), term(-1)
     to_right = jnp.concatenate(
         [(near_right[:half].astype(jnp.float32) + far_from_left).astype(jnp.bfloat16), near_right[half:]]

time: 159 us -> 160 us (level)
    dot_general x4 -> x3, matrix products: 4.05 us -> 3.3 us  [term(): jnp.dot(gated, cols, preferred_element_type=jnp.float32)]
where the time goes in v16:
time: 160 us; the launch traced here: 159 us
  waiting for transfers between devices  58.8 us (37%)
  matrix products  40.1 us (25%)
  starting transfers between devices  25.4 us (16%)
  local copies, waits for them, and re-layouts  18.5 us (12%)
  other arithmetic  10.5 us (7%)
  between operations  5.74 us (4%)
    ppermute x10, waiting for transfers between devices, ring(): lax.ppermute(x, 'tensor', [(i, (i + step) % size) for i in range(size)])  54 us
    ppermute x10, starting transfers between devices, ring(): lax.ppermute(x, 'tensor', [(i, (i + step) % size) for i in range(size)])  16.6 us
    dot_general x5, matrix products, projected(): out = jnp.dot(near, near_rows, preferred_element_type=jnp.float32)  13.7 us
    ppermute x3, starting transfers between devices, shifted(): return lax.ppermute(x, axis, pairs)  8.73 us
    dot_general x5, matrix products, projected(): jnp.dot(far, rows(2), preferred_element_type=jnp.float32)  6.17 us
    dot_general x1, matrix products, body(): jnp.einsum('ncd,ncv->ndv', k_decayed, v_float, precision=HIGH)  5.75 us
    ppermute x3, waiting for transfers between devices, shifted(): return lax.ppermute(x, axis, pairs)  4.78 us
    unnamed x63, local copies, waits for them, and re-layouts  4.14 us
  transfers between devices with their start and end apart: 13, of which 9 were waited for; matrix products, arithmetic and copies ran while one was open for 15% of the time, Pallas kernels for 0%

profile of v16, /device:TPU:2, one launch (start us, length us, event | category | flops | bytes accessed | tf_op | source)
XLA Modules:
  0.0 159.0 jit_solution(613933568984659114)
XLA Ops:
  1.4 1.6 %collective-permute-start = (bf16[512,512]{1,0:T(8,128)(2,1)S(1)}, bf16[512,512]{1,0:T(8,128)(2,1)}, u32[]{:S(2)}, u32[]{:S(2)}) collective-permute-start(bf16[512,512]{1,0:T(8,128)(2,1)S(1)} %get-tuple-element.115), channel_id=1, source_target_pairs={{0,1},{1,2},{2,3},{3,0},{4,5},{5,6},{6,7},{7,4},{8,9},{9,10},{10,1... | collective-permute-start | bytes 1572872 | tf_op jit(solution)/shard_map/ppermute | solution.py:19
  3.1 1.7 %collective-permute-start.1 = (bf16[512,512]{1,0:T(8,128)(2,1)S(1)}, bf16[512,512]{1,0:T(8,128)(2,1)}, u32[]{:S(2)}, u32[]{:S(2)}) collective-permute-start(bf16[512,512]{1,0:T(8,128)(2,1)S(1)} %get-tuple-element.114), channel_id=1, source_target_pairs={{0,3},{1,0},{2,1},{3,2},{4,7},{5,4},{6,5},{7,6},{8,11},{9,8},{10,9... | collective-permute-start | bytes 1572872 | tf_op jit(solution)/shard_map/ppermute | solution.py:19
  9.5 1.6 constant_dynamic-slice_fusion.5
  12.7 3.9 %collective-permute-done = bf16[512,512]{1,0:T(8,128)(2,1)} collective-permute-done((bf16[512,512]{1,0:T(8,128)(2,1)S(1)}, bf16[512,512]{1,0:T(8,128)(2,1)}, u32[]{:S(2)}, u32[]{:S(2)}) %collective-permute-start) | collective-permute-done | bytes 524320 | tf_op jit(solution)/shard_map/ppermute | solution.py:19
  18.2 1.7 %collective-permute-start.5 = (bf16[512,512]{1,0:T(8,128)(2,1)}, bf16[512,512]{1,0:T(8,128)(2,1)S(1)}, u32[]{:S(2)}, u32[]{:S(2)}) collective-permute-start(bf16[512,512]{1,0:T(8,128)(2,1)} %collective-permute-done.1), channel_id=1, source_target_pairs={{0,3},{1,0},{2,1},{3,2},{4,7},{5,4},{6,5},{7,6},{8,11},{9,8},{10,9... | collective-permute-start | bytes 1572872 | tf_op jit(solution)/shard_map/ppermute | solution.py:19
  20.5 2.9 %collective-permute-start.2 = (bf16[512,512]{1,0:T(8,128)(2,1)S(1)}, bf16[512,512]{1,0:T(8,128)(2,1)S(1)}, u32[]{:S(2)}, u32[]{:S(2)}) collective-permute-start(bf16[512,512]{1,0:T(8,128)(2,1)S(1)} %get-tuple-element.112), channel_id=1, source_target_pairs={{0,3},{1,0},{2,1},{3,2},{4,7},{5,4},{6,5},{7,6},{8,11},{9,8},{10,9... | collective-permute-start | bytes 1572872 | tf_op jit(solution)/shard_map/ppermute | solution.py:19
  23.4 9.4 %collective-permute-done.4 = bf16[512,512]{1,0:T(8,128)(2,1)S(1)} collective-permute-done((bf16[512,512]{1,0:T(8,128)(2,1)}, bf16[512,512]{1,0:T(8,128)(2,1)S(1)}, u32[]{:S(2)}, u32[]{:S(2)}) %collective-permute-start.4) | collective-permute-done | bytes 524320 | tf_op jit(solution)/shard_map/ppermute | solution.py:19
  34.5 1.8 %fusion.81 = f32[1024,512]{1,0:T(8,128)S(1)} fusion(bf16[1024,512]{1,0:T(8,128)(2,1)S(1)} %constant_dynamic-update-slice_fusion, bf16[2048,512]{1,0:T(8,128)(2,1)} %param.27, s32[]{:T(128)S(6)} %select_n.111), kind=kOutput, calls=%fused_computation.153 | convolution fusion | flops 536870912 | bytes 3670020 | tf_op jit(solution)/shard_map/dot_general | solution.py:47
  36.3 5.8 %collective-permute-done.3 = bf16[512,512]{1,0:T(8,128)(2,1)S(1)} collective-permute-done((bf16[512,512]{1,0:T(8,128)(2,1)S(1)}, bf16[512,512]{1,0:T(8,128)(2,1)S(1)}, u32[]{:S(2)}, u32[]{:S(2)}) %collective-permute-start.3) | collective-permute-done | bytes 524320 | tf_op jit(solution)/shard_map/ppermute | solution.py:19
  42.1 2.5 %convolution_add_fusion.3 = f32[1024,16]{0,1:T(8,128)S(1)} fusion(f32[1024,16]{0,1:T(8,128)S(1)} %fusion.163, bf16[512,16]{0,1:T(8,128)(2,1)S(1)} %get-tuple-element.140, bf16[512,16]{0,1:T(8,128)(2,1)S(1)} %get-tuple-element.139, bf16[512,16]{0,1:T(8,128)(2,1)S(1)} %get-tuple-element.138, bf16[512,512]{1,0:T(8,128)(2,1)S(1)} %collective-permute-done.3, ...), kind=kOutput, calls=%fused_computation.65 | convolution fusion | flops 66224128 | bytes 3325952 | tf_op jit(solution)/shard_map/dot_general | solution.py:46
  46.5 2.2 %fusion.17 = bf16[1024,256]{1,0:T(8,128)(2,1)S(1)} fusion(f32[1024,256]{1,0:T(8,128)S(1)} %fusion.120, bf16[512,256]{1,0:T(8,128)(2,1)S(1)} %get-tuple-element.108, bf16[512,256]{1,0:T(8,128)(2,1)S(1)} %get-tuple-element.107, bf16[512,256]{1,0:T(8,128)(2,1)S(1)} %get-tuple-element.106, bf16[512,512]{1,0:T(8,128)(2,1)S(1)} %collective-permute-done.3, ...), kind=kOutput, calls=%fused_computation.31 | convolution fusion | flops 823918592 | bytes 5505024 | tf_op jit(solution)/shard_map/dot_general | solution.py:46
  48.9 2.2 %fusion.16 = f32[1024,256]{1,0:T(8,128)S(1)} fusion(f32[1024,256]{1,0:T(8,128)S(1)} %fusion.122, bf16[512,256]{1,0:T(8,128)(2,1)S(1)} %get-tuple-element.163, bf16[512,256]{1,0:T(8,128)(2,1)S(1)} %get-tuple-element.164, bf16[512,256]{1,0:T(8,128)(2,1)S(1)} %get-tuple-element.165, bf16[512,512]{1,0:T(8,128)(2,1)S(1)} %collective-permute-done.3, ...), kind=kOutput, calls=%fused_computation.30 | convolution fusion | flops 824180736 | bytes 6029312 | tf_op jit(solution)/shard_map/dot_general | solution.py:46
  51.1 2.8 %multiply_convert_fusion.4 = (bf16[16,64,256]{2,0,1:T(8,128)(2,1)}, bf16[16,64,256]{2,0,1:T(8,128)(2,1)}, f32[16,64,256]{2,0,1:T(8,128)S(1)}, bf16[16,64,256]{2,0,1:T(8,128)(2,1)}, f32[16,64,256]{2,0,1:T(8,128)S(1)}) fusion(f32[16,64,256]{2,0,1:T(8,128)S(1)} %fusion.40, f32[16,64,256]{2,1,0:T(8,128)S(1)} %bitcast.314, f32[16,256]{1,0:T(8,128)S(1)} %get-tuple-element.105, ...), kind=kLoop, calls=%fused_computation.80 | loop fusion | flops 3145728 | bytes 6868992 | tf_op jit(solution)/shard_map/convert_element_type | solution.py:128
  54.5 3.4 %add_convert_fusion.1 = bf16[1024,512]{1,0:T(8,128)(2,1)S(1)} fusion(f32[1024,512]{1,0:T(8,128)S(1)} %fusion.81, bf16[512,512]{1,0:T(8,128)(2,1)S(1)} %get-tuple-element.99, bf16[512,512]{1,0:T(8,128)(2,1)S(1)} %get-tuple-element.98, bf16[512,512]{1,0:T(8,128)(2,1)S(1)} %get-tuple-element.97, bf16[512,512]{1,0:T(8,128)(2,1)S(1)} %collective-permute-done.3, ...), kind=kOutput, calls=%fused_computation.7 | convolution fusion | flops 1632108544 | bytes 7864320 | tf_op jit(solution)/shard_map/dot_general | solution.py:46
  57.9 5.7 %fusion.38 = f32[16,256,512]{2,1,0:T(8,128)} fusion(bf16[16,64,512]{2,1,0:T(8,128)(2,1)S(1)} %bitcast.315, f32[16,64,256]{2,0,1:T(8,128)S(1)} %get-tuple-element.100), kind=kOutput, calls=%fused_computation.70 | convolution fusion | flops 805306368 | bytes 10485760 | tf_op jit(solution)/shard_map/ncd,ncv->ndv/dot_general | solution.py:138
  63.9 3.7 %multiply_add_fusion.2 = (f32[1,256,512]{2,1,0:T(8,128)S(1)}, f32[1,256,512]{2,1,0:T(8,128)S(1)}, f32[1,256,512]{2,1,0:T(8,128)S(1)}, f32[1,256,512]{2,1,0:T(8,1...) fusion(f32[16,256,512]{2,1,0:T(8,128)} %fusion.38, ...), kind=kLoop, calls=%fused_computation.140 | loop fusion | flops 3538944 | bytes 11024384 | tf_op jit(solution)/shard_map/add | solution.py:152
  67.6 1.8 %copy-done.1 = f32[16,256,512]{2,1,0:T(8,128)S(1)} copy-done((f32[16,256,512]{2,1,0:T(8,128)S(1)}, f32[16,256,512]{2,1,0:T(8,128)}, u32[]{:S(2)}) %copy-start.1) | copy-done | bytes 8388632
  70.3 1.9 %collective-permute-start.6 = (bf16[258,512]{1,0:T(8,128)(2,1)S(1)}, bf16[258,512]{1,0:T(8,128)(2,1)S(1)}, u32[]{:S(2)}, u32[]{:S(2)}) collective-permute-start(bf16[258,512]{1,0:T(8,128)(2,1)S(1)} %pad_maximum_fusion.2), channel_id=1, source_target_pairs={{0,4},{4,8},{8,12},{12,16},{16,20},{20,24},{24,28},{28,32},{32,36}... | collective-permute-start | bytes 792584 | tf_op jit(solution)/shard_map/ppermute | solution.py:14
  72.2 4.0 %collective-permute-start.7 = (bf16[258,512]{1,0:T(8,128)(2,1)S(1)}, bf16[258,512]{1,0:T(8,128)(2,1)S(1)}, u32[]{:S(2)}, u32[]{:S(2)}) collective-permute-start(bf16[258,512]{1,0:T(8,128)(2,1)S(1)} %pad_maximum_fusion.2), channel_id=1, source_target_pairs={{0,8},{4,12},{8,16},{12,20},{16,24},{20,28},{24,32},{28,36},{32,40... | collective-permute-start | bytes 792584 | tf_op jit(solution)/shard_map/ppermute | solution.py:14
  81.4 2.3 %multiply_add_fusion.1 = f32[16,64,512]{2,1,0:T(8,128)} fusion(f32[16,64,512]{2,1,0:T(8,128)S(1)} %fusion.18, f32[16,64,64]{2,1,0:T(8,128)S(1)} %convolution_select_fusion, bf16[16,64,512]{2,1,0:T(8,128)(2,1)S(1)} %bitcast.316, f32[16,64]{1,0:T(8,128)S(1)} %compare_convert_fusion.1), kind=kOutput, calls=%fused_computation.6 | convolution fusion | flops 202375168 | bytes 5509120 | tf_op jit(solution)/shard_map/ncs,nsv->ncv/dot_general | solution.py:134
  90.3 2.8 %collective-permute-start.8 = (bf16[258,512]{1,0:T(8,128)(2,1)}, bf16[258,512]{1,0:T(8,128)(2,1)S(1)}, u32[]{:S(2)}, u32[]{:S(2)}) collective-permute-start(bf16[258,512]{1,0:T(8,128)(2,1)} %pad_maximum_fusion.3), channel_id=1, source_target_pairs={{0,8},{4,12},{8,16},{12,20},{16,24},{20,28},{24,32},{28,36},{32,40... | collective-permute-start | bytes 792584 | tf_op jit(solution)/shard_map/ppermute | solution.py:14
  93.1 3.2 %fusion.79 = f32[1024,512]{0,1:T(8,128)} fusion(bf16[1024,512]{1,0:T(8,128)(2,1)S(1)} %constant_dynamic-update-slice_fusion, bf16[2048,512]{1,0:T(8,128)(2,1)} %param.28, s32[]{:T(128)S(6)} %select_n.111), kind=kOutput, calls=%fused_computation.136 | convolution fusion | flops 536870912 | bytes 3670020 | tf_op jit(solution)/shard_map/dot_general | solution.py:47
  96.3 3.0 %copy.51 = f32[1024,512]{0,1:T(8,128)} copy(f32[1024,512]{1,0:T(8,128)} %bitcast.311) | data formatting | bytes 4194304 | tf_op jit(solution)/shard_map/reshape | solution.py:155
  99.9 3.7 %collective-permute-done.8 = bf16[258,512]{1,0:T(8,128)(2,1)S(1)} collective-permute-done((bf16[258,512]{1,0:T(8,128)(2,1)}, bf16[258,512]{1,0:T(8,128)(2,1)S(1)}, u32[]{:S(2)}, u32[]{:S(2)}) %collective-permute-start.8) | collective-permute-done | bytes 264224 | tf_op jit(solution)/shard_map/ppermute | solution.py:14
  105.7 3.1 %multiply_reduce_fusion = (f32[1024]{0:T(1024)S(1)}, f32[1024,512]{0,1:T(8,128)S(1)}) fusion(f32[1024,512]{0,1:T(8,128)} %copy.51, f32[1024]{0:T(1024)S(1)} %select_bitcast_fusion, f32[258,512]{1,0:T(8,128)S(1)} %convert_element_type.349, f32[256]{0:T(256)S(1)} %bitcast.359, f32[258,512]{1,0:T(8,128)S(1)} %copy-done.6, f32[256]{0:T(256)S(1)} %bitcast.357, ...), kind=kOutput, calls=%fused_computation.4 | convolution fusion | flops 272235520 | bytes 7874560 | tf_op jit(solution)/shard_map/dot_general | solution.py:187
  109.5 3.4 %multiply_convert_fusion = bf16[1024,512]{0,1:T(8,128)(2,1)S(1)} fusion(f32[1024,512]{0,1:T(8,128)S(1)} %copy-done.14, f32[1024,512]{0,1:T(8,128)S(1)} %get-tuple-element.162, bf16[512,512]{1,0:T(8,128)(2,1)S(1)} %copy-done.19, bf16[512,512]{1,0:T(8,128)(2,1)S(1)} %copy-done.18, bf16[512,512]{1,0:T(8,128)(2,1)S(1)} %copy-done.17, f32[512]{0:T(512)S(1)} %copy-done.29, ...), kind=kOutput, calls=%fused_computation.3 | convolution fusion | flops 1635778560 | bytes 9967616 | tf_op jit(solution)/shard_map/dot_general | solution.py:46
  113.9 2.9 %collective-permute-start.11 = (bf16[512,512]{1,0:T(8,128)(2,1)S(1)}, bf16[512,512]{1,0:T(8,128)(2,1)S(1)}, u32[]{:S(2)}, u32[]{:S(2)}) collective-permute-start(bf16[512,512]{1,0:T(8,128)(2,1)S(1)} %convolution_convert_fusion.3), channel_id=1, source_target_pairs={{0,3},{1,0},{2,1},{3,2},{4,7},{5,4},{6,5},{7,6},{8,11},{9,8},{10,9... | collective-permute-start | bytes 1572872 | tf_op jit(solution)/shard_map/ppermute | solution.py:19
  118.4 9.6 %collective-permute-done.11 = bf16[512,512]{1,0:T(8,128)(2,1)S(1)} collective-permute-done((bf16[512,512]{1,0:T(8,128)(2,1)S(1)}, bf16[512,512]{1,0:T(8,128)(2,1)S(1)}, u32[]{:S(2)}, u32[]{:S(2)}) %collective-permute-start.11) | collective-permute-done | bytes 524320 | tf_op jit(solution)/shard_map/ppermute | solution.py:19
  128.2 3.8 %collective-permute-start.12 = (bf16[1024,512]{1,0:T(8,128)(2,1)S(1)}, bf16[1024,512]{1,0:T(8,128)(2,1)S(1)}, u32[]{:S(2)}, u32[]{:S(2)}) collective-permute-start(bf16[1024,512]{1,0:T(8,128)(2,1)S(1)} %pad_maximum_fusion.1), channel_id=1, source_target_pairs={{0,3},{1,0},{2,1},{3,2},{4,7},{5,4},{6,5},{7,6},{8,11},{9,8},{10,9... | collective-permute-start | bytes 3145736 | tf_op jit(solution)/shard_map/ppermute | solution.py:19
  132.3 21.3 %collective-permute-done.12 = bf16[1024,512]{1,0:T(8,128)(2,1)S(1)} collective-permute-done((bf16[1024,512]{1,0:T(8,128)(2,1)S(1)}, bf16[1024,512]{1,0:T(8,128)(2,1)S(1)}, u32[]{:S(2)}, u32[]{:S(2)}) %collective-permute-start.12) | collective-permute-done | bytes 1048608 | tf_op jit(solution)/shard_map/ppermute | solution.py:19
  153.5 3.7 %collective-permute-done.10 = bf16[1024,512]{1,0:T(8,128)(2,1)S(1)} collective-permute-done((bf16[1024,512]{1,0:T(8,128)(2,1)S(1)}, bf16[1024,512]{1,0:T(8,128)(2,1)S(1)}, u32[]{:S(2)}, u32[]{:S(2)}) %collective-permute-start.10) | collective-permute-done | bytes 1048608 | tf_op jit(solution)/shard_map/ppermute | solution.py:19
  157.2 1.8 %add_convert_fusion = bf16[1024,512]{1,0:T(8,128)(2,1)} fusion(bf16[1024,512]{1,0:T(8,128)(2,1)S(1)} %collective-permute-done.12, bf16[1024,512]{1,0:T(8,128)(2,1)S(1)} %collective-permute-done.10, bf16[1024,512]{0,1:T(8,128)(2,1)S(1)} %multiply_convert_fusion, bf16[512,2048]{1,0:T(8,128)(2,1)S(1)} %copy-done, s32[]{:T(128)S(6)} %select_n.105), kind=kOutput, calls=%fused_computation.2 | convolution fusion | flops 540540928 | bytes 4718596 | tf_op jit(solution)/shard_map/dot_general | solution.py:60
  (157 shorter events, 28.4 us)
Async XLA Ops:
  0.0 112.9 %copy-start = (bf16[512,2048]{1,0:T(8,128)(2,1)S(1)}, bf16[512,2048]{1,0:T(8,128)(2,1)}, u32[]{:S(2)}) copy-start(bf16[512,2048]{1,0:T(8,128)(2,1)} %param.33) | copy-start | bytes 6291460
  0.0 4.7 %copy-start.23 = (s32[1024]{0:T(1024)S(1)}, s32[1024]{0:T(1024)}, u32[]{:S(2)}) copy-start(s32[1024]{0:T(1024)} %param.24) | copy-start | bytes 12292
  0.0 9.5 %copy-start.22 = (bf16[2048,16]{0,1:T(8,128)(2,1)S(1)}, bf16[2048,16]{0,1:T(8,128)(2,1)}, u32[]{:S(2)}) copy-start(bf16[2048,16]{0,1:T(8,128)(2,1)} %param.29) | copy-start | bytes 196612
  1.4 15.1 %collective-permute-start = (bf16[512,512]{1,0:T(8,128)(2,1)S(1)}, bf16[512,512]{1,0:T(8,128)(2,1)}, u32[]{:S(2)}, u32[]{:S(2)}) collective-permute-start(bf16[512,512]{1,0:T(8,128)(2,1)S(1)} %get-tuple-element.115), channel_id=1, source_target_pairs={{0,1},{1,2},{2,3},{3,0},{4,5},{5,6},{6,7},{7,4},{8,9},{9,10},{10,1... | collective-permute-start | bytes 1572872 | tf_op jit(solution)/shard_map/ppermute | solution.py:19
  3.1 13.5 %collective-permute-start.1 = (bf16[512,512]{1,0:T(8,128)(2,1)S(1)}, bf16[512,512]{1,0:T(8,128)(2,1)}, u32[]{:S(2)}, u32[]{:S(2)}) collective-permute-start(bf16[512,512]{1,0:T(8,128)(2,1)S(1)} %get-tuple-element.114), channel_id=1, source_target_pairs={{0,3},{1,0},{2,1},{3,2},{4,7},{5,4},{6,5},{7,6},{8,11},{9,8},{10,9... | collective-permute-start | bytes 1572872 | tf_op jit(solution)/shard_map/ppermute | solution.py:19
  11.4 8.5 %copy-start.15 = (bf16[2048,256]{1,0:T(8,128)(2,1)S(1)}, bf16[2048,256]{1,0:T(8,128)(2,1)}, u32[]{:S(2)}) copy-start(bf16[2048,256]{1,0:T(8,128)(2,1)} %param.25) | copy-start | bytes 3145732
  11.4 8.5 %copy-start.16 = (bf16[2048,256]{1,0:T(8,128)(2,1)S(1)}, bf16[2048,256]{1,0:T(8,128)(2,1)}, u32[]{:S(2)}) copy-start(bf16[2048,256]{1,0:T(8,128)(2,1)} %param.26) | copy-start | bytes 3145732
  12.7 7.4 %copy-start.8 = (bf16[1024,512]{1,0:T(8,128)(2,1)S(1)}, bf16[1024,512]{1,0:T(8,128)(2,1)}, u32[]{:S(2)}) copy-start(bf16[1024,512]{1,0:T(8,128)(2,1)} %param.23) | copy-start | bytes 3145732
  16.6 16.2 %collective-permute-start.4 = (bf16[512,512]{1,0:T(8,128)(2,1)}, bf16[512,512]{1,0:T(8,128)(2,1)S(1)}, u32[]{:S(2)}, u32[]{:S(2)}) collective-permute-start(bf16[512,512]{1,0:T(8,128)(2,1)} %collective-permute-done), channel_id=1, source_target_pairs={{0,1},{1,2},{2,3},{3,0},{4,5},{5,6},{6,7},{7,4},{8,9},{9,10},{10,1... | collective-permute-start | bytes 1572872 | tf_op jit(solution)/shard_map/ppermute | solution.py:19
  18.2 15.1 %collective-permute-start.5 = (bf16[512,512]{1,0:T(8,128)(2,1)}, bf16[512,512]{1,0:T(8,128)(2,1)S(1)}, u32[]{:S(2)}, u32[]{:S(2)}) collective-permute-start(bf16[512,512]{1,0:T(8,128)(2,1)} %collective-permute-done.1), channel_id=1, source_target_pairs={{0,3},{1,0},{2,1},{3,2},{4,7},{5,4},{6,5},{7,6},{8,11},{9,8},{10,9... | collective-permute-start | bytes 1572872 | tf_op jit(solution)/shard_map/ppermute | solution.py:19
  20.1 22.0 %collective-permute-start.3 = (bf16[512,512]{1,0:T(8,128)(2,1)S(1)}, bf16[512,512]{1,0:T(8,128)(2,1)S(1)}, u32[]{:S(2)}, u32[]{:S(2)}) collective-permute-start(bf16[512,512]{1,0:T(8,128)(2,1)S(1)} %get-tuple-element.113), channel_id=1, source_target_pairs={{0,1},{1,2},{2,3},{3,0},{4,5},{5,6},{6,7},{7,4},{8,9},{9,10},{10,1... | collective-permute-start | bytes 1572872 | tf_op jit(solution)/shard_map/ppermute | solution.py:19
  20.5 21.5 %collective-permute-start.2 = (bf16[512,512]{1,0:T(8,128)(2,1)S(1)}, bf16[512,512]{1,0:T(8,128)(2,1)S(1)}, u32[]{:S(2)}, u32[]{:S(2)}) collective-permute-start(bf16[512,512]{1,0:T(8,128)(2,1)S(1)} %get-tuple-element.112), channel_id=1, source_target_pairs={{0,3},{1,0},{2,1},{3,2},{4,7},{5,4},{6,5},{7,6},{8,11},{9,8},{10,9... | collective-permute-start | bytes 1572872 | tf_op jit(solution)/shard_map/ppermute | solution.py:19
  42.1 12.4 %copy-start.24 = (bf16[512,512]{1,0:T(8,128)(2,1)}, bf16[512,512]{1,0:T(8,128)(2,1)S(1)}, u32[]{:S(2)}) copy-start(bf16[512,512]{1,0:T(8,128)(2,1)S(1)} %collective-permute-done.3) | copy-start | bytes 1572868
  42.1 12.4 %copy-start.26 = (bf16[512,512]{1,0:T(8,128)(2,1)}, bf16[512,512]{1,0:T(8,128)(2,1)S(1)}, u32[]{:S(2)}) copy-start(bf16[512,512]{1,0:T(8,128)(2,1)S(1)} %collective-permute-done.2) | copy-start | bytes 1572868
  54.5 9.2 %copy-start.7 = (f32[16,64,256]{2,1,0:T(8,128)}, f32[16,64,256]{2,1,0:T(8,128)S(1)}, u32[]{:S(2)}) copy-start(f32[16,64,256]{2,1,0:T(8,128)S(1)} %copy.50) | copy-start | bytes 3145732
  57.9 5.8 %copy-start.11 = (bf16[1024,512]{1,0:T(8,128)(2,1)}, bf16[1024,512]{1,0:T(8,128)(2,1)S(1)}, u32[]{:S(2)}) copy-start(bf16[1024,512]{1,0:T(8,128)(2,1)S(1)} %add_convert_fusion.1) | copy-start | bytes 3145732
  63.9 5.6 %copy-start.1 = (f32[16,256,512]{2,1,0:T(8,128)S(1)}, f32[16,256,512]{2,1,0:T(8,128)}, u32[]{:S(2)}) copy-start(f32[16,256,512]{2,1,0:T(8,128)} %fusion.38) | copy-start | bytes 25165828
  69.4 6.8 %copy-start.2 = (bf16[16,64,256]{2,0,1:T(8,128)(2,1)S(1)}, bf16[16,64,256]{2,0,1:T(8,128)(2,1)}, u32[]{:S(2)}) copy-start(bf16[16,64,256]{2,0,1:T(8,128)(2,1)} %get-tuple-element.94) | copy-start | bytes 1572868
  70.3 13.4 %collective-permute-start.6 = (bf16[258,512]{1,0:T(8,128)(2,1)S(1)}, bf16[258,512]{1,0:T(8,128)(2,1)S(1)}, u32[]{:S(2)}, u32[]{:S(2)}) collective-permute-start(bf16[258,512]{1,0:T(8,128)(2,1)S(1)} %pad_maximum_fusion.2), channel_id=1, source_target_pairs={{0,4},{4,8},{8,12},{12,16},{16,20},{20,24},{24,28},{28,32},{32,36}... | collective-permute-start | bytes 792584 | tf_op jit(solution)/shard_map/ppermute | solution.py:14
  72.2 13.1 %collective-permute-start.7 = (bf16[258,512]{1,0:T(8,128)(2,1)S(1)}, bf16[258,512]{1,0:T(8,128)(2,1)S(1)}, u32[]{:S(2)}, u32[]{:S(2)}) collective-permute-start(bf16[258,512]{1,0:T(8,128)(2,1)S(1)} %pad_maximum_fusion.2), channel_id=1, source_target_pairs={{0,8},{4,12},{8,16},{12,20},{16,24},{20,28},{24,32},{28,36},{32,40... | collective-permute-start | bytes 792584 | tf_op jit(solution)/shard_map/ppermute | solution.py:14
  90.3 13.3 %collective-permute-start.8 = (bf16[258,512]{1,0:T(8,128)(2,1)}, bf16[258,512]{1,0:T(8,128)(2,1)S(1)}, u32[]{:S(2)}, u32[]{:S(2)}) collective-permute-start(bf16[258,512]{1,0:T(8,128)(2,1)} %pad_maximum_fusion.3), channel_id=1, source_target_pairs={{0,8},{4,12},{8,16},{12,20},{16,24},{20,28},{24,32},{28,36},{32,40... | collective-permute-start | bytes 792584 | tf_op jit(solution)/shard_map/ppermute | solution.py:14
  96.2 9.4 %copy-start.4 = (f32[258,512]{1,0:T(8,128)S(1)}, f32[258,512]{1,0:T(8,128)}, u32[]{:S(2)}) copy-start(f32[258,512]{1,0:T(8,128)} %copy-done.3) | copy-start | bytes 1585156
  96.3 9.4 %copy-start.6 = (f32[258,512]{1,0:T(8,128)S(1)}, f32[258,512]{1,0:T(8,128)}, u32[]{:S(2)}) copy-start(f32[258,512]{1,0:T(8,128)} %copy-done.5) | copy-start | bytes 1585156
  105.7 3.4 %copy-start.18 = (bf16[512,512]{1,0:T(8,128)(2,1)S(1)}, bf16[512,512]{1,0:T(8,128)(2,1)}, u32[]{:S(2)}) copy-start(bf16[512,512]{1,0:T(8,128)(2,1)} %get-tuple-element.91) | copy-start | bytes 1572868
  105.7 3.5 %copy-start.19 = (bf16[512,512]{1,0:T(8,128)(2,1)S(1)}, bf16[512,512]{1,0:T(8,128)(2,1)}, u32[]{:S(2)}) copy-start(bf16[512,512]{1,0:T(8,128)(2,1)} %get-tuple-element.92) | copy-start | bytes 1572868
  105.7 3.7 %copy-start.25 = (bf16[512,512]{1,0:T(8,128)(2,1)S(1)}, bf16[512,512]{1,0:T(8,128)(2,1)}, u32[]{:S(2)}) copy-start(bf16[512,512]{1,0:T(8,128)(2,1)} %copy-done.24) | copy-start | bytes 1572868
  105.7 3.8 %copy-start.27 = (bf16[512,512]{1,0:T(8,128)(2,1)S(1)}, bf16[512,512]{1,0:T(8,128)(2,1)}, u32[]{:S(2)}) copy-start(bf16[512,512]{1,0:T(8,128)(2,1)} %copy-done.26) | copy-start | bytes 1572868
  105.7 3.8 %copy-start.29 = (f32[512]{0:T(512)S(1)}, f32[512]{0:T(512)}, u32[]{:S(2)}) copy-start(f32[512]{0:T(512)} %param.32) | copy-start | bytes 6148
  113.9 14.1 %collective-permute-start.11 = (bf16[512,512]{1,0:T(8,128)(2,1)S(1)}, bf16[512,512]{1,0:T(8,128)(2,1)S(1)}, u32[]{:S(2)}, u32[]{:S(2)}) collective-permute-start(bf16[512,512]{1,0:T(8,128)(2,1)S(1)} %convolution_convert_fusion.3), channel_id=1, source_target_pairs={{0,3},{1,0},{2,1},{3,2},{4,7},{5,4},{6,5},{7,6},{8,11},{9,8},{10,9... | collective-permute-start | bytes 1572872 | tf_op jit(solution)/shard_map/ppermute | solution.py:19
  116.8 15.2 %collective-permute-start.9 = (bf16[512,512]{1,0:T(8,128)(2,1)S(1)}, bf16[512,512]{1,0:T(8,128)(2,1)S(1)}, u32[]{:S(2)}, u32[]{:S(2)}) collective-permute-start(bf16[512,512]{1,0:T(8,128)(2,1)S(1)} %convolution_convert_fusion.4), channel_id=1, source_target_pairs={{0,1},{1,2},{2,3},{3,0},{4,5},{5,6},{6,7},{7,4},{8,9},{9,10},{10,1... | collective-permute-start | bytes 1572872 | tf_op jit(solution)/shard_map/ppermute | solution.py:19
  128.2 25.3 %collective-permute-start.12 = (bf16[1024,512]{1,0:T(8,128)(2,1)S(1)}, bf16[1024,512]{1,0:T(8,128)(2,1)S(1)}, u32[]{:S(2)}, u32[]{:S(2)}) collective-permute-start(bf16[1024,512]{1,0:T(8,128)(2,1)S(1)} %pad_maximum_fusion.1), channel_id=1, source_target_pairs={{0,3},{1,0},{2,1},{3,2},{4,7},{5,4},{6,5},{7,6},{8,11},{9,8},{10,9... | collective-permute-start | bytes 3145736 | tf_op jit(solution)/shard_map/ppermute | solution.py:19
  132.2 25.0 %collective-permute-start.10 = (bf16[1024,512]{1,0:T(8,128)(2,1)S(1)}, bf16[1024,512]{1,0:T(8,128)(2,1)S(1)}, u32[]{:S(2)}, u32[]{:S(2)}) collective-permute-start(bf16[1024,512]{1,0:T(8,128)(2,1)S(1)} %pad_maximum_fusion), channel_id=1, source_target_pairs={{0,1},{1,2},{2,3},{3,0},{4,5},{5,6},{6,7},{7,4},{8,9},{9,10},{10,1... | collective-permute-start | bytes 3145736 | tf_op jit(solution)/shard_map/ppermute | solution.py:19
  (12 other events, 24.8 us)

commit v17 on v14

--- a/solution.py
+++ b/solution.py
@@ -21,14 +21,9 @@
 
 def gathered(local):
     half = local.shape[0] // 2
-    left_a = ring(local[:half], 1)
-    right_a = ring(local[half:], -1)
-    left_a, right_a, rest = lax.optimization_barrier((left_a, right_a, local))
-    left_b = ring(rest[half:], 1)
-    right_b = ring(rest[:half], -1)
-    far = jnp.concatenate([ring(left_a, 1), ring(right_a, -1)])
-    from_left = jnp.concatenate([left_a, left_b])
-    from_right = jnp.concatenate([right_b, right_a])
+    from_left = ring(local, 1)
+    from_right = ring(local, -1)
+    far = jnp.concatenate([ring(from_left[:half], 1), ring(from_right[half:], -1)])
     return jnp.concatenate([local, from_right, from_left], axis=1), far
 
 

time: 159 us -> 162 us (1.019)
  local copies, waits for them, and re-layouts: 18.6 us -> 31.6 us
  matrix products: 39.9 us -> 35.5 us
  waiting for transfers between devices: 59 us -> 55.2 us
  starting transfers between devices: 25.4 us -> 23.2 us
    unnamed x63 -> x73, local copies, waits for them, and re-layouts: 4.14 us -> 11.7 us
    dot_general x5, matrix products: 13.6 us -> 7.18 us  [projected(): out = jnp.dot(near, near_rows, preferred_element_type=jnp.float32)]
    ppermute x10 -> x8, waiting for transfers between devices: 54.3 us -> 50.9 us  [ring(): lax.ppermute(x, 'tensor', [(i, (i + step) % size) for i in range(size)])]
    ppermute x10 -> x8, starting transfers between devices: 16.7 us -> 14.1 us  [ring(): lax.ppermute(x, 'tensor', [(i, (i + step) % size) for i in range(size)])]
    concatenate x1 -> x2, local copies, waits for them, and re-layouts: 0.03 us -> 2.17 us  [the longest x1 1.09 us: gathered(): return (jnp.concatenate([local, from_right, from_left], axis=1), far)]
    dot_general x5, matrix products: 6.15 us -> 8.19 us  [projected(): jnp.dot(far, rows(2), preferred_element_type=jnp.float32)]
    dynamic_slice x4, local copies, waits for them, and re-layouts: 2.96 us -> 4.98 us  [rows(): lax.dynamic_slice_in_dim(weight, (index + offset) % size * width, width, 0)]
  transfers between devices with their start and end apart: 13 -> 11, of which waited for: 9 -> 8; matrix products, arithmetic and copies ran while one was open for 15% -> 21% of each run, Pallas kernels for 0% -> 0%
where the time goes in v17:
time: 162 us
  waiting for transfers between devices  55.2 us (34%)
  matrix products  35.5 us (22%)
  local copies, waits for them, and re-layouts  31.6 us (20%)
  starting transfers between devices  23.2 us (14%)
  other arithmetic  10.4 us (6%)
  between operations  5.79 us (4%)
    ppermute x8, waiting for transfers between devices, ring(): lax.ppermute(x, 'tensor', [(i, (i + step) % size) for i in range(size)])  50.9 us
    ppermute x8, starting transfers between devices, ring(): lax.ppermute(x, 'tensor', [(i, (i + step) % size) for i in range(size)])  14.1 us
    unnamed x73, local copies, waits for them, and re-layouts  11.7 us
    ppermute x3, starting transfers between devices, shifted(): return lax.ppermute(x, axis, pairs)  9.06 us
    dot_general x5, matrix products, projected(): jnp.dot(far, rows(2), preferred_element_type=jnp.float32)  8.19 us
    dot_general x5, matrix products, projected(): out = jnp.dot(near, near_rows, preferred_element_type=jnp.float32)  7.18 us
    dot_general x1, matrix products, body(): jnp.einsum('ncd,ncv->ndv', k_decayed, v_float, precision=HIGH)  5.74 us
    dynamic_slice x4, local copies, waits for them, and re-layouts, rows(): lax.dynamic_slice_in_dim(weight, (index + offset) % size * width, width, 0)  4.98 us
  transfers between devices with their start and end apart: 11, of which 8 were waited for; matrix products, arithmetic and copies ran while one was open for 21% of the time, Pallas kernels for 0%

profile of v17, /device:TPU:2, one launch (start us, length us, event | category | flops | bytes accessed | tf_op | source)
XLA Modules:
  0.0 161.7 jit_solution(13177699119494883810)
XLA Ops:
  0.0 1.6 collective-permute-start.1
  1.6 1.7 %collective-permute-start = (bf16[1024,512]{1,0:T(8,128)(2,1)}, bf16[1024,512]{1,0:T(8,128)(2,1)}, u32[]{:S(2)}, u32[]{:S(2)}) collective-permute-start(bf16[1024,512]{1,0:T(8,128)(2,1)} %param.23), channel_id=1, source_target_pairs={{0,3},{1,0},{2,1},{3,2},{4,7},{5,4},{6,5},{7,6},{8,11},{9,8},{10,9... | collective-permute-start | bytes 3145736 | tf_op jit(solution)/shard_map/ppermute | solution.py:19
  3.2 2.4 %constant_dynamic-update-slice_fusion.2 = bf16[1024,1536]{1,0:T(8,128)(2,1)} fusion(bf16[1024,512]{1,0:T(8,128)(2,1)} %param.23), kind=kLoop, calls=%fused_computation.199 | loop fusion | bytes 2097152
  7.0 2.7 %constant_dynamic-slice_fusion.5 = (bf16[512,512]{1,0:T(8,128)(2,1)}, bf16[512,512]{1,0:T(8,128)(2,1)}, bf16[512,512]{1,0:T(8,128)(2,1)}) fusion(bf16[2048,512]{1,0:T(8,128)(2,1)} %param.27, s32[]{:T(128)S(6)} %select_n.105, s32[]{:T(128)S(6)} %select_n.107, s32[]{:T(128)S(6)} %select_n.109), kind=kLoop, calls=%fused_computation.258 | loop fusion | bytes 3145740 | tf_op jit(solution)/shard_map/dynamic_slice | solution.py:38
  13.1 13.3 %collective-permute-done.1 = bf16[1024,512]{1,0:T(8,128)(2,1)S(1)} collective-permute-done((bf16[1024,512]{1,0:T(8,128)(2,1)}, bf16[1024,512]{1,0:T(8,128)(2,1)S(1)}, u32[]{:S(2)}, u32[]{:S(2)}) %collective-permute-start.1) | collective-permute-done | bytes 1048608 | tf_op jit(solution)/shard_map/ppermute | solution.py:19
  27.5 1.9 %slice.478 = bf16[512,512]{1,0:T(8,128)(2,1)} slice(bf16[1024,512]{1,0:T(8,128)(2,1)} %collective-permute-done), slice={[512:1024], [0:512]} | slice | bytes 1048576 | tf_op jit(solution)/shard_map/slice | solution.py:26
  29.4 2.9 %collective-permute-start.3 = (bf16[512,512]{1,0:T(8,128)(2,1)}, bf16[512,512]{1,0:T(8,128)(2,1)}, u32[]{:S(2)}, u32[]{:S(2)}) collective-permute-start(bf16[512,512]{1,0:T(8,128)(2,1)} %slice.478), channel_id=1, source_target_pairs={{0,3},{1,0},{2,1},{3,2},{4,7},{5,4},{6,5},{7,6},{8,11},{9,8},{10,9... | collective-permute-start | bytes 1572872 | tf_op jit(solution)/shard_map/ppermute | solution.py:19
  35.7 2.3 %constant_dynamic-update-slice_fusion.1 = bf16[1024,1536]{1,0:T(8,128)(2,1)} fusion(bf16[1024,1536]{1,0:T(8,128)(2,1)} %constant_dynamic-update-slice_fusion.2, bf16[1024,512]{1,0:T(8,128)(2,1)} %collective-permute-done), kind=kLoop, calls=%fused_computation.198 | loop fusion | bytes 2097152
  39.1 2.5 %collective-permute-done.2 = bf16[512,512]{1,0:T(8,128)(2,1)} collective-permute-done((bf16[512,512]{1,0:T(8,128)(2,1)}, bf16[512,512]{1,0:T(8,128)(2,1)}, u32[]{:S(2)}, u32[]{:S(2)}) %collective-permute-start.2) | collective-permute-done | bytes 524320 | tf_op jit(solution)/shard_map/ppermute | solution.py:19
  44.2 1.4 fusion.119
  45.6 1.4 fusion.117
  47.0 1.9 %fusion.80 = f32[1024,512]{1,0:T(8,128)S(1)} fusion(bf16[1024,512]{1,0:T(8,128)(2,1)S(1)} %constant_dynamic-update-slice_fusion.3, bf16[2048,512]{1,0:T(8,128)(2,1)} %param.27, s32[]{:T(128)S(6)} %select_n.111), kind=kOutput, calls=%fused_computation.150 | convolution fusion | flops 536870912 | bytes 3670020 | tf_op jit(solution)/shard_map/dot_general | solution.py:42
  54.2 2.6 %multiply_convert_fusion.4 = (bf16[16,64,256]{2,0,1:T(8,128)(2,1)}, bf16[16,64,256]{2,0,1:T(8,128)(2,1)}, f32[16,64,256]{2,0,1:T(8,128)S(1)}, bf16[16,64,256]{2,0,1:T(8,128)(2,1)}, f32[16,64,256]{2,0,1:T(8,128)S(1)}) fusion(f32[16,64,256]{2,0,1:T(8,128)S(1)} %fusion.40, f32[16,64,256]{2,1,0:T(8,128)S(1)} %bitcast.320, f32[16,256]{1,0:T(8,128)S(1)} %get-tuple-element.101, ...), kind=kLoop, calls=%fused_computation.78 | loop fusion | flops 3145728 | bytes 6868992 | tf_op jit(solution)/shard_map/convert_element_type | solution.py:121
  58.2 1.8 %add_convert_fusion.1 = bf16[1024,512]{1,0:T(8,128)(2,1)S(1)} fusion(f32[1024,512]{1,0:T(8,128)S(1)} %fusion.80, bf16[1024,1536]{1,0:T(8,128)(2,1)S(1)} %copy-done.2, bf16[512,512]{1,0:T(8,128)(2,1)S(1)} %copy-done.22, bf16[512,512]{1,0:T(8,128)(2,1)S(1)} %copy-done.21, bf16[512,512]{1,0:T(8,128)(2,1)S(1)} %copy-done.20), kind=kOutput, calls=%fused_computation.6 | convolution fusion | flops 1616379904 | bytes 7864320 | tf_op jit(solution)/shard_map/dot_general | solution.py:41
  60.0 5.7 %fusion.38 = f32[16,256,512]{2,1,0:T(8,128)} fusion(bf16[16,64,512]{2,1,0:T(8,128)(2,1)S(1)} %bitcast.321, f32[16,64,256]{2,0,1:T(8,128)S(1)} %get-tuple-element.94), kind=kOutput, calls=%fused_computation.68 | convolution fusion | flops 805306368 | bytes 10485760 | tf_op jit(solution)/shard_map/ncd,ncv->ndv/dot_general | solution.py:131
  65.9 3.7 %multiply_add_fusion.2 = (f32[1,256,512]{2,1,0:T(8,128)S(1)}, f32[1,256,512]{2,1,0:T(8,128)S(1)}, f32[1,256,512]{2,1,0:T(8,128)S(1)}, f32[1,256,512]{2,1,0:T(8,1...) fusion(f32[16,256,512]{2,1,0:T(8,128)} %fusion.38, ...), kind=kLoop, calls=%fused_computation.137 | loop fusion | flops 3538944 | bytes 11024384 | tf_op jit(solution)/shard_map/add | solution.py:145
  69.6 1.8 %copy-done.1 = f32[16,256,512]{2,1,0:T(8,128)S(1)} copy-done((f32[16,256,512]{2,1,0:T(8,128)S(1)}, f32[16,256,512]{2,1,0:T(8,128)}, u32[]{:S(2)}) %copy-start.1) | copy-done | bytes 8388632
  72.3 1.9 %collective-permute-start.4 = (bf16[258,512]{1,0:T(8,128)(2,1)S(1)}, bf16[258,512]{1,0:T(8,128)(2,1)S(1)}, u32[]{:S(2)}, u32[]{:S(2)}) collective-permute-start(bf16[258,512]{1,0:T(8,128)(2,1)S(1)} %pad_maximum_fusion.2), channel_id=1, source_target_pairs={{0,4},{4,8},{8,12},{12,16},{16,20},{20,24},{24,28},{28,32},{32,36}... | collective-permute-start | bytes 792584 | tf_op jit(solution)/shard_map/ppermute | solution.py:14
  74.3 4.1 %collective-permute-start.5 = (bf16[258,512]{1,0:T(8,128)(2,1)S(1)}, bf16[258,512]{1,0:T(8,128)(2,1)S(1)}, u32[]{:S(2)}, u32[]{:S(2)}) collective-permute-start(bf16[258,512]{1,0:T(8,128)(2,1)S(1)} %pad_maximum_fusion.2), channel_id=1, source_target_pairs={{0,8},{4,12},{8,16},{12,20},{16,24},{20,28},{24,32},{28,36},{32,40... | collective-permute-start | bytes 792584 | tf_op jit(solution)/shard_map/ppermute | solution.py:14
  83.5 2.3 %multiply_add_fusion.1 = f32[16,64,512]{2,1,0:T(8,128)} fusion(f32[16,64,512]{2,1,0:T(8,128)S(1)} %fusion.18, f32[16,64,64]{2,1,0:T(8,128)S(1)} %convolution_select_fusion, bf16[16,64,512]{2,1,0:T(8,128)(2,1)S(1)} %bitcast.322, f32[16,64]{1,0:T(8,128)S(1)} %compare_convert_fusion.1), kind=kOutput, calls=%fused_computation.5 | convolution fusion | flops 202375168 | bytes 5509120 | tf_op jit(solution)/shard_map/ncs,nsv->ncv/dot_general | solution.py:127
  92.1 3.1 %collective-permute-start.6 = (bf16[258,512]{1,0:T(8,128)(2,1)}, bf16[258,512]{1,0:T(8,128)(2,1)S(1)}, u32[]{:S(2)}, u32[]{:S(2)}) collective-permute-start(bf16[258,512]{1,0:T(8,128)(2,1)} %pad_maximum_fusion.3), channel_id=1, source_target_pairs={{0,8},{4,12},{8,16},{12,20},{16,24},{20,28},{24,32},{28,36},{32,40... | collective-permute-start | bytes 792584 | tf_op jit(solution)/shard_map/ppermute | solution.py:14
  95.2 3.1 %fusion.78 = f32[1024,512]{0,1:T(8,128)} fusion(bf16[1024,512]{1,0:T(8,128)(2,1)S(1)} %constant_dynamic-update-slice_fusion.3, bf16[2048,512]{1,0:T(8,128)(2,1)} %param.28, s32[]{:T(128)S(6)} %select_n.111), kind=kOutput, calls=%fused_computation.133 | convolution fusion | flops 536870912 | bytes 3670020 | tf_op jit(solution)/shard_map/dot_general | solution.py:42
  98.3 3.0 %copy.51 = f32[1024,512]{0,1:T(8,128)} copy(f32[1024,512]{1,0:T(8,128)} %bitcast.317) | data formatting | bytes 4194304 | tf_op jit(solution)/shard_map/reshape | solution.py:148
  102.1 3.5 %collective-permute-done.6 = bf16[258,512]{1,0:T(8,128)(2,1)S(1)} collective-permute-done((bf16[258,512]{1,0:T(8,128)(2,1)}, bf16[258,512]{1,0:T(8,128)(2,1)S(1)}, u32[]{:S(2)}, u32[]{:S(2)}) %collective-permute-start.6) | collective-permute-done | bytes 264224 | tf_op jit(solution)/shard_map/ppermute | solution.py:14
  107.6 3.1 %multiply_reduce_fusion = (f32[1024]{0:T(1024)S(1)}, f32[1024,512]{0,1:T(8,128)S(1)}) fusion(f32[1024,512]{0,1:T(8,128)} %copy.51, f32[1024]{0:T(1024)S(1)} %select_bitcast_fusion, f32[258,512]{1,0:T(8,128)S(1)} %convert_element_type.346, f32[256]{0:T(256)S(1)} %bitcast.365, f32[258,512]{1,0:T(8,128)S(1)} %copy-done.8, f32[256]{0:T(256)S(1)} %bitcast.363, ...), kind=kOutput, calls=%fused_computation.3 | convolution fusion | flops 272235520 | bytes 7874560 | tf_op jit(solution)/shard_map/dot_general | solution.py:180
  111.7 2.5 %multiply_convert_fusion = bf16[1024,512]{0,1:T(8,128)(2,1)S(1)} fusion(f32[1024,512]{0,1:T(8,128)S(1)} %copy-done.14, f32[1024,512]{0,1:T(8,128)S(1)} %get-tuple-element.154, bf16[1024,1536]{1,0:T(8,128)(2,1)S(1)} %copy-done.3, bf16[512,512]{1,0:T(8,128)(2,1)S(1)} %copy-done.19, bf16[512,512]{1,0:T(8,128)(2,1)S(1)} %copy-done.18, ...), kind=kOutput, calls=%fused_computation.2 | convolution fusion | flops 1620049920 | bytes 9967616 | tf_op jit(solution)/shard_map/dot_general | solution.py:41
  115.1 3.8 %collective-permute-start.9 = (bf16[512,512]{1,0:T(8,128)(2,1)S(1)}, bf16[512,512]{1,0:T(8,128)(2,1)S(1)}, u32[]{:S(2)}, u32[]{:S(2)}) collective-permute-start(bf16[512,512]{1,0:T(8,128)(2,1)S(1)} %get-tuple-element.97), channel_id=1, source_target_pairs={{0,3},{1,0},{2,1},{3,2},{4,7},{5,4},{6,5},{7,6},{8,11},{9,8},{10,9... | collective-permute-start | bytes 1572872 | tf_op jit(solution)/shard_map/ppermute | solution.py:19
  120.5 9.8 %collective-permute-done.9 = bf16[512,512]{1,0:T(8,128)(2,1)S(1)} collective-permute-done((bf16[512,512]{1,0:T(8,128)(2,1)S(1)}, bf16[512,512]{1,0:T(8,128)(2,1)S(1)}, u32[]{:S(2)}, u32[]{:S(2)}) %collective-permute-start.9) | collective-permute-done | bytes 524320 | tf_op jit(solution)/shard_map/ppermute | solution.py:19
  130.5 3.8 %collective-permute-start.10 = (bf16[1024,512]{1,0:T(8,128)(2,1)S(1)}, bf16[1024,512]{1,0:T(8,128)(2,1)S(1)}, u32[]{:S(2)}, u32[]{:S(2)}) collective-permute-start(bf16[1024,512]{1,0:T(8,128)(2,1)S(1)} %pad_maximum_fusion.1), channel_id=1, source_target_pairs={{0,3},{1,0},{2,1},{3,2},{4,7},{5,4},{6,5},{7,6},{8,11},{9,8},{10,9... | collective-permute-start | bytes 3145736 | tf_op jit(solution)/shard_map/ppermute | solution.py:19
  134.6 21.5 %collective-permute-done.10 = bf16[1024,512]{1,0:T(8,128)(2,1)S(1)} collective-permute-done((bf16[1024,512]{1,0:T(8,128)(2,1)S(1)}, bf16[1024,512]{1,0:T(8,128)(2,1)S(1)}, u32[]{:S(2)}, u32[]{:S(2)}) %collective-permute-start.10) | collective-permute-done | bytes 1048608 | tf_op jit(solution)/shard_map/ppermute | solution.py:19
  156.1 3.7 %collective-permute-done.8 = bf16[1024,512]{1,0:T(8,128)(2,1)S(1)} collective-permute-done((bf16[1024,512]{1,0:T(8,128)(2,1)S(1)}, bf16[1024,512]{1,0:T(8,128)(2,1)S(1)}, u32[]{:S(2)}, u32[]{:S(2)}) %collective-permute-start.8) | collective-permute-done | bytes 1048608 | tf_op jit(solution)/shard_map/ppermute | solution.py:19
  159.8 1.8 %add_convert_fusion = bf16[1024,512]{1,0:T(8,128)(2,1)} fusion(bf16[1024,512]{1,0:T(8,128)(2,1)S(1)} %collective-permute-done.10, bf16[1024,512]{1,0:T(8,128)(2,1)S(1)} %collective-permute-done.8, bf16[1024,512]{0,1:T(8,128)(2,1)S(1)} %multiply_convert_fusion, bf16[512,2048]{1,0:T(8,128)(2,1)S(1)} %copy-done, s32[]{:T(128)S(6)} %select_n.105), kind=kOutput, calls=%fused_computation.1 | convolution fusion | flops 540540928 | bytes 4718596 | tf_op jit(solution)/shard_map/dot_general | solution.py:55
  (164 shorter events, 33.2 us)
Async XLA Ops:
  0.0 114.2 %copy-start = (bf16[512,2048]{1,0:T(8,128)(2,1)S(1)}, bf16[512,2048]{1,0:T(8,128)(2,1)}, u32[]{:S(2)}) copy-start(bf16[512,2048]{1,0:T(8,128)(2,1)} %param.33) | copy-start | bytes 6291460
  0.0 5.6 %copy-start.31 = (s32[1024]{0:T(1024)S(1)}, s32[1024]{0:T(1024)}, u32[]{:S(2)}) copy-start(s32[1024]{0:T(1024)} %param.24) | copy-start | bytes 12292
  0.0 26.4 %collective-permute-start.1 = (bf16[1024,512]{1,0:T(8,128)(2,1)}, bf16[1024,512]{1,0:T(8,128)(2,1)S(1)}, u32[]{:S(2)}, u32[]{:S(2)}) collective-permute-start(bf16[1024,512]{1,0:T(8,128)(2,1)} %param.23), channel_id=1, source_target_pairs={{0,1},{1,2},{2,3},{3,0},{4,5},{5,6},{6,7},{7,4},{8,9},{9,10},{10,1... | collective-permute-start | bytes 3145736 | tf_op jit(solution)/shard_map/ppermute | solution.py:19
  1.6 26.0 %collective-permute-start = (bf16[1024,512]{1,0:T(8,128)(2,1)}, bf16[1024,512]{1,0:T(8,128)(2,1)}, u32[]{:S(2)}, u32[]{:S(2)}) collective-permute-start(bf16[1024,512]{1,0:T(8,128)(2,1)} %param.23), channel_id=1, source_target_pairs={{0,3},{1,0},{2,1},{3,2},{4,7},{5,4},{6,5},{7,6},{8,11},{9,8},{10,9... | collective-permute-start | bytes 3145736 | tf_op jit(solution)/shard_map/ppermute | solution.py:19
  7.0 2.7 %copy-start.13 = (bf16[2048,512]{1,0:T(8,128)(2,1)S(1)}, bf16[2048,512]{1,0:T(8,128)(2,1)}, u32[]{:S(2)}) copy-start(bf16[2048,512]{1,0:T(8,128)(2,1)} %param.28) | copy-start | bytes 6291460
  9.8 2.1 %copy-start.16 = (bf16[2048,256]{1,0:T(8,128)(2,1)S(1)}, bf16[2048,256]{1,0:T(8,128)(2,1)}, u32[]{:S(2)}) copy-start(bf16[2048,256]{1,0:T(8,128)(2,1)} %param.26) | copy-start | bytes 3145732
  11.9 23.8 %copy-start.30 = (bf16[2048,16]{0,1:T(8,128)(2,1)S(1)}, bf16[2048,16]{0,1:T(8,128)(2,1)}, u32[]{:S(2)}) copy-start(bf16[2048,16]{0,1:T(8,128)(2,1)} %param.29) | copy-start | bytes 196612
  27.2 14.4 %collective-permute-start.2 = (bf16[512,512]{1,0:T(8,128)(2,1)}, bf16[512,512]{1,0:T(8,128)(2,1)}, u32[]{:S(2)}, u32[]{:S(2)}) collective-permute-start(bf16[512,512]{1,0:T(8,128)(2,1)} %slice.477), channel_id=1, source_target_pairs={{0,1},{1,2},{2,3},{3,0},{4,5},{5,6},{6,7},{7,4},{8,9},{9,10},{10,1... | collective-permute-start | bytes 1572872 | tf_op jit(solution)/shard_map/ppermute | solution.py:19
  29.4 13.4 %collective-permute-start.3 = (bf16[512,512]{1,0:T(8,128)(2,1)}, bf16[512,512]{1,0:T(8,128)(2,1)}, u32[]{:S(2)}, u32[]{:S(2)}) collective-permute-start(bf16[512,512]{1,0:T(8,128)(2,1)} %slice.478), channel_id=1, source_target_pairs={{0,3},{1,0},{2,1},{3,2},{4,7},{5,4},{6,5},{7,6},{8,11},{9,8},{10,9... | collective-permute-start | bytes 1572872 | tf_op jit(solution)/shard_map/ppermute | solution.py:19
  47.0 2.0 %copy-start.2 = (bf16[1024,1536]{1,0:T(8,128)(2,1)S(1)}, bf16[1024,1536]{1,0:T(8,128)(2,1)}, u32[]{:S(2)}) copy-start(bf16[1024,1536]{1,0:T(8,128)(2,1)} %constant_dynamic-update-slice_fusion) | copy-start | bytes 9437188
  50.0 1.9 %copy-start.27 = (bf16[512,256]{1,0:T(8,128)(2,1)S(1)}, bf16[512,256]{1,0:T(8,128)(2,1)}, u32[]{:S(2)}) copy-start(bf16[512,256]{1,0:T(8,128)(2,1)} %get-tuple-element.102) | copy-start | bytes 786436
  50.0 1.9 %copy-start.28 = (bf16[512,256]{1,0:T(8,128)(2,1)S(1)}, bf16[512,256]{1,0:T(8,128)(2,1)}, u32[]{:S(2)}) copy-start(bf16[512,256]{1,0:T(8,128)(2,1)} %get-tuple-element.103) | copy-start | bytes 786436
  54.2 2.6 %copy-start.10 = (f32[1024,256]{1,0:T(8,128)}, f32[1024,256]{1,0:T(8,128)S(1)}, u32[]{:S(2)}) copy-start(f32[1024,256]{1,0:T(8,128)S(1)} %fusion.16) | copy-start | bytes 3145732
  57.4 8.3 %copy-start.9 = (f32[16,64,256]{2,1,0:T(8,128)}, f32[16,64,256]{2,1,0:T(8,128)S(1)}, u32[]{:S(2)}) copy-start(f32[16,64,256]{2,1,0:T(8,128)S(1)} %copy.50) | copy-start | bytes 3145732
  59.9 5.8 %copy-start.11 = (bf16[1024,512]{1,0:T(8,128)(2,1)}, bf16[1024,512]{1,0:T(8,128)(2,1)S(1)}, u32[]{:S(2)}) copy-start(bf16[1024,512]{1,0:T(8,128)(2,1)S(1)} %add_convert_fusion.1) | copy-start | bytes 3145732
  65.9 5.6 %copy-start.1 = (f32[16,256,512]{2,1,0:T(8,128)S(1)}, f32[16,256,512]{2,1,0:T(8,128)}, u32[]{:S(2)}) copy-start(f32[16,256,512]{2,1,0:T(8,128)} %fusion.38) | copy-start | bytes 25165828
  71.5 6.9 %copy-start.4 = (bf16[16,64,256]{2,0,1:T(8,128)(2,1)S(1)}, bf16[16,64,256]{2,0,1:T(8,128)(2,1)}, u32[]{:S(2)}) copy-start(bf16[16,64,256]{2,0,1:T(8,128)(2,1)} %get-tuple-element.88) | copy-start | bytes 1572868
  72.3 13.4 %collective-permute-start.4 = (bf16[258,512]{1,0:T(8,128)(2,1)S(1)}, bf16[258,512]{1,0:T(8,128)(2,1)S(1)}, u32[]{:S(2)}, u32[]{:S(2)}) collective-permute-start(bf16[258,512]{1,0:T(8,128)(2,1)S(1)} %pad_maximum_fusion.2), channel_id=1, source_target_pairs={{0,4},{4,8},{8,12},{12,16},{16,20},{20,24},{24,28},{28,32},{32,36}... | collective-permute-start | bytes 792584 | tf_op jit(solution)/shard_map/ppermute | solution.py:14
  74.3 12.9 %collective-permute-start.5 = (bf16[258,512]{1,0:T(8,128)(2,1)S(1)}, bf16[258,512]{1,0:T(8,128)(2,1)S(1)}, u32[]{:S(2)}, u32[]{:S(2)}) collective-permute-start(bf16[258,512]{1,0:T(8,128)(2,1)S(1)} %pad_maximum_fusion.2), channel_id=1, source_target_pairs={{0,8},{4,12},{8,16},{12,20},{16,24},{20,28},{24,32},{28,36},{32,40... | collective-permute-start | bytes 792584 | tf_op jit(solution)/shard_map/ppermute | solution.py:14
  92.1 13.5 %collective-permute-start.6 = (bf16[258,512]{1,0:T(8,128)(2,1)}, bf16[258,512]{1,0:T(8,128)(2,1)S(1)}, u32[]{:S(2)}, u32[]{:S(2)}) collective-permute-start(bf16[258,512]{1,0:T(8,128)(2,1)} %pad_maximum_fusion.3), channel_id=1, source_target_pairs={{0,8},{4,12},{8,16},{12,20},{16,24},{20,28},{24,32},{28,36},{32,40... | collective-permute-start | bytes 792584 | tf_op jit(solution)/shard_map/ppermute | solution.py:14
  98.3 9.2 %copy-start.6 = (f32[258,512]{1,0:T(8,128)S(1)}, f32[258,512]{1,0:T(8,128)}, u32[]{:S(2)}) copy-start(f32[258,512]{1,0:T(8,128)} %copy-done.5) | copy-start | bytes 1585156
  98.3 9.2 %copy-start.8 = (f32[258,512]{1,0:T(8,128)S(1)}, f32[258,512]{1,0:T(8,128)}, u32[]{:S(2)}) copy-start(f32[258,512]{1,0:T(8,128)} %copy-done.7) | copy-start | bytes 1585156
  107.5 3.2 %copy-start.3 = (bf16[1024,1536]{1,0:T(8,128)(2,1)S(1)}, bf16[1024,1536]{1,0:T(8,128)(2,1)}, u32[]{:S(2)}) copy-start(bf16[1024,1536]{1,0:T(8,128)(2,1)} %constant_dynamic-update-slice_fusion) | copy-start | bytes 9437188
  107.5 3.8 %copy-start.14 = (f32[1024,512]{0,1:T(8,128)S(1)}, f32[1024,512]{0,1:T(8,128)}, u32[]{:S(2)}) copy-start(f32[1024,512]{0,1:T(8,128)} %fusion.78) | copy-start | bytes 6291460
  107.5 3.9 %copy-start.17 = (bf16[512,512]{1,0:T(8,128)(2,1)S(1)}, bf16[512,512]{1,0:T(8,128)(2,1)}, u32[]{:S(2)}) copy-start(bf16[512,512]{1,0:T(8,128)(2,1)} %get-tuple-element.84) | copy-start | bytes 1572868
  107.5 4.0 %copy-start.18 = (bf16[512,512]{1,0:T(8,128)(2,1)S(1)}, bf16[512,512]{1,0:T(8,128)(2,1)}, u32[]{:S(2)}) copy-start(bf16[512,512]{1,0:T(8,128)(2,1)} %get-tuple-element.85) | copy-start | bytes 1572868
  107.5 4.1 %copy-start.19 = (bf16[512,512]{1,0:T(8,128)(2,1)S(1)}, bf16[512,512]{1,0:T(8,128)(2,1)}, u32[]{:S(2)}) copy-start(bf16[512,512]{1,0:T(8,128)(2,1)} %get-tuple-element.86) | copy-start | bytes 1572868
  107.5 4.1 %copy-start.33 = (f32[512]{0:T(512)S(1)}, f32[512]{0:T(512)}, u32[]{:S(2)}) copy-start(f32[512]{0:T(512)} %param.32) | copy-start | bytes 6148
  115.1 15.3 %collective-permute-start.9 = (bf16[512,512]{1,0:T(8,128)(2,1)S(1)}, bf16[512,512]{1,0:T(8,128)(2,1)S(1)}, u32[]{:S(2)}, u32[]{:S(2)}) collective-permute-start(bf16[512,512]{1,0:T(8,128)(2,1)S(1)} %get-tuple-element.97), channel_id=1, source_target_pairs={{0,3},{1,0},{2,1},{3,2},{4,7},{5,4},{6,5},{7,6},{8,11},{9,8},{10,9... | collective-permute-start | bytes 1572872 | tf_op jit(solution)/shard_map/ppermute | solution.py:19
  118.9 15.4 %collective-permute-start.7 = (bf16[512,512]{1,0:T(8,128)(2,1)S(1)}, bf16[512,512]{1,0:T(8,128)(2,1)S(1)}, u32[]{:S(2)}, u32[]{:S(2)}) collective-permute-start(bf16[512,512]{1,0:T(8,128)(2,1)S(1)} %get-tuple-element.96), channel_id=1, source_target_pairs={{0,1},{1,2},{2,3},{3,0},{4,5},{5,6},{6,7},{7,4},{8,9},{9,10},{10,1... | collective-permute-start | bytes 1572872 | tf_op jit(solution)/shard_map/ppermute | solution.py:19
  130.5 25.6 %collective-permute-start.10 = (bf16[1024,512]{1,0:T(8,128)(2,1)S(1)}, bf16[1024,512]{1,0:T(8,128)(2,1)S(1)}, u32[]{:S(2)}, u32[]{:S(2)}) collective-permute-start(bf16[1024,512]{1,0:T(8,128)(2,1)S(1)} %pad_maximum_fusion.1), channel_id=1, source_target_pairs={{0,3},{1,0},{2,1},{3,2},{4,7},{5,4},{6,5},{7,6},{8,11},{9,8},{10,9... | collective-permute-start | bytes 3145736 | tf_op jit(solution)/shard_map/ppermute | solution.py:19
  134.5 25.3 %collective-permute-start.8 = (bf16[1024,512]{1,0:T(8,128)(2,1)S(1)}, bf16[1024,512]{1,0:T(8,128)(2,1)S(1)}, u32[]{:S(2)}, u32[]{:S(2)}) collective-permute-start(bf16[1024,512]{1,0:T(8,128)(2,1)S(1)} %pad_maximum_fusion), channel_id=1, source_target_pairs={{0,1},{1,2},{2,3},{3,0},{4,5},{5,6},{6,7},{7,4},{8,9},{9,10},{10,1... | collective-permute-start | bytes 3145736 | tf_op jit(solution)/shard_map/ppermute | solution.py:19
  (14 other events, 16.8 us)

commit v18 on v14

--- a/solution.py
+++ b/solution.py
@@ -149,8 +149,9 @@
         )
         entering = chunk_decay[n][:, None] * entering + chunk_states[n]
     final_state = entering
-    inter = jnp.stack(inters) * live_blocks[:, :, None]
-    local_out = (intra + inter).reshape(tok_rows, value_width)
+    local_out = jnp.concatenate(
+        [intra[n] + inters[n] * live_blocks[n][:, None] for n in range(blocks)], axis=0
+    )
 
     devices = lax.axis_size("req")
     window = min(devices - 1, -(-SEG_MOST // tok_rows))

time: 159 us -> 159 us (level)
  waiting for transfers between devices: 59 us -> 62.5 us
  local copies, waits for them, and re-layouts: 18.6 us -> 16.3 us
    ppermute x3, waiting for transfers between devices: 4.62 us -> 11.6 us  [shifted(): return lax.ppermute(x, axis, pairs)]
    ppermute x10, waiting for transfers between devices: 54.3 us -> 50.9 us  [ring(): lax.ppermute(x, 'tensor', [(i, (i + step) % size) for i in range(size)])]
    reshape x1 -> x0, local copies, waits for them, and re-layouts: 2.98 us -> none  [body(): local_out = (intra + inter).reshape(tok_rows, value_width)]
    convert_element_type x1 -> x0, other arithmetic: 2.76 us -> none  [body(): q_scaled.astype(jnp.bfloat16)]
    another operation x5 -> x6, other arithmetic: 1.31 us -> 3.91 us
    dot_general x16, matrix products: 3.32 us -> 5.11 us  [body(): jnp.dot(q_decayed[n].astype(jnp.bfloat16), entering.astype(jnp.bfloat16),...]
    unnamed x63 -> x73, local copies, waits for them, and re-layouts: 4.14 us -> 3.78 us
  transfers between devices with their start and end apart: 13 -> 13, of which waited for: 9 -> 9; matrix products, arithmetic and copies ran while one was open for 15% -> 14% of each run, Pallas kernels for 0% -> 0%
where the time goes in v18:
time: 159 us
  waiting for transfers between devices  62.5 us (39%)
  matrix products  39.2 us (25%)
  starting transfers between devices  24.4 us (15%)
  local copies, waits for them, and re-layouts  16.3 us (10%)
  other arithmetic  10.4 us (7%)
  between operations  5.94 us (4%)
    ppermute x10, waiting for transfers between devices, ring(): lax.ppermute(x, 'tensor', [(i, (i + step) % size) for i in range(size)])  50.9 us
    ppermute x10, starting transfers between devices, ring(): lax.ppermute(x, 'tensor', [(i, (i + step) % size) for i in range(size)])  16.7 us
    dot_general x5, matrix products, projected(): out = jnp.dot(near, near_rows, preferred_element_type=jnp.float32)  13.7 us
    ppermute x3, waiting for transfers between devices, shifted(): return lax.ppermute(x, axis, pairs)  11.6 us
    ppermute x3, starting transfers between devices, shifted(): return lax.ppermute(x, axis, pairs)  7.78 us
    dot_general x1, matrix products, body(): jnp.einsum('ncd,ncv->ndv', k_decayed, v_float, precision=HIGH)  5.77 us
    dot_general x16, matrix products, body(): jnp.dot(q_decayed[n].astype(jnp.bfloat16), entering.astype(jnp.bfloat16),...  5.11 us
    dot_general x5, matrix products, projected(): jnp.dot(far, rows(2), preferred_element_type=jnp.float32)  5.1 us
  transfers between devices with their start and end apart: 13, of which 9 were waited for; matrix products, arithmetic and copies ran while one was open for 14% of the time, Pallas kernels for 0%

profile of v18, /device:TPU:2, one launch (start us, length us, event | category | flops | bytes accessed | tf_op | source)
XLA Modules:
  0.0 158.8 jit_solution(9989925011886854756)
XLA Ops:
  1.4 1.6 %collective-permute-start = (bf16[512,512]{1,0:T(8,128)(2,1)S(1)}, bf16[512,512]{1,0:T(8,128)(2,1)}, u32[]{:S(2)}, u32[]{:S(2)}) collective-permute-start(bf16[512,512]{1,0:T(8,128)(2,1)S(1)} %get-tuple-element.117), channel_id=1, source_target_pairs={{0,1},{1,2},{2,3},{3,0},{4,5},{5,6},{6,7},{7,4},{8,9},{9,10},{10,1... | collective-permute-start | bytes 1572872 | tf_op jit(solution)/shard_map/ppermute | solution.py:19
  3.1 1.7 %collective-permute-start.1 = (bf16[512,512]{1,0:T(8,128)(2,1)S(1)}, bf16[512,512]{1,0:T(8,128)(2,1)}, u32[]{:S(2)}, u32[]{:S(2)}) collective-permute-start(bf16[512,512]{1,0:T(8,128)(2,1)S(1)} %get-tuple-element.116), channel_id=1, source_target_pairs={{0,3},{1,0},{2,1},{3,2},{4,7},{5,4},{6,5},{7,6},{8,11},{9,8},{10,9... | collective-permute-start | bytes 1572872 | tf_op jit(solution)/shard_map/ppermute | solution.py:19
  9.5 1.6 %constant_dynamic-slice_fusion.5 = (bf16[512,512]{1,0:T(8,128)(2,1)S(1)}, bf16[512,512]{1,0:T(8,128)(2,1)S(1)}, bf16[512,512]{1,0:T(8,128)(2,1)S(1)}) fusion(bf16[2048,512]{1,0:T(8,128)(2,1)} %param.27, s32[]{:T(128)S(6)} %select_n.105, s32[]{:T(128)S(6)} %select_n.107, s32[]{:T(128)S(6)} %select_n.109), kind=kLoop, calls=%fused_computation.287 | loop fusion | bytes 3145740 | tf_op jit(solution)/shard_map/dynamic_slice | solution.py:43
  13.3 3.3 %collective-permute-done = bf16[512,512]{1,0:T(8,128)(2,1)} collective-permute-done((bf16[512,512]{1,0:T(8,128)(2,1)S(1)}, bf16[512,512]{1,0:T(8,128)(2,1)}, u32[]{:S(2)}, u32[]{:S(2)}) %collective-permute-start) | collective-permute-done | bytes 524320 | tf_op jit(solution)/shard_map/ppermute | solution.py:19
  18.2 1.7 %collective-permute-start.5 = (bf16[512,512]{1,0:T(8,128)(2,1)}, bf16[512,512]{1,0:T(8,128)(2,1)S(1)}, u32[]{:S(2)}, u32[]{:S(2)}) collective-permute-start(bf16[512,512]{1,0:T(8,128)(2,1)} %collective-permute-done.1), channel_id=1, source_target_pairs={{0,3},{1,0},{2,1},{3,2},{4,7},{5,4},{6,5},{7,6},{8,11},{9,8},{10,9... | collective-permute-start | bytes 1572872 | tf_op jit(solution)/shard_map/ppermute | solution.py:19
  20.6 2.9 %collective-permute-start.2 = (bf16[512,512]{1,0:T(8,128)(2,1)S(1)}, bf16[512,512]{1,0:T(8,128)(2,1)S(1)}, u32[]{:S(2)}, u32[]{:S(2)}) collective-permute-start(bf16[512,512]{1,0:T(8,128)(2,1)S(1)} %get-tuple-element.114), channel_id=1, source_target_pairs={{0,3},{1,0},{2,1},{3,2},{4,7},{5,4},{6,5},{7,6},{8,11},{9,8},{10,9... | collective-permute-start | bytes 1572872 | tf_op jit(solution)/shard_map/ppermute | solution.py:19
  23.5 9.3 %collective-permute-done.4 = bf16[512,512]{1,0:T(8,128)(2,1)S(1)} collective-permute-done((bf16[512,512]{1,0:T(8,128)(2,1)}, bf16[512,512]{1,0:T(8,128)(2,1)S(1)}, u32[]{:S(2)}, u32[]{:S(2)}) %collective-permute-start.4) | collective-permute-done | bytes 524320 | tf_op jit(solution)/shard_map/ppermute | solution.py:19
  33.3 2.1 %fusion.94 = f32[1024,512]{1,0:T(8,128)} fusion(bf16[1024,512]{1,0:T(8,128)(2,1)S(1)} %constant_dynamic-update-slice_fusion, bf16[2048,512]{1,0:T(8,128)(2,1)S(1)} %copy-done.12, s32[]{:T(128)S(6)} %select_n.111), kind=kOutput, calls=%fused_computation.149 | convolution fusion | flops 536870912 | bytes 3670020 | tf_op jit(solution)/shard_map/dot_general | solution.py:47
  36.6 1.8 %fusion.96 = f32[1024,512]{1,0:T(8,128)S(1)} fusion(bf16[1024,512]{1,0:T(8,128)(2,1)S(1)} %constant_dynamic-update-slice_fusion, bf16[2048,512]{1,0:T(8,128)(2,1)} %param.27, s32[]{:T(128)S(6)} %select_n.111), kind=kOutput, calls=%fused_computation.166 | convolution fusion | flops 536870912 | bytes 3670020 | tf_op jit(solution)/shard_map/dot_general | solution.py:47
  38.4 3.7 %collective-permute-done.3 = bf16[512,512]{1,0:T(8,128)(2,1)S(1)} collective-permute-done((bf16[512,512]{1,0:T(8,128)(2,1)S(1)}, bf16[512,512]{1,0:T(8,128)(2,1)S(1)}, u32[]{:S(2)}, u32[]{:S(2)}) %collective-permute-start.3) | collective-permute-done | bytes 524320 | tf_op jit(solution)/shard_map/ppermute | solution.py:19
  42.1 2.5 %convolution_add_fusion.3 = f32[1024,16]{0,1:T(8,128)S(1)} fusion(f32[1024,16]{0,1:T(8,128)S(1)} %fusion.176, bf16[512,16]{0,1:T(8,128)(2,1)S(1)} %get-tuple-element.142, bf16[512,16]{0,1:T(8,128)(2,1)S(1)} %get-tuple-element.141, bf16[512,16]{0,1:T(8,128)(2,1)S(1)} %get-tuple-element.140, bf16[512,512]{1,0:T(8,128)(2,1)S(1)} %collective-permute-done.3, ...), kind=kOutput, calls=%fused_computation.79 | convolution fusion | flops 66224128 | bytes 3325952 | tf_op jit(solution)/shard_map/dot_general | solution.py:46
  46.5 2.2 %fusion.17 = bf16[1024,256]{1,0:T(8,128)(2,1)S(1)} fusion(f32[1024,256]{1,0:T(8,128)S(1)} %fusion.133, bf16[512,256]{1,0:T(8,128)(2,1)S(1)} %get-tuple-element.113, bf16[512,256]{1,0:T(8,128)(2,1)S(1)} %get-tuple-element.112, bf16[512,256]{1,0:T(8,128)(2,1)S(1)} %get-tuple-element.111, bf16[512,512]{1,0:T(8,128)(2,1)S(1)} %collective-permute-done.3, ...), kind=kOutput, calls=%fused_computation.29 | convolution fusion | flops 823918592 | bytes 5505024 | tf_op jit(solution)/shard_map/dot_general | solution.py:46
  48.9 2.2 %fusion.16 = f32[1024,256]{1,0:T(8,128)S(1)} fusion(f32[1024,256]{1,0:T(8,128)S(1)} %fusion.135, bf16[512,256]{1,0:T(8,128)(2,1)S(1)} %get-tuple-element.181, bf16[512,256]{1,0:T(8,128)(2,1)S(1)} %get-tuple-element.182, bf16[512,256]{1,0:T(8,128)(2,1)S(1)} %get-tuple-element.183, bf16[512,512]{1,0:T(8,128)(2,1)S(1)} %collective-permute-done.3, ...), kind=kOutput, calls=%fused_computation.28 | convolution fusion | flops 824180736 | bytes 6029312 | tf_op jit(solution)/shard_map/dot_general | solution.py:46
  51.1 2.6 %multiply_convert_fusion.2 = (bf16[16,64,256]{2,0,1:T(8,128)(2,1)S(1)}, bf16[16,64,256]{2,0,1:T(8,128)(2,1)}, bf16[16,64,256]{2,0,1:T(8,128)(2,1)}, f32[16,64,256]{2,0,1:T(8,128)S(1)}, f32[16,64,256]{2,0,1:T(8,128)S(1)}) fusion(f32[16,64,256]{2,0,1:T(8,128)S(1)} %fusion.56, f32[16,64,256]{2,1,0:T(8,128)S(1)} %bitcast.347, ...), kind=kLoop, calls=%fused_computation.92 | loop fusion | flops 3145728 | bytes 6868992 | tf_op jit(solution)/shard_map/convert.27
  54.4 3.3 %add_convert_fusion.1 = bf16[1024,512]{1,0:T(8,128)(2,1)S(1)} fusion(f32[1024,512]{1,0:T(8,128)S(1)} %fusion.96, bf16[512,512]{1,0:T(8,128)(2,1)S(1)} %get-tuple-element.99, bf16[512,512]{1,0:T(8,128)(2,1)S(1)} %get-tuple-element.98, bf16[512,512]{1,0:T(8,128)(2,1)S(1)} %get-tuple-element.97, bf16[512,512]{1,0:T(8,128)(2,1)S(1)} %collective-permute-done.3, ...), kind=kOutput, calls=%fused_computation.6 | convolution fusion | flops 1632108544 | bytes 7864320 | tf_op jit(solution)/shard_map/dot_general | solution.py:46
  57.7 5.8 %fusion.54 = f32[16,256,512]{2,1,0:T(8,128)} fusion(bf16[16,64,512]{2,1,0:T(8,128)(2,1)S(1)} %bitcast.345, f32[16,64,256]{2,0,1:T(8,128)S(1)} %get-tuple-element.101), kind=kOutput, calls=%fused_computation.84 | convolution fusion | flops 805306368 | bytes 10485760 | tf_op jit(solution)/shard_map/ncd,ncv->ndv/dot_general | solution.py:136
  63.9 3.7 %multiply_add_fusion.1 = (f32[1,256,512]{2,1,0:T(8,128)S(1)}, f32[1,256,512]{2,1,0:T(8,128)S(1)}, f32[1,256,512]{2,1,0:T(8,128)S(1)}, f32[1,256,512]{2,1,0:T(8,1...) fusion(f32[16,256,512]{2,1,0:T(8,128)} %fusion.54, ...), kind=kLoop, calls=%fused_computation.153 | loop fusion | flops 3538944 | bytes 11024384 | tf_op jit(solution)/shard_map/add | solution.py:150
  67.6 1.8 %copy-done.1 = f32[16,256,512]{2,1,0:T(8,128)S(1)} copy-done((f32[16,256,512]{2,1,0:T(8,128)S(1)}, f32[16,256,512]{2,1,0:T(8,128)}, u32[]{:S(2)}) %copy-start.1) | copy-done | bytes 8388632
  70.4 2.1 %collective-permute-start.6 = (bf16[258,512]{1,0:T(8,128)(2,1)S(1)}, bf16[258,512]{1,0:T(8,128)(2,1)S(1)}, u32[]{:S(2)}, u32[]{:S(2)}) collective-permute-start(bf16[258,512]{1,0:T(8,128)(2,1)S(1)} %pad_maximum_fusion.2), channel_id=1, source_target_pairs={{0,4},{4,8},{8,12},{12,16},{16,20},{20,24},{24,28},{28,32},{32,36}... | collective-permute-start | bytes 792584 | tf_op jit(solution)/shard_map/ppermute | solution.py:14
  72.4 3.8 %collective-permute-start.7 = (bf16[258,512]{1,0:T(8,128)(2,1)S(1)}, bf16[258,512]{1,0:T(8,128)(2,1)S(1)}, u32[]{:S(2)}, u32[]{:S(2)}) collective-permute-start(bf16[258,512]{1,0:T(8,128)(2,1)S(1)} %pad_maximum_fusion.2), channel_id=1, source_target_pairs={{0,8},{4,12},{8,16},{12,20},{16,24},{20,28},{24,32},{28,36},{32,40... | collective-permute-start | bytes 792584 | tf_op jit(solution)/shard_map/ppermute | solution.py:14
  82.4 3.1 %collective-permute-done.7 = bf16[258,512]{1,0:T(8,128)(2,1)S(1)} collective-permute-done((bf16[258,512]{1,0:T(8,128)(2,1)S(1)}, bf16[258,512]{1,0:T(8,128)(2,1)S(1)}, u32[]{:S(2)}, u32[]{:S(2)}) %collective-permute-start.7) | collective-permute-done | bytes 264224 | tf_op jit(solution)/shard_map/ppermute | solution.py:14
  90.7 1.9 %collective-permute-start.8 = (bf16[258,512]{1,0:T(8,128)(2,1)}, bf16[258,512]{1,0:T(8,128)(2,1)S(1)}, u32[]{:S(2)}, u32[]{:S(2)}) collective-permute-start(bf16[258,512]{1,0:T(8,128)(2,1)} %pad_maximum_fusion.3), channel_id=1, source_target_pairs={{0,8},{4,12},{8,16},{12,20},{16,24},{20,28},{24,32},{28,36},{32,40... | collective-permute-start | bytes 792584 | tf_op jit(solution)/shard_map/ppermute | solution.py:14
  92.6 2.0 %fusion.19 = f32[1024,512]{1,0:T(8,128)} fusion(f32[1024,512]{1,0:T(8,128)} %copy-done.11, f32[16,256,512]{2,1,0:T(8,128)} %fusion.54, f32[1,256,512]{2,1,0:T(8,128)S(1)} %get-tuple-element.83, f32[256]{0:T(256)S(1)} %bitcast.386, f32[16,64,512]{2,1,0:T(8,128)} %copy-done.2, f32[64]{0:T(128)S(1)} %get-tuple-element.159, ...), kind=kOutput, calls=%fused_computation.33 | convolution fusion | flops 17235968 | bytes 1344768 | tf_op jit(solution)/shard_map/dot_general | solution.py:144
  95.3 8.5 %collective-permute-done.8 = bf16[258,512]{1,0:T(8,128)(2,1)S(1)} collective-permute-done((bf16[258,512]{1,0:T(8,128)(2,1)}, bf16[258,512]{1,0:T(8,128)(2,1)S(1)}, u32[]{:S(2)}, u32[]{:S(2)}) %collective-permute-start.8) | collective-permute-done | bytes 264224 | tf_op jit(solution)/shard_map/ppermute | solution.py:14
  105.9 3.3 %multiply_reduce_fusion = (f32[1024]{0:T(1024)S(1)}, f32[1024,512]{1,0:T(8,128)S(1)}) fusion(f32[1024,512]{1,0:T(8,128)} %fusion.19, f32[1024]{0:T(1024)S(1)} %select_bitcast_fusion, f32[258,512]{1,0:T(8,128)S(1)} %convert_element_type.342, f32[256]{0:T(256)S(1)} %bitcast.390, f32[258,512]{1,0:T(8,128)} %copy-done.4, f32[256]{0:T(256)S(1)} %bitcast.388, ...), kind=kOutput, calls=%fused_computation.4 | convolution fusion | flops 272235520 | bytes 7874560 | tf_op jit(solution)/shard_map/dot_general | solution.py:186
  109.8 3.4 %multiply_convert_fusion = bf16[1024,512]{1,0:T(8,128)(2,1)S(1)} fusion(f32[1024,512]{1,0:T(8,128)S(1)} %copy-done.3, f32[1024,512]{1,0:T(8,128)S(1)} %get-tuple-element.180, bf16[512,512]{1,0:T(8,128)(2,1)S(1)} %copy-done.17, bf16[512,512]{1,0:T(8,128)(2,1)S(1)} %copy-done.16, bf16[512,512]{1,0:T(8,128)(2,1)S(1)} %copy-done.15, f32[512]{0:T(512)S(1)} %copy-done.34, ...), kind=kOutput, calls=%fused_computation.3 | convolution fusion | flops 1635778560 | bytes 9967616 | tf_op jit(solution)/shard_map/dot_general | solution.py:46
  114.1 2.9 %collective-permute-start.11 = (bf16[512,512]{1,0:T(8,128)(2,1)S(1)}, bf16[512,512]{1,0:T(8,128)(2,1)S(1)}, u32[]{:S(2)}, u32[]{:S(2)}) collective-permute-start(bf16[512,512]{1,0:T(8,128)(2,1)S(1)} %get-tuple-element.103), channel_id=1, source_target_pairs={{0,3},{1,0},{2,1},{3,2},{4,7},{5,4},{6,5},{7,6},{8,11},{9,8},{10,9... | collective-permute-start | bytes 1572872 | tf_op jit(solution)/shard_map/ppermute | solution.py:19
  118.5 9.4 %collective-permute-done.11 = bf16[512,512]{1,0:T(8,128)(2,1)S(1)} collective-permute-done((bf16[512,512]{1,0:T(8,128)(2,1)S(1)}, bf16[512,512]{1,0:T(8,128)(2,1)S(1)}, u32[]{:S(2)}, u32[]{:S(2)}) %collective-permute-start.11) | collective-permute-done | bytes 524320 | tf_op jit(solution)/shard_map/ppermute | solution.py:19
  128.2 3.8 %collective-permute-start.12 = (bf16[1024,512]{1,0:T(8,128)(2,1)S(1)}, bf16[1024,512]{1,0:T(8,128)(2,1)S(1)}, u32[]{:S(2)}, u32[]{:S(2)}) collective-permute-start(bf16[1024,512]{1,0:T(8,128)(2,1)S(1)} %pad_maximum_fusion.1), channel_id=1, source_target_pairs={{0,3},{1,0},{2,1},{3,2},{4,7},{5,4},{6,5},{7,6},{8,11},{9,8},{10,9... | collective-permute-start | bytes 3145736 | tf_op jit(solution)/shard_map/ppermute | solution.py:19
  132.2 21.0 %collective-permute-done.12 = bf16[1024,512]{1,0:T(8,128)(2,1)S(1)} collective-permute-done((bf16[1024,512]{1,0:T(8,128)(2,1)S(1)}, bf16[1024,512]{1,0:T(8,128)(2,1)S(1)}, u32[]{:S(2)}, u32[]{:S(2)}) %collective-permute-start.12) | collective-permute-done | bytes 1048608 | tf_op jit(solution)/shard_map/ppermute | solution.py:19
  153.3 3.7 %collective-permute-done.10 = bf16[1024,512]{1,0:T(8,128)(2,1)S(1)} collective-permute-done((bf16[1024,512]{1,0:T(8,128)(2,1)S(1)}, bf16[1024,512]{1,0:T(8,128)(2,1)S(1)}, u32[]{:S(2)}, u32[]{:S(2)}) %collective-permute-start.10) | collective-permute-done | bytes 1048608 | tf_op jit(solution)/shard_map/ppermute | solution.py:19
  157.0 1.8 %add_convert_fusion = bf16[1024,512]{1,0:T(8,128)(2,1)} fusion(bf16[1024,512]{1,0:T(8,128)(2,1)S(1)} %collective-permute-done.12, bf16[1024,512]{1,0:T(8,128)(2,1)S(1)} %collective-permute-done.10, bf16[1024,512]{1,0:T(8,128)(2,1)S(1)} %multiply_convert_fusion, bf16[512,2048]{1,0:T(8,128)(2,1)S(1)} %copy-done, s32[]{:T(128)S(6)} %select_n.105), kind=kOutput, calls=%fused_computation.2 | convolution fusion | flops 540540928 | bytes 4718596 | tf_op jit(solution)/shard_map/dot_general | solution.py:60
  (167 shorter events, 28.3 us)
Async XLA Ops:
  0.0 113.2 %copy-start = (bf16[512,2048]{1,0:T(8,128)(2,1)S(1)}, bf16[512,2048]{1,0:T(8,128)(2,1)}, u32[]{:S(2)}) copy-start(bf16[512,2048]{1,0:T(8,128)(2,1)} %param.33) | copy-start | bytes 6291460
  0.0 4.7 %copy-start.21 = (s32[1024]{0:T(1024)S(1)}, s32[1024]{0:T(1024)}, u32[]{:S(2)}) copy-start(s32[1024]{0:T(1024)} %param.24) | copy-start | bytes 12292
  0.0 9.4 %copy-start.20 = (bf16[2048,16]{0,1:T(8,128)(2,1)S(1)}, bf16[2048,16]{0,1:T(8,128)(2,1)}, u32[]{:S(2)}) copy-start(bf16[2048,16]{0,1:T(8,128)(2,1)} %param.29) | copy-start | bytes 196612
  1.4 15.1 %collective-permute-start = (bf16[512,512]{1,0:T(8,128)(2,1)S(1)}, bf16[512,512]{1,0:T(8,128)(2,1)}, u32[]{:S(2)}, u32[]{:S(2)}) collective-permute-start(bf16[512,512]{1,0:T(8,128)(2,1)S(1)} %get-tuple-element.117), channel_id=1, source_target_pairs={{0,1},{1,2},{2,3},{3,0},{4,5},{5,6},{6,7},{7,4},{8,9},{9,10},{10,1... | collective-permute-start | bytes 1572872 | tf_op jit(solution)/shard_map/ppermute | solution.py:19
  3.1 13.5 %collective-permute-start.1 = (bf16[512,512]{1,0:T(8,128)(2,1)S(1)}, bf16[512,512]{1,0:T(8,128)(2,1)}, u32[]{:S(2)}, u32[]{:S(2)}) collective-permute-start(bf16[512,512]{1,0:T(8,128)(2,1)S(1)} %get-tuple-element.116), channel_id=1, source_target_pairs={{0,3},{1,0},{2,1},{3,2},{4,7},{5,4},{6,5},{7,6},{8,11},{9,8},{10,9... | collective-permute-start | bytes 1572872 | tf_op jit(solution)/shard_map/ppermute | solution.py:19
  11.5 8.4 %copy-start.13 = (bf16[2048,256]{1,0:T(8,128)(2,1)S(1)}, bf16[2048,256]{1,0:T(8,128)(2,1)}, u32[]{:S(2)}) copy-start(bf16[2048,256]{1,0:T(8,128)(2,1)} %param.25) | copy-start | bytes 3145732
  11.5 8.4 %copy-start.14 = (bf16[2048,256]{1,0:T(8,128)(2,1)S(1)}, bf16[2048,256]{1,0:T(8,128)(2,1)}, u32[]{:S(2)}) copy-start(bf16[2048,256]{1,0:T(8,128)(2,1)} %param.26) | copy-start | bytes 3145732
  12.7 7.4 %copy-start.8 = (bf16[1024,512]{1,0:T(8,128)(2,1)S(1)}, bf16[1024,512]{1,0:T(8,128)(2,1)}, u32[]{:S(2)}) copy-start(bf16[1024,512]{1,0:T(8,128)(2,1)} %param.23) | copy-start | bytes 3145732
  16.6 16.2 %collective-permute-start.4 = (bf16[512,512]{1,0:T(8,128)(2,1)}, bf16[512,512]{1,0:T(8,128)(2,1)S(1)}, u32[]{:S(2)}, u32[]{:S(2)}) collective-permute-start(bf16[512,512]{1,0:T(8,128)(2,1)} %collective-permute-done), channel_id=1, source_target_pairs={{0,1},{1,2},{2,3},{3,0},{4,5},{5,6},{6,7},{7,4},{8,9},{9,10},{10,1... | collective-permute-start | bytes 1572872 | tf_op jit(solution)/shard_map/ppermute | solution.py:19
  18.2 15.1 %collective-permute-start.5 = (bf16[512,512]{1,0:T(8,128)(2,1)}, bf16[512,512]{1,0:T(8,128)(2,1)S(1)}, u32[]{:S(2)}, u32[]{:S(2)}) collective-permute-start(bf16[512,512]{1,0:T(8,128)(2,1)} %collective-permute-done.1), channel_id=1, source_target_pairs={{0,3},{1,0},{2,1},{3,2},{4,7},{5,4},{6,5},{7,6},{8,11},{9,8},{10,9... | collective-permute-start | bytes 1572872 | tf_op jit(solution)/shard_map/ppermute | solution.py:19
  20.1 21.9 %collective-permute-start.3 = (bf16[512,512]{1,0:T(8,128)(2,1)S(1)}, bf16[512,512]{1,0:T(8,128)(2,1)S(1)}, u32[]{:S(2)}, u32[]{:S(2)}) collective-permute-start(bf16[512,512]{1,0:T(8,128)(2,1)S(1)} %get-tuple-element.115), channel_id=1, source_target_pairs={{0,1},{1,2},{2,3},{3,0},{4,5},{5,6},{6,7},{7,4},{8,9},{9,10},{10,1... | collective-permute-start | bytes 1572872 | tf_op jit(solution)/shard_map/ppermute | solution.py:19
  20.6 21.5 %collective-permute-start.2 = (bf16[512,512]{1,0:T(8,128)(2,1)S(1)}, bf16[512,512]{1,0:T(8,128)(2,1)S(1)}, u32[]{:S(2)}, u32[]{:S(2)}) collective-permute-start(bf16[512,512]{1,0:T(8,128)(2,1)S(1)} %get-tuple-element.114), channel_id=1, source_target_pairs={{0,3},{1,0},{2,1},{3,2},{4,7},{5,4},{6,5},{7,6},{8,11},{9,8},{10,9... | collective-permute-start | bytes 1572872 | tf_op jit(solution)/shard_map/ppermute | solution.py:19
  42.1 12.3 %copy-start.29 = (bf16[512,512]{1,0:T(8,128)(2,1)}, bf16[512,512]{1,0:T(8,128)(2,1)S(1)}, u32[]{:S(2)}) copy-start(bf16[512,512]{1,0:T(8,128)(2,1)S(1)} %collective-permute-done.3) | copy-start | bytes 1572868
  42.1 12.3 %copy-start.31 = (bf16[512,512]{1,0:T(8,128)(2,1)}, bf16[512,512]{1,0:T(8,128)(2,1)S(1)}, u32[]{:S(2)}) copy-start(bf16[512,512]{1,0:T(8,128)(2,1)S(1)} %collective-permute-done.2) | copy-start | bytes 1572868
  54.3 9.2 %copy-start.5 = (f32[16,64,256]{2,1,0:T(8,128)}, f32[16,64,256]{2,1,0:T(8,128)S(1)}, u32[]{:S(2)}) copy-start(f32[16,64,256]{2,1,0:T(8,128)S(1)} %copy.46) | copy-start | bytes 3145732
  57.7 5.8 %copy-start.6 = (bf16[1024,512]{1,0:T(8,128)(2,1)}, bf16[1024,512]{1,0:T(8,128)(2,1)S(1)}, u32[]{:S(2)}) copy-start(bf16[1024,512]{1,0:T(8,128)(2,1)S(1)} %add_convert_fusion.1) | copy-start | bytes 3145732
  63.9 5.6 %copy-start.1 = (f32[16,256,512]{2,1,0:T(8,128)S(1)}, f32[16,256,512]{2,1,0:T(8,128)}, u32[]{:S(2)}) copy-start(f32[16,256,512]{2,1,0:T(8,128)} %fusion.54) | copy-start | bytes 25165828
  69.5 6.8 %copy-start.18 = (bf16[16,64,256]{2,0,1:T(8,128)(2,1)S(1)}, bf16[16,64,256]{2,0,1:T(8,128)(2,1)}, u32[]{:S(2)}) copy-start(bf16[16,64,256]{2,0,1:T(8,128)(2,1)} %get-tuple-element.96) | copy-start | bytes 1572868
  69.5 6.8 %copy-start.19 = (bf16[16,64,256]{2,0,1:T(8,128)(2,1)S(1)}, bf16[16,64,256]{2,0,1:T(8,128)(2,1)}, u32[]{:S(2)}) copy-start(bf16[16,64,256]{2,0,1:T(8,128)(2,1)} %get-tuple-element.100) | copy-start | bytes 1572868
  70.3 6.4 %copy-start.7 = (bf16[1024,512]{1,0:T(8,128)(2,1)S(1)}, bf16[1024,512]{1,0:T(8,128)(2,1)}, u32[]{:S(2)}) copy-start(bf16[1024,512]{1,0:T(8,128)(2,1)} %copy-done.6) | copy-start | bytes 3145732
  70.4 11.3 %collective-permute-start.6 = (bf16[258,512]{1,0:T(8,128)(2,1)S(1)}, bf16[258,512]{1,0:T(8,128)(2,1)S(1)}, u32[]{:S(2)}, u32[]{:S(2)}) collective-permute-start(bf16[258,512]{1,0:T(8,128)(2,1)S(1)} %pad_maximum_fusion.2), channel_id=1, source_target_pairs={{0,4},{4,8},{8,12},{12,16},{16,20},{20,24},{24,28},{28,32},{32,36}... | collective-permute-start | bytes 792584 | tf_op jit(solution)/shard_map/ppermute | solution.py:14
  72.4 13.1 %collective-permute-start.7 = (bf16[258,512]{1,0:T(8,128)(2,1)S(1)}, bf16[258,512]{1,0:T(8,128)(2,1)S(1)}, u32[]{:S(2)}, u32[]{:S(2)}) collective-permute-start(bf16[258,512]{1,0:T(8,128)(2,1)S(1)} %pad_maximum_fusion.2), channel_id=1, source_target_pairs={{0,8},{4,12},{8,16},{12,20},{16,24},{20,28},{24,32},{28,36},{32,40... | collective-permute-start | bytes 792584 | tf_op jit(solution)/shard_map/ppermute | solution.py:14
  77.4 4.1 %copy-start.2 = (f32[16,64,512]{2,1,0:T(8,128)}, f32[16,64,512]{2,1,0:T(8,128)S(1)}, u32[]{:S(2)}) copy-start(f32[16,64,512]{2,1,0:T(8,128)S(1)} %fusion.206) | copy-start | bytes 6291460
  81.7 5.8 %copy-start.11 = (f32[1024,512]{1,0:T(8,128)}, f32[1024,512]{1,0:T(8,128)S(1)}, u32[]{:S(2)}) copy-start(f32[1024,512]{1,0:T(8,128)S(1)} %fusion.21) | copy-start | bytes 6291460
  90.7 13.1 %collective-permute-start.8 = (bf16[258,512]{1,0:T(8,128)(2,1)}, bf16[258,512]{1,0:T(8,128)(2,1)S(1)}, u32[]{:S(2)}, u32[]{:S(2)}) collective-permute-start(bf16[258,512]{1,0:T(8,128)(2,1)} %pad_maximum_fusion.3), channel_id=1, source_target_pairs={{0,8},{4,12},{8,16},{12,20},{16,24},{20,28},{24,32},{28,36},{32,40... | collective-permute-start | bytes 792584 | tf_op jit(solution)/shard_map/ppermute | solution.py:14
  105.8 3.8 %copy-start.30 = (bf16[512,512]{1,0:T(8,128)(2,1)S(1)}, bf16[512,512]{1,0:T(8,128)(2,1)}, u32[]{:S(2)}) copy-start(bf16[512,512]{1,0:T(8,128)(2,1)} %copy-done.29) | copy-start | bytes 1572868
  105.8 4.0 %copy-start.32 = (bf16[512,512]{1,0:T(8,128)(2,1)S(1)}, bf16[512,512]{1,0:T(8,128)(2,1)}, u32[]{:S(2)}) copy-start(bf16[512,512]{1,0:T(8,128)(2,1)} %copy-done.31) | copy-start | bytes 1572868
  105.9 4.0 %copy-start.34 = (f32[512]{0:T(512)S(1)}, f32[512]{0:T(512)}, u32[]{:S(2)}) copy-start(f32[512]{0:T(512)} %param.32) | copy-start | bytes 6148
  114.1 13.9 %collective-permute-start.11 = (bf16[512,512]{1,0:T(8,128)(2,1)S(1)}, bf16[512,512]{1,0:T(8,128)(2,1)S(1)}, u32[]{:S(2)}, u32[]{:S(2)}) collective-permute-start(bf16[512,512]{1,0:T(8,128)(2,1)S(1)} %get-tuple-element.103), channel_id=1, source_target_pairs={{0,3},{1,0},{2,1},{3,2},{4,7},{5,4},{6,5},{7,6},{8,11},{9,8},{10,9... | collective-permute-start | bytes 1572872 | tf_op jit(solution)/shard_map/ppermute | solution.py:19
  117.0 14.9 %collective-permute-start.9 = (bf16[512,512]{1,0:T(8,128)(2,1)S(1)}, bf16[512,512]{1,0:T(8,128)(2,1)S(1)}, u32[]{:S(2)}, u32[]{:S(2)}) collective-permute-start(bf16[512,512]{1,0:T(8,128)(2,1)S(1)} %get-tuple-element.102), channel_id=1, source_target_pairs={{0,1},{1,2},{2,3},{3,0},{4,5},{5,6},{6,7},{7,4},{8,9},{9,10},{10,1... | collective-permute-start | bytes 1572872 | tf_op jit(solution)/shard_map/ppermute | solution.py:19
  128.2 25.1 %collective-permute-start.12 = (bf16[1024,512]{1,0:T(8,128)(2,1)S(1)}, bf16[1024,512]{1,0:T(8,128)(2,1)S(1)}, u32[]{:S(2)}, u32[]{:S(2)}) collective-permute-start(bf16[1024,512]{1,0:T(8,128)(2,1)S(1)} %pad_maximum_fusion.1), channel_id=1, source_target_pairs={{0,3},{1,0},{2,1},{3,2},{4,7},{5,4},{6,5},{7,6},{8,11},{9,8},{10,9... | collective-permute-start | bytes 3145736 | tf_op jit(solution)/shard_map/ppermute | solution.py:19
  132.1 24.8 %collective-permute-start.10 = (bf16[1024,512]{1,0:T(8,128)(2,1)S(1)}, bf16[1024,512]{1,0:T(8,128)(2,1)S(1)}, u32[]{:S(2)}, u32[]{:S(2)}) collective-permute-start(bf16[1024,512]{1,0:T(8,128)(2,1)S(1)} %pad_maximum_fusion), channel_id=1, source_target_pairs={{0,1},{1,2},{2,3},{3,0},{4,5},{5,6},{6,7},{7,4},{8,9},{9,10},{10,1... | collective-permute-start | bytes 3145736 | tf_op jit(solution)/shard_map/ppermute | solution.py:19
  (17 other events, 35.0 us)
